TPU v7x, 512 devices: a whole 4x4x16 slice. The times are simulated.
512 devices in a mesh: cuts: 16 (over z_lo, core), stem: 32 (over z_hi, x, y).
Axes of the slice: x: 4, y: 4, z: 16 (z_hi: 2, z_lo: 8; z = z_hi * 8 + z_lo), core: 2. Of those that a mesh axis runs over, the one named last changes fastest.
Arguments:
- stem_tensor: bfloat16 [32, 16384, 2, 512], P('cuts', 'stem'), may hold values from -6 to 6
- branch_tensor: bfloat16 [32, 512, 2, 512], P('cuts', 'stem'), may hold values from -0.1875 to 0.1875
- open_tensor: bfloat16 [32, 16384, 2, 512], P('cuts', 'stem'), may hold values from -0.75 to 0.75
- open_order: int32 [32, 512], P('cuts'), may hold values from 0 to 511, each once within a row
Outputs:
- amplitudes: float32 [32, 512, 2, 512], P('stem', 'cuts')
Inputs may be any that keep to these rules, and one draw needn't show every extreme that they name: Each row of open_order holds every number of 0 to 511 once.
All inputs are finite; a program needn't handle non-finite values.
Results may differ from a plain program's by a relative error of at most 0.0003.
Values may be sent and summed in bfloat16 or wider, within the bound.
No kernel may reach another device: no remote copies, remote signals or barrier semaphores. Data moves between devices by JAX's collectives and lax.ppermute only.
A program may use at most 64 MiB of HBM per device.

v0:
```python
from functools import partial

import jax
import jax.numpy as jnp
from jax import lax
from jax.sharding import PartitionSpec as P


def from_behind(value, axis, steps):
    count = lax.axis_size(axis)
    pairs = [(source, (source + steps) % count) for source in range(count)]
    return lax.ppermute(value, axis, pairs)


def expand_branch(segment):
    top_rows = jnp.concatenate([segment[..., 0, :], segment[..., 1, :]], axis=-1)
    bottom_rows = jnp.concatenate([-segment[..., 1, :], segment[..., 0, :]], axis=-1)
    return jnp.concatenate([top_rows, bottom_rows], axis=-2)


def fold_rows(stem_block, running, segment, offset):
    stem_cols = stem_block
    stem_cols = stem_cols.reshape(stem_cols.shape[0], -1)
    product = jnp.dot(stem_cols, expand_branch(segment), preferred_element_type=jnp.float32)
    return product.reshape(running.shape)


def body(stem_tensor, branch_tensor, open_tensor, open_order):
    slice_count = stem_tensor.shape[0]
    row_count = stem_tensor.shape[1]
    width = stem_tensor.shape[3]
    image_list = []
    for slice_pos in range(slice_count):
        initial = jnp.zeros((row_count, 2, width), jnp.float32)
        folder = partial(fold_rows, stem_tensor[slice_pos])
        image_list.append(
            folder(
                initial,
                lax.all_gather(branch_tensor[slice_pos], "stem", axis=0, tiled=True),
                jnp.int32(0),
            )
        )
    local_sum = jnp.zeros((row_count, 2, width), jnp.float32)
    for slice_pos in range(slice_count):
        placed = jnp.take(image_list[slice_pos], open_order[slice_pos], axis=2)
        opened = open_tensor[slice_pos].astype(jnp.float32)
        real_part = placed[:, 0, :] * opened[:, 0, :] - placed[:, 1, :] * opened[:, 1, :]
        imag_part = placed[:, 0, :] * opened[:, 1, :] + placed[:, 1, :] * opened[:, 0, :]
        local_sum = local_sum + jnp.stack([real_part, imag_part], axis=1)
    cut_count = lax.axis_size("cuts")
    block_rows = row_count // cut_count
    cut_index = lax.axis_index("cuts")

    def pick_block(turn):
        start_row = (cut_index + cut_count - 1 - turn) % cut_count * block_rows
        return lax.dynamic_slice_in_dim(local_sum, start_row, block_rows, 0)

    def pass_along(turn, running):
        return from_behind(running, "cuts", 1) + pick_block(turn)

    running = lax.fori_loop(1, cut_count, pass_along, pick_block(0))
    return running.reshape(1, block_rows, 2, width)


def solution(mesh):
    return jax.shard_map(
        body,
        mesh=mesh,
        in_specs=(
            P("cuts", "stem", None, None),
            P("cuts", "stem", None, None),
            P("cuts", "stem", None, None),
            P("cuts", None),
        ),
        out_specs=P("stem", "cuts", None, None),
        check_vma=False,
    )
```

profile of v0, /device:TPU:1, one launch (start us, length us, event | category | flops | bytes accessed | tf_op | source)
XLA Modules:
  0.0 483.3 jit_solution(4633315407787686485)
XLA Ops:
  8.8 2.8 fusion.20
  11.7 2.3 fusion.21
  16.5 2.1 copy.18
  18.6 2.1 copy.16
  20.8 2.1 bitcast_convert_fusion
  22.9 2.0 bitcast_convert_fusion.1
  24.9 103.6 %all-gather.7.cloned.1.call-done = bf16[1,512,2,512]{3,1,2,0:T(8,128)(2,1)} async-done(((bf16[1,16,2,512]{3,1,2,0:T(8,128)(2,1)}), bf16[1,512,2,512]{3,1,2,0:T(8,128)(2,1)}) %all-gather.7.cloned.1.call-update) | async-done | bytes 1048592 | tf_op jit(solution)/shard_map/all_gather | solution.py:39
  130.9 104.0 %all-gather.5.cloned.1.call-done = bf16[1,512,2,512]{3,1,2,0:T(8,128)(2,1)} async-done(((bf16[1,16,2,512]{3,1,2,0:T(8,128)(2,1)}), bf16[1,512,2,512]{3,1,2,0:T(8,128)(2,1)}) %all-gather.5.cloned.1.call-update) | async-done | bytes 1048592 | tf_op jit(solution)/shard_map/all_gather | solution.py:39
  237.8 1.6 copy.11
  240.7 3.0 copy.8
  243.7 4.4 gather_fusion.1
  248.1 4.2 select_bitcast_fusion
  252.2 4.3 gather_fusion
  256.5 3.2 select_bitcast_fusion.1
  259.7 7.4 %multiply_subtract_fusion = (f32[512,1,512]{0,1,2:T(1,128)S(1)}, f32[512,1,512]{0,1,2:T(1,128)S(1)}, f32[512,1,512]{0,1,2:T(1,128)S(1)}, f32[512,1,512]{0,1,2:T(1,128)S(1)}) fusion(f32[512,2,512]{0,1,2:T(2,128)S(1)} %copy-done.1, f32[512,2,512]{0,1,2:T(2,128)} %select_bitcast_fusion, f32[512,2,512]{0,1,2:T(2,128)S(1)} %copy-done.2, ...), kind=kLoop, calls=%fused_computation.25 | loop fusion | flops 3145728 | bytes 12582912 | tf_op jit(solution)/shard_map/sub | solution.py:47
  267.1 3.5 maximum_add_fusion
  270.6 4.1 copy.14
  275.5 200.3 %while.15 = (s32[]{:T(128)}, f32[32,2,512]{2,1,0:T(2,128)S(1)}, s32[]{:T(128)}, f32[512,2,512]{2,1,0:T(2,128)}, s32[]{:T(128)}, /*index=5*/s32[]{:T(128)}, s32[]{:T(128)}, s32[]{:T(128)}, s32[]{:T(128)}, s32[]{:T(128)}) while((s32[]{:T(128)}, f32[32,2,512]{2,1,0:T(2,128)S(1)}, s32[]{:T(128)}, f32[512,2,512]{2,1,0:T(2,128)}, s32[]{:T(128)}, ...), condition=%wide.region_1.3_spmd, body=%wide.region_0.0_spmd.sunk | while | flops 32786 | bytes 917816 | solution.py:61
  275.5 1.9 collective-permute-start
  277.5 3.0 collective-permute-done
  281.5 3.2 collective-permute-start
  284.8 9.6 %collective-permute-done = f32[32,2,512]{2,1,0:T(2,128)S(1)} collective-permute-done((f32[32,2,512]{2,1,0:T(2,128)S(1)}, f32[32,2,512]{2,1,0:T(2,128)S(1)}, u32[]{:S(2)}, u32[]{:S(2)}) %collective-permute-start) | collective-permute-done | bytes 131104 | tf_op jit(solution)/shard_map/while/body/eval_jaxpr/ppermute | solution.py:12
  295.4 1.9 collective-permute-start
  297.3 10.9 %collective-permute-done = f32[32,2,512]{2,1,0:T(2,128)S(1)} collective-permute-done((f32[32,2,512]{2,1,0:T(2,128)S(1)}, f32[32,2,512]{2,1,0:T(2,128)S(1)}, u32[]{:S(2)}, u32[]{:S(2)}) %collective-permute-start) | collective-permute-done | bytes 131104 | tf_op jit(solution)/shard_map/while/body/eval_jaxpr/ppermute | solution.py:12
  309.3 1.9 collective-permute-start
  311.2 10.9 %collective-permute-done = f32[32,2,512]{2,1,0:T(2,128)S(1)} collective-permute-done((f32[32,2,512]{2,1,0:T(2,128)S(1)}, f32[32,2,512]{2,1,0:T(2,128)S(1)}, u32[]{:S(2)}, u32[]{:S(2)}) %collective-permute-start) | collective-permute-done | bytes 131104 | tf_op jit(solution)/shard_map/while/body/eval_jaxpr/ppermute | solution.py:12
  323.1 1.9 collective-permute-start
  325.1 10.9 %collective-permute-done = f32[32,2,512]{2,1,0:T(2,128)S(1)} collective-permute-done((f32[32,2,512]{2,1,0:T(2,128)S(1)}, f32[32,2,512]{2,1,0:T(2,128)S(1)}, u32[]{:S(2)}, u32[]{:S(2)}) %collective-permute-start) | collective-permute-done | bytes 131104 | tf_op jit(solution)/shard_map/while/body/eval_jaxpr/ppermute | solution.py:12
  337.0 1.9 collective-permute-start
  339.0 10.9 %collective-permute-done = f32[32,2,512]{2,1,0:T(2,128)S(1)} collective-permute-done((f32[32,2,512]{2,1,0:T(2,128)S(1)}, f32[32,2,512]{2,1,0:T(2,128)S(1)}, u32[]{:S(2)}, u32[]{:S(2)}) %collective-permute-start) | collective-permute-done | bytes 131104 | tf_op jit(solution)/shard_map/while/body/eval_jaxpr/ppermute | solution.py:12
  350.9 1.9 collective-permute-start
  352.8 10.9 %collective-permute-done = f32[32,2,512]{2,1,0:T(2,128)S(1)} collective-permute-done((f32[32,2,512]{2,1,0:T(2,128)S(1)}, f32[32,2,512]{2,1,0:T(2,128)S(1)}, u32[]{:S(2)}, u32[]{:S(2)}) %collective-permute-start) | collective-permute-done | bytes 131104 | tf_op jit(solution)/shard_map/while/body/eval_jaxpr/ppermute | solution.py:12
  364.8 1.9 collective-permute-start
  366.7 10.9 %collective-permute-done = f32[32,2,512]{2,1,0:T(2,128)S(1)} collective-permute-done((f32[32,2,512]{2,1,0:T(2,128)S(1)}, f32[32,2,512]{2,1,0:T(2,128)S(1)}, u32[]{:S(2)}, u32[]{:S(2)}) %collective-permute-start) | collective-permute-done | bytes 131104 | tf_op jit(solution)/shard_map/while/body/eval_jaxpr/ppermute | solution.py:12
  378.6 1.9 collective-permute-start
  380.6 10.9 %collective-permute-done = f32[32,2,512]{2,1,0:T(2,128)S(1)} collective-permute-done((f32[32,2,512]{2,1,0:T(2,128)S(1)}, f32[32,2,512]{2,1,0:T(2,128)S(1)}, u32[]{:S(2)}, u32[]{:S(2)}) %collective-permute-start) | collective-permute-done | bytes 131104 | tf_op jit(solution)/shard_map/while/body/eval_jaxpr/ppermute | solution.py:12
  392.5 1.9 collective-permute-start
  394.5 10.9 %collective-permute-done = f32[32,2,512]{2,1,0:T(2,128)S(1)} collective-permute-done((f32[32,2,512]{2,1,0:T(2,128)S(1)}, f32[32,2,512]{2,1,0:T(2,128)S(1)}, u32[]{:S(2)}, u32[]{:S(2)}) %collective-permute-start) | collective-permute-done | bytes 131104 | tf_op jit(solution)/shard_map/while/body/eval_jaxpr/ppermute | solution.py:12
  406.4 1.9 collective-permute-start
  408.4 10.9 %collective-permute-done = f32[32,2,512]{2,1,0:T(2,128)S(1)} collective-permute-done((f32[32,2,512]{2,1,0:T(2,128)S(1)}, f32[32,2,512]{2,1,0:T(2,128)S(1)}, u32[]{:S(2)}, u32[]{:S(2)}) %collective-permute-start) | collective-permute-done | bytes 131104 | tf_op jit(solution)/shard_map/while/body/eval_jaxpr/ppermute | solution.py:12
  420.3 1.9 collective-permute-start
  422.2 10.9 %collective-permute-done = f32[32,2,512]{2,1,0:T(2,128)S(1)} collective-permute-done((f32[32,2,512]{2,1,0:T(2,128)S(1)}, f32[32,2,512]{2,1,0:T(2,128)S(1)}, u32[]{:S(2)}, u32[]{:S(2)}) %collective-permute-start) | collective-permute-done | bytes 131104 | tf_op jit(solution)/shard_map/while/body/eval_jaxpr/ppermute | solution.py:12
  434.2 1.9 collective-permute-start
  436.1 10.9 %collective-permute-done = f32[32,2,512]{2,1,0:T(2,128)S(1)} collective-permute-done((f32[32,2,512]{2,1,0:T(2,128)S(1)}, f32[32,2,512]{2,1,0:T(2,128)S(1)}, u32[]{:S(2)}, u32[]{:S(2)}) %collective-permute-start) | collective-permute-done | bytes 131104 | tf_op jit(solution)/shard_map/while/body/eval_jaxpr/ppermute | solution.py:12
  448.0 1.9 collective-permute-start
  450.0 10.9 %collective-permute-done = f32[32,2,512]{2,1,0:T(2,128)S(1)} collective-permute-done((f32[32,2,512]{2,1,0:T(2,128)S(1)}, f32[32,2,512]{2,1,0:T(2,128)S(1)}, u32[]{:S(2)}, u32[]{:S(2)}) %collective-permute-start) | collective-permute-done | bytes 131104 | tf_op jit(solution)/shard_map/while/body/eval_jaxpr/ppermute | solution.py:12
  461.9 1.9 collective-permute-start
  463.9 10.9 %collective-permute-done = f32[32,2,512]{2,1,0:T(2,128)S(1)} collective-permute-done((f32[32,2,512]{2,1,0:T(2,128)S(1)}, f32[32,2,512]{2,1,0:T(2,128)S(1)}, u32[]{:S(2)}, u32[]{:S(2)}) %collective-permute-start) | collective-permute-done | bytes 131104 | tf_op jit(solution)/shard_map/while/body/eval_jaxpr/ppermute | solution.py:12
  (59 shorter events, 27.4 us)
Async XLA Ops:
  6.5 122.0 %all-gather.7.cloned.1.call-start = ((), (), s32[]{:S(2)}) async-start(), calls=%async_computation.1 | async-start | bytes 1081344 | tf_op jit(solution)/shard_map/all_gather | solution.py:39
  8.0 226.9 %all-gather.5.cloned.1.call-start = ((), (), s32[]{:S(2)}) async-start(), calls=%async_computation | async-start | bytes 1081344 | tf_op jit(solution)/shard_map/all_gather | solution.py:39
  8.8 2.9 copy-start.9
  8.8 2.9 copy-start.5
  15.2 1.3 copy-start.3
  130.9 105.6 %copy-start.7 = (bf16[64,8,2,512]{3,1,2,0:T(8,128)(2,1)S(1)}, bf16[64,8,2,512]{3,1,2,0:T(8,128)(2,1)}, u32[]{:S(2)}) copy-start(bf16[64,8,2,512]{3,1,2,0:T(8,128)(2,1)} %copy.20) | copy-start | bytes 3145732
  234.9 1.5 copy-start.4
  237.8 1.6 copy-start.6
  248.1 4.2 copy-start
  256.5 3.2 copy-start.1
  256.5 3.2 copy-start.2
  275.5 5.0 %collective-permute-start = (f32[32,2,512]{2,1,0:T(2,128)S(1)}, f32[32,2,512]{2,1,0:T(2,128)S(1)}, u32[]{:S(2)}, u32[]{:S(2)}) collective-permute-start(f32[32,2,512]{2,1,0:T(2,128)S(1)} %get-tuple-element.188), channel_id=1, source_target_pairs={{0,32},{32,64},{64,96},{96,128},{128,160},{160,192},{192,224},{224... | collective-permute-start | bytes 393224 | tf_op jit(solution)/shard_map/while/body/eval_jaxpr/ppermute | solution.py:12
  281.5 12.9 %collective-permute-start = (f32[32,2,512]{2,1,0:T(2,128)S(1)}, f32[32,2,512]{2,1,0:T(2,128)S(1)}, u32[]{:S(2)}, u32[]{:S(2)}) collective-permute-start(f32[32,2,512]{2,1,0:T(2,128)S(1)} %get-tuple-element.188), channel_id=1, source_target_pairs={{0,32},{32,64},{64,96},{96,128},{128,160},{160,192},{192,224},{224... | collective-permute-start | bytes 393224 | tf_op jit(solution)/shard_map/while/body/eval_jaxpr/ppermute | solution.py:12
  295.4 12.9 %collective-permute-start = (f32[32,2,512]{2,1,0:T(2,128)S(1)}, f32[32,2,512]{2,1,0:T(2,128)S(1)}, u32[]{:S(2)}, u32[]{:S(2)}) collective-permute-start(f32[32,2,512]{2,1,0:T(2,128)S(1)} %get-tuple-element.188), channel_id=1, source_target_pairs={{0,32},{32,64},{64,96},{96,128},{128,160},{160,192},{192,224},{224... | collective-permute-start | bytes 393224 | tf_op jit(solution)/shard_map/while/body/eval_jaxpr/ppermute | solution.py:12
  309.3 12.9 %collective-permute-start = (f32[32,2,512]{2,1,0:T(2,128)S(1)}, f32[32,2,512]{2,1,0:T(2,128)S(1)}, u32[]{:S(2)}, u32[]{:S(2)}) collective-permute-start(f32[32,2,512]{2,1,0:T(2,128)S(1)} %get-tuple-element.188), channel_id=1, source_target_pairs={{0,32},{32,64},{64,96},{96,128},{128,160},{160,192},{192,224},{224... | collective-permute-start | bytes 393224 | tf_op jit(solution)/shard_map/while/body/eval_jaxpr/ppermute | solution.py:12
  323.1 12.9 %collective-permute-start = (f32[32,2,512]{2,1,0:T(2,128)S(1)}, f32[32,2,512]{2,1,0:T(2,128)S(1)}, u32[]{:S(2)}, u32[]{:S(2)}) collective-permute-start(f32[32,2,512]{2,1,0:T(2,128)S(1)} %get-tuple-element.188), channel_id=1, source_target_pairs={{0,32},{32,64},{64,96},{96,128},{128,160},{160,192},{192,224},{224... | collective-permute-start | bytes 393224 | tf_op jit(solution)/shard_map/while/body/eval_jaxpr/ppermute | solution.py:12
  337.0 12.9 %collective-permute-start = (f32[32,2,512]{2,1,0:T(2,128)S(1)}, f32[32,2,512]{2,1,0:T(2,128)S(1)}, u32[]{:S(2)}, u32[]{:S(2)}) collective-permute-start(f32[32,2,512]{2,1,0:T(2,128)S(1)} %get-tuple-element.188), channel_id=1, source_target_pairs={{0,32},{32,64},{64,96},{96,128},{128,160},{160,192},{192,224},{224... | collective-permute-start | bytes 393224 | tf_op jit(solution)/shard_map/while/body/eval_jaxpr/ppermute | solution.py:12
  350.9 12.9 %collective-permute-start = (f32[32,2,512]{2,1,0:T(2,128)S(1)}, f32[32,2,512]{2,1,0:T(2,128)S(1)}, u32[]{:S(2)}, u32[]{:S(2)}) collective-permute-start(f32[32,2,512]{2,1,0:T(2,128)S(1)} %get-tuple-element.188), channel_id=1, source_target_pairs={{0,32},{32,64},{64,96},{96,128},{128,160},{160,192},{192,224},{224... | collective-permute-start | bytes 393224 | tf_op jit(solution)/shard_map/while/body/eval_jaxpr/ppermute | solution.py:12
  364.8 12.9 %collective-permute-start = (f32[32,2,512]{2,1,0:T(2,128)S(1)}, f32[32,2,512]{2,1,0:T(2,128)S(1)}, u32[]{:S(2)}, u32[]{:S(2)}) collective-permute-start(f32[32,2,512]{2,1,0:T(2,128)S(1)} %get-tuple-element.188), channel_id=1, source_target_pairs={{0,32},{32,64},{64,96},{96,128},{128,160},{160,192},{192,224},{224... | collective-permute-start | bytes 393224 | tf_op jit(solution)/shard_map/while/body/eval_jaxpr/ppermute | solution.py:12
  378.6 12.9 %collective-permute-start = (f32[32,2,512]{2,1,0:T(2,128)S(1)}, f32[32,2,512]{2,1,0:T(2,128)S(1)}, u32[]{:S(2)}, u32[]{:S(2)}) collective-permute-start(f32[32,2,512]{2,1,0:T(2,128)S(1)} %get-tuple-element.188), channel_id=1, source_target_pairs={{0,32},{32,64},{64,96},{96,128},{128,160},{160,192},{192,224},{224... | collective-permute-start | bytes 393224 | tf_op jit(solution)/shard_map/while/body/eval_jaxpr/ppermute | solution.py:12
  392.5 12.9 %collective-permute-start = (f32[32,2,512]{2,1,0:T(2,128)S(1)}, f32[32,2,512]{2,1,0:T(2,128)S(1)}, u32[]{:S(2)}, u32[]{:S(2)}) collective-permute-start(f32[32,2,512]{2,1,0:T(2,128)S(1)} %get-tuple-element.188), channel_id=1, source_target_pairs={{0,32},{32,64},{64,96},{96,128},{128,160},{160,192},{192,224},{224... | collective-permute-start | bytes 393224 | tf_op jit(solution)/shard_map/while/body/eval_jaxpr/ppermute | solution.py:12
  406.4 12.9 %collective-permute-start = (f32[32,2,512]{2,1,0:T(2,128)S(1)}, f32[32,2,512]{2,1,0:T(2,128)S(1)}, u32[]{:S(2)}, u32[]{:S(2)}) collective-permute-start(f32[32,2,512]{2,1,0:T(2,128)S(1)} %get-tuple-element.188), channel_id=1, source_target_pairs={{0,32},{32,64},{64,96},{96,128},{128,160},{160,192},{192,224},{224... | collective-permute-start | bytes 393224 | tf_op jit(solution)/shard_map/while/body/eval_jaxpr/ppermute | solution.py:12
  420.3 12.9 %collective-permute-start = (f32[32,2,512]{2,1,0:T(2,128)S(1)}, f32[32,2,512]{2,1,0:T(2,128)S(1)}, u32[]{:S(2)}, u32[]{:S(2)}) collective-permute-start(f32[32,2,512]{2,1,0:T(2,128)S(1)} %get-tuple-element.188), channel_id=1, source_target_pairs={{0,32},{32,64},{64,96},{96,128},{128,160},{160,192},{192,224},{224... | collective-permute-start | bytes 393224 | tf_op jit(solution)/shard_map/while/body/eval_jaxpr/ppermute | solution.py:12
  434.2 12.9 %collective-permute-start = (f32[32,2,512]{2,1,0:T(2,128)S(1)}, f32[32,2,512]{2,1,0:T(2,128)S(1)}, u32[]{:S(2)}, u32[]{:S(2)}) collective-permute-start(f32[32,2,512]{2,1,0:T(2,128)S(1)} %get-tuple-element.188), channel_id=1, source_target_pairs={{0,32},{32,64},{64,96},{96,128},{128,160},{160,192},{192,224},{224... | collective-permute-start | bytes 393224 | tf_op jit(solution)/shard_map/while/body/eval_jaxpr/ppermute | solution.py:12
  448.0 12.9 %collective-permute-start = (f32[32,2,512]{2,1,0:T(2,128)S(1)}, f32[32,2,512]{2,1,0:T(2,128)S(1)}, u32[]{:S(2)}, u32[]{:S(2)}) collective-permute-start(f32[32,2,512]{2,1,0:T(2,128)S(1)} %get-tuple-element.188), channel_id=1, source_target_pairs={{0,32},{32,64},{64,96},{96,128},{128,160},{160,192},{192,224},{224... | collective-permute-start | bytes 393224 | tf_op jit(solution)/shard_map/while/body/eval_jaxpr/ppermute | solution.py:12
  461.9 12.9 %collective-permute-start = (f32[32,2,512]{2,1,0:T(2,128)S(1)}, f32[32,2,512]{2,1,0:T(2,128)S(1)}, u32[]{:S(2)}, u32[]{:S(2)}) collective-permute-start(f32[32,2,512]{2,1,0:T(2,128)S(1)} %get-tuple-element.188), channel_id=1, source_target_pairs={{0,32},{32,64},{64,96},{96,128},{128,160},{160,192},{192,224},{224... | collective-permute-start | bytes 393224 | tf_op jit(solution)/shard_map/while/body/eval_jaxpr/ppermute | solution.py:12
  475.8 0.7 copy-start.8
Sparse Core Ops, SparseCore 0:
  11.8 116.6 all-gather.6
  132.9 101.9 all-gather.4
where the time goes:
time: 492 us; the launch traced here: 483 us
  waiting for transfers between devices  363 us (74%)
  other arithmetic  38 us (8%)
  local copies, waits for them, and re-layouts  35.6 us (7%)
  starting transfers between devices  30.2 us (6%)
  between operations  13.7 us (3%)
    all_gather x2, waiting for transfers between devices, body(): lax.all_gather(branch_tensor[slice_pos], 'stem', axis=0, tiled=True)  208 us
    ppermute x15, waiting for transfers between devices, from_behind(): return lax.ppermute(value, axis, pairs)  155 us
    ppermute x15, starting transfers between devices, from_behind(): return lax.ppermute(value, axis, pairs)  30.1 us
    add x15, other arithmetic, pass_along(): return from_behind(running, 'cuts', 1) + pick_block(turn)  14.6 us
  transfers between devices with their start and end apart: 17, of which 17 were waited for; matrix products, arithmetic and copies ran while one was open for 4% of the time, Pallas kernels for 0%

commit v1 on v0

v1 whole, which is shorter than its diff:
```python
import jax
import jax.numpy as jnp
from jax import lax
from jax.sharding import Mesh
from jax.sharding import PartitionSpec as P

CUTS = ("zl", "core")
STEM = ("zh", "x", "y")


def split_mesh(mesh):
    devices = mesh.devices.reshape(8, 2, 2, 4, 4)
    return Mesh(devices, CUTS + STEM)


def expand_branch(block):
    top_rows = jnp.concatenate([block[:, 0, :], block[:, 1, :]], axis=-1)
    bottom_rows = jnp.concatenate([-block[:, 1, :], block[:, 0, :]], axis=-1)
    return jnp.concatenate([top_rows, bottom_rows], axis=0)


def body(stem_tensor, branch_tensor, open_tensor, open_order):
    slice_count, row_count, _, width = stem_tensor.shape
    permuted = jnp.stack(
        [jnp.take(branch_tensor[t], open_order[t], axis=-1) for t in range(slice_count)]
    )
    pair = lax.all_gather(permuted, "zh", axis=1, tiled=False)
    gathered = lax.all_gather(pair, ("x", "y"), axis=1, tiled=False)
    gathered = jnp.swapaxes(gathered, 1, 2).reshape(slice_count, -1, 2, width)
    local_sum = None
    for t in range(slice_count):
        stem_cols = stem_tensor[t].reshape(row_count, 2 * width)
        placed = jnp.dot(stem_cols, expand_branch(gathered[t]), preferred_element_type=jnp.float32)
        placed = placed.reshape(row_count, 2, width)
        opened = open_tensor[t].astype(jnp.float32)
        real_part = placed[:, 0, :] * opened[:, 0, :] - placed[:, 1, :] * opened[:, 1, :]
        imag_part = placed[:, 0, :] * opened[:, 1, :] + placed[:, 1, :] * opened[:, 0, :]
        term = jnp.stack([real_part, imag_part], axis=1)
        local_sum = term if local_sum is None else local_sum + term
    zl_count = lax.axis_size("zl")
    core_count = lax.axis_size("core")
    block_rows = row_count // (zl_count * core_count)
    shaped = local_sum.reshape(zl_count, core_count, block_rows, 2, width)
    shaped = lax.psum_scatter(shaped, "core", scatter_dimension=1, tiled=True)
    shaped = lax.psum_scatter(shaped, "zl", scatter_dimension=0, tiled=True)
    return shaped.reshape(1, block_rows, 2, width)


def solution(mesh):
    fine = split_mesh(mesh)
    spec = P(CUTS, STEM, None, None)
    return jax.shard_map(
        body,
        mesh=fine,
        in_specs=(spec, spec, spec, P(CUTS, None)),
        out_specs=P(STEM, CUTS, None, None),
        check_vma=False,
    )
```

time: 492 us -> 225 us (0.46)
  the two profiles are of different devices: /device:TPU:1 before, /device:TPU:2 now
where the time goes in v1:
time: 225 us; the launch traced here: 224 us
  waiting for transfers between devices  147 us (65%)
  local copies, waits for them, and re-layouts  31 us (14%)
  blocking collectives  18.8 us (8%)
  between operations  13.3 us (6%)
  other arithmetic  9.84 us (4%)
  matrix products  4.45 us (2%)
    reduce_scatter x1, waiting for transfers between devices, body(): shaped = lax.psum_scatter(shaped, 'zl', scatter_dimension=0, tiled=True)  72.1 us
    all_gather x1, waiting for transfers between devices, body(): gathered = lax.all_gather(pair, ('x', 'y'), axis=1, tiled=False)  54.7 us
    reduce_scatter x1, waiting for transfers between devices, body(): shaped = lax.psum_scatter(shaped, 'core', scatter_dimension=1, tiled=True)  19.9 us
    all_gather x1, blocking collectives, body(): pair = lax.all_gather(permuted, 'zh', axis=1, tiled=False)  18.8 us
    unnamed x14, local copies, waits for them, and re-layouts  11.5 us
  transfers between devices with their start and end apart: 3, of which 3 were waited for; matrix products, arithmetic and copies ran while one was open for 3% of the time, Pallas kernels for 0%

profile of v1, /device:TPU:2, one launch (start us, length us, event | category | flops | bytes accessed | tf_op | source)
XLA Modules:
  0.0 224.5 jit_solution(11437526345782262937)
XLA Ops:
  6.5 0.0 all-gather.4.cloned.1.call-start
  6.5 0.9 fusion.30
  7.5 0.8 fusion.29
  8.3 0.2 copy.76
  8.5 0.2 copy.77
  8.7 2.1 gather_fusion
  10.8 2.1 gather_fusion.1
  12.9 2.2 fusion.18
  15.1 0.9 pad_maximum_fusion
  16.0 0.4 copy.62
  16.4 18.8 %all-gather = bf16[2,32,2,512]{3,2,0,1:T(2,128)(2,1)S(1)} all-gather(bf16[2,16,2,512]{3,2,0,1:T(2,128)(2,1)S(1)} %copy.62), channel_id=2, replica_groups=mesh['zl'=8,'core'=2,'zh'=2,'x'=4,'y'=4] {'zh'}, dimensions={1}, use_global_device_ids=true | all-gather | bytes 196608 | tf_op jit(solution)/shard_map/all_gather | solution.py:27
  35.1 0.7 copy.63
  35.8 0.0 all-gather.4.cloned.1.call-update
  35.8 0.2 reduce-scatter.3.cloned.1.call-start
  36.1 0.0 copy-done.1
  36.1 1.5 fusion.27
  37.6 0.0 copy-start.2
  37.6 1.2 copy.85
  38.8 0.2 copy.84
  39.1 0.5 copy-done.2
  39.6 1.5 fusion.24
  41.0 2.0 fusion.16
  43.0 54.7 %all-gather.4.cloned.1.call-done = bf16[2,32,16,2,512]{4,2,1,3,0:T(8,128)(2,1)} async-done(((bf16[2,2,16,2,512]{4,2,1,3,0:T(8,128)(2,1)}), bf16[2,32,16,2,512]{4,2,1,3,0:T(8,128)(2,1)}) %all-gather.4.cloned.1.call-update) | async-done | bytes 2097168 | tf_op jit(solution)/shard_map/all_gather | solution.py:28
  97.7 1.8 copy.64
  99.5 0.2 fusion.26
  99.8 0.1 copy.69
  99.9 0.8 fusion.23
  100.7 1.1 slice_bitcast_fusion
  101.8 0.1 copy.65
  101.9 0.1 slice_bitcast_fusion.2
  102.0 1.3 fusion
  103.3 1.5 fusion.28
  104.8 1.6 copy.78
  106.3 3.2 %fusion.8 = f32[1024,512]{1,0:T(8,128)S(1)} fusion(bf16[512,1024]{1,0:T(8,128)(2,1)} %bitcast.73, bf16[512,512]{1,0:T(8,128)(2,1)} %get-tuple-element.21, bf16[512,512]{1,0:T(8,128)(2,1)} %fusion.23, bf16[512,512]{1,0:T(8,128)(2,1)} %get-tuple-element.20), kind=kOutput, calls=%fused_computation.11 | convolution fusion | flops 1082130432 | bytes 4718592 | tf_op jit(solution)/shard_map/dot_general | solution.py:33
  109.5 1.5 fusion.25
  111.0 2.6 %copy.81 = f32[512,1,512]{2,0,1:T(8,128)} copy(f32[512,1,512]{0,2,1:T(8,128)} %get-tuple-element.12) | data formatting | bytes 2097152
  113.6 2.5 %copy.83 = f32[512,1,512]{2,0,1:T(8,128)} copy(f32[512,1,512]{0,2,1:T(8,128)} %get-tuple-element.13) | data formatting | bytes 2097152
  116.1 2.6 %copy.80 = f32[512,1,512]{2,0,1:T(8,128)} copy(f32[512,1,512]{0,2,1:T(8,128)} %get-tuple-element.19) | data formatting | bytes 2097152
  118.7 2.8 %multiply_subtract_fusion = (f32[512,1,512]{2,0,1:T(8,128)S(1)}, f32[512,1,512]{2,0,1:T(8,128)S(1)}) fusion(f32[512,1,512]{2,0,1:T(8,128)} %copy.83, f32[512,1,512]{2,0,1:T(8,128)} %copy.81, f32[512,2,512]{2,0,1:T(8,128)} %get-tuple-element.30), kind=kLoop, calls=%fused_computation.24 | loop fusion | flops 1572864 | bytes 6291456 | tf_op jit(solution)/shard_map/sub | solution.py:36
  121.5 0.5 multiply_subtract_fusion.1
  122.0 0.6 maximum_add_fusion
  122.6 1.5 copy.73
  124.1 0.0 reduce-scatter.3.cloned.1.call-update
  124.1 0.0 reduce-scatter.5.cloned.1.call-start
  124.2 19.9 %reduce-scatter.3.cloned.1.call-done = f32[8,1,32,2,512]{4,2,3,0,1:T(8,128)} async-done(((f32[8,2,32,2,512]{4,2,3,0,1:T(8,128)}), f32[8,1,32,2,512]{4,2,3,0,1:T(8,128)}) %reduce-scatter.3.cloned.1.call-update) | async-done | bytes 1048592 | tf_op jit(solution)/shard_map/reduce_scatter | solution.py:44
  144.1 0.0 reduce-scatter.5.cloned.1.call-update
  144.1 72.1 %reduce-scatter.5.cloned.1.call-done = f32[1,1,32,2,512]{4,2,3,1,0:T(8,128)} async-done(((f32[8,1,32,2,512]{4,2,3,1,0:T(8,128)}), f32[1,1,32,2,512]{4,2,3,1,0:T(8,128)}) %reduce-scatter.5.cloned.1.call-update) | async-done | bytes 131088 | tf_op jit(solution)/shard_map/reduce_scatter | solution.py:45
  216.3 1.7 copy.75
  (10 shorter events, 0.1 us)
Async XLA Ops:
  6.5 29.5 %copy-start.1 = (bf16[2,512,2,512]{3,2,1,0:T(2,128)(2,1)S(1)}, bf16[2,512,2,512]{3,2,1,0:T(2,128)(2,1)}, u32[]{:S(2)}) copy-start(bf16[2,512,2,512]{3,2,1,0:T(2,128)(2,1)} %param.6) | copy-start | bytes 6291460
  6.5 91.2 %all-gather.4.cloned.1.call-start = ((), (), s32[]{:S(2)}) async-start(), calls=%async_computation.4 | async-start | bytes 2228224 | tf_op jit(solution)/shard_map/all_gather | solution.py:28
  35.8 108.3 %reduce-scatter.3.cloned.1.call-start = ((), (), s32[]{:S(2)}) async-start(), calls=%async_computation.2 | async-start | bytes 3145728 | tf_op jit(solution)/shard_map/reduce_scatter | solution.py:44
  37.6 2.0 copy-start.2
  118.7 2.8 %copy-start = (f32[512,1,512]{2,0,1:T(8,128)S(1)}, f32[512,1,512]{2,0,1:T(8,128)}, u32[]{:S(2)}) copy-start(f32[512,1,512]{2,0,1:T(8,128)} %copy.80) | copy-start | bytes 3145732
  124.1 92.2 %reduce-scatter.5.cloned.1.call-start = ((), (), s32[]{:S(2)}) async-start(), calls=%async_computation.3 | async-start | bytes 1179648 | tf_op jit(solution)/shard_map/reduce_scatter | solution.py:45
Sparse Core Ops, SparseCore 0:
  36.0 61.7 all-gather.3
  124.2 19.8 reduce-scatter.2
  147.2 69.0 reduce-scatter.4

commit v2 on v1

--- a/solution.py
+++ b/solution.py
@@ -1,11 +1,13 @@
 import jax
 import jax.numpy as jnp
+import numpy as np
 from jax import lax
 from jax.sharding import Mesh
 from jax.sharding import PartitionSpec as P
 
 CUTS = ("zl", "core")
 STEM = ("zh", "x", "y")
+FOLDED = (0, 2, 4, 6, 7, 5, 3, 1)
 
 
 def split_mesh(mesh):
@@ -19,14 +21,53 @@
     return jnp.concatenate([top_rows, bottom_rows], axis=0)
 
 
+def shift_pairs(count, step):
+    return [(i, (i + step) % count) for i in range(count)]
+
+
+def ring_gather(block, axis):
+    count = lax.axis_size(axis)
+    me = lax.axis_index(axis)
+    from_left = lax.ppermute(block, axis, shift_pairs(count, 1))
+    from_right = lax.ppermute(block, axis, shift_pairs(count, -1))
+    half = block.shape[-1] // 2
+    far_a = lax.ppermute(from_left[..., :half], axis, shift_pairs(count, 1))
+    far_b = lax.ppermute(from_right[..., half:], axis, shift_pairs(count, -1))
+    far = jnp.concatenate([far_a, far_b], axis=-1)
+    relative = jnp.stack([block, from_right, far, from_left])
+    return jnp.roll(relative, me, axis=0)
+
+
+def zl_ring_scatter(blocks):
+    count = len(FOLDED)
+    position_of = np.zeros(count, np.int32)
+    for pos, chip in enumerate(FOLDED):
+        position_of[chip] = pos
+    chips = jnp.asarray(np.array(FOLDED, np.int32))
+    pos = jnp.asarray(position_of)[lax.axis_index("zl")]
+    pairs = [(FOLDED[i], FOLDED[(i + 1) % count]) for i in range(count)]
+
+    def own(step):
+        chip = chips[(pos - step - 1) % count]
+        return lax.dynamic_index_in_dim(blocks, chip, 0, keepdims=False)
+
+    running = own(0)
+    for step in range(1, count):
+        running = lax.ppermute(running, "zl", pairs) + own(step)
+    return running
+
+
 def body(stem_tensor, branch_tensor, open_tensor, open_order):
     slice_count, row_count, _, width = stem_tensor.shape
     permuted = jnp.stack(
         [jnp.take(branch_tensor[t], open_order[t], axis=-1) for t in range(slice_count)]
     )
-    pair = lax.all_gather(permuted, "zh", axis=1, tiled=False)
-    gathered = lax.all_gather(pair, ("x", "y"), axis=1, tiled=False)
-    gathered = jnp.swapaxes(gathered, 1, 2).reshape(slice_count, -1, 2, width)
+    other = lax.ppermute(permuted, "zh", shift_pairs(2, 1))
+    low = lax.axis_index("zh") == 0
+    pair = jnp.where(low, jnp.stack([permuted, other], axis=1), jnp.stack([other, permuted], axis=1))
+    gathered = ring_gather(pair, "y")
+    gathered = ring_gather(gathered, "x")
+    gathered = jnp.transpose(gathered, (2, 3, 0, 1, 4, 5, 6)).reshape(slice_count, -1, 2, width)
     local_sum = None
     for t in range(slice_count):
         stem_cols = stem_tensor[t].reshape(row_count, 2 * width)
@@ -38,12 +79,14 @@
         term = jnp.stack([real_part, imag_part], axis=1)
         local_sum = term if local_sum is None else local_sum + term
     zl_count = lax.axis_size("zl")
-    core_count = lax.axis_size("core")
-    block_rows = row_count // (zl_count * core_count)
-    shaped = local_sum.reshape(zl_count, core_count, block_rows, 2, width)
-    shaped = lax.psum_scatter(shaped, "core", scatter_dimension=1, tiled=True)
-    shaped = lax.psum_scatter(shaped, "zl", scatter_dimension=0, tiled=True)
-    return shaped.reshape(1, block_rows, 2, width)
+    block_rows = row_count // (zl_count * 2)
+    shaped = local_sum.reshape(zl_count, 2, block_rows, 2, width)
+    core = lax.axis_index("core")
+    mine = lax.dynamic_index_in_dim(shaped, core, 1, keepdims=False)
+    theirs = lax.dynamic_index_in_dim(shaped, 1 - core, 1, keepdims=False)
+    mine = mine + lax.ppermute(theirs, "core", shift_pairs(2, 1))
+    result = zl_ring_scatter(mine)
+    return result.reshape(1, block_rows, 2, width)
 
 
 def solution(mesh):

time: 225 us -> 206 us (0.916)
  the two profiles are of different devices: /device:TPU:2 before, /device:TPU:152 now
where the time goes in v2:
time: 206 us; the launch traced here: 204 us
  starting transfers between devices  65 us (32%)
  local copies, waits for them, and re-layouts  41.5 us (20%)
  waiting for transfers between devices  39.3 us (19%)
  other arithmetic  32.7 us (16%)
  between operations  21.4 us (10%)
  matrix products  4.44 us (2%)
    ppermute x7, waiting for transfers between devices, zl_ring_scatter(): running = lax.ppermute(running, 'zl', pairs) + own(step)  25.9 us
    ppermute x7, starting transfers between devices, zl_ring_scatter(): running = lax.ppermute(running, 'zl', pairs) + own(step)  25.9 us
    unnamed x42, local copies, waits for them, and re-layouts  22.8 us
    ppermute x1, starting transfers between devices, body(): other = lax.ppermute(permuted, 'zh', shift_pairs(2, 1))  10.9 us
    sub x2, other arithmetic, body(): placed[:, 0, :] * opened[:, 0, :] - placed[:, 1, :] * opened[:, 1, :]  7.45 us
    ppermute x2, starting transfers between devices, ring_gather(): from_right = lax.ppermute(block, axis, shift_pairs(count, -1))  7.37 us
    ppermute x2, starting transfers between devices, ring_gather(): far_b = lax.ppermute(from_right[..., half:], axis, shift_pairs(count, -1))  6.8 us
    ppermute x1, waiting for transfers between devices, body(): other = lax.ppermute(permuted, 'zh', shift_pairs(2, 1))  6.52 us
  transfers between devices with their start and end apart: 17, of which 12 were waited for; matrix products, arithmetic and copies ran while one was open for 7% of the time, Pallas kernels for 0%

profile of v2, /device:TPU:152, one launch (start us, length us, event | category | flops | bytes accessed | tf_op | source)
XLA Modules:
  0.0 204.4 jit_solution(16183176543431784127)
XLA Ops:
  1.8 2.1 %gather_fusion = bf16[512,16,2]{1,2,0:T(2,128)(2,1)S(1)} fusion(bf16[16,2,512]{0,1,2:T(2,128)(2,1)S(1)} %bitcast.154, s32[1024]{0:T(1024)S(1)} %pad_clamp_fusion.1), kind=kCustom, calls=%fused_computation.clone | custom fusion | bytes 67584 | tf_op jit(solution)/shard_map/jit(_take)/gather | solution.py:63
  3.9 1.8 fusion.18
  6.0 2.1 %gather_fusion.1 = bf16[512,16,2]{1,2,0:T(2,128)(2,1)S(1)} fusion(bf16[16,2,512]{0,1,2:T(2,128)(2,1)S(1)} %bitcast.155, s32[1024]{0:T(1024)S(1)} %pad_clamp_fusion), kind=kCustom, calls=%fused_computation.1.clone | custom fusion | bytes 67584 | tf_op jit(solution)/shard_map/jit(_take)/gather | solution.py:63
  8.2 1.8 fusion.19
  10.1 10.9 %collective-permute-start = (bf16[2,16,2,512]{3,1,2,0:T(8,128)(2,1)S(1)}, bf16[2,16,2,512]{3,1,2,0:T(8,128)(2,1)S(1)}, u32[]{:S(2)}, u32[]{:S(2)}) collective-permute-start(bf16[2,16,2,512]{3,1,2,0:T(8,128)(2,1)S(1)} %get-tuple-element.28), channel_id=1, source_target_pairs={{0,16},{16,0},{1,17},{17,1},{2,18},{18,2},{3,19},{19,3},{4,20},{20... | collective-permute-start | bytes 196616 | tf_op jit(solution)/shard_map/ppermute | solution.py:65
  21.0 6.5 %collective-permute-done = bf16[2,16,2,512]{3,1,2,0:T(8,128)(2,1)S(1)} collective-permute-done((bf16[2,16,2,512]{3,1,2,0:T(8,128)(2,1)S(1)}, bf16[2,16,2,512]{3,1,2,0:T(8,128)(2,1)S(1)}, u32[]{:S(2)}, u32[]{:S(2)}) %collective-permute-start) | collective-permute-done | bytes 65568 | tf_op jit(solution)/shard_map/ppermute | solution.py:65
  27.5 1.9 collective-permute-start.2
  29.5 3.9 %collective-permute-start.1 = (bf16[2,2,16,2,512]{4,2,3,1,0:T(8,128)(2,1)S(1)}, bf16[2,2,16,2,512]{4,2,3,1,0:T(8,128)(2,1)S(1)}, u32[]{:S(2)}, u32[]{:S(2)}) collective-permute-start(bf16[2,2,16,2,512]{4,2,3,1,0:T(8,128)(2,1)S(1)} %maximum_select_fusion.1), channel_id=1, source_target_pairs={{0,3},{1,0},{2,1},{3,2},{4,7},{5,4},{6,5},{7,6},{8,11},{9,8},{10,9... | collective-permute-start | bytes 393224 | tf_op jit(solution)/shard_map/ppermute | solution.py:32
  33.4 1.5 collective-permute-done.2
  35.0 2.6 %collective-permute-start.3 = (bf16[2,2,16,2,256]{4,2,3,1,0:T(8,128)(2,1)S(1)}, bf16[2,2,16,2,256]{4,2,3,1,0:T(8,128)(2,1)S(1)}, u32[]{:S(2)}, u32[]{:S(2)}) collective-permute-start(bf16[2,2,16,2,256]{4,2,3,1,0:T(8,128)(2,1)S(1)} %slice.122), channel_id=1, source_target_pairs={{0,1},{1,2},{2,3},{3,0},{4,5},{5,6},{6,7},{7,4},{8,9},{9,10},{10,1... | collective-permute-start | bytes 196616 | tf_op jit(solution)/shard_map/ppermute | solution.py:34
  37.6 3.4 %collective-permute-start.4 = (bf16[2,2,16,2,256]{4,2,3,1,0:T(8,128)(2,1)S(1)}, bf16[2,2,16,2,256]{4,2,3,1,0:T(8,128)(2,1)S(1)}, u32[]{:S(2)}, u32[]{:S(2)}) collective-permute-start(bf16[2,2,16,2,256]{4,2,3,1,0:T(8,128)(2,1)S(1)} %slice.123), channel_id=1, source_target_pairs={{0,3},{1,0},{2,1},{3,2},{4,7},{5,4},{6,5},{7,6},{8,11},{9,8},{10,9... | collective-permute-start | bytes 196616 | tf_op jit(solution)/shard_map/ppermute | solution.py:35
  41.1 3.8 %collective-permute-done.4 = bf16[2,2,16,2,256]{4,2,3,1,0:T(8,128)(2,1)S(1)} collective-permute-done((bf16[2,2,16,2,256]{4,2,3,1,0:T(8,128)(2,1)S(1)}, bf16[2,2,16,2,256]{4,2,3,1,0:T(8,128)(2,1)S(1)}, u32[]{:S(2)}, u32[]{:S(2)}) %collective-permute-start.4) | collective-permute-done | bytes 65568 | tf_op jit(solution)/shard_map/ppermute | solution.py:35
  45.9 3.9 %collective-permute-start.6 = (bf16[4,2,2,16,2,512]{5,3,4,2,1,0:T(8,128)(2,1)S(1)}, bf16[4,2,2,16,2,512]{5,3,4,2,1,0:T(8,128)(2,1)S(1)}, u32[]{:S(2)}, u32[]{:S(2)}) collective-permute-start(bf16[4,2,2,16,2,512]{5,3,4,2,1,0:T(8,128)(2,1)S(1)} %get-tuple-element.7), channel_id=1, source_target_pairs={{0,4},{4,8},{8,12},{12,0},{1,5},{5,9},{9,13},{13,1},{2,6},{6,10},{... | collective-permute-start | bytes 1572872 | tf_op jit(solution)/shard_map/ppermute | solution.py:31
  49.8 3.4 %collective-permute-start.5 = (bf16[4,2,2,16,2,512]{5,3,4,2,1,0:T(8,128)(2,1)S(1)}, bf16[4,2,2,16,2,512]{5,3,4,2,1,0:T(8,128)(2,1)S(1)}, u32[]{:S(2)}, u32[]{:S(2)}) collective-permute-start(bf16[4,2,2,16,2,512]{5,3,4,2,1,0:T(8,128)(2,1)S(1)} %get-tuple-element.7), channel_id=1, source_target_pairs={{0,12},{4,0},{8,4},{12,8},{1,13},{5,1},{9,5},{13,9},{2,14},{6,2},{... | collective-permute-start | bytes 1572872 | tf_op jit(solution)/shard_map/ppermute | solution.py:32
  53.3 4.4 %bitcast_convert_fusion = (f32[512,2,512]{2,1,0:T(2,128)}, f32[512,2,512]{2,1,0:T(2,128)S(1)}) fusion(bf16[2,512,2,512]{3,2,1,0:T(2,128)(2,1)} %param.10), kind=kLoop, calls=%fused_computation.21 | loop fusion | flops 1048576 | bytes 6291456 | tf_op jit(solution)/shard_map/convert_element_type | solution.py:76
  59.8 3.8 %collective-permute-start.7 = (bf16[4,2,2,16,2,256]{5,3,4,2,1,0:T(8,128)(2,1)}, bf16[4,2,2,16,2,256]{5,3,4,2,1,0:T(8,128)(2,1)S(1)}, u32[]{:S(2)}, u32[]{:S(2)}) collective-permute-start(bf16[4,2,2,16,2,256]{5,3,4,2,1,0:T(8,128)(2,1)} %slice.124), channel_id=1, source_target_pairs={{0,4},{4,8},{8,12},{12,0},{1,5},{5,9},{9,13},{13,1},{2,6},{6,10},{... | collective-permute-start | bytes 786440 | tf_op jit(solution)/shard_map/ppermute | solution.py:34
  64.4 3.4 %collective-permute-start.8 = (bf16[4,2,2,16,2,256]{5,3,4,2,1,0:T(8,128)(2,1)}, bf16[4,2,2,16,2,256]{5,3,4,2,1,0:T(8,128)(2,1)}, u32[]{:S(2)}, u32[]{:S(2)}) collective-permute-start(bf16[4,2,2,16,2,256]{5,3,4,2,1,0:T(8,128)(2,1)} %slice.125), channel_id=1, source_target_pairs={{0,12},{4,0},{8,4},{12,8},{1,13},{5,1},{9,5},{13,9},{2,14},{6,2},{... | collective-permute-start | bytes 786440 | tf_op jit(solution)/shard_map/ppermute | solution.py:35
  67.9 2.3 %fusion.31 = (bf16[1,512,2,512]{3,2,1,0:T(2,128)(2,1)}, bf16[1,512,2,512]{3,2,1,0:T(2,128)(2,1)S(1)}) fusion(bf16[2,512,2,512]{3,2,1,0:T(2,128)(2,1)S(1)} %copy-done.7), kind=kLoop, calls=%fused_computation.82 | loop fusion | bytes 4194304 | tf_op jit(solution)/shard_map/slice | solution.py:73
  70.2 2.5 %copy.46 = bf16[64,8,2,512]{3,1,2,0:T(8,128)(2,1)} copy(bf16[64,8,2,512]{3,2,1,0:T(2,128)(2,1)} %bitcast.142) | data formatting | bytes 2097152
  73.9 2.0 bitcast_dynamic-update-slice_fusion.2
  76.0 1.8 fusion.16
  80.3 1.8 fusion.17
  83.0 1.8 copy_bitcast_fusion
  88.3 1.5 fusion.29
  89.9 2.4 %copy.43 = f32[512,1,512]{2,1,0:T(1,128)S(1)} copy(f32[512,1,512]{0,2,1:T(8,128)} %get-tuple-element.14) | data formatting | bytes 2097152
  92.3 3.6 %copy.44 = f32[512,1,512]{2,1,0:T(1,128)} copy(f32[512,1,512]{0,2,1:T(8,128)} %get-tuple-element.15) | data formatting | bytes 2097152
  95.9 3.2 %fusion = f32[1024,512]{1,0:T(8,128)S(1)} fusion(bf16[512,1024]{1,0:T(8,128)(2,1)} %bitcast.149, bf16[512,512]{1,0:T(8,128)(2,1)} %get-tuple-element.25, bf16[512,512]{1,0:T(8,128)(2,1)} %fusion.27, bf16[512,512]{1,0:T(8,128)(2,1)} %get-tuple-element.24), kind=kOutput, calls=%fused_computation.2 | convolution fusion | flops 1082130432 | bytes 4718592 | tf_op jit(solution)/shard_map/dot_general | solution.py:74
  100.5 3.6 %copy.41 = f32[512,1,512]{2,1,0:T(1,128)} copy(f32[512,1,512]{0,2,1:T(8,128)} %get-tuple-element.20) | data formatting | bytes 2097152
  104.1 3.6 %copy.42 = f32[512,1,512]{2,1,0:T(1,128)} copy(f32[512,1,512]{0,2,1:T(8,128)} %get-tuple-element.21) | data formatting | bytes 2097152
  107.7 5.0 %multiply_subtract_fusion = (f32[512,1,512]{2,1,0:T(1,128)S(1)}, f32[512,1,512]{2,1,0:T(1,128)S(1)}) fusion(f32[512,1,512]{2,1,0:T(1,128)} %copy.44, f32[512,1,512]{2,1,0:T(1,128)S(1)} %copy.43, f32[512,2,512]{2,1,0:T(2,128)} %get-tuple-element.12), kind=kLoop, calls=%fused_computation.25 | loop fusion | flops 1572864 | bytes 6291456 | tf_op jit(solution)/shard_map/sub | solution.py:77
  112.8 2.4 %multiply_subtract_fusion.1 = (f32[512,1,512]{2,1,0:T(1,128)S(1)}, f32[512,1,512]{2,1,0:T(1,128)S(1)}) fusion(f32[512,1,512]{2,1,0:T(1,128)S(1)} %copy-done.2, f32[512,1,512]{2,1,0:T(1,128)S(1)} %copy-done.1, f32[512,2,512]{2,1,0:T(2,128)S(1)} %get-tuple-element.13), kind=kLoop, calls=%fused_computation.27 | loop fusion | flops 1572864 | bytes 6291456 | tf_op jit(solution)/shard_map/sub | solution.py:77
  115.2 3.6 %maximum_add_fusion = f32[8,2,32,2,512]{4,3,2,1,0:T(2,128)S(1)} fusion(f32[8,2,32,1,512]{4,3,2,1,0:T(1,128)S(1)} %bitcast.146, f32[8,2,32,1,512]{4,3,2,1,0:T(1,128)S(1)} %bitcast.145, f32[8,2,32,1,512]{4,3,2,1,0:T(1,128)S(1)} %bitcast.144, f32[8,2,32,1,512]{4,3,2,1,0:T(1,128)S(1)} %bitcast.143), kind=kLoop, calls=%fused_computation.10 | loop fusion | flops 1572864 | bytes 6291456 | tf_op jit(solution)/shard_map/add | solution.py:80
  119.2 1.9 collective-permute-start.9
  129.8 1.8 bitcast_add_fusion
  131.6 7.9 %collective-permute-start.10 = (f32[32,2,512]{2,1,0:T(2,128)S(1)}, f32[32,2,512]{2,1,0:T(2,128)S(1)}, u32[]{:S(2)}, u32[]{:S(2)}) collective-permute-start(f32[32,2,512]{2,1,0:T(2,128)S(1)} %dynamic-slice_bitcast_fusion.1), channel_id=1, source_target_pairs={{0,128},{128,256},{256,384},{384,448},{448,320},{320,192},{192,64}... | collective-permute-start | bytes 393224 | tf_op jit(solution)/shard_map/ppermute | solution.py:56
  143.9 5.3 %collective-permute-start.11 = (f32[32,2,512]{2,1,0:T(2,128)S(1)}, f32[32,2,512]{2,1,0:T(2,128)S(1)}, u32[]{:S(2)}, u32[]{:S(2)}) collective-permute-start(f32[32,2,512]{2,1,0:T(2,128)S(1)} %bitcast_add_fusion.7), channel_id=1, source_target_pairs={{0,128},{128,256},{256,384},{384,448},{448,320},{320,192},{192,64}... | collective-permute-start | bytes 393224 | tf_op jit(solution)/shard_map/ppermute | solution.py:56
  151.2 1.8 collective-permute-done.11
  154.0 4.1 %collective-permute-start.12 = (f32[32,2,512]{2,1,0:T(2,128)S(1)}, f32[32,2,512]{2,1,0:T(2,128)S(1)}, u32[]{:S(2)}, u32[]{:S(2)}) collective-permute-start(f32[32,2,512]{2,1,0:T(2,128)S(1)} %bitcast_add_fusion.6), channel_id=1, source_target_pairs={{0,128},{128,256},{256,384},{384,448},{448,320},{320,192},{192,64}... | collective-permute-start | bytes 393224 | tf_op jit(solution)/shard_map/ppermute | solution.py:56
  159.8 3.2 %collective-permute-done.12 = f32[32,2,512]{2,1,0:T(2,128)S(1)} collective-permute-done((f32[32,2,512]{2,1,0:T(2,128)S(1)}, f32[32,2,512]{2,1,0:T(2,128)S(1)}, u32[]{:S(2)}, u32[]{:S(2)}) %collective-permute-start.12) | collective-permute-done | bytes 131104 | tf_op jit(solution)/shard_map/ppermute | solution.py:56
  163.9 2.9 %collective-permute-start.13 = (f32[32,2,512]{2,1,0:T(2,128)S(1)}, f32[32,2,512]{2,1,0:T(2,128)S(1)}, u32[]{:S(2)}, u32[]{:S(2)}) collective-permute-start(f32[32,2,512]{2,1,0:T(2,128)S(1)} %bitcast_add_fusion.5), channel_id=1, source_target_pairs={{0,128},{128,256},{256,384},{384,448},{448,320},{320,192},{192,64}... | collective-permute-start | bytes 393224 | tf_op jit(solution)/shard_map/ppermute | solution.py:56
  168.5 4.4 %collective-permute-done.13 = f32[32,2,512]{2,1,0:T(2,128)S(1)} collective-permute-done((f32[32,2,512]{2,1,0:T(2,128)S(1)}, f32[32,2,512]{2,1,0:T(2,128)S(1)}, u32[]{:S(2)}, u32[]{:S(2)}) %collective-permute-start.13) | collective-permute-done | bytes 131104 | tf_op jit(solution)/shard_map/ppermute | solution.py:56
  173.9 1.9 collective-permute-start.14
  177.9 5.0 %collective-permute-done.14 = f32[32,2,512]{2,1,0:T(2,128)S(1)} collective-permute-done((f32[32,2,512]{2,1,0:T(2,128)S(1)}, f32[32,2,512]{2,1,0:T(2,128)S(1)}, u32[]{:S(2)}, u32[]{:S(2)}) %collective-permute-start.14) | collective-permute-done | bytes 131104 | tf_op jit(solution)/shard_map/ppermute | solution.py:56
  183.8 1.9 collective-permute-start.15
  187.6 5.2 %collective-permute-done.15 = f32[32,2,512]{2,1,0:T(2,128)S(1)} collective-permute-done((f32[32,2,512]{2,1,0:T(2,128)S(1)}, f32[32,2,512]{2,1,0:T(2,128)S(1)}, u32[]{:S(2)}, u32[]{:S(2)}) %collective-permute-start.15) | collective-permute-done | bytes 131104 | tf_op jit(solution)/shard_map/ppermute | solution.py:56
  193.8 1.9 collective-permute-start.16
  197.6 5.1 %collective-permute-done.16 = f32[32,2,512]{2,1,0:T(2,128)S(1)} collective-permute-done((f32[32,2,512]{2,1,0:T(2,128)S(1)}, f32[32,2,512]{2,1,0:T(2,128)S(1)}, u32[]{:S(2)}, u32[]{:S(2)}) %collective-permute-start.16) | collective-permute-done | bytes 131104 | tf_op jit(solution)/shard_map/ppermute | solution.py:56
  202.7 1.6 fusion.20
  (81 shorter events, 25.0 us)
Async XLA Ops:
  10.1 17.4 %collective-permute-start = (bf16[2,16,2,512]{3,1,2,0:T(8,128)(2,1)S(1)}, bf16[2,16,2,512]{3,1,2,0:T(8,128)(2,1)S(1)}, u32[]{:S(2)}, u32[]{:S(2)}) collective-permute-start(bf16[2,16,2,512]{3,1,2,0:T(8,128)(2,1)S(1)} %get-tuple-element.28), channel_id=1, source_target_pairs={{0,16},{16,0},{1,17},{17,1},{2,18},{18,2},{3,19},{19,3},{4,20},{20... | collective-permute-start | bytes 196616 | tf_op jit(solution)/shard_map/ppermute | solution.py:65
  27.5 7.4 %collective-permute-start.2 = (bf16[2,2,16,2,512]{4,2,3,1,0:T(8,128)(2,1)S(1)}, bf16[2,2,16,2,512]{4,2,3,1,0:T(8,128)(2,1)S(1)}, u32[]{:S(2)}, u32[]{:S(2)}) collective-permute-start(bf16[2,2,16,2,512]{4,2,3,1,0:T(8,128)(2,1)S(1)} %maximum_select_fusion.1), channel_id=1, source_target_pairs={{0,1},{1,2},{2,3},{3,0},{4,5},{5,6},{6,7},{7,4},{8,9},{9,10},{10,1... | collective-permute-start | bytes 393224 | tf_op jit(solution)/shard_map/ppermute | solution.py:31
  29.5 8.1 %collective-permute-start.1 = (bf16[2,2,16,2,512]{4,2,3,1,0:T(8,128)(2,1)S(1)}, bf16[2,2,16,2,512]{4,2,3,1,0:T(8,128)(2,1)S(1)}, u32[]{:S(2)}, u32[]{:S(2)}) collective-permute-start(bf16[2,2,16,2,512]{4,2,3,1,0:T(8,128)(2,1)S(1)} %maximum_select_fusion.1), channel_id=1, source_target_pairs={{0,3},{1,0},{2,1},{3,2},{4,7},{5,4},{6,5},{7,6},{8,11},{9,8},{10,9... | collective-permute-start | bytes 393224 | tf_op jit(solution)/shard_map/ppermute | solution.py:32
  35.0 6.1 %collective-permute-start.3 = (bf16[2,2,16,2,256]{4,2,3,1,0:T(8,128)(2,1)S(1)}, bf16[2,2,16,2,256]{4,2,3,1,0:T(8,128)(2,1)S(1)}, u32[]{:S(2)}, u32[]{:S(2)}) collective-permute-start(bf16[2,2,16,2,256]{4,2,3,1,0:T(8,128)(2,1)S(1)} %slice.122), channel_id=1, source_target_pairs={{0,1},{1,2},{2,3},{3,0},{4,5},{5,6},{6,7},{7,4},{8,9},{9,10},{10,1... | collective-permute-start | bytes 196616 | tf_op jit(solution)/shard_map/ppermute | solution.py:34
  37.6 7.4 %collective-permute-start.4 = (bf16[2,2,16,2,256]{4,2,3,1,0:T(8,128)(2,1)S(1)}, bf16[2,2,16,2,256]{4,2,3,1,0:T(8,128)(2,1)S(1)}, u32[]{:S(2)}, u32[]{:S(2)}) collective-permute-start(bf16[2,2,16,2,256]{4,2,3,1,0:T(8,128)(2,1)S(1)} %slice.123), channel_id=1, source_target_pairs={{0,3},{1,0},{2,1},{3,2},{4,7},{5,4},{6,5},{7,6},{8,11},{9,8},{10,9... | collective-permute-start | bytes 196616 | tf_op jit(solution)/shard_map/ppermute | solution.py:35
  45.9 11.7 %copy-start.8 = (bf16[4,2,2,16,2,512]{5,3,4,2,1,0:T(8,128)(2,1)}, bf16[4,2,2,16,2,512]{5,3,4,2,1,0:T(8,128)(2,1)S(1)}, u32[]{:S(2)}) copy-start(bf16[4,2,2,16,2,512]{5,3,4,2,1,0:T(8,128)(2,1)S(1)} %get-tuple-element.7) | copy-start | bytes 1572868
  45.9 21.9 %copy-start.7 = (bf16[2,512,2,512]{3,2,1,0:T(2,128)(2,1)S(1)}, bf16[2,512,2,512]{3,2,1,0:T(2,128)(2,1)}, u32[]{:S(2)}) copy-start(bf16[2,512,2,512]{3,2,1,0:T(2,128)(2,1)} %param.8) | copy-start | bytes 6291460
  45.9 13.1 %collective-permute-start.6 = (bf16[4,2,2,16,2,512]{5,3,4,2,1,0:T(8,128)(2,1)S(1)}, bf16[4,2,2,16,2,512]{5,3,4,2,1,0:T(8,128)(2,1)S(1)}, u32[]{:S(2)}, u32[]{:S(2)}) collective-permute-start(bf16[4,2,2,16,2,512]{5,3,4,2,1,0:T(8,128)(2,1)S(1)} %get-tuple-element.7), channel_id=1, source_target_pairs={{0,4},{4,8},{8,12},{12,0},{1,5},{5,9},{9,13},{13,1},{2,6},{6,10},{... | collective-permute-start | bytes 1572872 | tf_op jit(solution)/shard_map/ppermute | solution.py:31
  49.8 13.8 %collective-permute-start.5 = (bf16[4,2,2,16,2,512]{5,3,4,2,1,0:T(8,128)(2,1)S(1)}, bf16[4,2,2,16,2,512]{5,3,4,2,1,0:T(8,128)(2,1)S(1)}, u32[]{:S(2)}, u32[]{:S(2)}) collective-permute-start(bf16[4,2,2,16,2,512]{5,3,4,2,1,0:T(8,128)(2,1)S(1)} %get-tuple-element.7), channel_id=1, source_target_pairs={{0,12},{4,0},{8,4},{12,8},{1,13},{5,1},{9,5},{13,9},{2,14},{6,2},{... | collective-permute-start | bytes 1572872 | tf_op jit(solution)/shard_map/ppermute | solution.py:32
  59.0 5.4 %copy-start.3 = (bf16[4,2,2,16,2,512]{5,3,4,2,1,0:T(8,128)(2,1)}, bf16[4,2,2,16,2,512]{5,3,4,2,1,0:T(8,128)(2,1)S(1)}, u32[]{:S(2)}) copy-start(bf16[4,2,2,16,2,512]{5,3,4,2,1,0:T(8,128)(2,1)S(1)} %collective-permute-done.6) | copy-start | bytes 1572868
  59.8 16.1 %collective-permute-start.7 = (bf16[4,2,2,16,2,256]{5,3,4,2,1,0:T(8,128)(2,1)}, bf16[4,2,2,16,2,256]{5,3,4,2,1,0:T(8,128)(2,1)S(1)}, u32[]{:S(2)}, u32[]{:S(2)}) collective-permute-start(bf16[4,2,2,16,2,256]{5,3,4,2,1,0:T(8,128)(2,1)} %slice.124), channel_id=1, source_target_pairs={{0,4},{4,8},{8,12},{12,0},{1,5},{5,9},{9,13},{13,1},{2,6},{6,10},{... | collective-permute-start | bytes 786440 | tf_op jit(solution)/shard_map/ppermute | solution.py:34
  63.6 4.2 %copy-start.5 = (bf16[4,2,2,16,2,512]{5,3,4,2,1,0:T(8,128)(2,1)}, bf16[4,2,2,16,2,512]{5,3,4,2,1,0:T(8,128)(2,1)S(1)}, u32[]{:S(2)}) copy-start(bf16[4,2,2,16,2,512]{5,3,4,2,1,0:T(8,128)(2,1)S(1)} %collective-permute-done.5) | copy-start | bytes 1572868
  64.4 11.5 %collective-permute-start.8 = (bf16[4,2,2,16,2,256]{5,3,4,2,1,0:T(8,128)(2,1)}, bf16[4,2,2,16,2,256]{5,3,4,2,1,0:T(8,128)(2,1)}, u32[]{:S(2)}, u32[]{:S(2)}) collective-permute-start(bf16[4,2,2,16,2,256]{5,3,4,2,1,0:T(8,128)(2,1)} %slice.125), channel_id=1, source_target_pairs={{0,12},{4,0},{8,4},{12,8},{1,13},{5,1},{9,5},{13,9},{2,14},{6,2},{... | collective-permute-start | bytes 786440 | tf_op jit(solution)/shard_map/ppermute | solution.py:35
  73.9 3.9 %copy-start.4 = (bf16[4,2,2,16,2,512]{5,3,4,2,1,0:T(8,128)(2,1)S(1)}, bf16[4,2,2,16,2,512]{5,3,4,2,1,0:T(8,128)(2,1)}, u32[]{:S(2)}) copy-start(bf16[4,2,2,16,2,512]{5,3,4,2,1,0:T(8,128)(2,1)} %copy-done.3) | copy-start | bytes 1572868
  73.9 4.7 %copy-start.9 = (bf16[4,2,2,16,2,512]{5,3,4,2,1,0:T(8,128)(2,1)S(1)}, bf16[4,2,2,16,2,512]{5,3,4,2,1,0:T(8,128)(2,1)}, u32[]{:S(2)}) copy-start(bf16[4,2,2,16,2,512]{5,3,4,2,1,0:T(8,128)(2,1)} %copy-done.8) | copy-start | bytes 1572868
  73.9 5.6 %copy-start.6 = (bf16[4,2,2,16,2,512]{5,3,4,2,1,0:T(8,128)(2,1)S(1)}, bf16[4,2,2,16,2,512]{5,3,4,2,1,0:T(8,128)(2,1)}, u32[]{:S(2)}) copy-start(bf16[4,2,2,16,2,512]{5,3,4,2,1,0:T(8,128)(2,1)} %copy-done.5) | copy-start | bytes 1572868
  85.1 1.9 copy-start.10
  107.7 5.0 %copy-start.1 = (f32[512,1,512]{2,1,0:T(1,128)S(1)}, f32[512,1,512]{2,1,0:T(1,128)}, u32[]{:S(2)}) copy-start(f32[512,1,512]{2,1,0:T(1,128)} %copy.41) | copy-start | bytes 3145732
  107.7 5.1 %copy-start.2 = (f32[512,1,512]{2,1,0:T(1,128)S(1)}, f32[512,1,512]{2,1,0:T(1,128)}, u32[]{:S(2)}) copy-start(f32[512,1,512]{2,1,0:T(1,128)} %copy.42) | copy-start | bytes 3145732
  118.8 2.3 %copy-start.12 = (s32[8]{0:T(128)S(1)}, s32[8]{0:T(128)}, u32[]{:S(2)}) copy-start(s32[8]{0:T(128)} %constant.185.clone) | copy-start | bytes 100
  118.8 8.2 %copy-start.11 = (s32[8]{0:T(128)S(1)}, s32[8]{0:T(128)}, u32[]{:S(2)}) copy-start(s32[8]{0:T(128)} %constant.184.clone) | copy-start | bytes 100
  119.2 10.6 %collective-permute-start.9 = (f32[8,32,2,512]{3,2,1,0:T(2,128)S(1)}, f32[8,32,2,512]{3,2,1,0:T(2,128)}, u32[]{:S(2)}, u32[]{:S(2)}) collective-permute-start(f32[8,32,2,512]{3,2,1,0:T(2,128)S(1)} %dynamic-slice_bitcast_fusion), channel_id=1, source_target_pairs={{0,32},{32,0},{1,33},{33,1},{2,34},{34,2},{3,35},{35,3},{4,36},{36... | collective-permute-start | bytes 3145736 | tf_op jit(solution)/shard_map/ppermute | solution.py:87
  131.6 11.3 %copy-start = (f32[8,32,2,512]{3,2,1,0:T(2,128)}, f32[8,32,2,512]{3,2,1,0:T(2,128)S(1)}, u32[]{:S(2)}) copy-start(f32[8,32,2,512]{3,2,1,0:T(2,128)S(1)} %bitcast_add_fusion) | copy-start | bytes 3145732
  131.6 11.3 %collective-permute-start.10 = (f32[32,2,512]{2,1,0:T(2,128)S(1)}, f32[32,2,512]{2,1,0:T(2,128)S(1)}, u32[]{:S(2)}, u32[]{:S(2)}) collective-permute-start(f32[32,2,512]{2,1,0:T(2,128)S(1)} %dynamic-slice_bitcast_fusion.1), channel_id=1, source_target_pairs={{0,128},{128,256},{256,384},{384,448},{448,320},{320,192},{192,64}... | collective-permute-start | bytes 393224 | tf_op jit(solution)/shard_map/ppermute | solution.py:56
  143.9 9.1 %collective-permute-start.11 = (f32[32,2,512]{2,1,0:T(2,128)S(1)}, f32[32,2,512]{2,1,0:T(2,128)S(1)}, u32[]{:S(2)}, u32[]{:S(2)}) collective-permute-start(f32[32,2,512]{2,1,0:T(2,128)S(1)} %bitcast_add_fusion.7), channel_id=1, source_target_pairs={{0,128},{128,256},{256,384},{384,448},{448,320},{320,192},{192,64}... | collective-permute-start | bytes 393224 | tf_op jit(solution)/shard_map/ppermute | solution.py:56
  154.0 9.0 %collective-permute-start.12 = (f32[32,2,512]{2,1,0:T(2,128)S(1)}, f32[32,2,512]{2,1,0:T(2,128)S(1)}, u32[]{:S(2)}, u32[]{:S(2)}) collective-permute-start(f32[32,2,512]{2,1,0:T(2,128)S(1)} %bitcast_add_fusion.6), channel_id=1, source_target_pairs={{0,128},{128,256},{256,384},{384,448},{448,320},{320,192},{192,64}... | collective-permute-start | bytes 393224 | tf_op jit(solution)/shard_map/ppermute | solution.py:56
  163.9 9.0 %collective-permute-start.13 = (f32[32,2,512]{2,1,0:T(2,128)S(1)}, f32[32,2,512]{2,1,0:T(2,128)S(1)}, u32[]{:S(2)}, u32[]{:S(2)}) collective-permute-start(f32[32,2,512]{2,1,0:T(2,128)S(1)} %bitcast_add_fusion.5), channel_id=1, source_target_pairs={{0,128},{128,256},{256,384},{384,448},{448,320},{320,192},{192,64}... | collective-permute-start | bytes 393224 | tf_op jit(solution)/shard_map/ppermute | solution.py:56
  173.9 9.0 %collective-permute-start.14 = (f32[32,2,512]{2,1,0:T(2,128)S(1)}, f32[32,2,512]{2,1,0:T(2,128)S(1)}, u32[]{:S(2)}, u32[]{:S(2)}) collective-permute-start(f32[32,2,512]{2,1,0:T(2,128)S(1)} %bitcast_add_fusion.4), channel_id=1, source_target_pairs={{0,128},{128,256},{256,384},{384,448},{448,320},{320,192},{192,64}... | collective-permute-start | bytes 393224 | tf_op jit(solution)/shard_map/ppermute | solution.py:56
  183.8 9.0 %collective-permute-start.15 = (f32[32,2,512]{2,1,0:T(2,128)S(1)}, f32[32,2,512]{2,1,0:T(2,128)S(1)}, u32[]{:S(2)}, u32[]{:S(2)}) collective-permute-start(f32[32,2,512]{2,1,0:T(2,128)S(1)} %bitcast_add_fusion.3), channel_id=1, source_target_pairs={{0,128},{128,256},{256,384},{384,448},{448,320},{320,192},{192,64}... | collective-permute-start | bytes 393224 | tf_op jit(solution)/shard_map/ppermute | solution.py:56
  193.8 9.0 %collective-permute-start.16 = (f32[32,2,512]{2,1,0:T(2,128)S(1)}, f32[32,2,512]{2,1,0:T(2,128)S(1)}, u32[]{:S(2)}, u32[]{:S(2)}) collective-permute-start(f32[32,2,512]{2,1,0:T(2,128)S(1)} %bitcast_add_fusion.2), channel_id=1, source_target_pairs={{0,128},{128,256},{256,384},{384,448},{448,320},{320,192},{192,64}... | collective-permute-start | bytes 393224 | tf_op jit(solution)/shard_map/ppermute | solution.py:56

commit v3 on v1

v3 whole, which is shorter than its diff:
```python
import jax
import jax.numpy as jnp
from jax import lax
from jax.experimental import pallas as pl
from jax.sharding import Mesh
from jax.sharding import PartitionSpec as P

CUTS = ("zl", "core")
STEM = ("zh", "x", "y")
ROW_TILE = 256


def split_mesh(mesh):
    devices = mesh.devices.reshape(8, 2, 2, 4, 4)
    return Mesh(devices, CUTS + STEM)


def shift_pairs(count, step):
    return [(i, (i + step) % count) for i in range(count)]


def ring_gather(block, axis, along):
    count = lax.axis_size(axis)
    me = lax.axis_index(axis)
    from_left = lax.ppermute(block, axis, shift_pairs(count, 1))
    from_right = lax.ppermute(block, axis, shift_pairs(count, -1))
    half = block.shape[-1] // 2
    far_a = lax.ppermute(from_left[..., :half], axis, shift_pairs(count, 1))
    far_b = lax.ppermute(from_right[..., half:], axis, shift_pairs(count, -1))
    far = jnp.concatenate([far_a, far_b], axis=-1)
    relative = jnp.concatenate([block, from_right, far, from_left], axis=along)
    return jnp.roll(relative, me * block.shape[along], axis=along)


def permute_columns(block, order):
    width = block.shape[-1]
    one_hot = (lax.broadcasted_iota(jnp.int32, (width, width), 0) == order[None, :]).astype(block.dtype)
    flat = block.reshape(-1, width)
    moved = jnp.dot(flat, one_hot, preferred_element_type=jnp.float32)
    return moved.astype(block.dtype).reshape(block.shape)


def contract_kernel(s_ref, b_ref, o_ref, out_ref):
    f32 = jnp.float32
    for t in range(s_ref.shape[0]):
        sr = s_ref[t, 0]
        si = s_ref[t, 1]
        br = b_ref[t, 0]
        bi = b_ref[t, 1]
        pr = jnp.dot(sr, br, preferred_element_type=f32) - jnp.dot(si, bi, preferred_element_type=f32)
        pi = jnp.dot(sr, bi, preferred_element_type=f32) + jnp.dot(si, br, preferred_element_type=f32)
        o_r = o_ref[t, 0].astype(f32)
        o_i = o_ref[t, 1].astype(f32)
        re = pr * o_r - pi * o_i
        im = pr * o_i + pi * o_r
        if t == 0:
            out_ref[0] = re
            out_ref[1] = im
        else:
            out_ref[0] += re
            out_ref[1] += im


def contract(stem_t, branch_t, open_t):
    slices, _, rows, width = stem_t.shape
    tile = min(ROW_TILE, rows)
    flops = slices * 8 * rows * width * width
    moved = 2 * (stem_t.size + branch_t.size + open_t.size) + 4 * 2 * rows * width
    return pl.pallas_call(
        contract_kernel,
        out_shape=jax.ShapeDtypeStruct((2, rows, width), jnp.float32),
        grid=(rows // tile,),
        in_specs=[
            pl.BlockSpec((slices, 2, tile, width), lambda i: (0, 0, i, 0)),
            pl.BlockSpec((slices, 2, width, width), lambda i: (0, 0, 0, 0)),
            pl.BlockSpec((slices, 2, tile, width), lambda i: (0, 0, i, 0)),
        ],
        out_specs=pl.BlockSpec((2, tile, width), lambda i: (0, i, 0)),
        cost_estimate=pl.CostEstimate(flops=flops, bytes_accessed=moved, transcendentals=0),
    )(stem_t, branch_t, open_t)


def halving_scatter(blocks, axis):
    count = lax.axis_size(axis)
    me = lax.axis_index(axis)
    shaped = blocks.reshape((2,) + (2,) * 3 + blocks.shape[2:])
    for bit_pos in range(3):
        along = 3 - bit_pos
        bit = (me >> bit_pos) & 1
        keep = lax.dynamic_index_in_dim(shaped, bit, along, keepdims=False)
        send = lax.dynamic_index_in_dim(shaped, 1 - bit, along, keepdims=False)
        pairs = [(i, i ^ (1 << bit_pos)) for i in range(count)]
        shaped = keep + lax.ppermute(send, axis, pairs)
    return shaped


def body(stem_tensor, branch_tensor, open_tensor, open_order):
    slice_count, row_count, _, width = stem_tensor.shape
    permuted = jnp.stack([permute_columns(branch_tensor[t], open_order[t]) for t in range(slice_count)])
    other = lax.ppermute(permuted, "zh", shift_pairs(2, 1))
    low = lax.axis_index("zh") == 0
    pair = jnp.where(low, jnp.stack([permuted, other], axis=1), jnp.stack([other, permuted], axis=1))
    pair = pair[:, :, None, None]
    gathered = ring_gather(pair, "y", 3)
    gathered = ring_gather(gathered, "x", 2)
    gathered = gathered.reshape(slice_count, -1, 2, width)
    branch_t = jnp.transpose(gathered, (0, 2, 1, 3))
    stem_t = jnp.transpose(stem_tensor, (0, 2, 1, 3))
    open_t = jnp.transpose(open_tensor, (0, 2, 1, 3))
    local_sum = contract(stem_t, branch_t, open_t)
    zl_count = lax.axis_size("zl")
    block_rows = row_count // (zl_count * 2)
    shaped = local_sum.reshape(2, zl_count, 2, block_rows, width)
    core = lax.axis_index("core")
    mine = lax.dynamic_index_in_dim(shaped, core, 2, keepdims=False)
    theirs = lax.dynamic_index_in_dim(shaped, 1 - core, 2, keepdims=False)
    mine = mine + lax.ppermute(theirs, "core", shift_pairs(2, 1))
    result = halving_scatter(mine, "zl")
    return jnp.transpose(result, (1, 0, 2)).reshape(1, block_rows, 2, width)


def solution(mesh):
    fine = split_mesh(mesh)
    spec = P(CUTS, STEM, None, None)
    return jax.shard_map(
        body,
        mesh=fine,
        in_specs=(spec, spec, spec, P(CUTS, None)),
        out_specs=P(STEM, CUTS, None, None),
        check_vma=False,
    )
```

time: 225 us -> 143 us (0.64)
  the two profiles are of different devices: /device:TPU:2 before, /device:TPU:1 now
where the time goes in v3:
time: 143 us; the launch traced here: 142 us
  starting transfers between devices  67.2 us (47%)
  waiting for transfers between devices  47.7 us (33%)
  local copies, waits for them, and re-layouts  14.9 us (10%)
  Pallas kernels  6.24 us (4%)
  other arithmetic  4.65 us (3%)
    ppermute x3, waiting for transfers between devices, halving_scatter(): shaped = keep + lax.ppermute(send, axis, pairs)  36.5 us
    ppermute x1, starting transfers between devices, body(): other = lax.ppermute(permuted, 'zh', shift_pairs(2, 1))  16.3 us
    ppermute x3, starting transfers between devices, halving_scatter(): shaped = keep + lax.ppermute(send, axis, pairs)  15 us
    ppermute x1, starting transfers between devices, body(): mine = mine + lax.ppermute(theirs, 'core', shift_pairs(2, 1))  9.9 us
    ppermute x2, starting transfers between devices, ring_gather(): far_b = lax.ppermute(from_right[..., half:], axis, shift_pairs(count, -1))  8.9 us
    ppermute x2, starting transfers between devices, ring_gather(): from_right = lax.ppermute(block, axis, shift_pairs(count, -1))  6.73 us
    ppermute x2, starting transfers between devices, ring_gather(): from_left = lax.ppermute(block, axis, shift_pairs(count, 1))  6.31 us
    pallas_call x1, Pallas kernels, contract(): pl.pallas_call(contract_kernel, out_shape=jax.ShapeDtypeStruct((2, rows,...  6.24 us
  transfers between devices with their start and end apart: 13, of which 10 were waited for; matrix products, arithmetic and copies ran while one was open for 3% of the time, Pallas kernels for 0%

profile of v3, /device:TPU:1, one launch (start us, length us, event | category | flops | bytes accessed | tf_op | source)
XLA Modules:
  0.0 141.7 jit_solution(513579414314293227)
XLA Ops:
  0.0 0.8 fusion.9
  0.8 0.8 fusion.10
  1.6 0.3 fusion
  2.0 0.3 fusion.1
  2.3 16.3 %collective-permute-start = (bf16[2,16,2,512]{3,1,2,0:T(8,128)(2,1)S(1)}, bf16[2,16,2,512]{3,1,2,0:T(8,128)(2,1)S(1)}, u32[]{:S(2)}, u32[]{:S(2)}) collective-permute-start(bf16[2,16,2,512]{3,1,2,0:T(8,128)(2,1)S(1)} %constant_dynamic-update-slice_fusion), channel_id=1, source_target_pairs={{0,16},{16,0},{1,17},{17,1},{2,18},{18,2},{3,19},{19,3},{4,20},{20... | collective-permute-start | bytes 196616 | tf_op jit(solution)/shard_map/ppermute | solution.py:100
  18.6 1.8 %collective-permute-done = bf16[2,16,2,512]{3,1,2,0:T(8,128)(2,1)S(1)} collective-permute-done((bf16[2,16,2,512]{3,1,2,0:T(8,128)(2,1)S(1)}, bf16[2,16,2,512]{3,1,2,0:T(8,128)(2,1)S(1)}, u32[]{:S(2)}, u32[]{:S(2)}) %collective-permute-start) | collective-permute-done | bytes 65568 | tf_op jit(solution)/shard_map/ppermute | solution.py:100
  20.5 3.2 %collective-permute-start.2 = (bf16[2,2,1,1,16,2,512]{6,4,3,2,1,5,0:T(8,128)(2,1)S(1)}, bf16[2,2,1,1,16,2,512]{6,4,3,2,1,5,0:T(8,128)(2,1)S(1)}, u32[]{:S(2)}, u32[]{:S(2)}) collective-permute-start(bf16[2,2,1,1,16,2,512]{6,4,3,2,1,5,0:T(8,128)(2,1)S(1)} %get-tuple-element.8), channel_id=1, source_target_pairs={{0,1},{1,2},{2,3},{3,0},{4,5},{5,6},{6,7},{7,4},{8,9},{9,10},{10,1... | collective-permute-start | bytes 393224 | tf_op jit(solution)/shard_map/ppermute | solution.py:25
  23.7 3.4 %collective-permute-start.1 = (bf16[2,2,1,1,16,2,512]{6,4,3,2,1,5,0:T(8,128)(2,1)S(1)}, bf16[2,2,1,1,16,2,512]{6,4,3,2,1,5,0:T(8,128)(2,1)S(1)}, u32[]{:S(2)}, u32[]{:S(2)}) collective-permute-start(bf16[2,2,1,1,16,2,512]{6,4,3,2,1,5,0:T(8,128)(2,1)S(1)} %get-tuple-element.8), channel_id=1, source_target_pairs={{0,3},{1,0},{2,1},{3,2},{4,7},{5,4},{6,5},{7,6},{8,11},{9,8},{10,9... | collective-permute-start | bytes 393224 | tf_op jit(solution)/shard_map/ppermute | solution.py:26
  27.1 0.0 copy-start
  27.1 0.0 copy-start.1
  27.1 0.4 collective-permute-done.2
  27.5 2.2 %collective-permute-start.3 = (bf16[2,2,1,1,16,2,256]{6,4,3,2,1,5,0:T(8,128)(2,1)S(1)}, bf16[2,2,1,1,16,2,256]{6,4,3,2,1,5,0:T(8,128)(2,1)S(1)}, u32[]{:S(2)}, u32[]{:S(2)}) collective-permute-start(bf16[2,2,1,1,16,2,256]{6,4,3,2,1,5,0:T(8,128)(2,1)S(1)} %slice.32), channel_id=1, source_target_pairs={{0,1},{1,2},{2,3},{3,0},{4,5},{5,6},{6,7},{7,4},{8,9},{9,10},{10,1... | collective-permute-start | bytes 196616 | tf_op jit(solution)/shard_map/ppermute | solution.py:28
  29.7 4.6 %collective-permute-start.4 = (bf16[2,2,1,1,16,2,256]{6,4,3,2,1,5,0:T(8,128)(2,1)S(1)}, bf16[2,2,1,1,16,2,256]{6,4,3,2,1,5,0:T(8,128)(2,1)S(1)}, u32[]{:S(2)}, u32[]{:S(2)}) collective-permute-start(bf16[2,2,1,1,16,2,256]{6,4,3,2,1,5,0:T(8,128)(2,1)S(1)} %slice.33), channel_id=1, source_target_pairs={{0,3},{1,0},{2,1},{3,2},{4,7},{5,4},{6,5},{7,6},{8,11},{9,8},{10,9... | collective-permute-start | bytes 196616 | tf_op jit(solution)/shard_map/ppermute | solution.py:29
  34.3 0.0 collective-permute-done.3
  34.3 1.3 collective-permute-done.4
  35.7 0.9 constant_dynamic-update-slice_fusion.13
  36.6 3.1 %collective-permute-start.6 = (bf16[2,2,1,4,16,2,512]{6,4,3,2,1,5,0:T(8,128)(2,1)S(1)}, bf16[2,2,1,4,16,2,512]{6,4,3,2,1,5,0:T(8,128)(2,1)S(1)}, u32[]{:S(2)}, u32[]{:S(2)}) collective-permute-start(bf16[2,2,1,4,16,2,512]{6,4,3,2,1,5,0:T(8,128)(2,1)S(1)} %get-tuple-element.6), channel_id=1, source_target_pairs={{0,4},{4,8},{8,12},{12,0},{1,5},{5,9},{9,13},{13,1},{2,6},{6,10},{... | collective-permute-start | bytes 1572872 | tf_op jit(solution)/shard_map/ppermute | solution.py:25
  39.7 3.4 %collective-permute-start.5 = (bf16[2,2,1,4,16,2,512]{6,4,3,2,1,5,0:T(8,128)(2,1)S(1)}, bf16[2,2,1,4,16,2,512]{6,4,3,2,1,5,0:T(8,128)(2,1)S(1)}, u32[]{:S(2)}, u32[]{:S(2)}) collective-permute-start(bf16[2,2,1,4,16,2,512]{6,4,3,2,1,5,0:T(8,128)(2,1)S(1)} %get-tuple-element.6), channel_id=1, source_target_pairs={{0,12},{4,0},{8,4},{12,8},{1,13},{5,1},{9,5},{13,9},{2,14},{6,2},{... | collective-permute-start | bytes 1572872 | tf_op jit(solution)/shard_map/ppermute | solution.py:26
  43.1 4.6 %collective-permute-done.6 = bf16[2,2,1,4,16,2,512]{6,4,3,2,1,5,0:T(8,128)(2,1)S(1)} collective-permute-done((bf16[2,2,1,4,16,2,512]{6,4,3,2,1,5,0:T(8,128)(2,1)S(1)}, bf16[2,2,1,4,16,2,512]{6,4,3,2,1,5,0:T(8,128)(2,1)S(1)}, u32[]{:S(2)}, u32[]{:S(2)}) %collective-permute-start.6) | collective-permute-done | bytes 524320 | tf_op jit(solution)/shard_map/ppermute | solution.py:25
  47.8 1.9 %collective-permute-start.7 = (bf16[2,2,1,4,16,2,256]{6,4,3,2,1,5,0:T(8,128)(2,1)S(1)}, bf16[2,2,1,4,16,2,256]{6,4,3,2,1,5,0:T(8,128)(2,1)S(1)}, u32[]{:S(2)}, u32[]{:S(2)}) collective-permute-start(bf16[2,2,1,4,16,2,256]{6,4,3,2,1,5,0:T(8,128)(2,1)S(1)} %slice.34), channel_id=1, source_target_pairs={{0,4},{4,8},{8,12},{12,0},{1,5},{5,9},{9,13},{13,1},{2,6},{6,10},{... | collective-permute-start | bytes 786440 | tf_op jit(solution)/shard_map/ppermute | solution.py:28
  49.7 0.3 collective-permute-done.5
  50.0 4.3 %collective-permute-start.8 = (bf16[2,2,1,4,16,2,256]{6,4,3,2,1,5,0:T(8,128)(2,1)S(1)}, bf16[2,2,1,4,16,2,256]{6,4,3,2,1,5,0:T(8,128)(2,1)S(1)}, u32[]{:S(2)}, u32[]{:S(2)}) collective-permute-start(bf16[2,2,1,4,16,2,256]{6,4,3,2,1,5,0:T(8,128)(2,1)S(1)} %slice.35), channel_id=1, source_target_pairs={{0,12},{4,0},{8,4},{12,8},{1,13},{5,1},{9,5},{13,9},{2,14},{6,2},{... | collective-permute-start | bytes 786440 | tf_op jit(solution)/shard_map/ppermute | solution.py:29
  54.3 2.7 %copy_bitcast_fusion = (bf16[2,2,512,512]{3,2,1,0:T(8,128)(2,1)}, bf16[2,2,512,512]{3,2,1,0:T(8,128)(2,1)}) fusion(bf16[2,512,2,512]{3,2,1,0:T(2,128)(2,1)S(1)} %copy-done, bf16[2,512,2,512]{3,2,1,0:T(2,128)(2,1)S(1)} %copy-done.1), kind=kLoop, calls=%fused_computation | loop fusion | bytes 8388608 | tf_op jit(solution)/shard_map/transpose | solution.py:109
  57.1 0.9 constant_dynamic-update-slice_fusion.12
  58.0 0.6 collective-permute-done.8
  58.6 0.9 fusion.5
  59.5 0.9 constant_dynamic-update-slice_fusion.11
  60.4 0.8 constant_dynamic-update-slice_fusion.10
  61.2 0.8 constant_dynamic-update-slice_fusion.9
  62.1 0.9 fusion.4
  62.9 0.9 constant_dynamic-update-slice_fusion.8
  63.8 3.3 %constant_dynamic-slice_fusion.2 = bf16[2,2,4,4,16,2,512]{6,4,3,2,1,5,0:T(8,128)(2,1)} fusion(bf16[2,2,8,4,16,2,512]{6,4,3,2,1,5,0:T(8,128)(2,1)} %constant_dynamic-update-slice_fusion.8, s32[]{:T(128)S(6)} %select_n.71), kind=kLoop, calls=%fused_computation.42 | loop fusion | bytes 4194308 | tf_op jit(solution)/shard_map/jit(_roll_dynamic)/dynamic_slice | solution.py:32
  67.1 6.2 %shard_map.46 = f32[2,512,512]{2,1,0:T(8,128)} custom-call(bf16[2,2,512,512]{3,2,1,0:T(8,128)(2,1)} %get-tuple-element.16.s_ref, bf16[2,2,512,512]{3,2,1,0:T(8,128)(2,1)} %bitcast.44, bf16[2,2,512,512]{3,2,1,0:T(8,128)(2,1)} %get-tuple-element.15.o_ref), custom_call_target="tpu_custom_call" | custom-call | flops 2147483648 | bytes 8388608 | tf_op jit(solution)/shard_map/pallas_call | solution.py:69
  73.3 1.3 dynamic-slice_bitcast_fusion
  74.6 9.9 %collective-permute-start.9 = (f32[2,8,32,512]{3,2,1,0:T(8,128)S(1)}, f32[2,8,32,512]{3,2,1,0:T(8,128)S(1)}, u32[]{:S(2)}, u32[]{:S(2)}) collective-permute-start(f32[2,8,32,512]{3,2,1,0:T(8,128)S(1)} %dynamic-slice_bitcast_fusion), channel_id=1, source_target_pairs={{0,32},{32,0},{1,33},{33,1},{2,34},{34,2},{3,35},{35,3},{4,36},{36... | collective-permute-start | bytes 3145736 | tf_op jit(solution)/shard_map/ppermute | solution.py:117
  84.5 2.3 %collective-permute-done.9 = f32[2,8,32,512]{3,2,1,0:T(8,128)S(1)} collective-permute-done((f32[2,8,32,512]{3,2,1,0:T(8,128)S(1)}, f32[2,8,32,512]{3,2,1,0:T(8,128)S(1)}, u32[]{:S(2)}, u32[]{:S(2)}) %collective-permute-start.9) | collective-permute-done | bytes 1048608 | tf_op jit(solution)/shard_map/ppermute | solution.py:117
  86.8 1.4 %bitcast_add_fusion = f32[2,8,32,512]{3,2,1,0:T(8,128)S(1)} fusion(f32[2,8,32,512]{3,2,1,0:T(8,128)S(1)} %collective-permute-done.9, f32[2,8,2,32,512]{4,3,2,1,0:T(8,128)} %bitcast.43, s32[]{:T(128)S(6)} %select_n.72), kind=kLoop, calls=%fused_computation.6 | loop fusion | flops 262144 | bytes 3145732 | tf_op jit(solution)/shard_map/add | solution.py:117
  88.2 0.1 constant_dynamic-slice_fusion.1
  88.3 0.4 copy.17
  88.8 1.9 %collective-permute-start.10 = (f32[2,2,2,32,512]{4,0,3,1,2:T(2,128)S(1)}, f32[2,2,2,32,512]{4,0,3,1,2:T(2,128)S(1)}, u32[]{:S(2)}, u32[]{:S(2)}) collective-permute-start(f32[2,2,2,32,512]{4,0,3,1,2:T(2,128)S(1)} %bitcast.46), channel_id=1, source_target_pairs={{0,64},{64,0},{128,192},{192,128},{256,320},{320,256},{384,448},{4... | collective-permute-start | bytes 1572872 | tf_op jit(solution)/shard_map/ppermute | solution.py:93
  90.7 13.1 %collective-permute-done.10 = f32[2,2,2,32,512]{4,0,3,1,2:T(2,128)S(1)} collective-permute-done((f32[2,2,2,32,512]{4,0,3,1,2:T(2,128)S(1)}, f32[2,2,2,32,512]{4,0,3,1,2:T(2,128)S(1)}, u32[]{:S(2)}, u32[]{:S(2)}) %collective-permute-start.10) | collective-permute-done | bytes 524320 | tf_op jit(solution)/shard_map/ppermute | solution.py:93
  103.8 0.5 bitcast_add_fusion.1
  104.4 3.7 %collective-permute-start.11 = (f32[2,2,32,512]{3,0,2,1:T(2,128)S(1)}, f32[2,2,32,512]{3,0,2,1:T(2,128)S(1)}, u32[]{:S(2)}, u32[]{:S(2)}) collective-permute-start(f32[2,2,32,512]{3,0,2,1:T(2,128)S(1)} %dynamic-slice_bitcast_fusion.1), channel_id=1, source_target_pairs={{0,128},{64,192},{128,0},{192,64},{256,384},{320,448},{384,256},{4... | collective-permute-start | bytes 786440 | tf_op jit(solution)/shard_map/ppermute | solution.py:93
  108.1 12.5 %collective-permute-done.11 = f32[2,2,32,512]{3,0,2,1:T(2,128)S(1)} collective-permute-done((f32[2,2,32,512]{3,0,2,1:T(2,128)S(1)}, f32[2,2,32,512]{3,0,2,1:T(2,128)S(1)}, u32[]{:S(2)}, u32[]{:S(2)}) %collective-permute-start.11) | collective-permute-done | bytes 262176 | tf_op jit(solution)/shard_map/ppermute | solution.py:93
  120.6 0.1 bitcast_add_fusion.2
  120.8 9.4 %collective-permute-start.12 = (f32[2,32,512]{2,0,1:T(2,128)S(1)}, f32[2,32,512]{2,0,1:T(2,128)S(1)}, u32[]{:S(2)}, u32[]{:S(2)}) collective-permute-start(f32[2,32,512]{2,0,1:T(2,128)S(1)} %dynamic-slice_bitcast_fusion.2), channel_id=1, source_target_pairs={{0,256},{64,320},{128,384},{192,448},{256,0},{320,64},{384,128},{4... | collective-permute-start | bytes 393224 | tf_op jit(solution)/shard_map/ppermute | solution.py:93
  130.2 10.8 %collective-permute-done.12 = f32[2,32,512]{2,0,1:T(2,128)S(1)} collective-permute-done((f32[2,32,512]{2,0,1:T(2,128)S(1)}, f32[2,32,512]{2,0,1:T(2,128)S(1)}, u32[]{:S(2)}, u32[]{:S(2)}) %collective-permute-start.12) | collective-permute-done | bytes 131104 | tf_op jit(solution)/shard_map/ppermute | solution.py:93
  141.0 0.7 fusion.6
  (24 shorter events, 0.3 us)
Async XLA Ops:
  2.3 18.1 %collective-permute-start = (bf16[2,16,2,512]{3,1,2,0:T(8,128)(2,1)S(1)}, bf16[2,16,2,512]{3,1,2,0:T(8,128)(2,1)S(1)}, u32[]{:S(2)}, u32[]{:S(2)}) collective-permute-start(bf16[2,16,2,512]{3,1,2,0:T(8,128)(2,1)S(1)} %constant_dynamic-update-slice_fusion), channel_id=1, source_target_pairs={{0,16},{16,0},{1,17},{17,1},{2,18},{18,2},{3,19},{19,3},{4,20},{20... | collective-permute-start | bytes 196616 | tf_op jit(solution)/shard_map/ppermute | solution.py:100
  20.5 7.0 %collective-permute-start.2 = (bf16[2,2,1,1,16,2,512]{6,4,3,2,1,5,0:T(8,128)(2,1)S(1)}, bf16[2,2,1,1,16,2,512]{6,4,3,2,1,5,0:T(8,128)(2,1)S(1)}, u32[]{:S(2)}, u32[]{:S(2)}) collective-permute-start(bf16[2,2,1,1,16,2,512]{6,4,3,2,1,5,0:T(8,128)(2,1)S(1)} %get-tuple-element.8), channel_id=1, source_target_pairs={{0,1},{1,2},{2,3},{3,0},{4,5},{5,6},{6,7},{7,4},{8,9},{9,10},{10,1... | collective-permute-start | bytes 393224 | tf_op jit(solution)/shard_map/ppermute | solution.py:25
  23.7 6.0 %collective-permute-start.1 = (bf16[2,2,1,1,16,2,512]{6,4,3,2,1,5,0:T(8,128)(2,1)S(1)}, bf16[2,2,1,1,16,2,512]{6,4,3,2,1,5,0:T(8,128)(2,1)S(1)}, u32[]{:S(2)}, u32[]{:S(2)}) collective-permute-start(bf16[2,2,1,1,16,2,512]{6,4,3,2,1,5,0:T(8,128)(2,1)S(1)} %get-tuple-element.8), channel_id=1, source_target_pairs={{0,3},{1,0},{2,1},{3,2},{4,7},{5,4},{6,5},{7,6},{8,11},{9,8},{10,9... | collective-permute-start | bytes 393224 | tf_op jit(solution)/shard_map/ppermute | solution.py:26
  27.1 27.2 %copy-start = (bf16[2,512,2,512]{3,2,1,0:T(2,128)(2,1)S(1)}, bf16[2,512,2,512]{3,2,1,0:T(2,128)(2,1)}, u32[]{:S(2)}) copy-start(bf16[2,512,2,512]{3,2,1,0:T(2,128)(2,1)} %param.6) | copy-start | bytes 6291460
  27.1 27.2 %copy-start.1 = (bf16[2,512,2,512]{3,2,1,0:T(2,128)(2,1)S(1)}, bf16[2,512,2,512]{3,2,1,0:T(2,128)(2,1)}, u32[]{:S(2)}) copy-start(bf16[2,512,2,512]{3,2,1,0:T(2,128)(2,1)} %param.4) | copy-start | bytes 6291460
  27.5 6.8 %collective-permute-start.3 = (bf16[2,2,1,1,16,2,256]{6,4,3,2,1,5,0:T(8,128)(2,1)S(1)}, bf16[2,2,1,1,16,2,256]{6,4,3,2,1,5,0:T(8,128)(2,1)S(1)}, u32[]{:S(2)}, u32[]{:S(2)}) collective-permute-start(bf16[2,2,1,1,16,2,256]{6,4,3,2,1,5,0:T(8,128)(2,1)S(1)} %slice.32), channel_id=1, source_target_pairs={{0,1},{1,2},{2,3},{3,0},{4,5},{5,6},{6,7},{7,4},{8,9},{9,10},{10,1... | collective-permute-start | bytes 196616 | tf_op jit(solution)/shard_map/ppermute | solution.py:28
  29.7 5.9 %collective-permute-start.4 = (bf16[2,2,1,1,16,2,256]{6,4,3,2,1,5,0:T(8,128)(2,1)S(1)}, bf16[2,2,1,1,16,2,256]{6,4,3,2,1,5,0:T(8,128)(2,1)S(1)}, u32[]{:S(2)}, u32[]{:S(2)}) collective-permute-start(bf16[2,2,1,1,16,2,256]{6,4,3,2,1,5,0:T(8,128)(2,1)S(1)} %slice.33), channel_id=1, source_target_pairs={{0,3},{1,0},{2,1},{3,2},{4,7},{5,4},{6,5},{7,6},{8,11},{9,8},{10,9... | collective-permute-start | bytes 196616 | tf_op jit(solution)/shard_map/ppermute | solution.py:29
  36.6 11.1 %collective-permute-start.6 = (bf16[2,2,1,4,16,2,512]{6,4,3,2,1,5,0:T(8,128)(2,1)S(1)}, bf16[2,2,1,4,16,2,512]{6,4,3,2,1,5,0:T(8,128)(2,1)S(1)}, u32[]{:S(2)}, u32[]{:S(2)}) collective-permute-start(bf16[2,2,1,4,16,2,512]{6,4,3,2,1,5,0:T(8,128)(2,1)S(1)} %get-tuple-element.6), channel_id=1, source_target_pairs={{0,4},{4,8},{8,12},{12,0},{1,5},{5,9},{9,13},{13,1},{2,6},{6,10},{... | collective-permute-start | bytes 1572872 | tf_op jit(solution)/shard_map/ppermute | solution.py:25
  39.7 10.2 %collective-permute-start.5 = (bf16[2,2,1,4,16,2,512]{6,4,3,2,1,5,0:T(8,128)(2,1)S(1)}, bf16[2,2,1,4,16,2,512]{6,4,3,2,1,5,0:T(8,128)(2,1)S(1)}, u32[]{:S(2)}, u32[]{:S(2)}) collective-permute-start(bf16[2,2,1,4,16,2,512]{6,4,3,2,1,5,0:T(8,128)(2,1)S(1)} %get-tuple-element.6), channel_id=1, source_target_pairs={{0,12},{4,0},{8,4},{12,8},{1,13},{5,1},{9,5},{13,9},{2,14},{6,2},{... | collective-permute-start | bytes 1572872 | tf_op jit(solution)/shard_map/ppermute | solution.py:26
  47.8 10.2 %collective-permute-start.7 = (bf16[2,2,1,4,16,2,256]{6,4,3,2,1,5,0:T(8,128)(2,1)S(1)}, bf16[2,2,1,4,16,2,256]{6,4,3,2,1,5,0:T(8,128)(2,1)S(1)}, u32[]{:S(2)}, u32[]{:S(2)}) collective-permute-start(bf16[2,2,1,4,16,2,256]{6,4,3,2,1,5,0:T(8,128)(2,1)S(1)} %slice.34), channel_id=1, source_target_pairs={{0,4},{4,8},{8,12},{12,0},{1,5},{5,9},{9,13},{13,1},{2,6},{6,10},{... | collective-permute-start | bytes 786440 | tf_op jit(solution)/shard_map/ppermute | solution.py:28
  50.0 8.6 %collective-permute-start.8 = (bf16[2,2,1,4,16,2,256]{6,4,3,2,1,5,0:T(8,128)(2,1)S(1)}, bf16[2,2,1,4,16,2,256]{6,4,3,2,1,5,0:T(8,128)(2,1)S(1)}, u32[]{:S(2)}, u32[]{:S(2)}) collective-permute-start(bf16[2,2,1,4,16,2,256]{6,4,3,2,1,5,0:T(8,128)(2,1)S(1)} %slice.35), channel_id=1, source_target_pairs={{0,12},{4,0},{8,4},{12,8},{1,13},{5,1},{9,5},{13,9},{2,14},{6,2},{... | collective-permute-start | bytes 786440 | tf_op jit(solution)/shard_map/ppermute | solution.py:29
  74.6 12.2 %collective-permute-start.9 = (f32[2,8,32,512]{3,2,1,0:T(8,128)S(1)}, f32[2,8,32,512]{3,2,1,0:T(8,128)S(1)}, u32[]{:S(2)}, u32[]{:S(2)}) collective-permute-start(f32[2,8,32,512]{3,2,1,0:T(8,128)S(1)} %dynamic-slice_bitcast_fusion), channel_id=1, source_target_pairs={{0,32},{32,0},{1,33},{33,1},{2,34},{34,2},{3,35},{35,3},{4,36},{36... | collective-permute-start | bytes 3145736 | tf_op jit(solution)/shard_map/ppermute | solution.py:117
  88.8 15.0 %collective-permute-start.10 = (f32[2,2,2,32,512]{4,0,3,1,2:T(2,128)S(1)}, f32[2,2,2,32,512]{4,0,3,1,2:T(2,128)S(1)}, u32[]{:S(2)}, u32[]{:S(2)}) collective-permute-start(f32[2,2,2,32,512]{4,0,3,1,2:T(2,128)S(1)} %bitcast.46), channel_id=1, source_target_pairs={{0,64},{64,0},{128,192},{192,128},{256,320},{320,256},{384,448},{4... | collective-permute-start | bytes 1572872 | tf_op jit(solution)/shard_map/ppermute | solution.py:93
  104.4 16.2 %collective-permute-start.11 = (f32[2,2,32,512]{3,0,2,1:T(2,128)S(1)}, f32[2,2,32,512]{3,0,2,1:T(2,128)S(1)}, u32[]{:S(2)}, u32[]{:S(2)}) collective-permute-start(f32[2,2,32,512]{3,0,2,1:T(2,128)S(1)} %dynamic-slice_bitcast_fusion.1), channel_id=1, source_target_pairs={{0,128},{64,192},{128,0},{192,64},{256,384},{320,448},{384,256},{4... | collective-permute-start | bytes 786440 | tf_op jit(solution)/shard_map/ppermute | solution.py:93
  120.8 20.2 %collective-permute-start.12 = (f32[2,32,512]{2,0,1:T(2,128)S(1)}, f32[2,32,512]{2,0,1:T(2,128)S(1)}, u32[]{:S(2)}, u32[]{:S(2)}) collective-permute-start(f32[2,32,512]{2,0,1:T(2,128)S(1)} %dynamic-slice_bitcast_fusion.2), channel_id=1, source_target_pairs={{0,256},{64,320},{128,384},{192,448},{256,0},{320,64},{384,128},{4... | collective-permute-start | bytes 393224 | tf_op jit(solution)/shard_map/ppermute | solution.py:93

commit v4 on v3

--- a/solution.py
+++ b/solution.py
@@ -19,17 +19,15 @@
     return [(i, (i + step) % count) for i in range(count)]
 
 
-def ring_gather(block, axis, along):
+def ring_gather(block, axis):
     count = lax.axis_size(axis)
-    me = lax.axis_index(axis)
     from_left = lax.ppermute(block, axis, shift_pairs(count, 1))
     from_right = lax.ppermute(block, axis, shift_pairs(count, -1))
     half = block.shape[-1] // 2
     far_a = lax.ppermute(from_left[..., :half], axis, shift_pairs(count, 1))
     far_b = lax.ppermute(from_right[..., half:], axis, shift_pairs(count, -1))
     far = jnp.concatenate([far_a, far_b], axis=-1)
-    relative = jnp.concatenate([block, from_right, far, from_left], axis=along)
-    return jnp.roll(relative, me * block.shape[along], axis=along)
+    return [block, from_right, far, from_left]
 
 
 def permute_columns(block, order):
@@ -97,15 +95,23 @@
 def body(stem_tensor, branch_tensor, open_tensor, open_order):
     slice_count, row_count, _, width = stem_tensor.shape
     permuted = jnp.stack([permute_columns(branch_tensor[t], open_order[t]) for t in range(slice_count)])
+    permuted = jnp.transpose(permuted, (0, 2, 1, 3))
     other = lax.ppermute(permuted, "zh", shift_pairs(2, 1))
     low = lax.axis_index("zh") == 0
-    pair = jnp.where(low, jnp.stack([permuted, other], axis=1), jnp.stack([other, permuted], axis=1))
-    pair = pair[:, :, None, None]
-    gathered = ring_gather(pair, "y", 3)
-    gathered = ring_gather(gathered, "x", 2)
-    gathered = gathered.reshape(slice_count, -1, 2, width)
-    branch_t = jnp.transpose(gathered, (0, 2, 1, 3))
-    stem_t = jnp.transpose(stem_tensor, (0, 2, 1, 3))
+    pair = jnp.where(low, jnp.stack([permuted, other], axis=2), jnp.stack([other, permuted], axis=2))
+    y_block = jnp.stack(ring_gather(pair, "y"), axis=3)
+    x_pieces = ring_gather(y_block, "x")
+    branch_t = jnp.concatenate(
+        [piece.reshape(slice_count, 2, -1, width) for piece in x_pieces], axis=2
+    )
+    x = lax.axis_index("x")
+    y = lax.axis_index("y")
+    x_count = lax.axis_size("x")
+    y_count = lax.axis_size("y")
+    stem6 = stem_tensor.reshape(slice_count, row_count, 2, 2, x_count, y_count, -1)
+    stem6 = jnp.roll(stem6, -x, axis=4)
+    stem6 = jnp.roll(stem6, -y, axis=5)
+    stem_t = jnp.transpose(stem6, (0, 2, 1, 4, 3, 5, 6)).reshape(slice_count, 2, row_count, width)
     open_t = jnp.transpose(open_tensor, (0, 2, 1, 3))
     local_sum = contract(stem_t, branch_t, open_t)
     zl_count = lax.axis_size("zl")

time: 143 us -> 142 us (level)
  waiting for transfers between devices: 47.7 us -> 43.3 us
  other arithmetic: 4.65 us -> 8.05 us
    ppermute x2, waiting for transfers between devices: 5 us -> 0.42 us  [ring_gather(): from_left = lax.ppermute(block, axis, shift_pairs(count, 1))]
    concatenate x0 -> x3, other arithmetic: none -> 4.38 us  [the longest x1 2.55 us: body(): jnp.concatenate([piece.reshape(slice_count, 2, -1, width) for piece in x_...]
    unnamed x14 -> x5, local copies, waits for them, and re-layouts: 4.45 us -> 8.01 us
    dynamic_slice x1 -> x0, local copies, waits for them, and re-layouts: 3.25 us -> none  [ring_gather(): return jnp.roll(relative, me * block.shape[along], axis=along)]
    transpose x1, local copies, waits for them, and re-layouts: 2.74 us -> 0.27 us  [body(): jnp.transpose(stem6, (0, 2, 1, 4, 3, 5, 6))]
    reshape x0 -> x1, local copies, waits for them, and re-layouts: none -> 2.41 us  [body(): jnp.transpose(stem6, (0, 2, 1, 4, 3, 5, 6))]
    unnamed x5 -> x0, other arithmetic: 1.82 us -> none
    slice x2, local copies, waits for them, and re-layouts: 0.02 us -> 1.68 us  [ring_gather(): far_b = lax.ppermute(from_right[..., half:], axis, shift_pairs(count, -1))]
  transfers between devices with their start and end apart: 13 -> 13, of which waited for: 10 -> 8; matrix products, arithmetic and copies ran while one was open for 3% -> 10% of each run, Pallas kernels for 0% -> 0%
where the time goes in v4:
time: 142 us; the launch traced here: 141 us
  starting transfers between devices  66.7 us (47%)
  waiting for transfers between devices  43.3 us (30%)
  local copies, waits for them, and re-layouts  16.1 us (11%)
  other arithmetic  8.05 us (6%)
  Pallas kernels  6.3 us (4%)
    ppermute x3, waiting for transfers between devices, halving_scatter(): shaped = keep + lax.ppermute(send, axis, pairs)  37.3 us
    ppermute x1, starting transfers between devices, body(): other = lax.ppermute(permuted, 'zh', shift_pairs(2, 1))  16.3 us
    ppermute x3, starting transfers between devices, halving_scatter(): shaped = keep + lax.ppermute(send, axis, pairs)  14.4 us
    ppermute x1, starting transfers between devices, body(): mine = mine + lax.ppermute(theirs, 'core', shift_pairs(2, 1))  10 us
    ppermute x2, starting transfers between devices, ring_gather(): far_b = lax.ppermute(from_right[..., half:], axis, shift_pairs(count, -1))  9.07 us
    unnamed x5, local copies, waits for them, and re-layouts  8.01 us
    ppermute x2, starting transfers between devices, ring_gather(): from_right = lax.ppermute(block, axis, shift_pairs(count, -1))  6.73 us
    ppermute x2, starting transfers between devices, ring_gather(): from_left = lax.ppermute(block, axis, shift_pairs(count, 1))  6.32 us
  transfers between devices with their start and end apart: 13, of which 8 were waited for; matrix products, arithmetic and copies ran while one was open for 10% of the time, Pallas kernels for 0%

profile of v4, /device:TPU:1, one launch (start us, length us, event | category | flops | bytes accessed | tf_op | source)
XLA Modules:
  0.0 141.4 jit_solution(3426156788692716315)
XLA Ops:
  0.0 0.8 fusion.8
  0.8 0.8 fusion.9
  1.6 0.3 fusion.3
  2.0 0.3 fusion.4
  2.3 16.3 %collective-permute-start = (bf16[2,2,16,512]{3,2,1,0:T(8,128)(2,1)S(1)}, bf16[2,2,16,512]{3,2,1,0:T(8,128)(2,1)S(1)}, u32[]{:S(2)}, u32[]{:S(2)}) collective-permute-start(bf16[2,2,16,512]{3,2,1,0:T(8,128)(2,1)S(1)} %bitcast.69), channel_id=1, source_target_pairs={{0,16},{16,0},{1,17},{17,1},{2,18},{18,2},{3,19},{19,3},{4,20},{20... | collective-permute-start | bytes 196616 | tf_op jit(solution)/shard_map/ppermute | solution.py:99
  18.6 1.8 %collective-permute-done = bf16[2,2,16,512]{3,2,1,0:T(8,128)(2,1)S(1)} collective-permute-done((bf16[2,2,16,512]{3,2,1,0:T(8,128)(2,1)S(1)}, bf16[2,2,16,512]{3,2,1,0:T(8,128)(2,1)S(1)}, u32[]{:S(2)}, u32[]{:S(2)}) %collective-permute-start) | collective-permute-done | bytes 65568 | tf_op jit(solution)/shard_map/ppermute | solution.py:99
  20.5 3.2 %collective-permute-start.2 = (bf16[2,2,2,16,512]{4,3,2,1,0:T(8,128)(2,1)S(1)}, bf16[2,2,2,16,512]{4,3,2,1,0:T(8,128)(2,1)S(1)}, u32[]{:S(2)}, u32[]{:S(2)}) collective-permute-start(bf16[2,2,2,16,512]{4,3,2,1,0:T(8,128)(2,1)S(1)} %maximum_select_fusion.1), channel_id=1, source_target_pairs={{0,1},{1,2},{2,3},{3,0},{4,5},{5,6},{6,7},{7,4},{8,9},{9,10},{10,1... | collective-permute-start | bytes 393224 | tf_op jit(solution)/shard_map/ppermute | solution.py:24
  23.7 3.4 %collective-permute-start.1 = (bf16[2,2,2,16,512]{4,3,2,1,0:T(8,128)(2,1)S(1)}, bf16[2,2,2,16,512]{4,3,2,1,0:T(8,128)(2,1)S(1)}, u32[]{:S(2)}, u32[]{:S(2)}) collective-permute-start(bf16[2,2,2,16,512]{4,3,2,1,0:T(8,128)(2,1)S(1)} %maximum_select_fusion.1), channel_id=1, source_target_pairs={{0,3},{1,0},{2,1},{3,2},{4,7},{5,4},{6,5},{7,6},{8,11},{9,8},{10,9... | collective-permute-start | bytes 393224 | tf_op jit(solution)/shard_map/ppermute | solution.py:25
  27.0 0.4 collective-permute-done.2
  27.5 1.9 %collective-permute-start.3 = (bf16[2,2,2,16,256]{4,3,2,1,0:T(8,128)(2,1)S(1)}, bf16[2,2,2,16,256]{4,3,2,1,0:T(8,128)(2,1)S(1)}, u32[]{:S(2)}, u32[]{:S(2)}) collective-permute-start(bf16[2,2,2,16,256]{4,3,2,1,0:T(8,128)(2,1)S(1)} %slice.32), channel_id=1, source_target_pairs={{0,1},{1,2},{2,3},{3,0},{4,5},{5,6},{6,7},{7,4},{8,9},{9,10},{10,1... | collective-permute-start | bytes 196616 | tf_op jit(solution)/shard_map/ppermute | solution.py:27
  29.4 0.0 collective-permute-done.1
  29.4 4.6 %collective-permute-start.4 = (bf16[2,2,2,16,256]{4,3,2,1,0:T(8,128)(2,1)S(1)}, bf16[2,2,2,16,256]{4,3,2,1,0:T(8,128)(2,1)S(1)}, u32[]{:S(2)}, u32[]{:S(2)}) collective-permute-start(bf16[2,2,2,16,256]{4,3,2,1,0:T(8,128)(2,1)S(1)} %slice.33), channel_id=1, source_target_pairs={{0,3},{1,0},{2,1},{3,2},{4,7},{5,4},{6,5},{7,6},{8,11},{9,8},{10,9... | collective-permute-start | bytes 196616 | tf_op jit(solution)/shard_map/ppermute | solution.py:28
  34.0 0.0 collective-permute-done.3
  34.0 1.3 collective-permute-done.4
  35.3 0.1 pad_maximum_fusion.1
  35.4 3.1 %collective-permute-start.6 = (bf16[2,2,2,4,16,512]{5,4,3,2,1,0:T(8,128)(2,1)S(1)}, bf16[2,2,2,4,16,512]{5,4,3,2,1,0:T(8,128)(2,1)S(1)}, u32[]{:S(2)}, u32[]{:S(2)}) collective-permute-start(bf16[2,2,2,4,16,512]{5,4,3,2,1,0:T(8,128)(2,1)S(1)} %pad_maximum_fusion.1), channel_id=1, source_target_pairs={{0,4},{4,8},{8,12},{12,0},{1,5},{5,9},{9,13},{13,1},{2,6},{6,10},{... | collective-permute-start | bytes 1572872 | tf_op jit(solution)/shard_map/ppermute | solution.py:24
  38.5 3.4 %collective-permute-start.5 = (bf16[2,2,2,4,16,512]{5,4,3,2,1,0:T(8,128)(2,1)S(1)}, bf16[2,2,2,4,16,512]{5,4,3,2,1,0:T(8,128)(2,1)}, u32[]{:S(2)}, u32[]{:S(2)}) collective-permute-start(bf16[2,2,2,4,16,512]{5,4,3,2,1,0:T(8,128)(2,1)S(1)} %pad_maximum_fusion.1), channel_id=1, source_target_pairs={{0,12},{4,0},{8,4},{12,8},{1,13},{5,1},{9,5},{13,9},{2,14},{6,2},{... | collective-permute-start | bytes 1572872 | tf_op jit(solution)/shard_map/ppermute | solution.py:25
  41.9 4.7 %copy.15 = bf16[2,512,2,512]{1,3,2,0:T(8,128)(2,1)S(1)} copy(bf16[2,512,2,512]{3,2,1,0:T(2,128)(2,1)} %param.4) | data formatting | bytes 4194304 | tf_op args[0]
  46.7 0.0 collective-permute-done.6
  46.7 1.9 %collective-permute-start.7 = (bf16[2,2,2,4,16,256]{5,4,3,2,1,0:T(8,128)(2,1)S(1)}, bf16[2,2,2,4,16,256]{5,4,3,2,1,0:T(8,128)(2,1)}, u32[]{:S(2)}, u32[]{:S(2)}) collective-permute-start(bf16[2,2,2,4,16,256]{5,4,3,2,1,0:T(8,128)(2,1)S(1)} %slice.34), channel_id=1, source_target_pairs={{0,4},{4,8},{8,12},{12,0},{1,5},{5,9},{9,13},{13,1},{2,6},{6,10},{... | collective-permute-start | bytes 786440 | tf_op jit(solution)/shard_map/ppermute | solution.py:27
  48.6 0.1 collective-permute-done.5
  48.7 1.7 %slice.35 = bf16[2,2,2,4,16,256]{5,4,3,2,1,0:T(8,128)(2,1)} slice(bf16[2,2,2,4,16,512]{5,4,3,2,1,0:T(8,128)(2,1)} %collective-permute-done.5), slice={[0:2], [0:2], [0:2], [0:4], [0:16], [256:512]} | slice | bytes 524288 | tf_op jit(solution)/shard_map/slice | solution.py:28
  50.4 4.5 %collective-permute-start.8 = (bf16[2,2,2,4,16,256]{5,4,3,2,1,0:T(8,128)(2,1)}, bf16[2,2,2,4,16,256]{5,4,3,2,1,0:T(8,128)(2,1)}, u32[]{:S(2)}, u32[]{:S(2)}) collective-permute-start(bf16[2,2,2,4,16,256]{5,4,3,2,1,0:T(8,128)(2,1)} %slice.35), channel_id=1, source_target_pairs={{0,12},{4,0},{8,4},{12,8},{1,13},{5,1},{9,5},{13,9},{2,14},{6,2},{... | collective-permute-start | bytes 786440 | tf_op jit(solution)/shard_map/ppermute | solution.py:28
  54.9 0.8 fusion.2
  55.7 0.8 fusion.1
  56.4 0.3 copy.16
  56.7 2.4 %copy.23.s_ref = bf16[2,2,512,512]{3,2,1,0:T(8,128)(2,1)} copy(bf16[2,2,512,512]{2,3,1,0:T(8,128)(2,1)S(1)} %bitcast.60) | data formatting | bytes 4194304 | tf_op jit(solution)/shard_map/reshape | solution.py:114
  59.1 3.3 %copy.33 = bf16[2,512,2,512]{3,1,2,0:T(8,128)(2,1)} copy(bf16[2,512,2,512]{3,2,1,0:T(2,128)(2,1)} %param.6) | data formatting | bytes 4194304 | tf_op args[2]
  62.4 0.0 collective-permute-done.7
  62.4 0.0 collective-permute-done.8
  62.4 1.1 pad_maximum_fusion.2
  63.5 2.5 %pad_maximum_fusion.b_ref = bf16[2,2,512,512]{3,2,1,0:T(8,128)(2,1)} fusion(bf16[2,2,128,512]{3,2,1,0:T(8,128)(2,1)S(1)} %bitcast.67, bf16[2,2,128,512]{3,2,1,0:T(8,128)(2,1)S(1)} %bitcast.65, bf16[2,2,128,512]{3,2,1,0:T(8,128)(2,1)} %bitcast.20, bf16[2,2,128,512]{3,2,1,0:T(8,128)(2,1)S(1)} %bitcast.66), kind=kLoop, calls=%fused_computation.7 | loop fusion | flops 8388608 | bytes 4194304 | tf_op jit(solution)/shard_map/concatenate | solution.py:104
  66.0 6.3 %shard_map.46 = f32[2,512,512]{2,1,0:T(8,128)} custom-call(bf16[2,2,512,512]{3,2,1,0:T(8,128)(2,1)} %copy.23.s_ref, bf16[2,2,512,512]{3,2,1,0:T(8,128)(2,1)} %pad_maximum_fusion.b_ref, bf16[2,2,512,512]{3,2,1,0:T(8,128)(2,1)} %bitcast.63), custom_call_target="tpu_custom_call" | custom-call | flops 2147483648 | bytes 8388608 | tf_op jit(solution)/shard_map/pallas_call | solution.py:67
  72.3 1.5 %dynamic-slice_bitcast_fusion = f32[2,8,32,512]{3,2,1,0:T(8,128)S(1)} fusion(f32[2,8,2,32,512]{4,3,2,1,0:T(8,128)} %bitcast.61, s32[]{:T(128)S(6)} %select_n.79), kind=kLoop, calls=%fused_computation.14 | loop fusion | bytes 2097156 | tf_op jit(solution)/shard_map/jit(dynamic_index_in_dim)/squeeze | solution.py:122
  73.8 10.0 %collective-permute-start.9 = (f32[2,8,32,512]{3,2,1,0:T(8,128)S(1)}, f32[2,8,32,512]{3,2,1,0:T(8,128)}, u32[]{:S(2)}, u32[]{:S(2)}) collective-permute-start(f32[2,8,32,512]{3,2,1,0:T(8,128)S(1)} %dynamic-slice_bitcast_fusion), channel_id=1, source_target_pairs={{0,32},{32,0},{1,33},{33,1},{2,34},{34,2},{3,35},{35,3},{4,36},{36... | collective-permute-start | bytes 3145736 | tf_op jit(solution)/shard_map/ppermute | solution.py:123
  83.8 2.4 %collective-permute-done.9 = f32[2,8,32,512]{3,2,1,0:T(8,128)} collective-permute-done((f32[2,8,32,512]{3,2,1,0:T(8,128)S(1)}, f32[2,8,32,512]{3,2,1,0:T(8,128)}, u32[]{:S(2)}, u32[]{:S(2)}) %collective-permute-start.9) | collective-permute-done | bytes 1048608 | tf_op jit(solution)/shard_map/ppermute | solution.py:123
  86.2 1.4 %bitcast_add_fusion = f32[2,8,32,512]{3,2,1,0:T(8,128)S(1)} fusion(f32[2,8,32,512]{3,2,1,0:T(8,128)} %collective-permute-done.9, f32[2,8,2,32,512]{4,3,2,1,0:T(8,128)S(1)} %bitcast.62, s32[]{:T(128)S(6)} %select_n.78), kind=kLoop, calls=%fused_computation.13 | loop fusion | flops 262144 | bytes 3145732 | tf_op jit(solution)/shard_map/add | solution.py:123
  87.6 0.1 constant_dynamic-slice_fusion.1
  87.7 0.4 copy.34
  88.2 1.9 %collective-permute-start.10 = (f32[2,2,2,32,512]{4,0,3,1,2:T(2,128)S(1)}, f32[2,2,2,32,512]{4,0,3,1,2:T(2,128)S(1)}, u32[]{:S(2)}, u32[]{:S(2)}) collective-permute-start(f32[2,2,2,32,512]{4,0,3,1,2:T(2,128)S(1)} %bitcast.68), channel_id=1, source_target_pairs={{0,64},{64,0},{128,192},{192,128},{256,320},{320,256},{384,448},{4... | collective-permute-start | bytes 1572872 | tf_op jit(solution)/shard_map/ppermute | solution.py:91
  90.1 13.1 %collective-permute-done.10 = f32[2,2,2,32,512]{4,0,3,1,2:T(2,128)S(1)} collective-permute-done((f32[2,2,2,32,512]{4,0,3,1,2:T(2,128)S(1)}, f32[2,2,2,32,512]{4,0,3,1,2:T(2,128)S(1)}, u32[]{:S(2)}, u32[]{:S(2)}) %collective-permute-start.10) | collective-permute-done | bytes 524320 | tf_op jit(solution)/shard_map/ppermute | solution.py:91
  103.2 0.5 bitcast_add_fusion.1
  103.8 3.2 %collective-permute-start.11 = (f32[2,2,32,512]{3,0,2,1:T(2,128)S(1)}, f32[2,2,32,512]{3,0,2,1:T(2,128)S(1)}, u32[]{:S(2)}, u32[]{:S(2)}) collective-permute-start(f32[2,2,32,512]{3,0,2,1:T(2,128)S(1)} %dynamic-slice_bitcast_fusion.1), channel_id=1, source_target_pairs={{0,128},{64,192},{128,0},{192,64},{256,384},{320,448},{384,256},{4... | collective-permute-start | bytes 786440 | tf_op jit(solution)/shard_map/ppermute | solution.py:91
  107.0 13.4 %collective-permute-done.11 = f32[2,2,32,512]{3,0,2,1:T(2,128)S(1)} collective-permute-done((f32[2,2,32,512]{3,0,2,1:T(2,128)S(1)}, f32[2,2,32,512]{3,0,2,1:T(2,128)S(1)}, u32[]{:S(2)}, u32[]{:S(2)}) %collective-permute-start.11) | collective-permute-done | bytes 262176 | tf_op jit(solution)/shard_map/ppermute | solution.py:91
  120.4 0.1 bitcast_add_fusion.2
  120.5 9.3 %collective-permute-start.12 = (f32[2,32,512]{2,0,1:T(2,128)S(1)}, f32[2,32,512]{2,0,1:T(2,128)S(1)}, u32[]{:S(2)}, u32[]{:S(2)}) collective-permute-start(f32[2,32,512]{2,0,1:T(2,128)S(1)} %dynamic-slice_bitcast_fusion.2), channel_id=1, source_target_pairs={{0,256},{64,320},{128,384},{192,448},{256,0},{320,64},{384,128},{4... | collective-permute-start | bytes 393224 | tf_op jit(solution)/shard_map/ppermute | solution.py:91
  129.8 10.8 %collective-permute-done.12 = f32[2,32,512]{2,0,1:T(2,128)S(1)} collective-permute-done((f32[2,32,512]{2,0,1:T(2,128)S(1)}, f32[2,32,512]{2,0,1:T(2,128)S(1)}, u32[]{:S(2)}, u32[]{:S(2)}) %collective-permute-start.12) | collective-permute-done | bytes 131104 | tf_op jit(solution)/shard_map/ppermute | solution.py:91
  140.7 0.7 fusion.7
  (15 shorter events, 0.2 us)
Async XLA Ops:
  2.3 18.1 %collective-permute-start = (bf16[2,2,16,512]{3,2,1,0:T(8,128)(2,1)S(1)}, bf16[2,2,16,512]{3,2,1,0:T(8,128)(2,1)S(1)}, u32[]{:S(2)}, u32[]{:S(2)}) collective-permute-start(bf16[2,2,16,512]{3,2,1,0:T(8,128)(2,1)S(1)} %bitcast.69), channel_id=1, source_target_pairs={{0,16},{16,0},{1,17},{17,1},{2,18},{18,2},{3,19},{19,3},{4,20},{20... | collective-permute-start | bytes 196616 | tf_op jit(solution)/shard_map/ppermute | solution.py:99
  20.5 7.0 %collective-permute-start.2 = (bf16[2,2,2,16,512]{4,3,2,1,0:T(8,128)(2,1)S(1)}, bf16[2,2,2,16,512]{4,3,2,1,0:T(8,128)(2,1)S(1)}, u32[]{:S(2)}, u32[]{:S(2)}) collective-permute-start(bf16[2,2,2,16,512]{4,3,2,1,0:T(8,128)(2,1)S(1)} %maximum_select_fusion.1), channel_id=1, source_target_pairs={{0,1},{1,2},{2,3},{3,0},{4,5},{5,6},{6,7},{7,4},{8,9},{9,10},{10,1... | collective-permute-start | bytes 393224 | tf_op jit(solution)/shard_map/ppermute | solution.py:24
  23.7 5.7 %collective-permute-start.1 = (bf16[2,2,2,16,512]{4,3,2,1,0:T(8,128)(2,1)S(1)}, bf16[2,2,2,16,512]{4,3,2,1,0:T(8,128)(2,1)S(1)}, u32[]{:S(2)}, u32[]{:S(2)}) collective-permute-start(bf16[2,2,2,16,512]{4,3,2,1,0:T(8,128)(2,1)S(1)} %maximum_select_fusion.1), channel_id=1, source_target_pairs={{0,3},{1,0},{2,1},{3,2},{4,7},{5,4},{6,5},{7,6},{8,11},{9,8},{10,9... | collective-permute-start | bytes 393224 | tf_op jit(solution)/shard_map/ppermute | solution.py:25
  27.5 6.5 %collective-permute-start.3 = (bf16[2,2,2,16,256]{4,3,2,1,0:T(8,128)(2,1)S(1)}, bf16[2,2,2,16,256]{4,3,2,1,0:T(8,128)(2,1)S(1)}, u32[]{:S(2)}, u32[]{:S(2)}) collective-permute-start(bf16[2,2,2,16,256]{4,3,2,1,0:T(8,128)(2,1)S(1)} %slice.32), channel_id=1, source_target_pairs={{0,1},{1,2},{2,3},{3,0},{4,5},{5,6},{6,7},{7,4},{8,9},{9,10},{10,1... | collective-permute-start | bytes 196616 | tf_op jit(solution)/shard_map/ppermute | solution.py:27
  29.4 5.9 %collective-permute-start.4 = (bf16[2,2,2,16,256]{4,3,2,1,0:T(8,128)(2,1)S(1)}, bf16[2,2,2,16,256]{4,3,2,1,0:T(8,128)(2,1)S(1)}, u32[]{:S(2)}, u32[]{:S(2)}) collective-permute-start(bf16[2,2,2,16,256]{4,3,2,1,0:T(8,128)(2,1)S(1)} %slice.33), channel_id=1, source_target_pairs={{0,3},{1,0},{2,1},{3,2},{4,7},{5,4},{6,5},{7,6},{8,11},{9,8},{10,9... | collective-permute-start | bytes 196616 | tf_op jit(solution)/shard_map/ppermute | solution.py:28
  35.4 11.3 %collective-permute-start.6 = (bf16[2,2,2,4,16,512]{5,4,3,2,1,0:T(8,128)(2,1)S(1)}, bf16[2,2,2,4,16,512]{5,4,3,2,1,0:T(8,128)(2,1)S(1)}, u32[]{:S(2)}, u32[]{:S(2)}) collective-permute-start(bf16[2,2,2,4,16,512]{5,4,3,2,1,0:T(8,128)(2,1)S(1)} %pad_maximum_fusion.1), channel_id=1, source_target_pairs={{0,4},{4,8},{8,12},{12,0},{1,5},{5,9},{9,13},{13,1},{2,6},{6,10},{... | collective-permute-start | bytes 1572872 | tf_op jit(solution)/shard_map/ppermute | solution.py:24
  38.5 10.2 %collective-permute-start.5 = (bf16[2,2,2,4,16,512]{5,4,3,2,1,0:T(8,128)(2,1)S(1)}, bf16[2,2,2,4,16,512]{5,4,3,2,1,0:T(8,128)(2,1)}, u32[]{:S(2)}, u32[]{:S(2)}) collective-permute-start(bf16[2,2,2,4,16,512]{5,4,3,2,1,0:T(8,128)(2,1)S(1)} %pad_maximum_fusion.1), channel_id=1, source_target_pairs={{0,12},{4,0},{8,4},{12,8},{1,13},{5,1},{9,5},{13,9},{2,14},{6,2},{... | collective-permute-start | bytes 1572872 | tf_op jit(solution)/shard_map/ppermute | solution.py:25
  46.7 15.7 %collective-permute-start.7 = (bf16[2,2,2,4,16,256]{5,4,3,2,1,0:T(8,128)(2,1)S(1)}, bf16[2,2,2,4,16,256]{5,4,3,2,1,0:T(8,128)(2,1)}, u32[]{:S(2)}, u32[]{:S(2)}) collective-permute-start(bf16[2,2,2,4,16,256]{5,4,3,2,1,0:T(8,128)(2,1)S(1)} %slice.34), channel_id=1, source_target_pairs={{0,4},{4,8},{8,12},{12,0},{1,5},{5,9},{9,13},{13,1},{2,6},{6,10},{... | collective-permute-start | bytes 786440 | tf_op jit(solution)/shard_map/ppermute | solution.py:27
  50.4 12.0 %collective-permute-start.8 = (bf16[2,2,2,4,16,256]{5,4,3,2,1,0:T(8,128)(2,1)}, bf16[2,2,2,4,16,256]{5,4,3,2,1,0:T(8,128)(2,1)}, u32[]{:S(2)}, u32[]{:S(2)}) collective-permute-start(bf16[2,2,2,4,16,256]{5,4,3,2,1,0:T(8,128)(2,1)} %slice.35), channel_id=1, source_target_pairs={{0,12},{4,0},{8,4},{12,8},{1,13},{5,1},{9,5},{13,9},{2,14},{6,2},{... | collective-permute-start | bytes 786440 | tf_op jit(solution)/shard_map/ppermute | solution.py:28
  72.3 13.9 %copy-start = (f32[2,512,512]{2,1,0:T(8,128)S(1)}, f32[2,512,512]{2,1,0:T(8,128)}, u32[]{:S(2)}) copy-start(f32[2,512,512]{2,1,0:T(8,128)} %shard_map.46) | copy-start | bytes 6291460
  73.8 12.4 %collective-permute-start.9 = (f32[2,8,32,512]{3,2,1,0:T(8,128)S(1)}, f32[2,8,32,512]{3,2,1,0:T(8,128)}, u32[]{:S(2)}, u32[]{:S(2)}) collective-permute-start(f32[2,8,32,512]{3,2,1,0:T(8,128)S(1)} %dynamic-slice_bitcast_fusion), channel_id=1, source_target_pairs={{0,32},{32,0},{1,33},{33,1},{2,34},{34,2},{3,35},{35,3},{4,36},{36... | collective-permute-start | bytes 3145736 | tf_op jit(solution)/shard_map/ppermute | solution.py:123
  88.2 15.0 %collective-permute-start.10 = (f32[2,2,2,32,512]{4,0,3,1,2:T(2,128)S(1)}, f32[2,2,2,32,512]{4,0,3,1,2:T(2,128)S(1)}, u32[]{:S(2)}, u32[]{:S(2)}) collective-permute-start(f32[2,2,2,32,512]{4,0,3,1,2:T(2,128)S(1)} %bitcast.68), channel_id=1, source_target_pairs={{0,64},{64,0},{128,192},{192,128},{256,320},{320,256},{384,448},{4... | collective-permute-start | bytes 1572872 | tf_op jit(solution)/shard_map/ppermute | solution.py:91
  103.8 16.6 %collective-permute-start.11 = (f32[2,2,32,512]{3,0,2,1:T(2,128)S(1)}, f32[2,2,32,512]{3,0,2,1:T(2,128)S(1)}, u32[]{:S(2)}, u32[]{:S(2)}) collective-permute-start(f32[2,2,32,512]{3,0,2,1:T(2,128)S(1)} %dynamic-slice_bitcast_fusion.1), channel_id=1, source_target_pairs={{0,128},{64,192},{128,0},{192,64},{256,384},{320,448},{384,256},{4... | collective-permute-start | bytes 786440 | tf_op jit(solution)/shard_map/ppermute | solution.py:91
  120.5 20.2 %collective-permute-start.12 = (f32[2,32,512]{2,0,1:T(2,128)S(1)}, f32[2,32,512]{2,0,1:T(2,128)S(1)}, u32[]{:S(2)}, u32[]{:S(2)}) collective-permute-start(f32[2,32,512]{2,0,1:T(2,128)S(1)} %dynamic-slice_bitcast_fusion.2), channel_id=1, source_target_pairs={{0,256},{64,320},{128,384},{192,448},{256,0},{320,64},{384,128},{4... | collective-permute-start | bytes 393224 | tf_op jit(solution)/shard_map/ppermute | solution.py:91

commit v5 on v4

--- a/solution.py
+++ b/solution.py
@@ -99,19 +99,15 @@
     other = lax.ppermute(permuted, "zh", shift_pairs(2, 1))
     low = lax.axis_index("zh") == 0
     pair = jnp.where(low, jnp.stack([permuted, other], axis=2), jnp.stack([other, permuted], axis=2))
-    y_block = jnp.stack(ring_gather(pair, "y"), axis=3)
-    x_pieces = ring_gather(y_block, "x")
-    branch_t = jnp.concatenate(
-        [piece.reshape(slice_count, 2, -1, width) for piece in x_pieces], axis=2
-    )
-    x = lax.axis_index("x")
-    y = lax.axis_index("y")
+    plane = lax.axis_size("x") * lax.axis_size("y")
+    copies = jnp.broadcast_to(pair[:, :, None], pair.shape[:2] + (plane,) + pair.shape[2:])
+    copies = copies.reshape(slice_count, 2, plane, -1, width)
+    gathered = lax.all_to_all(copies, ("x", "y"), 2, 2, tiled=True)
+    branch_t = gathered.reshape(slice_count, 2, -1, width)
     x_count = lax.axis_size("x")
     y_count = lax.axis_size("y")
     stem6 = stem_tensor.reshape(slice_count, row_count, 2, 2, x_count, y_count, -1)
-    stem6 = jnp.roll(stem6, -x, axis=4)
-    stem6 = jnp.roll(stem6, -y, axis=5)
-    stem_t = jnp.transpose(stem6, (0, 2, 1, 4, 3, 5, 6)).reshape(slice_count, 2, row_count, width)
+    stem_t = jnp.transpose(stem6, (0, 2, 1, 4, 5, 3, 6)).reshape(slice_count, 2, row_count, width)
     open_t = jnp.transpose(open_tensor, (0, 2, 1, 3))
     local_sum = contract(stem_t, branch_t, open_t)
     zl_count = lax.axis_size("zl")

time: 142 us -> 130 us (0.915)
  starting transfers between devices: 66.7 us -> 47 us
  local copies, waits for them, and re-layouts: 16.1 us -> 23.5 us
  waiting for transfers between devices: 43.3 us -> 49.3 us
  other arithmetic: 8.05 us -> 2.84 us
    ppermute x8 -> x0, starting transfers between devices: 26 us -> none  [the longest x2 9.07 us: ring_gather(): far_b = lax.ppermute(from_right[..., half:], axis, shift_pairs(count, -1))]
    all_to_all x0 -> x1, waiting for transfers between devices: none -> 8.31 us  [body(): gathered = lax.all_to_all(copies, ('x', 'y'), 2, 2, tiled=True)]
    all_to_all x0 -> x1, starting transfers between devices: none -> 6.75 us  [body(): gathered = lax.all_to_all(copies, ('x', 'y'), 2, 2, tiled=True)]
    concatenate x3 -> x0, other arithmetic: 4.38 us -> none  [the longest x1 2.55 us: body(): jnp.concatenate([piece.reshape(slice_count, 2, -1, width) for piece in x_...]
    transpose x1, local copies, waits for them, and re-layouts: 0.27 us -> 3.18 us  [body(): jnp.transpose(stem6, (0, 2, 1, 4, 5, 3, 6))]
    ppermute x1, starting transfers between devices: 10 us -> 7.91 us  [body(): mine = mine + lax.ppermute(theirs, 'core', shift_pairs(2, 1))]
    ppermute x8 -> x0, waiting for transfers between devices: 1.8 us -> none  [the longest x2 1.3 us: ring_gather(): far_b = lax.ppermute(from_right[..., half:], axis, shift_pairs(count, -1))]
    reshape x1, local copies, waits for them, and re-layouts: 2.41 us -> 4.14 us  [body(): jnp.transpose(stem6, (0, 2, 1, 4, 5, 3, 6))]
  transfers between devices with their start and end apart: 13 -> 6, of which waited for: 8 -> 6; matrix products, arithmetic and copies ran while one was open for 10% -> 13% of each run, Pallas kernels for 0% -> 0%
where the time goes in v5:
time: 130 us
  waiting for transfers between devices  49.3 us (38%)
  starting transfers between devices  47 us (36%)
  local copies, waits for them, and re-layouts  23.5 us (18%)
  Pallas kernels  6.22 us (5%)
  other arithmetic  2.84 us (2%)
    ppermute x3, waiting for transfers between devices, halving_scatter(): shaped = keep + lax.ppermute(send, axis, pairs)  36.8 us
    ppermute x1, starting transfers between devices, body(): other = lax.ppermute(permuted, 'zh', shift_pairs(2, 1))  16.3 us
    ppermute x3, starting transfers between devices, halving_scatter(): shaped = keep + lax.ppermute(send, axis, pairs)  16 us
    unnamed x5, local copies, waits for them, and re-layouts  9.44 us
    all_to_all x1, waiting for transfers between devices, body(): gathered = lax.all_to_all(copies, ('x', 'y'), 2, 2, tiled=True)  8.31 us
    ppermute x1, starting transfers between devices, body(): mine = mine + lax.ppermute(theirs, 'core', shift_pairs(2, 1))  7.91 us
    all_to_all x1, starting transfers between devices, body(): gathered = lax.all_to_all(copies, ('x', 'y'), 2, 2, tiled=True)  6.75 us
    pallas_call x1, Pallas kernels, contract(): pl.pallas_call(contract_kernel, out_shape=jax.ShapeDtypeStruct((2, rows,...  6.22 us
  transfers between devices with their start and end apart: 6, of which 6 were waited for; matrix products, arithmetic and copies ran while one was open for 13% of the time, Pallas kernels for 0%

profile of v5, /device:TPU:1, one launch (start us, length us, event | category | flops | bytes accessed | tf_op | source)
XLA Modules:
  0.0 129.7 jit_solution(5334668842836636088)
XLA Ops:
  0.0 0.8 fusion.5
  0.8 0.8 fusion.6
  1.6 0.3 fusion
  2.0 0.3 fusion.1
  2.3 16.3 %collective-permute-start = (bf16[2,2,16,512]{3,2,1,0:T(8,128)(2,1)S(1)}, bf16[2,2,16,512]{3,2,1,0:T(8,128)(2,1)S(1)}, u32[]{:S(2)}, u32[]{:S(2)}) collective-permute-start(bf16[2,2,16,512]{3,2,1,0:T(8,128)(2,1)S(1)} %bitcast.55), channel_id=1, source_target_pairs={{0,16},{16,0},{1,17},{17,1},{2,18},{18,2},{3,19},{19,3},{4,20},{20... | collective-permute-start | bytes 196616 | tf_op jit(solution)/shard_map/ppermute | solution.py:99
  18.6 1.8 %collective-permute-done = bf16[2,2,16,512]{3,2,1,0:T(8,128)(2,1)S(1)} collective-permute-done((bf16[2,2,16,512]{3,2,1,0:T(8,128)(2,1)S(1)}, bf16[2,2,16,512]{3,2,1,0:T(8,128)(2,1)S(1)}, u32[]{:S(2)}, u32[]{:S(2)}) %collective-permute-start) | collective-permute-done | bytes 65568 | tf_op jit(solution)/shard_map/ppermute | solution.py:99
  20.5 1.6 %broadcast_in_dim.2 = bf16[2,2,16,32,512]{4,3,1,0,2:T(8,128)(2,1)} broadcast(bf16[2,2,32,512]{3,2,1,0:T(8,128)(2,1)S(1)} %bitcast.53), dimensions={0,1,3,4} | broadcast | bytes 2228224 | tf_op jit(solution)/shard_map/broadcast_in_dim | solution.py:103
  22.0 6.8 %all-to-all-start = ((bf16[2,2,16,32,512]{4,3,1,0,2:T(8,128)(2,1)}), bf16[2,2,16,32,512]{4,3,1,0,2:T(8,128)(2,1)S(1)}, u32[]{:S(2)}, u32[]{:S(2)}) async-start(bf16[2,2,16,32,512]{4,3,1,0,2:T(8,128)(2,1)} %broadcast_in_dim.2), calls=%async_computation | async-start | bytes 4194304 | tf_op jit(solution)/shard_map/all_to_all | solution.py:105
  28.8 6.2 %copy.17 = bf16[2,512,2,512]{1,3,2,0:T(8,128)(2,1)} copy(bf16[2,512,2,512]{3,2,1,0:T(2,128)(2,1)} %param.4) | data formatting | bytes 4194304 | tf_op args[0]
  35.0 3.2 %copy.18 = bf16[2,2,512,4,4,2,16]{2,6,5,4,3,1,0:T(8,128)(2,1)} copy(bf16[2,2,512,4,4,2,16]{2,6,4,3,5,1,0:T(8,128)(2,1)} %bitcast.47) | data formatting | bytes 4194304 | tf_op jit(solution)/shard_map/transpose | solution.py:110
  38.1 4.1 %copy.23.s_ref = bf16[2,2,512,512]{3,2,1,0:T(8,128)(2,1)} copy(bf16[2,2,512,512]{2,3,1,0:T(8,128)(2,1)} %bitcast.46) | data formatting | bytes 4194304 | tf_op jit(solution)/shard_map/reshape | solution.py:110
  42.3 3.3 %copy.31 = bf16[2,512,2,512]{3,1,2,0:T(8,128)(2,1)} copy(bf16[2,512,2,512]{3,2,1,0:T(2,128)(2,1)} %param.6) | data formatting | bytes 4194304 | tf_op args[2]
  45.6 8.3 %all-to-all-done = bf16[2,2,16,32,512]{4,3,1,0,2:T(8,128)(2,1)S(1)} async-done(((bf16[2,2,16,32,512]{4,3,1,0,2:T(8,128)(2,1)}), bf16[2,2,16,32,512]{4,3,1,0,2:T(8,128)(2,1)S(1)}, u32[]{:S(2)}, u32[]{:S(2)}) %all-to-all-start) | async-done | bytes 2097184 | tf_op jit(solution)/shard_map/all_to_all | solution.py:105
  53.9 1.5 %copy.21 = bf16[2,2,16,32,512]{4,3,2,1,0:T(8,128)(2,1)} copy(bf16[2,2,16,32,512]{4,3,1,0,2:T(8,128)(2,1)S(1)} %all-to-all-done) | data formatting | bytes 4194304 | tf_op jit(solution)/shard_map/all_to_all | solution.py:105
  55.3 6.2 %shard_map.46 = f32[2,512,512]{2,1,0:T(8,128)} custom-call(bf16[2,2,512,512]{3,2,1,0:T(8,128)(2,1)} %copy.23.s_ref, bf16[2,2,512,512]{3,2,1,0:T(8,128)(2,1)} %bitcast.51, bf16[2,2,512,512]{3,2,1,0:T(8,128)(2,1)} %bitcast.50), custom_call_target="tpu_custom_call" | custom-call | flops 2147483648 | bytes 8388608 | tf_op jit(solution)/shard_map/pallas_call | solution.py:67
  61.6 0.0 copy-start
  61.6 1.5 %dynamic-slice_bitcast_fusion = f32[2,8,32,512]{3,2,1,0:T(8,128)S(1)} fusion(f32[2,8,2,32,512]{4,3,2,1,0:T(8,128)} %bitcast.48, s32[]{:T(128)S(6)} %select_n.47), kind=kLoop, calls=%fused_computation.6 | loop fusion | bytes 2097156 | tf_op jit(solution)/shard_map/jit(dynamic_index_in_dim)/squeeze | solution.py:118
  63.0 7.9 %collective-permute-start.1 = (f32[2,8,32,512]{3,2,1,0:T(8,128)S(1)}, f32[2,8,32,512]{3,2,1,0:T(8,128)}, u32[]{:S(2)}, u32[]{:S(2)}) collective-permute-start(f32[2,8,32,512]{3,2,1,0:T(8,128)S(1)} %dynamic-slice_bitcast_fusion), channel_id=1, source_target_pairs={{0,32},{32,0},{1,33},{33,1},{2,34},{34,2},{3,35},{35,3},{4,36},{36... | collective-permute-start | bytes 3145736 | tf_op jit(solution)/shard_map/ppermute | solution.py:119
  71.0 2.4 %collective-permute-done.1 = f32[2,8,32,512]{3,2,1,0:T(8,128)} collective-permute-done((f32[2,8,32,512]{3,2,1,0:T(8,128)S(1)}, f32[2,8,32,512]{3,2,1,0:T(8,128)}, u32[]{:S(2)}, u32[]{:S(2)}) %collective-permute-start.1) | collective-permute-done | bytes 1048608 | tf_op jit(solution)/shard_map/ppermute | solution.py:119
  73.4 0.0 copy-done
  73.4 1.4 %bitcast_add_fusion = f32[2,8,32,512]{3,2,1,0:T(8,128)S(1)} fusion(f32[2,8,32,512]{3,2,1,0:T(8,128)} %collective-permute-done.1, f32[2,8,2,32,512]{4,3,2,1,0:T(8,128)S(1)} %bitcast.49, s32[]{:T(128)S(6)} %select_n.46), kind=kLoop, calls=%fused_computation.5 | loop fusion | flops 262144 | bytes 3145732 | tf_op jit(solution)/shard_map/add | solution.py:119
  74.8 0.1 constant_dynamic-slice_fusion.1
  74.9 0.4 copy.32
  75.3 2.4 %collective-permute-start.2 = (f32[2,2,2,32,512]{4,0,3,1,2:T(2,128)S(1)}, f32[2,2,2,32,512]{4,0,3,1,2:T(2,128)S(1)}, u32[]{:S(2)}, u32[]{:S(2)}) collective-permute-start(f32[2,2,2,32,512]{4,0,3,1,2:T(2,128)S(1)} %bitcast.54), channel_id=1, source_target_pairs={{0,64},{64,0},{128,192},{192,128},{256,320},{320,256},{384,448},{4... | collective-permute-start | bytes 1572872 | tf_op jit(solution)/shard_map/ppermute | solution.py:91
  77.8 12.6 %collective-permute-done.2 = f32[2,2,2,32,512]{4,0,3,1,2:T(2,128)S(1)} collective-permute-done((f32[2,2,2,32,512]{4,0,3,1,2:T(2,128)S(1)}, f32[2,2,2,32,512]{4,0,3,1,2:T(2,128)S(1)}, u32[]{:S(2)}, u32[]{:S(2)}) %collective-permute-start.2) | collective-permute-done | bytes 524320 | tf_op jit(solution)/shard_map/ppermute | solution.py:91
  90.4 0.5 bitcast_add_fusion.1
  90.9 3.0 %collective-permute-start.3 = (f32[2,2,32,512]{3,0,2,1:T(2,128)S(1)}, f32[2,2,32,512]{3,0,2,1:T(2,128)S(1)}, u32[]{:S(2)}, u32[]{:S(2)}) collective-permute-start(f32[2,2,32,512]{3,0,2,1:T(2,128)S(1)} %dynamic-slice_bitcast_fusion.1), channel_id=1, source_target_pairs={{0,128},{64,192},{128,0},{192,64},{256,384},{320,448},{384,256},{4... | collective-permute-start | bytes 786440 | tf_op jit(solution)/shard_map/ppermute | solution.py:91
  93.9 13.4 %collective-permute-done.3 = f32[2,2,32,512]{3,0,2,1:T(2,128)S(1)} collective-permute-done((f32[2,2,32,512]{3,0,2,1:T(2,128)S(1)}, f32[2,2,32,512]{3,0,2,1:T(2,128)S(1)}, u32[]{:S(2)}, u32[]{:S(2)}) %collective-permute-start.3) | collective-permute-done | bytes 262176 | tf_op jit(solution)/shard_map/ppermute | solution.py:91
  107.3 0.1 bitcast_add_fusion.2
  107.5 10.6 %collective-permute-start.4 = (f32[2,32,512]{2,0,1:T(2,128)S(1)}, f32[2,32,512]{2,0,1:T(2,128)S(1)}, u32[]{:S(2)}, u32[]{:S(2)}) collective-permute-start(f32[2,32,512]{2,0,1:T(2,128)S(1)} %dynamic-slice_bitcast_fusion.2), channel_id=1, source_target_pairs={{0,256},{64,320},{128,384},{192,448},{256,0},{320,64},{384,128},{4... | collective-permute-start | bytes 393224 | tf_op jit(solution)/shard_map/ppermute | solution.py:91
  118.1 10.8 %collective-permute-done.4 = f32[2,32,512]{2,0,1:T(2,128)S(1)} collective-permute-done((f32[2,32,512]{2,0,1:T(2,128)S(1)}, f32[2,32,512]{2,0,1:T(2,128)S(1)}, u32[]{:S(2)}, u32[]{:S(2)}) %collective-permute-start.4) | collective-permute-done | bytes 131104 | tf_op jit(solution)/shard_map/ppermute | solution.py:91
  128.9 0.7 fusion.4
  (9 shorter events, 0.2 us)
Async XLA Ops:
  2.3 18.1 %collective-permute-start = (bf16[2,2,16,512]{3,2,1,0:T(8,128)(2,1)S(1)}, bf16[2,2,16,512]{3,2,1,0:T(8,128)(2,1)S(1)}, u32[]{:S(2)}, u32[]{:S(2)}) collective-permute-start(bf16[2,2,16,512]{3,2,1,0:T(8,128)(2,1)S(1)} %bitcast.55), channel_id=1, source_target_pairs={{0,16},{16,0},{1,17},{17,1},{2,18},{18,2},{3,19},{19,3},{4,20},{20... | collective-permute-start | bytes 196616 | tf_op jit(solution)/shard_map/ppermute | solution.py:99
  22.0 31.8 %all-to-all-start = ((bf16[2,2,16,32,512]{4,3,1,0,2:T(8,128)(2,1)}), bf16[2,2,16,32,512]{4,3,1,0,2:T(8,128)(2,1)S(1)}, u32[]{:S(2)}, u32[]{:S(2)}) async-start(bf16[2,2,16,32,512]{4,3,1,0,2:T(8,128)(2,1)} %broadcast_in_dim.2), calls=%async_computation | async-start | bytes 4194304 | tf_op jit(solution)/shard_map/all_to_all | solution.py:105
  61.6 11.8 %copy-start = (f32[2,512,512]{2,1,0:T(8,128)S(1)}, f32[2,512,512]{2,1,0:T(8,128)}, u32[]{:S(2)}) copy-start(f32[2,512,512]{2,1,0:T(8,128)} %shard_map.46) | copy-start | bytes 6291460
  63.0 10.3 %collective-permute-start.1 = (f32[2,8,32,512]{3,2,1,0:T(8,128)S(1)}, f32[2,8,32,512]{3,2,1,0:T(8,128)}, u32[]{:S(2)}, u32[]{:S(2)}) collective-permute-start(f32[2,8,32,512]{3,2,1,0:T(8,128)S(1)} %dynamic-slice_bitcast_fusion), channel_id=1, source_target_pairs={{0,32},{32,0},{1,33},{33,1},{2,34},{34,2},{3,35},{35,3},{4,36},{36... | collective-permute-start | bytes 3145736 | tf_op jit(solution)/shard_map/ppermute | solution.py:119
  75.3 15.0 %collective-permute-start.2 = (f32[2,2,2,32,512]{4,0,3,1,2:T(2,128)S(1)}, f32[2,2,2,32,512]{4,0,3,1,2:T(2,128)S(1)}, u32[]{:S(2)}, u32[]{:S(2)}) collective-permute-start(f32[2,2,2,32,512]{4,0,3,1,2:T(2,128)S(1)} %bitcast.54), channel_id=1, source_target_pairs={{0,64},{64,0},{128,192},{192,128},{256,320},{320,256},{384,448},{4... | collective-permute-start | bytes 1572872 | tf_op jit(solution)/shard_map/ppermute | solution.py:91
  90.9 16.4 %collective-permute-start.3 = (f32[2,2,32,512]{3,0,2,1:T(2,128)S(1)}, f32[2,2,32,512]{3,0,2,1:T(2,128)S(1)}, u32[]{:S(2)}, u32[]{:S(2)}) collective-permute-start(f32[2,2,32,512]{3,0,2,1:T(2,128)S(1)} %dynamic-slice_bitcast_fusion.1), channel_id=1, source_target_pairs={{0,128},{64,192},{128,0},{192,64},{256,384},{320,448},{384,256},{4... | collective-permute-start | bytes 786440 | tf_op jit(solution)/shard_map/ppermute | solution.py:91
  107.5 21.5 %collective-permute-start.4 = (f32[2,32,512]{2,0,1:T(2,128)S(1)}, f32[2,32,512]{2,0,1:T(2,128)S(1)}, u32[]{:S(2)}, u32[]{:S(2)}) collective-permute-start(f32[2,32,512]{2,0,1:T(2,128)S(1)} %dynamic-slice_bitcast_fusion.2), channel_id=1, source_target_pairs={{0,256},{64,320},{128,384},{192,448},{256,0},{320,64},{384,128},{4... | collective-permute-start | bytes 393224 | tf_op jit(solution)/shard_map/ppermute | solution.py:91

commit v6 on v5

--- a/solution.py
+++ b/solution.py
@@ -41,14 +41,14 @@
 def contract_kernel(s_ref, b_ref, o_ref, out_ref):
     f32 = jnp.float32
     for t in range(s_ref.shape[0]):
-        sr = s_ref[t, 0]
-        si = s_ref[t, 1]
+        sr = s_ref[t, :, 0, :]
+        si = s_ref[t, :, 1, :]
         br = b_ref[t, 0]
         bi = b_ref[t, 1]
         pr = jnp.dot(sr, br, preferred_element_type=f32) - jnp.dot(si, bi, preferred_element_type=f32)
         pi = jnp.dot(sr, bi, preferred_element_type=f32) + jnp.dot(si, br, preferred_element_type=f32)
-        o_r = o_ref[t, 0].astype(f32)
-        o_i = o_ref[t, 1].astype(f32)
+        o_r = o_ref[t, :, 0, :].astype(f32)
+        o_i = o_ref[t, :, 1, :].astype(f32)
         re = pr * o_r - pi * o_i
         im = pr * o_i + pi * o_r
         if t == 0:
@@ -60,7 +60,7 @@
 
 
 def contract(stem_t, branch_t, open_t):
-    slices, _, rows, width = stem_t.shape
+    slices, rows, _, width = stem_t.shape
     tile = min(ROW_TILE, rows)
     flops = slices * 8 * rows * width * width
     moved = 2 * (stem_t.size + branch_t.size + open_t.size) + 4 * 2 * rows * width
@@ -69,9 +69,9 @@
         out_shape=jax.ShapeDtypeStruct((2, rows, width), jnp.float32),
         grid=(rows // tile,),
         in_specs=[
-            pl.BlockSpec((slices, 2, tile, width), lambda i: (0, 0, i, 0)),
+            pl.BlockSpec((slices, tile, 2, width), lambda i: (0, i, 0, 0)),
             pl.BlockSpec((slices, 2, width, width), lambda i: (0, 0, 0, 0)),
-            pl.BlockSpec((slices, 2, tile, width), lambda i: (0, 0, i, 0)),
+            pl.BlockSpec((slices, tile, 2, width), lambda i: (0, i, 0, 0)),
         ],
         out_specs=pl.BlockSpec((2, tile, width), lambda i: (0, i, 0)),
         cost_estimate=pl.CostEstimate(flops=flops, bytes_accessed=moved, transcendentals=0),
@@ -101,14 +101,10 @@
     pair = jnp.where(low, jnp.stack([permuted, other], axis=2), jnp.stack([other, permuted], axis=2))
     plane = lax.axis_size("x") * lax.axis_size("y")
     copies = jnp.broadcast_to(pair[:, :, None], pair.shape[:2] + (plane,) + pair.shape[2:])
-    copies = copies.reshape(slice_count, 2, plane, -1, width)
-    gathered = lax.all_to_all(copies, ("x", "y"), 2, 2, tiled=True)
+    gathered = lax.all_to_all(copies, ("x", "y"), 2, 4, tiled=True)
     branch_t = gathered.reshape(slice_count, 2, -1, width)
-    x_count = lax.axis_size("x")
-    y_count = lax.axis_size("y")
-    stem6 = stem_tensor.reshape(slice_count, row_count, 2, 2, x_count, y_count, -1)
-    stem_t = jnp.transpose(stem6, (0, 2, 1, 4, 5, 3, 6)).reshape(slice_count, 2, row_count, width)
-    open_t = jnp.transpose(open_tensor, (0, 2, 1, 3))
+    stem_t = stem_tensor
+    open_t = open_tensor
     local_sum = contract(stem_t, branch_t, open_t)
     zl_count = lax.axis_size("zl")
     block_rows = row_count // (zl_count * 2)

time: 130 us -> 134 us (1.031)
  waiting for transfers between devices: 49.3 us -> 66.1 us
  local copies, waits for them, and re-layouts: 23.5 us -> 6.91 us
  Pallas kernels: 6.22 us -> 10.2 us
    all_to_all x1, waiting for transfers between devices: 8.31 us -> 25 us  [body(): gathered = lax.all_to_all(copies, ('x', 'y'), 2, 4, tiled=True)]
    unnamed x5 -> x3, local copies, waits for them, and re-layouts: 9.44 us -> 0.03 us
    reshape x1 -> x0, local copies, waits for them, and re-layouts: 4.14 us -> none  [body(): jnp.transpose(stem6, (0, 2, 1, 4, 5, 3, 6))]
    pallas_call x1, Pallas kernels: 6.22 us -> 10.2 us  [contract(): pl.pallas_call(contract_kernel, out_shape=jax.ShapeDtypeStruct((2, rows,...]
    transpose x1 -> x0, local copies, waits for them, and re-layouts: 3.18 us -> none  [body(): jnp.transpose(stem6, (0, 2, 1, 4, 5, 3, 6))]
  transfers between devices with their start and end apart: 6 -> 6, of which waited for: 6 -> 6; matrix products, arithmetic and copies ran while one was open for 13% -> 0% of each run, Pallas kernels for 0% -> 0%
where the time goes in v6:
time: 134 us
  waiting for transfers between devices  66.1 us (49%)
  starting transfers between devices  46.9 us (35%)
  Pallas kernels  10.2 us (8%)
  local copies, waits for them, and re-layouts  6.91 us (5%)
  other arithmetic  3.02 us (2%)
    ppermute x3, waiting for transfers between devices, halving_scatter(): shaped = keep + lax.ppermute(send, axis, pairs)  36.9 us
    all_to_all x1, waiting for transfers between devices, body(): gathered = lax.all_to_all(copies, ('x', 'y'), 2, 4, tiled=True)  25 us
    ppermute x1, starting transfers between devices, body(): other = lax.ppermute(permuted, 'zh', shift_pairs(2, 1))  16.3 us
    ppermute x3, starting transfers between devices, halving_scatter(): shaped = keep + lax.ppermute(send, axis, pairs)  16 us
    pallas_call x1, Pallas kernels, contract(): pl.pallas_call(contract_kernel, out_shape=jax.ShapeDtypeStruct((2, rows,...  10.2 us
    ppermute x1, starting transfers between devices, body(): mine = mine + lax.ppermute(theirs, 'core', shift_pairs(2, 1))  7.91 us
    all_to_all x1, starting transfers between devices, body(): gathered = lax.all_to_all(copies, ('x', 'y'), 2, 4, tiled=True)  6.75 us
  transfers between devices with their start and end apart: 6, of which 6 were waited for; matrix products, arithmetic and copies ran while one was open for 0% of the time, Pallas kernels for 0%

profile of v6, /device:TPU:1, one launch (start us, length us, event | category | flops | bytes accessed | tf_op | source)
XLA Modules:
  0.0 133.9 jit_solution(16896589645436677604)
XLA Ops:
  0.0 0.8 fusion.5
  0.8 0.8 fusion.6
  1.6 0.3 fusion
  2.0 0.3 fusion.1
  2.4 16.3 %collective-permute-start = (bf16[2,2,16,512]{3,1,2,0:T(2,128)(2,1)S(1)}, bf16[2,2,16,512]{3,1,2,0:T(2,128)(2,1)S(1)}, u32[]{:S(2)}, u32[]{:S(2)}) collective-permute-start(bf16[2,2,16,512]{3,1,2,0:T(2,128)(2,1)S(1)} %bitcast.47), channel_id=1, source_target_pairs={{0,16},{16,0},{1,17},{17,1},{2,18},{18,2},{3,19},{19,3},{4,20},{20... | collective-permute-start | bytes 196616 | tf_op jit(solution)/shard_map/ppermute | solution.py:99
  18.6 1.8 %collective-permute-done = bf16[2,2,16,512]{3,1,2,0:T(2,128)(2,1)S(1)} collective-permute-done((bf16[2,2,16,512]{3,1,2,0:T(2,128)(2,1)S(1)}, bf16[2,2,16,512]{3,1,2,0:T(2,128)(2,1)S(1)}, u32[]{:S(2)}, u32[]{:S(2)}) %collective-permute-start) | collective-permute-done | bytes 65568 | tf_op jit(solution)/shard_map/ppermute | solution.py:99
  20.5 0.2 broadcast_select_fusion
  20.7 1.6 %broadcast_in_dim.2 = bf16[2,2,16,2,16,512]{5,4,3,1,0,2:T(8,128)(2,1)} broadcast(bf16[2,2,2,16,512]{4,3,2,1,0:T(8,128)(2,1)S(1)} %copy.8), dimensions={0,1,3,4,5} | broadcast | bytes 2228224 | tf_op jit(solution)/shard_map/broadcast_in_dim | solution.py:103
  22.3 6.8 %all-to-all-start = ((bf16[2,2,16,2,16,512]{5,4,3,1,0,2:T(8,128)(2,1)}), bf16[2,2,16,2,16,512]{5,4,3,1,0,2:T(8,128)(2,1)S(1)}, u32[]{:S(2)}, u32[]{:S(2)}) async-start(bf16[2,2,16,2,16,512]{5,4,3,1,0,2:T(8,128)(2,1)} %broadcast_in_dim.2), calls=%async_computation | async-start | bytes 4194304 | tf_op jit(solution)/shard_map/all_to_all | solution.py:104
  29.1 25.0 %all-to-all-done = bf16[2,2,16,2,16,512]{5,4,3,1,0,2:T(8,128)(2,1)S(1)} async-done(((bf16[2,2,16,2,16,512]{5,4,3,1,0,2:T(8,128)(2,1)}), bf16[2,2,16,2,16,512]{5,4,3,1,0,2:T(8,128)(2,1)S(1)}, u32[]{:S(2)}, u32[]{:S(2)}) %all-to-all-start) | async-done | bytes 2097184 | tf_op jit(solution)/shard_map/all_to_all | solution.py:104
  54.1 1.6 %copy.9 = bf16[2,2,1,2,16,16,512]{6,5,4,3,1,0,2:T(8,128)(2,1)} copy(bf16[2,2,1,2,16,16,512]{6,5,3,1,0,4,2:T(8,128)(2,1)S(1)} %bitcast.41) | data formatting | bytes 4194304 | tf_op jit(solution)/shard_map/all_to_all | solution.py:104
  55.7 10.2 %shard_map.46 = f32[2,512,512]{2,1,0:T(8,128)} custom-call(bf16[2,512,2,512]{3,2,1,0:T(2,128)(2,1)} %s_ref.1, bf16[2,2,512,512]{3,2,1,0:T(8,128)(2,1)} %bitcast.44, bf16[2,512,2,512]{3,2,1,0:T(2,128)(2,1)} %o_ref.1), custom_call_target="tpu_custom_call" | custom-call | flops 2147483648 | bytes 8388608 | tf_op jit(solution)/shard_map/pallas_call | solution.py:67
  65.8 0.0 copy-start
  65.8 1.5 %dynamic-slice_bitcast_fusion = f32[2,8,32,512]{3,2,1,0:T(8,128)S(1)} fusion(f32[2,8,2,32,512]{4,3,2,1,0:T(8,128)} %bitcast.42, s32[]{:T(128)S(6)} %select_n.43), kind=kLoop, calls=%fused_computation.5 | loop fusion | bytes 2097156 | tf_op jit(solution)/shard_map/jit(dynamic_index_in_dim)/squeeze | solution.py:114
  67.3 7.9 %collective-permute-start.1 = (f32[2,8,32,512]{3,2,1,0:T(8,128)S(1)}, f32[2,8,32,512]{3,2,1,0:T(8,128)}, u32[]{:S(2)}, u32[]{:S(2)}) collective-permute-start(f32[2,8,32,512]{3,2,1,0:T(8,128)S(1)} %dynamic-slice_bitcast_fusion), channel_id=1, source_target_pairs={{0,32},{32,0},{1,33},{33,1},{2,34},{34,2},{3,35},{35,3},{4,36},{36... | collective-permute-start | bytes 3145736 | tf_op jit(solution)/shard_map/ppermute | solution.py:115
  75.2 2.4 %collective-permute-done.1 = f32[2,8,32,512]{3,2,1,0:T(8,128)} collective-permute-done((f32[2,8,32,512]{3,2,1,0:T(8,128)S(1)}, f32[2,8,32,512]{3,2,1,0:T(8,128)}, u32[]{:S(2)}, u32[]{:S(2)}) %collective-permute-start.1) | collective-permute-done | bytes 1048608 | tf_op jit(solution)/shard_map/ppermute | solution.py:115
  77.6 0.0 copy-done
  77.6 1.4 %bitcast_add_fusion = f32[2,8,32,512]{3,2,1,0:T(8,128)S(1)} fusion(f32[2,8,32,512]{3,2,1,0:T(8,128)} %collective-permute-done.1, f32[2,8,2,32,512]{4,3,2,1,0:T(8,128)S(1)} %bitcast.43, s32[]{:T(128)S(6)} %select_n.42), kind=kLoop, calls=%fused_computation.4 | loop fusion | flops 262144 | bytes 3145732 | tf_op jit(solution)/shard_map/add | solution.py:115
  79.0 0.1 constant_dynamic-slice_fusion.1
  79.1 0.4 copy.14
  79.6 2.4 %collective-permute-start.2 = (f32[2,2,2,32,512]{4,0,3,1,2:T(2,128)S(1)}, f32[2,2,2,32,512]{4,0,3,1,2:T(2,128)S(1)}, u32[]{:S(2)}, u32[]{:S(2)}) collective-permute-start(f32[2,2,2,32,512]{4,0,3,1,2:T(2,128)S(1)} %bitcast.46), channel_id=1, source_target_pairs={{0,64},{64,0},{128,192},{192,128},{256,320},{320,256},{384,448},{4... | collective-permute-start | bytes 1572872 | tf_op jit(solution)/shard_map/ppermute | solution.py:91
  82.0 12.6 %collective-permute-done.2 = f32[2,2,2,32,512]{4,0,3,1,2:T(2,128)S(1)} collective-permute-done((f32[2,2,2,32,512]{4,0,3,1,2:T(2,128)S(1)}, f32[2,2,2,32,512]{4,0,3,1,2:T(2,128)S(1)}, u32[]{:S(2)}, u32[]{:S(2)}) %collective-permute-start.2) | collective-permute-done | bytes 524320 | tf_op jit(solution)/shard_map/ppermute | solution.py:91
  94.6 0.5 bitcast_add_fusion.1
  95.2 3.0 %collective-permute-start.3 = (f32[2,2,32,512]{3,0,2,1:T(2,128)S(1)}, f32[2,2,32,512]{3,0,2,1:T(2,128)S(1)}, u32[]{:S(2)}, u32[]{:S(2)}) collective-permute-start(f32[2,2,32,512]{3,0,2,1:T(2,128)S(1)} %dynamic-slice_bitcast_fusion.1), channel_id=1, source_target_pairs={{0,128},{64,192},{128,0},{192,64},{256,384},{320,448},{384,256},{4... | collective-permute-start | bytes 786440 | tf_op jit(solution)/shard_map/ppermute | solution.py:91
  98.2 13.4 %collective-permute-done.3 = f32[2,2,32,512]{3,0,2,1:T(2,128)S(1)} collective-permute-done((f32[2,2,32,512]{3,0,2,1:T(2,128)S(1)}, f32[2,2,32,512]{3,0,2,1:T(2,128)S(1)}, u32[]{:S(2)}, u32[]{:S(2)}) %collective-permute-start.3) | collective-permute-done | bytes 262176 | tf_op jit(solution)/shard_map/ppermute | solution.py:91
  111.6 0.1 bitcast_add_fusion.2
  111.7 10.6 %collective-permute-start.4 = (f32[2,32,512]{2,0,1:T(2,128)S(1)}, f32[2,32,512]{2,0,1:T(2,128)S(1)}, u32[]{:S(2)}, u32[]{:S(2)}) collective-permute-start(f32[2,32,512]{2,0,1:T(2,128)S(1)} %dynamic-slice_bitcast_fusion.2), channel_id=1, source_target_pairs={{0,256},{64,320},{128,384},{192,448},{256,0},{320,64},{384,128},{4... | collective-permute-start | bytes 393224 | tf_op jit(solution)/shard_map/ppermute | solution.py:91
  122.3 10.8 %collective-permute-done.4 = f32[2,32,512]{2,0,1:T(2,128)S(1)} collective-permute-done((f32[2,32,512]{2,0,1:T(2,128)S(1)}, f32[2,32,512]{2,0,1:T(2,128)S(1)}, u32[]{:S(2)}, u32[]{:S(2)}) %collective-permute-start.4) | collective-permute-done | bytes 131104 | tf_op jit(solution)/shard_map/ppermute | solution.py:91
  133.2 0.7 fusion.4
  (9 shorter events, 0.2 us)
Async XLA Ops:
  2.4 18.1 %collective-permute-start = (bf16[2,2,16,512]{3,1,2,0:T(2,128)(2,1)S(1)}, bf16[2,2,16,512]{3,1,2,0:T(2,128)(2,1)S(1)}, u32[]{:S(2)}, u32[]{:S(2)}) collective-permute-start(bf16[2,2,16,512]{3,1,2,0:T(2,128)(2,1)S(1)} %bitcast.47), channel_id=1, source_target_pairs={{0,16},{16,0},{1,17},{17,1},{2,18},{18,2},{3,19},{19,3},{4,20},{20... | collective-permute-start | bytes 196616 | tf_op jit(solution)/shard_map/ppermute | solution.py:99
  22.3 31.8 %all-to-all-start = ((bf16[2,2,16,2,16,512]{5,4,3,1,0,2:T(8,128)(2,1)}), bf16[2,2,16,2,16,512]{5,4,3,1,0,2:T(8,128)(2,1)S(1)}, u32[]{:S(2)}, u32[]{:S(2)}) async-start(bf16[2,2,16,2,16,512]{5,4,3,1,0,2:T(8,128)(2,1)} %broadcast_in_dim.2), calls=%async_computation | async-start | bytes 4194304 | tf_op jit(solution)/shard_map/all_to_all | solution.py:104
  65.8 11.8 %copy-start = (f32[2,512,512]{2,1,0:T(8,128)S(1)}, f32[2,512,512]{2,1,0:T(8,128)}, u32[]{:S(2)}) copy-start(f32[2,512,512]{2,1,0:T(8,128)} %shard_map.46) | copy-start | bytes 6291460
  67.3 10.3 %collective-permute-start.1 = (f32[2,8,32,512]{3,2,1,0:T(8,128)S(1)}, f32[2,8,32,512]{3,2,1,0:T(8,128)}, u32[]{:S(2)}, u32[]{:S(2)}) collective-permute-start(f32[2,8,32,512]{3,2,1,0:T(8,128)S(1)} %dynamic-slice_bitcast_fusion), channel_id=1, source_target_pairs={{0,32},{32,0},{1,33},{33,1},{2,34},{34,2},{3,35},{35,3},{4,36},{36... | collective-permute-start | bytes 3145736 | tf_op jit(solution)/shard_map/ppermute | solution.py:115
  79.6 15.0 %collective-permute-start.2 = (f32[2,2,2,32,512]{4,0,3,1,2:T(2,128)S(1)}, f32[2,2,2,32,512]{4,0,3,1,2:T(2,128)S(1)}, u32[]{:S(2)}, u32[]{:S(2)}) collective-permute-start(f32[2,2,2,32,512]{4,0,3,1,2:T(2,128)S(1)} %bitcast.46), channel_id=1, source_target_pairs={{0,64},{64,0},{128,192},{192,128},{256,320},{320,256},{384,448},{4... | collective-permute-start | bytes 1572872 | tf_op jit(solution)/shard_map/ppermute | solution.py:91
  95.2 16.4 %collective-permute-start.3 = (f32[2,2,32,512]{3,0,2,1:T(2,128)S(1)}, f32[2,2,32,512]{3,0,2,1:T(2,128)S(1)}, u32[]{:S(2)}, u32[]{:S(2)}) collective-permute-start(f32[2,2,32,512]{3,0,2,1:T(2,128)S(1)} %dynamic-slice_bitcast_fusion.1), channel_id=1, source_target_pairs={{0,128},{64,192},{128,0},{192,64},{256,384},{320,448},{384,256},{4... | collective-permute-start | bytes 786440 | tf_op jit(solution)/shard_map/ppermute | solution.py:91
  111.7 21.4 %collective-permute-start.4 = (f32[2,32,512]{2,0,1:T(2,128)S(1)}, f32[2,32,512]{2,0,1:T(2,128)S(1)}, u32[]{:S(2)}, u32[]{:S(2)}) collective-permute-start(f32[2,32,512]{2,0,1:T(2,128)S(1)} %dynamic-slice_bitcast_fusion.2), channel_id=1, source_target_pairs={{0,256},{64,320},{128,384},{192,448},{256,0},{320,64},{384,128},{4... | collective-permute-start | bytes 393224 | tf_op jit(solution)/shard_map/ppermute | solution.py:91

commit v7 on v5

--- a/solution.py
+++ b/solution.py
@@ -59,19 +59,20 @@
             out_ref[1] += im
 
 
-def contract(stem_t, branch_t, open_t):
-    slices, _, rows, width = stem_t.shape
+def contract(stem_t, branch_t, open_t, column_block):
+    slices, _, rows, depth = stem_t.shape
+    width = branch_t.shape[-1]
     tile = min(ROW_TILE, rows)
-    flops = slices * 8 * rows * width * width
-    moved = 2 * (stem_t.size + branch_t.size + open_t.size) + 4 * 2 * rows * width
+    flops = slices * 8 * rows * depth * width
+    moved = 2 * (stem_t.size + branch_t.size) + 2 * slices * 2 * rows * width + 4 * 2 * rows * width
     return pl.pallas_call(
         contract_kernel,
         out_shape=jax.ShapeDtypeStruct((2, rows, width), jnp.float32),
         grid=(rows // tile,),
         in_specs=[
-            pl.BlockSpec((slices, 2, tile, width), lambda i: (0, 0, i, 0)),
-            pl.BlockSpec((slices, 2, width, width), lambda i: (0, 0, 0, 0)),
-            pl.BlockSpec((slices, 2, tile, width), lambda i: (0, 0, i, 0)),
+            pl.BlockSpec((slices, 2, tile, depth), lambda i: (0, 0, i, 0)),
+            pl.BlockSpec((slices, 2, depth, width), lambda i: (0, 0, 0, 0)),
+            pl.BlockSpec((slices, 2, tile, width), lambda i: (0, 0, i, column_block)),
         ],
         out_specs=pl.BlockSpec((2, tile, width), lambda i: (0, i, 0)),
         cost_estimate=pl.CostEstimate(flops=flops, bytes_accessed=moved, transcendentals=0),
@@ -102,22 +103,32 @@
     plane = lax.axis_size("x") * lax.axis_size("y")
     copies = jnp.broadcast_to(pair[:, :, None], pair.shape[:2] + (plane,) + pair.shape[2:])
     copies = copies.reshape(slice_count, 2, plane, -1, width)
-    gathered = lax.all_to_all(copies, ("x", "y"), 2, 2, tiled=True)
-    branch_t = gathered.reshape(slice_count, 2, -1, width)
+    halves = 2
+    span = width // halves
     x_count = lax.axis_size("x")
     y_count = lax.axis_size("y")
     stem6 = stem_tensor.reshape(slice_count, row_count, 2, 2, x_count, y_count, -1)
     stem_t = jnp.transpose(stem6, (0, 2, 1, 4, 5, 3, 6)).reshape(slice_count, 2, row_count, width)
     open_t = jnp.transpose(open_tensor, (0, 2, 1, 3))
-    local_sum = contract(stem_t, branch_t, open_t)
     zl_count = lax.axis_size("zl")
     block_rows = row_count // (zl_count * 2)
-    shaped = local_sum.reshape(2, zl_count, 2, block_rows, width)
     core = lax.axis_index("core")
-    mine = lax.dynamic_index_in_dim(shaped, core, 2, keepdims=False)
-    theirs = lax.dynamic_index_in_dim(shaped, 1 - core, 2, keepdims=False)
-    mine = mine + lax.ppermute(theirs, "core", shift_pairs(2, 1))
-    result = halving_scatter(mine, "zl")
+    results = []
+    previous = None
+    for h in range(halves):
+        part = copies[..., h * span:(h + 1) * span]
+        if previous is not None:
+            part, previous = lax.optimization_barrier((part, previous))
+        gathered = lax.all_to_all(part, ("x", "y"), 2, 2, tiled=True)
+        previous = gathered
+        branch_t = gathered.reshape(slice_count, 2, -1, span)
+        local_sum = contract(stem_t, branch_t, open_t, h)
+        shaped = local_sum.reshape(2, zl_count, 2, block_rows, span)
+        mine = lax.dynamic_index_in_dim(shaped, core, 2, keepdims=False)
+        theirs = lax.dynamic_index_in_dim(shaped, 1 - core, 2, keepdims=False)
+        mine = mine + lax.ppermute(theirs, "core", shift_pairs(2, 1))
+        results.append(halving_scatter(mine, "zl"))
+    result = jnp.concatenate(results, axis=-1)
     return jnp.transpose(result, (1, 0, 2)).reshape(1, block_rows, 2, width)
 
 

time: 130 us -> 128 us (0.985)
  the two profiles are of different devices: /device:TPU:1 before, /device:TPU:2 now
where the time goes in v7:
time: 128 us; the launch traced here: 127 us
  starting transfers between devices  55.6 us (43%)
  local copies, waits for them, and re-layouts  21.7 us (17%)
  blocking collectives  19.7 us (15%)
  waiting for transfers between devices  19.5 us (15%)
  Pallas kernels  8.28 us (6%)
  other arithmetic  1.63 us (1%)
    ppermute x6, starting transfers between devices, halving_scatter(): shaped = keep + lax.ppermute(send, axis, pairs)  29.9 us
    all_to_all x1, blocking collectives, body(): gathered = lax.all_to_all(part, ('x', 'y'), 2, 2, tiled=True)  19.7 us
    ppermute x1, starting transfers between devices, body(): other = lax.ppermute(permuted, 'zh', shift_pairs(2, 1))  15.7 us
    ppermute x6, waiting for transfers between devices, halving_scatter(): shaped = keep + lax.ppermute(send, axis, pairs)  13.6 us
    pallas_call x2, Pallas kernels, contract(): pl.pallas_call(contract_kernel, out_shape=jax.ShapeDtypeStruct((2, rows,...  8.28 us
    unnamed x11, local copies, waits for them, and re-layouts  7.97 us
    all_to_all x1, starting transfers between devices, body(): gathered = lax.all_to_all(part, ('x', 'y'), 2, 2, tiled=True)  5.72 us
    ppermute x2, starting transfers between devices, body(): mine = mine + lax.ppermute(theirs, 'core', shift_pairs(2, 1))  4.3 us
  transfers between devices with their start and end apart: 10, of which 7 were waited for; matrix products, arithmetic and copies ran while one was open for 15% of the time, Pallas kernels for 7%

profile of v7, /device:TPU:2, one launch (start us, length us, event | category | flops | bytes accessed | tf_op | source)
XLA Modules:
  0.0 127.3 jit_solution(17915134631443638884)
XLA Ops:
  0.0 0.8 fusion.6
  0.8 0.8 fusion.5
  1.6 0.3 fusion.1
  2.0 0.3 fusion
  2.3 15.7 %collective-permute-start = (bf16[2,2,16,512]{3,2,1,0:T(8,128)(2,1)S(1)}, bf16[2,2,16,512]{3,2,1,0:T(8,128)(2,1)S(1)}, u32[]{:S(2)}, u32[]{:S(2)}) collective-permute-start(bf16[2,2,16,512]{3,2,1,0:T(8,128)(2,1)S(1)} %bitcast.79), channel_id=1, source_target_pairs={{0,16},{16,0},{1,17},{17,1},{2,18},{18,2},{3,19},{19,3},{4,20},{20... | collective-permute-start | bytes 196616 | tf_op jit(solution)/shard_map/ppermute | solution.py:100
  18.0 4.2 %collective-permute-done = bf16[2,2,16,512]{3,2,1,0:T(8,128)(2,1)S(1)} collective-permute-done((bf16[2,2,16,512]{3,2,1,0:T(8,128)(2,1)S(1)}, bf16[2,2,16,512]{3,2,1,0:T(8,128)(2,1)S(1)}, u32[]{:S(2)}, u32[]{:S(2)}) %collective-permute-start) | collective-permute-done | bytes 65568 | tf_op jit(solution)/shard_map/ppermute | solution.py:100
  22.3 0.1 broadcast_in_dim.8
  22.4 19.7 %all_to_all.10 = bf16[2,2,16,32,256]{4,3,1,0,2:T(8,128)(2,1)} all-to-all(bf16[2,2,16,32,256]{4,3,1,0,2:T(8,128)(2,1)S(1)} %broadcast_in_dim.8), channel_id=1, replica_groups=mesh['zl'=8,'core'=2,'zh'=2,'x'=4,'y'=4] {'x','y'}, dimensions={2} | all-to-all | bytes 2097152 | tf_op jit(solution)/shard_map/all_to_all | solution.py:122
  42.1 1.1 broadcast_in_dim.9
  43.2 5.7 %all-to-all-start.1 = ((bf16[2,2,16,32,256]{4,3,1,0,2:T(8,128)(2,1)}), bf16[2,2,16,32,256]{4,3,1,0,2:T(8,128)(2,1)S(1)}, u32[]{:S(2)}, u32[]{:S(2)}) async-start(bf16[2,2,16,32,256]{4,3,1,0,2:T(8,128)(2,1)} %broadcast_in_dim.9), calls=%async_computation.1 | async-start | bytes 2097152 | tf_op jit(solution)/shard_map/all_to_all | solution.py:122
  49.0 4.6 %copy.22 = bf16[2,512,2,512]{1,3,2,0:T(8,128)(2,1)} copy(bf16[2,512,2,512]{3,2,1,0:T(2,128)(2,1)S(1)} %copy-done.3) | data formatting | bytes 4194304 | tf_op args[0]
  53.6 1.8 %copy.23 = bf16[2,2,512,4,4,2,16]{2,6,5,4,3,1,0:T(8,128)(2,1)S(1)} copy(bf16[2,2,512,4,4,2,16]{2,6,4,3,5,1,0:T(8,128)(2,1)} %bitcast.67) | data formatting | bytes 4194304 | tf_op jit(solution)/shard_map/transpose | solution.py:111
  55.4 2.4 %copy.28.s_ref = bf16[2,2,512,512]{3,2,1,0:T(8,128)(2,1)} copy(bf16[2,2,512,512]{2,3,1,0:T(8,128)(2,1)S(1)} %bitcast.66) | data formatting | bytes 4194304 | tf_op jit(solution)/shard_map/reshape | solution.py:111
  57.8 3.3 %copy.42 = bf16[2,512,2,512]{3,1,2,0:T(8,128)(2,1)} copy(bf16[2,512,2,512]{3,2,1,0:T(2,128)(2,1)} %param.6) | data formatting | bytes 4194304 | tf_op args[2]
  61.2 1.1 copy.26
  62.2 4.1 %shard_map.46 = f32[2,512,256]{2,1,0:T(8,128)} custom-call(bf16[2,2,512,512]{3,2,1,0:T(8,128)(2,1)} %copy.28.s_ref, bf16[2,2,512,256]{3,2,1,0:T(8,128)(2,1)} %bitcast.73, bf16[2,2,512,512]{3,2,1,0:T(8,128)(2,1)} %bitcast.64), custom_call_target="tpu_custom_call" | custom-call | flops 1073741824 | bytes 5242880 | tf_op jit(solution)/shard_map/pallas_call | solution.py:68
  66.3 1.9 %dynamic-slice_bitcast_fusion.1 = f32[2,8,32,256]{3,2,1,0:T(8,128)} fusion(f32[2,8,2,32,256]{4,3,2,1,0:T(8,128)} %bitcast.68, s32[]{:T(128)S(6)} %select_n.55), kind=kLoop, calls=%fused_computation.10 | loop fusion | bytes 1048580 | tf_op jit(solution)/shard_map/jit(dynamic_index_in_dim)/squeeze | solution.py:128
  68.2 1.9 %collective-permute-start.1 = (f32[2,8,32,256]{3,2,1,0:T(8,128)}, f32[2,8,32,256]{3,2,1,0:T(8,128)S(1)}, u32[]{:S(2)}, u32[]{:S(2)}) collective-permute-start(f32[2,8,32,256]{3,2,1,0:T(8,128)} %dynamic-slice_bitcast_fusion.1), channel_id=1, source_target_pairs={{0,32},{32,0},{1,33},{33,1},{2,34},{34,2},{3,35},{35,3},{4,36},{36... | collective-permute-start | bytes 1572872 | tf_op jit(solution)/shard_map/ppermute | solution.py:129
  70.1 0.0 all-to-all-done.1
  70.1 1.1 copy.31
  71.2 4.2 %shard_map.47 = f32[2,512,256]{2,1,0:T(8,128)} custom-call(bf16[2,2,512,512]{3,2,1,0:T(8,128)(2,1)} %copy.28.s_ref, bf16[2,2,512,256]{3,2,1,0:T(8,128)(2,1)} %bitcast.72, bf16[2,2,512,512]{3,2,1,0:T(8,128)(2,1)} %bitcast.65), custom_call_target="tpu_custom_call" | custom-call | flops 1073741824 | bytes 5242880 | tf_op jit(solution)/shard_map/pallas_call | solution.py:68
  75.4 2.0 %dynamic-slice_bitcast_fusion = f32[2,8,32,256]{3,2,1,0:T(8,128)} fusion(f32[2,8,2,32,256]{4,3,2,1,0:T(8,128)} %bitcast.70, s32[]{:T(128)S(6)} %select_n.55), kind=kLoop, calls=%fused_computation.9 | loop fusion | bytes 1048580 | tf_op jit(solution)/shard_map/jit(dynamic_index_in_dim)/squeeze | solution.py:128
  77.4 2.4 %collective-permute-start.5 = (f32[2,8,32,256]{3,2,1,0:T(8,128)}, f32[2,8,32,256]{3,2,1,0:T(8,128)S(1)}, u32[]{:S(2)}, u32[]{:S(2)}) collective-permute-start(f32[2,8,32,256]{3,2,1,0:T(8,128)} %dynamic-slice_bitcast_fusion), channel_id=1, source_target_pairs={{0,32},{32,0},{1,33},{33,1},{2,34},{34,2},{3,35},{35,3},{4,36},{36... | collective-permute-start | bytes 1572872 | tf_op jit(solution)/shard_map/ppermute | solution.py:129
  79.8 0.0 collective-permute-done.1
  79.8 0.0 copy-done.1
  79.8 0.1 bitcast_add_fusion.1
  79.9 1.6 %collective-permute-done.5 = f32[2,8,32,256]{3,2,1,0:T(8,128)S(1)} collective-permute-done((f32[2,8,32,256]{3,2,1,0:T(8,128)}, f32[2,8,32,256]{3,2,1,0:T(8,128)S(1)}, u32[]{:S(2)}, u32[]{:S(2)}) %collective-permute-start.5) | collective-permute-done | bytes 524320 | tf_op jit(solution)/shard_map/ppermute | solution.py:129
  81.5 0.1 bitcast_add_fusion
  81.6 0.1 constant_dynamic-slice_fusion.1
  81.7 0.2 copy.44
  81.9 2.7 %collective-permute-start.2 = (f32[2,2,2,32,256]{4,0,3,1,2:T(2,128)S(1)}, f32[2,2,2,32,256]{4,0,3,1,2:T(2,128)S(1)}, u32[]{:S(2)}, u32[]{:S(2)}) collective-permute-start(f32[2,2,2,32,256]{4,0,3,1,2:T(2,128)S(1)} %bitcast.77), channel_id=1, source_target_pairs={{0,64},{64,0},{128,192},{192,128},{256,320},{320,256},{384,448},{4... | collective-permute-start | bytes 786440 | tf_op jit(solution)/shard_map/ppermute | solution.py:92
  84.7 0.2 copy.43
  84.9 3.1 %collective-permute-start.6 = (f32[2,2,2,32,256]{4,0,3,1,2:T(2,128)S(1)}, f32[2,2,2,32,256]{4,0,3,1,2:T(2,128)S(1)}, u32[]{:S(2)}, u32[]{:S(2)}) collective-permute-start(f32[2,2,2,32,256]{4,0,3,1,2:T(2,128)S(1)} %bitcast.78), channel_id=1, source_target_pairs={{0,64},{64,0},{128,192},{192,128},{256,320},{320,256},{384,448},{4... | collective-permute-start | bytes 786440 | tf_op jit(solution)/shard_map/ppermute | solution.py:92
  88.0 4.9 %collective-permute-done.2 = f32[2,2,2,32,256]{4,0,3,1,2:T(2,128)S(1)} collective-permute-done((f32[2,2,2,32,256]{4,0,3,1,2:T(2,128)S(1)}, f32[2,2,2,32,256]{4,0,3,1,2:T(2,128)S(1)}, u32[]{:S(2)}, u32[]{:S(2)}) %collective-permute-start.2) | collective-permute-done | bytes 262176 | tf_op jit(solution)/shard_map/ppermute | solution.py:92
  93.0 0.3 bitcast_add_fusion.3
  93.2 3.3 %collective-permute-start.3 = (f32[2,2,32,256]{3,0,2,1:T(2,128)S(1)}, f32[2,2,32,256]{3,0,2,1:T(2,128)S(1)}, u32[]{:S(2)}, u32[]{:S(2)}) collective-permute-start(f32[2,2,32,256]{3,0,2,1:T(2,128)S(1)} %dynamic-slice_bitcast_fusion.3), channel_id=1, source_target_pairs={{0,128},{64,192},{128,0},{192,64},{256,384},{320,448},{384,256},{4... | collective-permute-start | bytes 393224 | tf_op jit(solution)/shard_map/ppermute | solution.py:92
  96.6 2.5 %collective-permute-done.6 = f32[2,2,2,32,256]{4,0,3,1,2:T(2,128)S(1)} collective-permute-done((f32[2,2,2,32,256]{4,0,3,1,2:T(2,128)S(1)}, f32[2,2,2,32,256]{4,0,3,1,2:T(2,128)S(1)}, u32[]{:S(2)}, u32[]{:S(2)}) %collective-permute-start.6) | collective-permute-done | bytes 262176 | tf_op jit(solution)/shard_map/ppermute | solution.py:92
  99.0 0.3 bitcast_add_fusion.2
  99.3 2.8 %collective-permute-start.7 = (f32[2,2,32,256]{3,0,2,1:T(2,128)S(1)}, f32[2,2,32,256]{3,0,2,1:T(2,128)S(1)}, u32[]{:S(2)}, u32[]{:S(2)}) collective-permute-start(f32[2,2,32,256]{3,0,2,1:T(2,128)S(1)} %dynamic-slice_bitcast_fusion.2), channel_id=1, source_target_pairs={{0,128},{64,192},{128,0},{192,64},{256,384},{320,448},{384,256},{4... | collective-permute-start | bytes 393224 | tf_op jit(solution)/shard_map/ppermute | solution.py:92
  102.2 1.1 collective-permute-done.3
  103.3 0.1 bitcast_add_fusion.5
  103.3 12.3 %collective-permute-start.4 = (f32[2,32,256]{2,0,1:T(2,128)S(1)}, f32[2,32,256]{2,0,1:T(2,128)S(1)}, u32[]{:S(2)}, u32[]{:S(2)}) collective-permute-start(f32[2,32,256]{2,0,1:T(2,128)S(1)} %dynamic-slice_bitcast_fusion.5), channel_id=1, source_target_pairs={{0,256},{64,320},{128,384},{192,448},{256,0},{320,64},{384,128},{4... | collective-permute-start | bytes 196616 | tf_op jit(solution)/shard_map/ppermute | solution.py:92
  115.7 0.0 collective-permute-done.7
  115.7 0.1 bitcast_add_fusion.4
  115.8 5.6 %collective-permute-start.8 = (f32[2,32,256]{2,0,1:T(2,128)S(1)}, f32[2,32,256]{2,0,1:T(2,128)S(1)}, u32[]{:S(2)}, u32[]{:S(2)}) collective-permute-start(f32[2,32,256]{2,0,1:T(2,128)S(1)} %dynamic-slice_bitcast_fusion.4), channel_id=1, source_target_pairs={{0,256},{64,320},{128,384},{192,448},{256,0},{320,64},{384,128},{4... | collective-permute-start | bytes 196616 | tf_op jit(solution)/shard_map/ppermute | solution.py:92
  121.4 0.6 collective-permute-done.4
  122.1 4.5 %collective-permute-done.8 = f32[2,32,256]{2,0,1:T(2,128)S(1)} collective-permute-done((f32[2,32,256]{2,0,1:T(2,128)S(1)}, f32[2,32,256]{2,0,1:T(2,128)S(1)}, u32[]{:S(2)}, u32[]{:S(2)}) %collective-permute-start.8) | collective-permute-done | bytes 65568 | tf_op jit(solution)/shard_map/ppermute | solution.py:92
  126.6 0.7 maximum_bitcast_fusion
  (21 shorter events, 0.3 us)
Async XLA Ops:
  2.3 19.9 %collective-permute-start = (bf16[2,2,16,512]{3,2,1,0:T(8,128)(2,1)S(1)}, bf16[2,2,16,512]{3,2,1,0:T(8,128)(2,1)S(1)}, u32[]{:S(2)}, u32[]{:S(2)}) collective-permute-start(bf16[2,2,16,512]{3,2,1,0:T(8,128)(2,1)S(1)} %bitcast.79), channel_id=1, source_target_pairs={{0,16},{16,0},{1,17},{17,1},{2,18},{18,2},{3,19},{19,3},{4,20},{20... | collective-permute-start | bytes 196616 | tf_op jit(solution)/shard_map/ppermute | solution.py:100
  42.1 6.9 %copy-start.3 = (bf16[2,512,2,512]{3,2,1,0:T(2,128)(2,1)S(1)}, bf16[2,512,2,512]{3,2,1,0:T(2,128)(2,1)}, u32[]{:S(2)}) copy-start(bf16[2,512,2,512]{3,2,1,0:T(2,128)(2,1)} %param.4) | copy-start | bytes 6291460
  43.2 26.9 %all-to-all-start.1 = ((bf16[2,2,16,32,256]{4,3,1,0,2:T(8,128)(2,1)}), bf16[2,2,16,32,256]{4,3,1,0,2:T(8,128)(2,1)S(1)}, u32[]{:S(2)}, u32[]{:S(2)}) async-start(bf16[2,2,16,32,256]{4,3,1,0,2:T(8,128)(2,1)} %broadcast_in_dim.9), calls=%async_computation.1 | async-start | bytes 2097152 | tf_op jit(solution)/shard_map/all_to_all | solution.py:122
  57.8 3.4 %copy-start = (bf16[2,2,16,32,256]{4,3,1,0,2:T(8,128)(2,1)S(1)}, bf16[2,2,16,32,256]{4,3,1,0,2:T(8,128)(2,1)}, u32[]{:S(2)}) copy-start(bf16[2,2,16,32,256]{4,3,1,0,2:T(8,128)(2,1)} %all_to_all.10) | copy-start | bytes 3145732
  68.2 11.6 %collective-permute-start.1 = (f32[2,8,32,256]{3,2,1,0:T(8,128)}, f32[2,8,32,256]{3,2,1,0:T(8,128)S(1)}, u32[]{:S(2)}, u32[]{:S(2)}) collective-permute-start(f32[2,8,32,256]{3,2,1,0:T(8,128)} %dynamic-slice_bitcast_fusion.1), channel_id=1, source_target_pairs={{0,32},{32,0},{1,33},{33,1},{2,34},{34,2},{3,35},{35,3},{4,36},{36... | collective-permute-start | bytes 1572872 | tf_op jit(solution)/shard_map/ppermute | solution.py:129
  71.2 8.6 %copy-start.1 = (f32[2,512,256]{2,1,0:T(8,128)S(1)}, f32[2,512,256]{2,1,0:T(8,128)}, u32[]{:S(2)}) copy-start(f32[2,512,256]{2,1,0:T(8,128)} %shard_map.46) | copy-start | bytes 3145732
  75.4 6.1 %copy-start.2 = (f32[2,512,256]{2,1,0:T(8,128)S(1)}, f32[2,512,256]{2,1,0:T(8,128)}, u32[]{:S(2)}) copy-start(f32[2,512,256]{2,1,0:T(8,128)} %shard_map.47) | copy-start | bytes 3145732
  77.4 4.1 %collective-permute-start.5 = (f32[2,8,32,256]{3,2,1,0:T(8,128)}, f32[2,8,32,256]{3,2,1,0:T(8,128)S(1)}, u32[]{:S(2)}, u32[]{:S(2)}) collective-permute-start(f32[2,8,32,256]{3,2,1,0:T(8,128)} %dynamic-slice_bitcast_fusion), channel_id=1, source_target_pairs={{0,32},{32,0},{1,33},{33,1},{2,34},{34,2},{3,35},{35,3},{4,36},{36... | collective-permute-start | bytes 1572872 | tf_op jit(solution)/shard_map/ppermute | solution.py:129
  81.9 11.0 %collective-permute-start.2 = (f32[2,2,2,32,256]{4,0,3,1,2:T(2,128)S(1)}, f32[2,2,2,32,256]{4,0,3,1,2:T(2,128)S(1)}, u32[]{:S(2)}, u32[]{:S(2)}) collective-permute-start(f32[2,2,2,32,256]{4,0,3,1,2:T(2,128)S(1)} %bitcast.77), channel_id=1, source_target_pairs={{0,64},{64,0},{128,192},{192,128},{256,320},{320,256},{384,448},{4... | collective-permute-start | bytes 786440 | tf_op jit(solution)/shard_map/ppermute | solution.py:92
  84.9 14.2 %collective-permute-start.6 = (f32[2,2,2,32,256]{4,0,3,1,2:T(2,128)S(1)}, f32[2,2,2,32,256]{4,0,3,1,2:T(2,128)S(1)}, u32[]{:S(2)}, u32[]{:S(2)}) collective-permute-start(f32[2,2,2,32,256]{4,0,3,1,2:T(2,128)S(1)} %bitcast.78), channel_id=1, source_target_pairs={{0,64},{64,0},{128,192},{192,128},{256,320},{320,256},{384,448},{4... | collective-permute-start | bytes 786440 | tf_op jit(solution)/shard_map/ppermute | solution.py:92
  93.2 10.0 %collective-permute-start.3 = (f32[2,2,32,256]{3,0,2,1:T(2,128)S(1)}, f32[2,2,32,256]{3,0,2,1:T(2,128)S(1)}, u32[]{:S(2)}, u32[]{:S(2)}) collective-permute-start(f32[2,2,32,256]{3,0,2,1:T(2,128)S(1)} %dynamic-slice_bitcast_fusion.3), channel_id=1, source_target_pairs={{0,128},{64,192},{128,0},{192,64},{256,384},{320,448},{384,256},{4... | collective-permute-start | bytes 393224 | tf_op jit(solution)/shard_map/ppermute | solution.py:92
  99.3 16.4 %collective-permute-start.7 = (f32[2,2,32,256]{3,0,2,1:T(2,128)S(1)}, f32[2,2,32,256]{3,0,2,1:T(2,128)S(1)}, u32[]{:S(2)}, u32[]{:S(2)}) collective-permute-start(f32[2,2,32,256]{3,0,2,1:T(2,128)S(1)} %dynamic-slice_bitcast_fusion.2), channel_id=1, source_target_pairs={{0,128},{64,192},{128,0},{192,64},{256,384},{320,448},{384,256},{4... | collective-permute-start | bytes 393224 | tf_op jit(solution)/shard_map/ppermute | solution.py:92
  103.3 18.7 %collective-permute-start.4 = (f32[2,32,256]{2,0,1:T(2,128)S(1)}, f32[2,32,256]{2,0,1:T(2,128)S(1)}, u32[]{:S(2)}, u32[]{:S(2)}) collective-permute-start(f32[2,32,256]{2,0,1:T(2,128)S(1)} %dynamic-slice_bitcast_fusion.5), channel_id=1, source_target_pairs={{0,256},{64,320},{128,384},{192,448},{256,0},{320,64},{384,128},{4... | collective-permute-start | bytes 196616 | tf_op jit(solution)/shard_map/ppermute | solution.py:92
  115.8 10.8 %collective-permute-start.8 = (f32[2,32,256]{2,0,1:T(2,128)S(1)}, f32[2,32,256]{2,0,1:T(2,128)S(1)}, u32[]{:S(2)}, u32[]{:S(2)}) collective-permute-start(f32[2,32,256]{2,0,1:T(2,128)S(1)} %dynamic-slice_bitcast_fusion.4), channel_id=1, source_target_pairs={{0,256},{64,320},{128,384},{192,448},{256,0},{320,64},{384,128},{4... | collective-permute-start | bytes 196616 | tf_op jit(solution)/shard_map/ppermute | solution.py:92

commit v8 on v7

--- a/solution.py
+++ b/solution.py
@@ -41,14 +41,14 @@
 def contract_kernel(s_ref, b_ref, o_ref, out_ref):
     f32 = jnp.float32
     for t in range(s_ref.shape[0]):
-        sr = s_ref[t, 0]
-        si = s_ref[t, 1]
+        sr = s_ref[t, :, 0, :]
+        si = s_ref[t, :, 1, :]
         br = b_ref[t, 0]
         bi = b_ref[t, 1]
         pr = jnp.dot(sr, br, preferred_element_type=f32) - jnp.dot(si, bi, preferred_element_type=f32)
         pi = jnp.dot(sr, bi, preferred_element_type=f32) + jnp.dot(si, br, preferred_element_type=f32)
-        o_r = o_ref[t, 0].astype(f32)
-        o_i = o_ref[t, 1].astype(f32)
+        o_r = o_ref[t, :, 0, :].astype(f32)
+        o_i = o_ref[t, :, 1, :].astype(f32)
         re = pr * o_r - pi * o_i
         im = pr * o_i + pi * o_r
         if t == 0:
@@ -60,7 +60,7 @@
 
 
 def contract(stem_t, branch_t, open_t, column_block):
-    slices, _, rows, depth = stem_t.shape
+    slices, rows, _, depth = stem_t.shape
     width = branch_t.shape[-1]
     tile = min(ROW_TILE, rows)
     flops = slices * 8 * rows * depth * width
@@ -70,9 +70,9 @@
         out_shape=jax.ShapeDtypeStruct((2, rows, width), jnp.float32),
         grid=(rows // tile,),
         in_specs=[
-            pl.BlockSpec((slices, 2, tile, depth), lambda i: (0, 0, i, 0)),
+            pl.BlockSpec((slices, tile, 2, depth), lambda i: (0, i, 0, 0)),
             pl.BlockSpec((slices, 2, depth, width), lambda i: (0, 0, 0, 0)),
-            pl.BlockSpec((slices, 2, tile, width), lambda i: (0, 0, i, column_block)),
+            pl.BlockSpec((slices, tile, 2, width), lambda i: (0, i, 0, column_block)),
         ],
         out_specs=pl.BlockSpec((2, tile, width), lambda i: (0, i, 0)),
         cost_estimate=pl.CostEstimate(flops=flops, bytes_accessed=moved, transcendentals=0),
@@ -102,14 +102,10 @@
     pair = jnp.where(low, jnp.stack([permuted, other], axis=2), jnp.stack([other, permuted], axis=2))
     plane = lax.axis_size("x") * lax.axis_size("y")
     copies = jnp.broadcast_to(pair[:, :, None], pair.shape[:2] + (plane,) + pair.shape[2:])
-    copies = copies.reshape(slice_count, 2, plane, -1, width)
     halves = 2
     span = width // halves
-    x_count = lax.axis_size("x")
-    y_count = lax.axis_size("y")
-    stem6 = stem_tensor.reshape(slice_count, row_count, 2, 2, x_count, y_count, -1)
-    stem_t = jnp.transpose(stem6, (0, 2, 1, 4, 5, 3, 6)).reshape(slice_count, 2, row_count, width)
-    open_t = jnp.transpose(open_tensor, (0, 2, 1, 3))
+    stem_t = stem_tensor
+    open_t = open_tensor
     zl_count = lax.axis_size("zl")
     block_rows = row_count // (zl_count * 2)
     core = lax.axis_index("core")
@@ -119,7 +115,7 @@
         part = copies[..., h * span:(h + 1) * span]
         if previous is not None:
             part, previous = lax.optimization_barrier((part, previous))
-        gathered = lax.all_to_all(part, ("x", "y"), 2, 2, tiled=True)
+        gathered = lax.all_to_all(part, ("x", "y"), 2, 4, tiled=True)
         previous = gathered
         branch_t = gathered.reshape(slice_count, 2, -1, span)
         local_sum = contract(stem_t, branch_t, open_t, h)

time: 128 us -> 128 us (level)
  the two profiles are of different devices: /device:TPU:2 before, /device:TPU:1 now
where the time goes in v8:
time: 128 us; the launch traced here: 125 us
  starting transfers between devices  70.4 us (55%)
  waiting for transfers between devices  24.6 us (19%)
  Pallas kernels  17.1 us (13%)
  local copies, waits for them, and re-layouts  10.7 us (8%)
  other arithmetic  1.82 us (1%)
    ppermute x6, starting transfers between devices, halving_scatter(): shaped = keep + lax.ppermute(send, axis, pairs)  31.9 us
    pallas_call x2, Pallas kernels, contract(): pl.pallas_call(contract_kernel, out_shape=jax.ShapeDtypeStruct((2, rows,...  17.1 us
    ppermute x1, starting transfers between devices, body(): other = lax.ppermute(permuted, 'zh', shift_pairs(2, 1))  16.3 us
    all_to_all x2, starting transfers between devices, body(): gathered = lax.all_to_all(part, ('x', 'y'), 2, 4, tiled=True)  13.7 us
    all_to_all x2, waiting for transfers between devices, body(): gathered = lax.all_to_all(part, ('x', 'y'), 2, 4, tiled=True)  10.7 us
    ppermute x6, waiting for transfers between devices, halving_scatter(): shaped = keep + lax.ppermute(send, axis, pairs)  10.4 us
    ppermute x2, starting transfers between devices, body(): mine = mine + lax.ppermute(theirs, 'core', shift_pairs(2, 1))  8.48 us
    squeeze x2, local copies, waits for them, and re-layouts, body(): theirs = lax.dynamic_index_in_dim(shaped, 1 - core, 2, keepdims=False)  3.87 us
  transfers between devices with their start and end apart: 11, of which 6 were waited for; matrix products, arithmetic and copies ran while one was open for 7% of the time, Pallas kernels for 14%

profile of v8, /device:TPU:1, one launch (start us, length us, event | category | flops | bytes accessed | tf_op | source)
XLA Modules:
  0.0 125.5 jit_solution(9058986863874085963)
XLA Ops:
  0.0 0.8 fusion.5
  0.8 0.8 fusion.6
  1.6 0.3 fusion
  2.0 0.3 fusion.1
  2.4 16.3 %collective-permute-start = (bf16[2,2,16,512]{3,1,2,0:T(2,128)(2,1)S(1)}, bf16[2,2,16,512]{3,1,2,0:T(2,128)(2,1)S(1)}, u32[]{:S(2)}, u32[]{:S(2)}) collective-permute-start(bf16[2,2,16,512]{3,1,2,0:T(2,128)(2,1)S(1)} %bitcast.74), channel_id=1, source_target_pairs={{0,16},{16,0},{1,17},{17,1},{2,18},{18,2},{3,19},{19,3},{4,20},{20... | collective-permute-start | bytes 196616 | tf_op jit(solution)/shard_map/ppermute | solution.py:100
  18.6 1.8 %collective-permute-done = bf16[2,2,16,512]{3,1,2,0:T(2,128)(2,1)S(1)} collective-permute-done((bf16[2,2,16,512]{3,1,2,0:T(2,128)(2,1)S(1)}, bf16[2,2,16,512]{3,1,2,0:T(2,128)(2,1)S(1)}, u32[]{:S(2)}, u32[]{:S(2)}) %collective-permute-start) | collective-permute-done | bytes 65568 | tf_op jit(solution)/shard_map/ppermute | solution.py:100
  20.5 0.2 broadcast_select_fusion
  20.7 0.1 fusion.4
  20.8 1.1 broadcast_in_dim.8
  21.9 6.8 %all-to-all-start = ((bf16[2,2,16,2,16,256]{5,4,3,1,0,2:T(8,128)(2,1)}), bf16[2,2,16,2,16,256]{5,4,3,1,0,2:T(8,128)(2,1)S(1)}, u32[]{:S(2)}, u32[]{:S(2)}) async-start(bf16[2,2,16,2,16,256]{5,4,3,1,0,2:T(8,128)(2,1)} %broadcast_in_dim.8), calls=%async_computation | async-start | bytes 2097152 | tf_op jit(solution)/shard_map/all_to_all | solution.py:118
  28.7 1.1 broadcast_in_dim.9
  29.8 10.7 %all-to-all-done = bf16[2,2,16,2,16,256]{5,4,3,1,0,2:T(8,128)(2,1)S(1)} async-done(((bf16[2,2,16,2,16,256]{5,4,3,1,0,2:T(8,128)(2,1)}), bf16[2,2,16,2,16,256]{5,4,3,1,0,2:T(8,128)(2,1)S(1)}, u32[]{:S(2)}, u32[]{:S(2)}) %all-to-all-start) | async-done | bytes 1048608 | tf_op jit(solution)/shard_map/all_to_all | solution.py:118
  40.5 6.9 %all-to-all-start.1 = ((bf16[2,2,16,2,16,256]{5,4,3,1,0,2:T(8,128)(2,1)}), bf16[2,2,16,2,16,256]{5,4,3,1,0,2:T(8,128)(2,1)S(1)}, u32[]{:S(2)}, u32[]{:S(2)}) async-start(bf16[2,2,16,2,16,256]{5,4,3,1,0,2:T(8,128)(2,1)} %broadcast_in_dim.9), calls=%async_computation.1 | async-start | bytes 2097152 | tf_op jit(solution)/shard_map/all_to_all | solution.py:118
  47.5 1.1 copy.12
  48.5 8.5 %shard_map.46 = f32[2,512,256]{2,1,0:T(8,128)} custom-call(bf16[2,512,2,512]{3,2,1,0:T(2,128)(2,1)} %s_ref.3, bf16[2,2,512,256]{3,2,1,0:T(8,128)(2,1)} %bitcast.68, bf16[2,512,2,512]{3,2,1,0:T(2,128)(2,1)} %o_ref.3), custom_call_target="tpu_custom_call" | custom-call | flops 1073741824 | bytes 5242880 | tf_op jit(solution)/shard_map/pallas_call | solution.py:68
  57.0 1.9 %dynamic-slice_bitcast_fusion.1 = f32[2,8,32,256]{3,2,1,0:T(8,128)} fusion(f32[2,8,2,32,256]{4,3,2,1,0:T(8,128)} %bitcast.64, s32[]{:T(128)S(6)} %select_n.51), kind=kLoop, calls=%fused_computation.9 | loop fusion | bytes 1048580 | tf_op jit(solution)/shard_map/jit(dynamic_index_in_dim)/squeeze | solution.py:124
  58.9 4.8 %collective-permute-start.1 = (f32[2,8,32,256]{3,2,1,0:T(8,128)}, f32[2,8,32,256]{3,2,1,0:T(8,128)S(1)}, u32[]{:S(2)}, u32[]{:S(2)}) collective-permute-start(f32[2,8,32,256]{3,2,1,0:T(8,128)} %dynamic-slice_bitcast_fusion.1), channel_id=1, source_target_pairs={{0,32},{32,0},{1,33},{33,1},{2,34},{34,2},{3,35},{35,3},{4,36},{36... | collective-permute-start | bytes 1572872 | tf_op jit(solution)/shard_map/ppermute | solution.py:125
  63.8 0.0 all-to-all-done.1
  63.8 1.1 copy.16
  64.8 8.6 %shard_map.47 = f32[2,512,256]{2,1,0:T(8,128)} custom-call(bf16[2,512,2,512]{3,2,1,0:T(2,128)(2,1)} %s_ref.3, bf16[2,2,512,256]{3,2,1,0:T(8,128)(2,1)} %bitcast.69, bf16[2,512,2,512]{3,2,1,0:T(2,128)(2,1)} %o_ref.3), custom_call_target="tpu_custom_call" | custom-call | flops 1073741824 | bytes 5242880 | tf_op jit(solution)/shard_map/pallas_call | solution.py:68
  73.5 2.0 %dynamic-slice_bitcast_fusion = f32[2,8,32,256]{3,2,1,0:T(8,128)} fusion(f32[2,8,2,32,256]{4,3,2,1,0:T(8,128)} %bitcast.66, s32[]{:T(128)S(6)} %select_n.51), kind=kLoop, calls=%fused_computation.8 | loop fusion | bytes 1048580 | tf_op jit(solution)/shard_map/jit(dynamic_index_in_dim)/squeeze | solution.py:124
  75.4 3.7 %collective-permute-start.5 = (f32[2,8,32,256]{3,2,1,0:T(8,128)}, f32[2,8,32,256]{3,2,1,0:T(8,128)S(1)}, u32[]{:S(2)}, u32[]{:S(2)}) collective-permute-start(f32[2,8,32,256]{3,2,1,0:T(8,128)} %dynamic-slice_bitcast_fusion), channel_id=1, source_target_pairs={{0,32},{32,0},{1,33},{33,1},{2,34},{34,2},{3,35},{35,3},{4,36},{36... | collective-permute-start | bytes 1572872 | tf_op jit(solution)/shard_map/ppermute | solution.py:125
  79.1 0.0 collective-permute-done.1
  79.1 0.0 copy-done
  79.1 0.1 bitcast_add_fusion.1
  79.2 1.6 %collective-permute-done.5 = f32[2,8,32,256]{3,2,1,0:T(8,128)S(1)} collective-permute-done((f32[2,8,32,256]{3,2,1,0:T(8,128)}, f32[2,8,32,256]{3,2,1,0:T(8,128)S(1)}, u32[]{:S(2)}, u32[]{:S(2)}) %collective-permute-start.5) | collective-permute-done | bytes 524320 | tf_op jit(solution)/shard_map/ppermute | solution.py:125
  80.8 0.0 copy-done.1
  80.8 0.1 bitcast_add_fusion
  80.9 0.1 constant_dynamic-slice_fusion.1
  81.0 0.2 copy.24
  81.2 2.7 %collective-permute-start.2 = (f32[2,2,2,32,256]{4,0,3,1,2:T(2,128)S(1)}, f32[2,2,2,32,256]{4,0,3,1,2:T(2,128)S(1)}, u32[]{:S(2)}, u32[]{:S(2)}) collective-permute-start(f32[2,2,2,32,256]{4,0,3,1,2:T(2,128)S(1)} %bitcast.72), channel_id=1, source_target_pairs={{0,64},{64,0},{128,192},{192,128},{256,320},{320,256},{384,448},{4... | collective-permute-start | bytes 786440 | tf_op jit(solution)/shard_map/ppermute | solution.py:92
  83.9 0.2 copy.23
  84.1 2.6 %collective-permute-start.6 = (f32[2,2,2,32,256]{4,0,3,1,2:T(2,128)S(1)}, f32[2,2,2,32,256]{4,0,3,1,2:T(2,128)S(1)}, u32[]{:S(2)}, u32[]{:S(2)}) collective-permute-start(f32[2,2,2,32,256]{4,0,3,1,2:T(2,128)S(1)} %bitcast.73), channel_id=1, source_target_pairs={{0,64},{64,0},{128,192},{192,128},{256,320},{320,256},{384,448},{4... | collective-permute-start | bytes 786440 | tf_op jit(solution)/shard_map/ppermute | solution.py:92
  86.7 3.9 %collective-permute-done.2 = f32[2,2,2,32,256]{4,0,3,1,2:T(2,128)S(1)} collective-permute-done((f32[2,2,2,32,256]{4,0,3,1,2:T(2,128)S(1)}, f32[2,2,2,32,256]{4,0,3,1,2:T(2,128)S(1)}, u32[]{:S(2)}, u32[]{:S(2)}) %collective-permute-start.2) | collective-permute-done | bytes 262176 | tf_op jit(solution)/shard_map/ppermute | solution.py:92
  90.6 0.3 bitcast_add_fusion.3
  90.9 3.3 %collective-permute-start.3 = (f32[2,2,32,256]{3,0,2,1:T(2,128)S(1)}, f32[2,2,32,256]{3,0,2,1:T(2,128)S(1)}, u32[]{:S(2)}, u32[]{:S(2)}) collective-permute-start(f32[2,2,32,256]{3,0,2,1:T(2,128)S(1)} %dynamic-slice_bitcast_fusion.3), channel_id=1, source_target_pairs={{0,128},{64,192},{128,0},{192,64},{256,384},{320,448},{384,256},{4... | collective-permute-start | bytes 393224 | tf_op jit(solution)/shard_map/ppermute | solution.py:92
  94.2 2.0 %collective-permute-done.6 = f32[2,2,2,32,256]{4,0,3,1,2:T(2,128)S(1)} collective-permute-done((f32[2,2,2,32,256]{4,0,3,1,2:T(2,128)S(1)}, f32[2,2,2,32,256]{4,0,3,1,2:T(2,128)S(1)}, u32[]{:S(2)}, u32[]{:S(2)}) %collective-permute-start.6) | collective-permute-done | bytes 262176 | tf_op jit(solution)/shard_map/ppermute | solution.py:92
  96.3 0.3 bitcast_add_fusion.2
  96.6 3.3 %collective-permute-start.7 = (f32[2,2,32,256]{3,0,2,1:T(2,128)S(1)}, f32[2,2,32,256]{3,0,2,1:T(2,128)S(1)}, u32[]{:S(2)}, u32[]{:S(2)}) collective-permute-start(f32[2,2,32,256]{3,0,2,1:T(2,128)S(1)} %dynamic-slice_bitcast_fusion.2), channel_id=1, source_target_pairs={{0,128},{64,192},{128,0},{192,64},{256,384},{320,448},{384,256},{4... | collective-permute-start | bytes 393224 | tf_op jit(solution)/shard_map/ppermute | solution.py:92
  99.8 0.0 collective-permute-done.3
  99.9 0.1 bitcast_add_fusion.5
  100.0 11.9 %collective-permute-start.4 = (f32[2,32,256]{2,0,1:T(2,128)S(1)}, f32[2,32,256]{2,0,1:T(2,128)S(1)}, u32[]{:S(2)}, u32[]{:S(2)}) collective-permute-start(f32[2,32,256]{2,0,1:T(2,128)S(1)} %dynamic-slice_bitcast_fusion.5), channel_id=1, source_target_pairs={{0,256},{64,320},{128,384},{192,448},{256,0},{320,64},{384,128},{4... | collective-permute-start | bytes 196616 | tf_op jit(solution)/shard_map/ppermute | solution.py:92
  111.9 0.0 collective-permute-done.7
  111.9 0.1 bitcast_add_fusion.4
  112.0 8.2 %collective-permute-start.8 = (f32[2,32,256]{2,0,1:T(2,128)S(1)}, f32[2,32,256]{2,0,1:T(2,128)S(1)}, u32[]{:S(2)}, u32[]{:S(2)}) collective-permute-start(f32[2,32,256]{2,0,1:T(2,128)S(1)} %dynamic-slice_bitcast_fusion.4), channel_id=1, source_target_pairs={{0,256},{64,320},{128,384},{192,448},{256,0},{320,64},{384,128},{4... | collective-permute-start | bytes 196616 | tf_op jit(solution)/shard_map/ppermute | solution.py:92
  120.2 0.0 collective-permute-done.4
  120.3 4.5 %collective-permute-done.8 = f32[2,32,256]{2,0,1:T(2,128)S(1)} collective-permute-done((f32[2,32,256]{2,0,1:T(2,128)S(1)}, f32[2,32,256]{2,0,1:T(2,128)S(1)}, u32[]{:S(2)}, u32[]{:S(2)}) %collective-permute-start.8) | collective-permute-done | bytes 65568 | tf_op jit(solution)/shard_map/ppermute | solution.py:92
  124.8 0.7 maximum_bitcast_fusion
  (16 shorter events, 0.3 us)
Async XLA Ops:
  2.4 18.1 %collective-permute-start = (bf16[2,2,16,512]{3,1,2,0:T(2,128)(2,1)S(1)}, bf16[2,2,16,512]{3,1,2,0:T(2,128)(2,1)S(1)}, u32[]{:S(2)}, u32[]{:S(2)}) collective-permute-start(bf16[2,2,16,512]{3,1,2,0:T(2,128)(2,1)S(1)} %bitcast.74), channel_id=1, source_target_pairs={{0,16},{16,0},{1,17},{17,1},{2,18},{18,2},{3,19},{19,3},{4,20},{20... | collective-permute-start | bytes 196616 | tf_op jit(solution)/shard_map/ppermute | solution.py:100
  21.9 18.6 %all-to-all-start = ((bf16[2,2,16,2,16,256]{5,4,3,1,0,2:T(8,128)(2,1)}), bf16[2,2,16,2,16,256]{5,4,3,1,0,2:T(8,128)(2,1)S(1)}, u32[]{:S(2)}, u32[]{:S(2)}) async-start(bf16[2,2,16,2,16,256]{5,4,3,1,0,2:T(8,128)(2,1)} %broadcast_in_dim.8), calls=%async_computation | async-start | bytes 2097152 | tf_op jit(solution)/shard_map/all_to_all | solution.py:118
  40.5 23.2 %all-to-all-start.1 = ((bf16[2,2,16,2,16,256]{5,4,3,1,0,2:T(8,128)(2,1)}), bf16[2,2,16,2,16,256]{5,4,3,1,0,2:T(8,128)(2,1)S(1)}, u32[]{:S(2)}, u32[]{:S(2)}) async-start(bf16[2,2,16,2,16,256]{5,4,3,1,0,2:T(8,128)(2,1)} %broadcast_in_dim.9), calls=%async_computation.1 | async-start | bytes 2097152 | tf_op jit(solution)/shard_map/all_to_all | solution.py:118
  58.9 20.2 %collective-permute-start.1 = (f32[2,8,32,256]{3,2,1,0:T(8,128)}, f32[2,8,32,256]{3,2,1,0:T(8,128)S(1)}, u32[]{:S(2)}, u32[]{:S(2)}) collective-permute-start(f32[2,8,32,256]{3,2,1,0:T(8,128)} %dynamic-slice_bitcast_fusion.1), channel_id=1, source_target_pairs={{0,32},{32,0},{1,33},{33,1},{2,34},{34,2},{3,35},{35,3},{4,36},{36... | collective-permute-start | bytes 1572872 | tf_op jit(solution)/shard_map/ppermute | solution.py:125
  64.8 14.3 %copy-start = (f32[2,512,256]{2,1,0:T(8,128)S(1)}, f32[2,512,256]{2,1,0:T(8,128)}, u32[]{:S(2)}) copy-start(f32[2,512,256]{2,1,0:T(8,128)} %shard_map.46) | copy-start | bytes 3145732
  73.5 7.4 %copy-start.1 = (f32[2,512,256]{2,1,0:T(8,128)S(1)}, f32[2,512,256]{2,1,0:T(8,128)}, u32[]{:S(2)}) copy-start(f32[2,512,256]{2,1,0:T(8,128)} %shard_map.47) | copy-start | bytes 3145732
  75.4 5.4 %collective-permute-start.5 = (f32[2,8,32,256]{3,2,1,0:T(8,128)}, f32[2,8,32,256]{3,2,1,0:T(8,128)S(1)}, u32[]{:S(2)}, u32[]{:S(2)}) collective-permute-start(f32[2,8,32,256]{3,2,1,0:T(8,128)} %dynamic-slice_bitcast_fusion), channel_id=1, source_target_pairs={{0,32},{32,0},{1,33},{33,1},{2,34},{34,2},{3,35},{35,3},{4,36},{36... | collective-permute-start | bytes 1572872 | tf_op jit(solution)/shard_map/ppermute | solution.py:125
  81.2 9.4 %collective-permute-start.2 = (f32[2,2,2,32,256]{4,0,3,1,2:T(2,128)S(1)}, f32[2,2,2,32,256]{4,0,3,1,2:T(2,128)S(1)}, u32[]{:S(2)}, u32[]{:S(2)}) collective-permute-start(f32[2,2,2,32,256]{4,0,3,1,2:T(2,128)S(1)} %bitcast.72), channel_id=1, source_target_pairs={{0,64},{64,0},{128,192},{192,128},{256,320},{320,256},{384,448},{4... | collective-permute-start | bytes 786440 | tf_op jit(solution)/shard_map/ppermute | solution.py:92
  84.1 12.1 %collective-permute-start.6 = (f32[2,2,2,32,256]{4,0,3,1,2:T(2,128)S(1)}, f32[2,2,2,32,256]{4,0,3,1,2:T(2,128)S(1)}, u32[]{:S(2)}, u32[]{:S(2)}) collective-permute-start(f32[2,2,2,32,256]{4,0,3,1,2:T(2,128)S(1)} %bitcast.73), channel_id=1, source_target_pairs={{0,64},{64,0},{128,192},{192,128},{256,320},{320,256},{384,448},{4... | collective-permute-start | bytes 786440 | tf_op jit(solution)/shard_map/ppermute | solution.py:92
  90.9 8.9 %collective-permute-start.3 = (f32[2,2,32,256]{3,0,2,1:T(2,128)S(1)}, f32[2,2,32,256]{3,0,2,1:T(2,128)S(1)}, u32[]{:S(2)}, u32[]{:S(2)}) collective-permute-start(f32[2,2,32,256]{3,0,2,1:T(2,128)S(1)} %dynamic-slice_bitcast_fusion.3), channel_id=1, source_target_pairs={{0,128},{64,192},{128,0},{192,64},{256,384},{320,448},{384,256},{4... | collective-permute-start | bytes 393224 | tf_op jit(solution)/shard_map/ppermute | solution.py:92
  96.6 15.3 %collective-permute-start.7 = (f32[2,2,32,256]{3,0,2,1:T(2,128)S(1)}, f32[2,2,32,256]{3,0,2,1:T(2,128)S(1)}, u32[]{:S(2)}, u32[]{:S(2)}) collective-permute-start(f32[2,2,32,256]{3,0,2,1:T(2,128)S(1)} %dynamic-slice_bitcast_fusion.2), channel_id=1, source_target_pairs={{0,128},{64,192},{128,0},{192,64},{256,384},{320,448},{384,256},{4... | collective-permute-start | bytes 393224 | tf_op jit(solution)/shard_map/ppermute | solution.py:92
  100.0 20.2 %collective-permute-start.4 = (f32[2,32,256]{2,0,1:T(2,128)S(1)}, f32[2,32,256]{2,0,1:T(2,128)S(1)}, u32[]{:S(2)}, u32[]{:S(2)}) collective-permute-start(f32[2,32,256]{2,0,1:T(2,128)S(1)} %dynamic-slice_bitcast_fusion.5), channel_id=1, source_target_pairs={{0,256},{64,320},{128,384},{192,448},{256,0},{320,64},{384,128},{4... | collective-permute-start | bytes 196616 | tf_op jit(solution)/shard_map/ppermute | solution.py:92
  112.0 12.8 %collective-permute-start.8 = (f32[2,32,256]{2,0,1:T(2,128)S(1)}, f32[2,32,256]{2,0,1:T(2,128)S(1)}, u32[]{:S(2)}, u32[]{:S(2)}) collective-permute-start(f32[2,32,256]{2,0,1:T(2,128)S(1)} %dynamic-slice_bitcast_fusion.4), channel_id=1, source_target_pairs={{0,256},{64,320},{128,384},{192,448},{256,0},{320,64},{384,128},{4... | collective-permute-start | bytes 196616 | tf_op jit(solution)/shard_map/ppermute | solution.py:92

commit v9 on v8

--- a/solution.py
+++ b/solution.py
@@ -41,8 +41,8 @@
 def contract_kernel(s_ref, b_ref, o_ref, out_ref):
     f32 = jnp.float32
     for t in range(s_ref.shape[0]):
-        sr = s_ref[t, :, 0, :]
-        si = s_ref[t, :, 1, :]
+        sr = s_ref[t, 0]
+        si = s_ref[t, 1]
         br = b_ref[t, 0]
         bi = b_ref[t, 1]
         pr = jnp.dot(sr, br, preferred_element_type=f32) - jnp.dot(si, bi, preferred_element_type=f32)
@@ -60,7 +60,7 @@
 
 
 def contract(stem_t, branch_t, open_t, column_block):
-    slices, rows, _, depth = stem_t.shape
+    slices, _, rows, depth = stem_t.shape
     width = branch_t.shape[-1]
     tile = min(ROW_TILE, rows)
     flops = slices * 8 * rows * depth * width
@@ -70,7 +70,7 @@
         out_shape=jax.ShapeDtypeStruct((2, rows, width), jnp.float32),
         grid=(rows // tile,),
         in_specs=[
-            pl.BlockSpec((slices, tile, 2, depth), lambda i: (0, i, 0, 0)),
+            pl.BlockSpec((slices, 2, tile, depth), lambda i: (0, 0, i, 0)),
             pl.BlockSpec((slices, 2, depth, width), lambda i: (0, 0, 0, 0)),
             pl.BlockSpec((slices, tile, 2, width), lambda i: (0, i, 0, column_block)),
         ],
@@ -104,7 +104,7 @@
     copies = jnp.broadcast_to(pair[:, :, None], pair.shape[:2] + (plane,) + pair.shape[2:])
     halves = 2
     span = width // halves
-    stem_t = stem_tensor
+    stem_t = jnp.transpose(stem_tensor, (0, 2, 1, 3))
     open_t = open_tensor
     zl_count = lax.axis_size("zl")
     block_rows = row_count // (zl_count * 2)

time: 128 us -> 124 us (0.969)
  Pallas kernels: 17.1 us -> 9.37 us
  local copies, waits for them, and re-layouts: 10.7 us -> 14 us
    pallas_call x2, Pallas kernels: 17.1 us -> 9.37 us  [contract(): pl.pallas_call(contract_kernel, out_shape=jax.ShapeDtypeStruct((2, rows,...]
    unnamed x5 -> x6, local copies, waits for them, and re-layouts: 0.03 us -> 3.31 us
  transfers between devices with their start and end apart: 11 -> 11, of which waited for: 6 -> 6; matrix products, arithmetic and copies ran while one was open for 7% -> 9% of each run, Pallas kernels for 14% -> 8%
where the time goes in v9:
time: 124 us; the launch traced here: 122 us
  starting transfers between devices  70.9 us (57%)
  waiting for transfers between devices  24.6 us (20%)
  local copies, waits for them, and re-layouts  14 us (11%)
  Pallas kernels  9.37 us (8%)
  other arithmetic  1.82 us (1%)
    ppermute x6, starting transfers between devices, halving_scatter(): shaped = keep + lax.ppermute(send, axis, pairs)  32 us
    ppermute x1, starting transfers between devices, body(): other = lax.ppermute(permuted, 'zh', shift_pairs(2, 1))  16.3 us
    all_to_all x2, starting transfers between devices, body(): gathered = lax.all_to_all(part, ('x', 'y'), 2, 4, tiled=True)  13.7 us
    all_to_all x2, waiting for transfers between devices, body(): gathered = lax.all_to_all(part, ('x', 'y'), 2, 4, tiled=True)  10.7 us
    ppermute x6, waiting for transfers between devices, halving_scatter(): shaped = keep + lax.ppermute(send, axis, pairs)  10.4 us
    pallas_call x2, Pallas kernels, contract(): pl.pallas_call(contract_kernel, out_shape=jax.ShapeDtypeStruct((2, rows,...  9.37 us
    ppermute x2, starting transfers between devices, body(): mine = mine + lax.ppermute(theirs, 'core', shift_pairs(2, 1))  9.02 us
    squeeze x2, local copies, waits for them, and re-layouts, body(): theirs = lax.dynamic_index_in_dim(shaped, 1 - core, 2, keepdims=False)  3.9 us
  transfers between devices with their start and end apart: 11, of which 6 were waited for; matrix products, arithmetic and copies ran while one was open for 9% of the time, Pallas kernels for 8%

profile of v9, /device:TPU:1, one launch (start us, length us, event | category | flops | bytes accessed | tf_op | source)
XLA Modules:
  0.0 121.6 jit_solution(11313009360410356662)
XLA Ops:
  0.0 0.8 fusion.5
  0.8 0.8 fusion.6
  1.6 0.3 fusion
  2.0 0.3 fusion.1
  2.4 16.3 %collective-permute-start = (bf16[2,2,16,512]{3,1,2,0:T(2,128)(2,1)S(1)}, bf16[2,2,16,512]{3,1,2,0:T(2,128)(2,1)S(1)}, u32[]{:S(2)}, u32[]{:S(2)}) collective-permute-start(bf16[2,2,16,512]{3,1,2,0:T(2,128)(2,1)S(1)} %bitcast.79), channel_id=1, source_target_pairs={{0,16},{16,0},{1,17},{17,1},{2,18},{18,2},{3,19},{19,3},{4,20},{20... | collective-permute-start | bytes 196616 | tf_op jit(solution)/shard_map/ppermute | solution.py:100
  18.6 1.8 %collective-permute-done = bf16[2,2,16,512]{3,1,2,0:T(2,128)(2,1)S(1)} collective-permute-done((bf16[2,2,16,512]{3,1,2,0:T(2,128)(2,1)S(1)}, bf16[2,2,16,512]{3,1,2,0:T(2,128)(2,1)S(1)}, u32[]{:S(2)}, u32[]{:S(2)}) %collective-permute-start) | collective-permute-done | bytes 65568 | tf_op jit(solution)/shard_map/ppermute | solution.py:100
  20.5 0.2 broadcast_select_fusion
  20.7 0.1 fusion.4
  20.8 1.1 broadcast_in_dim.8
  21.9 6.8 %all-to-all-start = ((bf16[2,2,16,2,16,256]{5,4,3,1,0,2:T(8,128)(2,1)}), bf16[2,2,16,2,16,256]{5,4,3,1,0,2:T(8,128)(2,1)S(1)}, u32[]{:S(2)}, u32[]{:S(2)}) async-start(bf16[2,2,16,2,16,256]{5,4,3,1,0,2:T(8,128)(2,1)} %broadcast_in_dim.8), calls=%async_computation | async-start | bytes 2097152 | tf_op jit(solution)/shard_map/all_to_all | solution.py:118
  28.7 1.1 broadcast_in_dim.9
  29.8 10.7 %all-to-all-done = bf16[2,2,16,2,16,256]{5,4,3,1,0,2:T(8,128)(2,1)S(1)} async-done(((bf16[2,2,16,2,16,256]{5,4,3,1,0,2:T(8,128)(2,1)}), bf16[2,2,16,2,16,256]{5,4,3,1,0,2:T(8,128)(2,1)S(1)}, u32[]{:S(2)}, u32[]{:S(2)}) %all-to-all-start) | async-done | bytes 1048608 | tf_op jit(solution)/shard_map/all_to_all | solution.py:118
  40.5 6.9 %all-to-all-start.1 = ((bf16[2,2,16,2,16,256]{5,4,3,1,0,2:T(8,128)(2,1)}), bf16[2,2,16,2,16,256]{5,4,3,1,0,2:T(8,128)(2,1)S(1)}, u32[]{:S(2)}, u32[]{:S(2)}) async-start(bf16[2,2,16,2,16,256]{5,4,3,1,0,2:T(8,128)(2,1)} %broadcast_in_dim.9), calls=%async_computation.1 | async-start | bytes 2097152 | tf_op jit(solution)/shard_map/all_to_all | solution.py:118
  47.5 3.3 %copy.26 = bf16[2,512,2,512]{3,1,2,0:T(8,128)(2,1)} copy(bf16[2,512,2,512]{3,2,1,0:T(2,128)(2,1)} %param.4) | data formatting | bytes 4194304 | tf_op args[0]
  50.8 1.1 copy.14
  51.8 4.6 %shard_map.46 = f32[2,512,256]{2,1,0:T(8,128)} custom-call(bf16[2,2,512,512]{3,2,1,0:T(8,128)(2,1)} %bitcast.65, bf16[2,2,512,256]{3,2,1,0:T(8,128)(2,1)} %bitcast.74, bf16[2,512,2,512]{3,2,1,0:T(2,128)(2,1)} %o_ref.3), custom_call_target="tpu_custom_call" | custom-call | flops 1073741824 | bytes 5242880 | tf_op jit(solution)/shard_map/pallas_call | solution.py:68
  56.5 1.9 %dynamic-slice_bitcast_fusion.1 = f32[2,8,32,256]{3,2,1,0:T(8,128)} fusion(f32[2,8,2,32,256]{4,3,2,1,0:T(8,128)} %bitcast.69, s32[]{:T(128)S(6)} %select_n.51), kind=kLoop, calls=%fused_computation.10 | loop fusion | bytes 1048580 | tf_op jit(solution)/shard_map/jit(dynamic_index_in_dim)/squeeze | solution.py:124
  58.4 4.8 %collective-permute-start.1 = (f32[2,8,32,256]{3,2,1,0:T(8,128)}, f32[2,8,32,256]{3,2,1,0:T(8,128)S(1)}, u32[]{:S(2)}, u32[]{:S(2)}) collective-permute-start(f32[2,8,32,256]{3,2,1,0:T(8,128)} %dynamic-slice_bitcast_fusion.1), channel_id=1, source_target_pairs={{0,32},{32,0},{1,33},{33,1},{2,34},{34,2},{3,35},{35,3},{4,36},{36... | collective-permute-start | bytes 1572872 | tf_op jit(solution)/shard_map/ppermute | solution.py:125
  63.2 0.0 all-to-all-done.1
  63.2 1.1 copy.18
  64.3 4.7 %shard_map.47 = f32[2,512,256]{2,1,0:T(8,128)} custom-call(bf16[2,2,512,512]{3,2,1,0:T(8,128)(2,1)} %bitcast.66, bf16[2,2,512,256]{3,2,1,0:T(8,128)(2,1)} %bitcast.73, bf16[2,512,2,512]{3,2,1,0:T(2,128)(2,1)} %o_ref.3), custom_call_target="tpu_custom_call" | custom-call | flops 1073741824 | bytes 5242880 | tf_op jit(solution)/shard_map/pallas_call | solution.py:68
  69.0 2.0 %dynamic-slice_bitcast_fusion = f32[2,8,32,256]{3,2,1,0:T(8,128)} fusion(f32[2,8,2,32,256]{4,3,2,1,0:T(8,128)} %bitcast.71, s32[]{:T(128)S(6)} %select_n.51), kind=kLoop, calls=%fused_computation.9 | loop fusion | bytes 1048580 | tf_op jit(solution)/shard_map/jit(dynamic_index_in_dim)/squeeze | solution.py:124
  71.0 4.2 %collective-permute-start.5 = (f32[2,8,32,256]{3,2,1,0:T(8,128)}, f32[2,8,32,256]{3,2,1,0:T(8,128)S(1)}, u32[]{:S(2)}, u32[]{:S(2)}) collective-permute-start(f32[2,8,32,256]{3,2,1,0:T(8,128)} %dynamic-slice_bitcast_fusion), channel_id=1, source_target_pairs={{0,32},{32,0},{1,33},{33,1},{2,34},{34,2},{3,35},{35,3},{4,36},{36... | collective-permute-start | bytes 1572872 | tf_op jit(solution)/shard_map/ppermute | solution.py:125
  75.2 0.0 collective-permute-done.1
  75.2 0.1 bitcast_add_fusion.1
  75.3 1.6 %collective-permute-done.5 = f32[2,8,32,256]{3,2,1,0:T(8,128)S(1)} collective-permute-done((f32[2,8,32,256]{3,2,1,0:T(8,128)}, f32[2,8,32,256]{3,2,1,0:T(8,128)S(1)}, u32[]{:S(2)}, u32[]{:S(2)}) %collective-permute-start.5) | collective-permute-done | bytes 524320 | tf_op jit(solution)/shard_map/ppermute | solution.py:125
  76.9 0.0 copy-done.1
  77.0 0.1 bitcast_add_fusion
  77.0 0.1 constant_dynamic-slice_fusion.1
  77.1 0.2 copy.28
  77.3 2.7 %collective-permute-start.2 = (f32[2,2,2,32,256]{4,0,3,1,2:T(2,128)S(1)}, f32[2,2,2,32,256]{4,0,3,1,2:T(2,128)S(1)}, u32[]{:S(2)}, u32[]{:S(2)}) collective-permute-start(f32[2,2,2,32,256]{4,0,3,1,2:T(2,128)S(1)} %bitcast.77), channel_id=1, source_target_pairs={{0,64},{64,0},{128,192},{192,128},{256,320},{320,256},{384,448},{4... | collective-permute-start | bytes 786440 | tf_op jit(solution)/shard_map/ppermute | solution.py:92
  80.0 0.2 copy.27
  80.3 2.6 %collective-permute-start.6 = (f32[2,2,2,32,256]{4,0,3,1,2:T(2,128)S(1)}, f32[2,2,2,32,256]{4,0,3,1,2:T(2,128)S(1)}, u32[]{:S(2)}, u32[]{:S(2)}) collective-permute-start(f32[2,2,2,32,256]{4,0,3,1,2:T(2,128)S(1)} %bitcast.78), channel_id=1, source_target_pairs={{0,64},{64,0},{128,192},{192,128},{256,320},{320,256},{384,448},{4... | collective-permute-start | bytes 786440 | tf_op jit(solution)/shard_map/ppermute | solution.py:92
  82.9 3.9 %collective-permute-done.2 = f32[2,2,2,32,256]{4,0,3,1,2:T(2,128)S(1)} collective-permute-done((f32[2,2,2,32,256]{4,0,3,1,2:T(2,128)S(1)}, f32[2,2,2,32,256]{4,0,3,1,2:T(2,128)S(1)}, u32[]{:S(2)}, u32[]{:S(2)}) %collective-permute-start.2) | collective-permute-done | bytes 262176 | tf_op jit(solution)/shard_map/ppermute | solution.py:92
  86.8 0.3 bitcast_add_fusion.3
  87.1 3.3 %collective-permute-start.3 = (f32[2,2,32,256]{3,0,2,1:T(2,128)S(1)}, f32[2,2,32,256]{3,0,2,1:T(2,128)S(1)}, u32[]{:S(2)}, u32[]{:S(2)}) collective-permute-start(f32[2,2,32,256]{3,0,2,1:T(2,128)S(1)} %dynamic-slice_bitcast_fusion.3), channel_id=1, source_target_pairs={{0,128},{64,192},{128,0},{192,64},{256,384},{320,448},{384,256},{4... | collective-permute-start | bytes 393224 | tf_op jit(solution)/shard_map/ppermute | solution.py:92
  90.3 2.0 %collective-permute-done.6 = f32[2,2,2,32,256]{4,0,3,1,2:T(2,128)S(1)} collective-permute-done((f32[2,2,2,32,256]{4,0,3,1,2:T(2,128)S(1)}, f32[2,2,2,32,256]{4,0,3,1,2:T(2,128)S(1)}, u32[]{:S(2)}, u32[]{:S(2)}) %collective-permute-start.6) | collective-permute-done | bytes 262176 | tf_op jit(solution)/shard_map/ppermute | solution.py:92
  92.4 0.3 bitcast_add_fusion.2
  92.7 3.3 %collective-permute-start.7 = (f32[2,2,32,256]{3,0,2,1:T(2,128)S(1)}, f32[2,2,32,256]{3,0,2,1:T(2,128)S(1)}, u32[]{:S(2)}, u32[]{:S(2)}) collective-permute-start(f32[2,2,32,256]{3,0,2,1:T(2,128)S(1)} %dynamic-slice_bitcast_fusion.2), channel_id=1, source_target_pairs={{0,128},{64,192},{128,0},{192,64},{256,384},{320,448},{384,256},{4... | collective-permute-start | bytes 393224 | tf_op jit(solution)/shard_map/ppermute | solution.py:92
  96.0 0.0 collective-permute-done.3
  96.0 0.1 bitcast_add_fusion.5
  96.1 11.9 %collective-permute-start.4 = (f32[2,32,256]{2,0,1:T(2,128)S(1)}, f32[2,32,256]{2,0,1:T(2,128)S(1)}, u32[]{:S(2)}, u32[]{:S(2)}) collective-permute-start(f32[2,32,256]{2,0,1:T(2,128)S(1)} %dynamic-slice_bitcast_fusion.5), channel_id=1, source_target_pairs={{0,256},{64,320},{128,384},{192,448},{256,0},{320,64},{384,128},{4... | collective-permute-start | bytes 196616 | tf_op jit(solution)/shard_map/ppermute | solution.py:92
  108.0 0.0 collective-permute-done.7
  108.0 0.1 bitcast_add_fusion.4
  108.1 8.2 %collective-permute-start.8 = (f32[2,32,256]{2,0,1:T(2,128)S(1)}, f32[2,32,256]{2,0,1:T(2,128)S(1)}, u32[]{:S(2)}, u32[]{:S(2)}) collective-permute-start(f32[2,32,256]{2,0,1:T(2,128)S(1)} %dynamic-slice_bitcast_fusion.4), channel_id=1, source_target_pairs={{0,256},{64,320},{128,384},{192,448},{256,0},{320,64},{384,128},{4... | collective-permute-start | bytes 196616 | tf_op jit(solution)/shard_map/ppermute | solution.py:92
  116.3 0.0 collective-permute-done.4
  116.4 4.5 %collective-permute-done.8 = f32[2,32,256]{2,0,1:T(2,128)S(1)} collective-permute-done((f32[2,32,256]{2,0,1:T(2,128)S(1)}, f32[2,32,256]{2,0,1:T(2,128)S(1)}, u32[]{:S(2)}, u32[]{:S(2)}) %collective-permute-start.8) | collective-permute-done | bytes 65568 | tf_op jit(solution)/shard_map/ppermute | solution.py:92
  120.9 0.7 maximum_bitcast_fusion
  (17 shorter events, 0.3 us)
Async XLA Ops:
  2.4 18.1 %collective-permute-start = (bf16[2,2,16,512]{3,1,2,0:T(2,128)(2,1)S(1)}, bf16[2,2,16,512]{3,1,2,0:T(2,128)(2,1)S(1)}, u32[]{:S(2)}, u32[]{:S(2)}) collective-permute-start(bf16[2,2,16,512]{3,1,2,0:T(2,128)(2,1)S(1)} %bitcast.79), channel_id=1, source_target_pairs={{0,16},{16,0},{1,17},{17,1},{2,18},{18,2},{3,19},{19,3},{4,20},{20... | collective-permute-start | bytes 196616 | tf_op jit(solution)/shard_map/ppermute | solution.py:100
  21.9 18.6 %all-to-all-start = ((bf16[2,2,16,2,16,256]{5,4,3,1,0,2:T(8,128)(2,1)}), bf16[2,2,16,2,16,256]{5,4,3,1,0,2:T(8,128)(2,1)S(1)}, u32[]{:S(2)}, u32[]{:S(2)}) async-start(bf16[2,2,16,2,16,256]{5,4,3,1,0,2:T(8,128)(2,1)} %broadcast_in_dim.8), calls=%async_computation | async-start | bytes 2097152 | tf_op jit(solution)/shard_map/all_to_all | solution.py:118
  40.5 22.7 %all-to-all-start.1 = ((bf16[2,2,16,2,16,256]{5,4,3,1,0,2:T(8,128)(2,1)}), bf16[2,2,16,2,16,256]{5,4,3,1,0,2:T(8,128)(2,1)S(1)}, u32[]{:S(2)}, u32[]{:S(2)}) async-start(bf16[2,2,16,2,16,256]{5,4,3,1,0,2:T(8,128)(2,1)} %broadcast_in_dim.9), calls=%async_computation.1 | async-start | bytes 2097152 | tf_op jit(solution)/shard_map/all_to_all | solution.py:118
  58.4 16.8 %collective-permute-start.1 = (f32[2,8,32,256]{3,2,1,0:T(8,128)}, f32[2,8,32,256]{3,2,1,0:T(8,128)S(1)}, u32[]{:S(2)}, u32[]{:S(2)}) collective-permute-start(f32[2,8,32,256]{3,2,1,0:T(8,128)} %dynamic-slice_bitcast_fusion.1), channel_id=1, source_target_pairs={{0,32},{32,0},{1,33},{33,1},{2,34},{34,2},{3,35},{35,3},{4,36},{36... | collective-permute-start | bytes 1572872 | tf_op jit(solution)/shard_map/ppermute | solution.py:125
  64.3 10.9 %copy-start = (f32[2,512,256]{2,1,0:T(8,128)S(1)}, f32[2,512,256]{2,1,0:T(8,128)}, u32[]{:S(2)}) copy-start(f32[2,512,256]{2,1,0:T(8,128)} %shard_map.46) | copy-start | bytes 3145732
  69.0 7.9 %copy-start.1 = (f32[2,512,256]{2,1,0:T(8,128)S(1)}, f32[2,512,256]{2,1,0:T(8,128)}, u32[]{:S(2)}) copy-start(f32[2,512,256]{2,1,0:T(8,128)} %shard_map.47) | copy-start | bytes 3145732
  71.0 5.9 %collective-permute-start.5 = (f32[2,8,32,256]{3,2,1,0:T(8,128)}, f32[2,8,32,256]{3,2,1,0:T(8,128)S(1)}, u32[]{:S(2)}, u32[]{:S(2)}) collective-permute-start(f32[2,8,32,256]{3,2,1,0:T(8,128)} %dynamic-slice_bitcast_fusion), channel_id=1, source_target_pairs={{0,32},{32,0},{1,33},{33,1},{2,34},{34,2},{3,35},{35,3},{4,36},{36... | collective-permute-start | bytes 1572872 | tf_op jit(solution)/shard_map/ppermute | solution.py:125
  77.3 9.4 %collective-permute-start.2 = (f32[2,2,2,32,256]{4,0,3,1,2:T(2,128)S(1)}, f32[2,2,2,32,256]{4,0,3,1,2:T(2,128)S(1)}, u32[]{:S(2)}, u32[]{:S(2)}) collective-permute-start(f32[2,2,2,32,256]{4,0,3,1,2:T(2,128)S(1)} %bitcast.77), channel_id=1, source_target_pairs={{0,64},{64,0},{128,192},{192,128},{256,320},{320,256},{384,448},{4... | collective-permute-start | bytes 786440 | tf_op jit(solution)/shard_map/ppermute | solution.py:92
  80.3 12.1 %collective-permute-start.6 = (f32[2,2,2,32,256]{4,0,3,1,2:T(2,128)S(1)}, f32[2,2,2,32,256]{4,0,3,1,2:T(2,128)S(1)}, u32[]{:S(2)}, u32[]{:S(2)}) collective-permute-start(f32[2,2,2,32,256]{4,0,3,1,2:T(2,128)S(1)} %bitcast.78), channel_id=1, source_target_pairs={{0,64},{64,0},{128,192},{192,128},{256,320},{320,256},{384,448},{4... | collective-permute-start | bytes 786440 | tf_op jit(solution)/shard_map/ppermute | solution.py:92
  87.1 8.9 %collective-permute-start.3 = (f32[2,2,32,256]{3,0,2,1:T(2,128)S(1)}, f32[2,2,32,256]{3,0,2,1:T(2,128)S(1)}, u32[]{:S(2)}, u32[]{:S(2)}) collective-permute-start(f32[2,2,32,256]{3,0,2,1:T(2,128)S(1)} %dynamic-slice_bitcast_fusion.3), channel_id=1, source_target_pairs={{0,128},{64,192},{128,0},{192,64},{256,384},{320,448},{384,256},{4... | collective-permute-start | bytes 393224 | tf_op jit(solution)/shard_map/ppermute | solution.py:92
  92.7 15.3 %collective-permute-start.7 = (f32[2,2,32,256]{3,0,2,1:T(2,128)S(1)}, f32[2,2,32,256]{3,0,2,1:T(2,128)S(1)}, u32[]{:S(2)}, u32[]{:S(2)}) collective-permute-start(f32[2,2,32,256]{3,0,2,1:T(2,128)S(1)} %dynamic-slice_bitcast_fusion.2), channel_id=1, source_target_pairs={{0,128},{64,192},{128,0},{192,64},{256,384},{320,448},{384,256},{4... | collective-permute-start | bytes 393224 | tf_op jit(solution)/shard_map/ppermute | solution.py:92
  96.1 20.2 %collective-permute-start.4 = (f32[2,32,256]{2,0,1:T(2,128)S(1)}, f32[2,32,256]{2,0,1:T(2,128)S(1)}, u32[]{:S(2)}, u32[]{:S(2)}) collective-permute-start(f32[2,32,256]{2,0,1:T(2,128)S(1)} %dynamic-slice_bitcast_fusion.5), channel_id=1, source_target_pairs={{0,256},{64,320},{128,384},{192,448},{256,0},{320,64},{384,128},{4... | collective-permute-start | bytes 196616 | tf_op jit(solution)/shard_map/ppermute | solution.py:92
  108.1 12.8 %collective-permute-start.8 = (f32[2,32,256]{2,0,1:T(2,128)S(1)}, f32[2,32,256]{2,0,1:T(2,128)S(1)}, u32[]{:S(2)}, u32[]{:S(2)}) collective-permute-start(f32[2,32,256]{2,0,1:T(2,128)S(1)} %dynamic-slice_bitcast_fusion.4), channel_id=1, source_target_pairs={{0,256},{64,320},{128,384},{192,448},{256,0},{320,64},{384,128},{4... | collective-permute-start | bytes 196616 | tf_op jit(solution)/shard_map/ppermute | solution.py:92

commit v10 on v9

--- a/solution.py
+++ b/solution.py
@@ -5,13 +5,13 @@
 from jax.sharding import Mesh
 from jax.sharding import PartitionSpec as P
 
-CUTS = ("zl", "core")
+CUTS = ("zq", "zb", "core")
 STEM = ("zh", "x", "y")
 ROW_TILE = 256
 
 
 def split_mesh(mesh):
-    devices = mesh.devices.reshape(8, 2, 2, 4, 4)
+    devices = mesh.devices.reshape(4, 2, 2, 2, 4, 4)
     return Mesh(devices, CUTS + STEM)
 
 
@@ -79,18 +79,14 @@
     )(stem_t, branch_t, open_t)
 
 
-def halving_scatter(blocks, axis):
-    count = lax.axis_size(axis)
-    me = lax.axis_index(axis)
-    shaped = blocks.reshape((2,) + (2,) * 3 + blocks.shape[2:])
-    for bit_pos in range(3):
-        along = 3 - bit_pos
-        bit = (me >> bit_pos) & 1
-        keep = lax.dynamic_index_in_dim(shaped, bit, along, keepdims=False)
-        send = lax.dynamic_index_in_dim(shaped, 1 - bit, along, keepdims=False)
-        pairs = [(i, i ^ (1 << bit_pos)) for i in range(count)]
-        shaped = keep + lax.ppermute(send, axis, pairs)
-    return shaped
+def cuts_scatter(blocks):
+    zb = lax.axis_index("zb")
+    shaped = blocks.reshape((2, lax.axis_size("zq"), 2) + blocks.shape[2:])
+    keep = lax.dynamic_index_in_dim(shaped, zb, 2, keepdims=False)
+    send = lax.dynamic_index_in_dim(shaped, 1 - zb, 2, keepdims=False)
+    part = keep + lax.ppermute(send, "zb", shift_pairs(2, 1))
+    got = lax.all_to_all(part, "zq", 1, 1, tiled=True)
+    return jnp.sum(got, axis=1)
 
 
 def body(stem_tensor, branch_tensor, open_tensor, open_order):
@@ -106,7 +102,7 @@
     span = width // halves
     stem_t = jnp.transpose(stem_tensor, (0, 2, 1, 3))
     open_t = open_tensor
-    zl_count = lax.axis_size("zl")
+    zl_count = lax.axis_size("zq") * lax.axis_size("zb")
     block_rows = row_count // (zl_count * 2)
     core = lax.axis_index("core")
     results = []
@@ -123,7 +119,7 @@
         mine = lax.dynamic_index_in_dim(shaped, core, 2, keepdims=False)
         theirs = lax.dynamic_index_in_dim(shaped, 1 - core, 2, keepdims=False)
         mine = mine + lax.ppermute(theirs, "core", shift_pairs(2, 1))
-        results.append(halving_scatter(mine, "zl"))
+        results.append(cuts_scatter(mine))
     result = jnp.concatenate(results, axis=-1)
     return jnp.transpose(result, (1, 0, 2)).reshape(1, block_rows, 2, width)
 

time: 124 us -> 142 us (1.15)
  waiting for transfers between devices: 24.6 us -> 51.4 us
  starting transfers between devices: 70.9 us -> 63.2 us
    ppermute x6 -> x2, starting transfers between devices: 32 us -> 4.81 us  [cuts_scatter(): part = keep + lax.ppermute(send, 'zb', shift_pairs(2, 1))]
    all_to_all x0 -> x2, waiting for transfers between devices: none -> 23.7 us  [cuts_scatter(): got = lax.all_to_all(part, 'zq', 1, 1, tiled=True)]
    all_to_all x0 -> x2, starting transfers between devices: none -> 18.5 us  [cuts_scatter(): got = lax.all_to_all(part, 'zq', 1, 1, tiled=True)]
    ppermute x6 -> x2, waiting for transfers between devices: 10.4 us -> 15.1 us  [cuts_scatter(): part = keep + lax.ppermute(send, 'zb', shift_pairs(2, 1))]
    ppermute x2, waiting for transfers between devices: 1.62 us -> 0.01 us  [body(): mine = mine + lax.ppermute(theirs, 'core', shift_pairs(2, 1))]
    add x0 -> x2, local copies, waits for them, and re-layouts: none -> 1.47 us  [cuts_scatter(): part = keep + lax.ppermute(send, 'zb', shift_pairs(2, 1))]
  transfers between devices with their start and end apart: 11 -> 9, of which waited for: 6 -> 6; matrix products, arithmetic and copies ran while one was open for 9% -> 9% of each run, Pallas kernels for 8% -> 7%
where the time goes in v10:
time: 142 us; the launch traced here: 141 us
  starting transfers between devices  63.2 us (45%)
  waiting for transfers between devices  51.4 us (36%)
  local copies, waits for them, and re-layouts  14.7 us (10%)
  Pallas kernels  9.44 us (7%)
  other arithmetic  1.5 us (1%)
    all_to_all x2, waiting for transfers between devices, cuts_scatter(): got = lax.all_to_all(part, 'zq', 1, 1, tiled=True)  23.7 us
    all_to_all x2, starting transfers between devices, cuts_scatter(): got = lax.all_to_all(part, 'zq', 1, 1, tiled=True)  18.5 us
    ppermute x1, starting transfers between devices, body(): other = lax.ppermute(permuted, 'zh', shift_pairs(2, 1))  16.3 us
    ppermute x2, waiting for transfers between devices, cuts_scatter(): part = keep + lax.ppermute(send, 'zb', shift_pairs(2, 1))  15.1 us
    all_to_all x2, starting transfers between devices, body(): gathered = lax.all_to_all(part, ('x', 'y'), 2, 4, tiled=True)  13.7 us
    all_to_all x2, waiting for transfers between devices, body(): gathered = lax.all_to_all(part, ('x', 'y'), 2, 4, tiled=True)  10.7 us
    ppermute x2, starting transfers between devices, body(): mine = mine + lax.ppermute(theirs, 'core', shift_pairs(2, 1))  9.96 us
    pallas_call x2, Pallas kernels, contract(): pl.pallas_call(contract_kernel, out_shape=jax.ShapeDtypeStruct((2, rows,...  9.44 us
  transfers between devices with their start and end apart: 9, of which 6 were waited for; matrix products, arithmetic and copies ran while one was open for 9% of the time, Pallas kernels for 7%

profile of v10, /device:TPU:1, one launch (start us, length us, event | category | flops | bytes accessed | tf_op | source)
XLA Modules:
  0.0 141.0 jit_solution(17794613651635992490)
XLA Ops:
  0.0 0.8 fusion.5
  0.8 0.8 fusion.6
  1.6 0.3 fusion
  2.0 0.3 fusion.1
  2.4 16.3 %collective-permute-start = (bf16[2,2,16,512]{3,1,2,0:T(2,128)(2,1)S(1)}, bf16[2,2,16,512]{3,1,2,0:T(2,128)(2,1)S(1)}, u32[]{:S(2)}, u32[]{:S(2)}) collective-permute-start(bf16[2,2,16,512]{3,1,2,0:T(2,128)(2,1)S(1)} %bitcast.61), channel_id=1, source_target_pairs={{0,16},{16,0},{1,17},{17,1},{2,18},{18,2},{3,19},{19,3},{4,20},{20... | collective-permute-start | bytes 196616 | tf_op jit(solution)/shard_map/ppermute | solution.py:96
  18.6 1.8 %collective-permute-done = bf16[2,2,16,512]{3,1,2,0:T(2,128)(2,1)S(1)} collective-permute-done((bf16[2,2,16,512]{3,1,2,0:T(2,128)(2,1)S(1)}, bf16[2,2,16,512]{3,1,2,0:T(2,128)(2,1)S(1)}, u32[]{:S(2)}, u32[]{:S(2)}) %collective-permute-start) | collective-permute-done | bytes 65568 | tf_op jit(solution)/shard_map/ppermute | solution.py:96
  20.5 0.2 broadcast_select_fusion
  20.7 0.1 fusion.4
  20.8 1.1 broadcast_in_dim.8
  21.9 6.8 %all-to-all-start = ((bf16[2,2,16,2,16,256]{5,4,3,1,0,2:T(8,128)(2,1)}), bf16[2,2,16,2,16,256]{5,4,3,1,0,2:T(8,128)(2,1)S(1)}, u32[]{:S(2)}, u32[]{:S(2)}) async-start(bf16[2,2,16,2,16,256]{5,4,3,1,0,2:T(8,128)(2,1)} %broadcast_in_dim.8), calls=%async_computation | async-start | bytes 2097152 | tf_op jit(solution)/shard_map/all_to_all | solution.py:114
  28.7 1.1 broadcast_in_dim.9
  29.8 10.7 %all-to-all-done = bf16[2,2,16,2,16,256]{5,4,3,1,0,2:T(8,128)(2,1)S(1)} async-done(((bf16[2,2,16,2,16,256]{5,4,3,1,0,2:T(8,128)(2,1)}), bf16[2,2,16,2,16,256]{5,4,3,1,0,2:T(8,128)(2,1)S(1)}, u32[]{:S(2)}, u32[]{:S(2)}) %all-to-all-start) | async-done | bytes 1048608 | tf_op jit(solution)/shard_map/all_to_all | solution.py:114
  40.5 6.9 %all-to-all-start.2 = ((bf16[2,2,16,2,16,256]{5,4,3,1,0,2:T(8,128)(2,1)}), bf16[2,2,16,2,16,256]{5,4,3,1,0,2:T(8,128)(2,1)S(1)}, u32[]{:S(2)}, u32[]{:S(2)}) async-start(bf16[2,2,16,2,16,256]{5,4,3,1,0,2:T(8,128)(2,1)} %broadcast_in_dim.9), calls=%async_computation.2 | async-start | bytes 2097152 | tf_op jit(solution)/shard_map/all_to_all | solution.py:114
  47.5 3.3 %copy.37 = bf16[2,512,2,512]{3,1,2,0:T(8,128)(2,1)} copy(bf16[2,512,2,512]{3,2,1,0:T(2,128)(2,1)} %param.4) | data formatting | bytes 4194304 | tf_op args[0]
  50.7 1.1 copy.26
  51.8 4.7 %shard_map.46 = f32[2,512,256]{2,1,0:T(8,128)} custom-call(bf16[2,2,512,512]{3,2,1,0:T(8,128)(2,1)} %bitcast.47, bf16[2,2,512,256]{3,2,1,0:T(8,128)(2,1)} %bitcast.56, bf16[2,512,2,512]{3,2,1,0:T(2,128)(2,1)} %o_ref.3), custom_call_target="tpu_custom_call" | custom-call | flops 1073741824 | bytes 5242880 | tf_op jit(solution)/shard_map/pallas_call | solution.py:68
  56.5 1.1 dynamic-slice_bitcast_fusion.1
  57.6 4.8 %collective-permute-start.1 = (f32[2,8,32,256]{3,2,1,0:T(8,128)S(1)}, f32[2,8,32,256]{3,2,1,0:T(8,128)S(1)}, u32[]{:S(2)}, u32[]{:S(2)}) collective-permute-start(f32[2,8,32,256]{3,2,1,0:T(8,128)S(1)} %dynamic-slice_bitcast_fusion.1), channel_id=1, source_target_pairs={{0,32},{32,0},{1,33},{33,1},{2,34},{34,2},{3,35},{35,3},{4,36},{36... | collective-permute-start | bytes 1572872 | tf_op jit(solution)/shard_map/ppermute | solution.py:121
  62.4 0.0 all-to-all-done.2
  62.4 1.1 copy.30
  63.5 0.0 copy-start
  63.5 4.8 %shard_map.47 = f32[2,512,256]{2,1,0:T(8,128)} custom-call(bf16[2,2,512,512]{3,2,1,0:T(8,128)(2,1)} %bitcast.48, bf16[2,2,512,256]{3,2,1,0:T(8,128)(2,1)} %bitcast.55, bf16[2,512,2,512]{3,2,1,0:T(2,128)(2,1)} %o_ref.3), custom_call_target="tpu_custom_call" | custom-call | flops 1073741824 | bytes 5242880 | tf_op jit(solution)/shard_map/pallas_call | solution.py:68
  68.3 1.9 %dynamic-slice_bitcast_fusion = f32[2,8,32,256]{3,2,1,0:T(8,128)} fusion(f32[2,8,2,32,256]{4,3,2,1,0:T(8,128)} %bitcast.53, s32[]{:T(128)S(6)} %select_n.33), kind=kLoop, calls=%fused_computation.9 | loop fusion | bytes 1048580 | tf_op jit(solution)/shard_map/jit(dynamic_index_in_dim)/squeeze | solution.py:120
  70.1 0.0 copy-start.1
  70.1 5.1 %collective-permute-start.3 = (f32[2,8,32,256]{3,2,1,0:T(8,128)}, f32[2,8,32,256]{3,2,1,0:T(8,128)}, u32[]{:S(2)}, u32[]{:S(2)}) collective-permute-start(f32[2,8,32,256]{3,2,1,0:T(8,128)} %dynamic-slice_bitcast_fusion), channel_id=1, source_target_pairs={{0,32},{32,0},{1,33},{33,1},{2,34},{34,2},{3,35},{35,3},{4,36},{36... | collective-permute-start | bytes 1572872 | tf_op jit(solution)/shard_map/ppermute | solution.py:121
  75.3 0.0 collective-permute-done.1
  75.3 0.0 copy-done
  75.3 0.1 bitcast_add_fusion.1
  75.4 2.7 %collective-permute-start.2 = (f32[2,4,32,256]{3,2,1,0:T(8,128)S(1)}, f32[2,4,32,256]{3,2,1,0:T(8,128)S(1)}, u32[]{:S(2)}, u32[]{:S(2)}) collective-permute-start(f32[2,4,32,256]{3,2,1,0:T(8,128)S(1)} %dynamic-slice_bitcast_fusion.3), channel_id=1, source_target_pairs={{0,64},{64,0},{1,65},{65,1},{2,66},{66,2},{3,67},{67,3},{4,68},{68... | collective-permute-start | bytes 786440 | tf_op jit(solution)/shard_map/ppermute | solution.py:87
  78.1 7.1 %collective-permute-done.2 = f32[2,4,32,256]{3,2,1,0:T(8,128)S(1)} collective-permute-done((f32[2,4,32,256]{3,2,1,0:T(8,128)S(1)}, f32[2,4,32,256]{3,2,1,0:T(8,128)S(1)}, u32[]{:S(2)}, u32[]{:S(2)}) %collective-permute-start.2) | collective-permute-done | bytes 262176 | tf_op jit(solution)/shard_map/ppermute | solution.py:87
  85.3 0.7 copy.27
  86.0 12.3 %all-to-all-start.1 = ((f32[2,4,32,256]{3,2,0,1:T(8,128)}), f32[2,4,32,256]{3,2,0,1:T(8,128)S(1)}, u32[]{:S(2)}, u32[]{:S(2)}) async-start(f32[2,4,32,256]{3,2,0,1:T(8,128)} %copy.27), calls=%async_computation.1 | async-start | bytes 524288 | tf_op jit(solution)/shard_map/all_to_all | solution.py:88
  98.4 0.0 collective-permute-done.3
  98.4 0.0 copy-done.1
  98.4 1.1 bitcast_add_fusion
  99.5 2.1 %collective-permute-start.4 = (f32[2,4,32,256]{3,2,1,0:T(8,128)S(1)}, f32[2,4,32,256]{3,2,1,0:T(8,128)S(1)}, u32[]{:S(2)}, u32[]{:S(2)}) collective-permute-start(f32[2,4,32,256]{3,2,1,0:T(8,128)S(1)} %dynamic-slice_bitcast_fusion.2), channel_id=1, source_target_pairs={{0,64},{64,0},{1,65},{65,1},{2,66},{66,2},{3,67},{67,3},{4,68},{68... | collective-permute-start | bytes 786440 | tf_op jit(solution)/shard_map/ppermute | solution.py:87
  101.7 7.9 %collective-permute-done.4 = f32[2,4,32,256]{3,2,1,0:T(8,128)S(1)} collective-permute-done((f32[2,4,32,256]{3,2,1,0:T(8,128)S(1)}, f32[2,4,32,256]{3,2,1,0:T(8,128)S(1)}, u32[]{:S(2)}, u32[]{:S(2)}) %collective-permute-start.4) | collective-permute-done | bytes 262176 | tf_op jit(solution)/shard_map/ppermute | solution.py:87
  109.6 0.7 copy.31
  110.3 5.9 %all-to-all-done.1 = f32[2,4,32,256]{3,2,0,1:T(8,128)S(1)} async-done(((f32[2,4,32,256]{3,2,0,1:T(8,128)}), f32[2,4,32,256]{3,2,0,1:T(8,128)S(1)}, u32[]{:S(2)}, u32[]{:S(2)}) %all-to-all-start.1) | async-done | bytes 262176 | tf_op jit(solution)/shard_map/all_to_all | solution.py:88
  116.3 6.1 %all-to-all-start.3 = ((f32[2,4,32,256]{3,2,0,1:T(8,128)}), f32[2,4,32,256]{3,2,0,1:T(8,128)S(1)}, u32[]{:S(2)}, u32[]{:S(2)}) async-start(f32[2,4,32,256]{3,2,0,1:T(8,128)} %copy.31), calls=%async_computation.3 | async-start | bytes 524288 | tf_op jit(solution)/shard_map/all_to_all | solution.py:88
  122.4 17.8 %all-to-all-done.3 = f32[2,4,32,256]{3,2,0,1:T(8,128)S(1)} async-done(((f32[2,4,32,256]{3,2,0,1:T(8,128)}), f32[2,4,32,256]{3,2,0,1:T(8,128)S(1)}, u32[]{:S(2)}, u32[]{:S(2)}) %all-to-all-start.3) | async-done | bytes 262176 | tf_op jit(solution)/shard_map/all_to_all | solution.py:88
  140.3 0.8 copy.33
  (15 shorter events, 0.3 us)
Async XLA Ops:
  2.4 18.1 %collective-permute-start = (bf16[2,2,16,512]{3,1,2,0:T(2,128)(2,1)S(1)}, bf16[2,2,16,512]{3,1,2,0:T(2,128)(2,1)S(1)}, u32[]{:S(2)}, u32[]{:S(2)}) collective-permute-start(bf16[2,2,16,512]{3,1,2,0:T(2,128)(2,1)S(1)} %bitcast.61), channel_id=1, source_target_pairs={{0,16},{16,0},{1,17},{17,1},{2,18},{18,2},{3,19},{19,3},{4,20},{20... | collective-permute-start | bytes 196616 | tf_op jit(solution)/shard_map/ppermute | solution.py:96
  21.9 18.6 %all-to-all-start = ((bf16[2,2,16,2,16,256]{5,4,3,1,0,2:T(8,128)(2,1)}), bf16[2,2,16,2,16,256]{5,4,3,1,0,2:T(8,128)(2,1)S(1)}, u32[]{:S(2)}, u32[]{:S(2)}) async-start(bf16[2,2,16,2,16,256]{5,4,3,1,0,2:T(8,128)(2,1)} %broadcast_in_dim.8), calls=%async_computation | async-start | bytes 2097152 | tf_op jit(solution)/shard_map/all_to_all | solution.py:114
  40.5 21.9 %all-to-all-start.2 = ((bf16[2,2,16,2,16,256]{5,4,3,1,0,2:T(8,128)(2,1)}), bf16[2,2,16,2,16,256]{5,4,3,1,0,2:T(8,128)(2,1)S(1)}, u32[]{:S(2)}, u32[]{:S(2)}) async-start(bf16[2,2,16,2,16,256]{5,4,3,1,0,2:T(8,128)(2,1)} %broadcast_in_dim.9), calls=%async_computation.2 | async-start | bytes 2097152 | tf_op jit(solution)/shard_map/all_to_all | solution.py:114
  57.6 17.7 %collective-permute-start.1 = (f32[2,8,32,256]{3,2,1,0:T(8,128)S(1)}, f32[2,8,32,256]{3,2,1,0:T(8,128)S(1)}, u32[]{:S(2)}, u32[]{:S(2)}) collective-permute-start(f32[2,8,32,256]{3,2,1,0:T(8,128)S(1)} %dynamic-slice_bitcast_fusion.1), channel_id=1, source_target_pairs={{0,32},{32,0},{1,33},{33,1},{2,34},{34,2},{3,35},{35,3},{4,36},{36... | collective-permute-start | bytes 1572872 | tf_op jit(solution)/shard_map/ppermute | solution.py:121
  63.5 11.8 %copy-start = (f32[2,512,256]{2,1,0:T(8,128)S(1)}, f32[2,512,256]{2,1,0:T(8,128)}, u32[]{:S(2)}) copy-start(f32[2,512,256]{2,1,0:T(8,128)} %shard_map.46) | copy-start | bytes 3145732
  70.1 28.2 %copy-start.1 = (f32[2,512,256]{2,1,0:T(8,128)S(1)}, f32[2,512,256]{2,1,0:T(8,128)}, u32[]{:S(2)}) copy-start(f32[2,512,256]{2,1,0:T(8,128)} %shard_map.47) | copy-start | bytes 3145732
  70.1 28.2 %collective-permute-start.3 = (f32[2,8,32,256]{3,2,1,0:T(8,128)}, f32[2,8,32,256]{3,2,1,0:T(8,128)}, u32[]{:S(2)}, u32[]{:S(2)}) collective-permute-start(f32[2,8,32,256]{3,2,1,0:T(8,128)} %dynamic-slice_bitcast_fusion), channel_id=1, source_target_pairs={{0,32},{32,0},{1,33},{33,1},{2,34},{34,2},{3,35},{35,3},{4,36},{36... | collective-permute-start | bytes 1572872 | tf_op jit(solution)/shard_map/ppermute | solution.py:121
  75.4 9.8 %collective-permute-start.2 = (f32[2,4,32,256]{3,2,1,0:T(8,128)S(1)}, f32[2,4,32,256]{3,2,1,0:T(8,128)S(1)}, u32[]{:S(2)}, u32[]{:S(2)}) collective-permute-start(f32[2,4,32,256]{3,2,1,0:T(8,128)S(1)} %dynamic-slice_bitcast_fusion.3), channel_id=1, source_target_pairs={{0,64},{64,0},{1,65},{65,1},{2,66},{66,2},{3,67},{67,3},{4,68},{68... | collective-permute-start | bytes 786440 | tf_op jit(solution)/shard_map/ppermute | solution.py:87
  86.0 30.3 %all-to-all-start.1 = ((f32[2,4,32,256]{3,2,0,1:T(8,128)}), f32[2,4,32,256]{3,2,0,1:T(8,128)S(1)}, u32[]{:S(2)}, u32[]{:S(2)}) async-start(f32[2,4,32,256]{3,2,0,1:T(8,128)} %copy.27), calls=%async_computation.1 | async-start | bytes 524288 | tf_op jit(solution)/shard_map/all_to_all | solution.py:88
  99.5 10.1 %collective-permute-start.4 = (f32[2,4,32,256]{3,2,1,0:T(8,128)S(1)}, f32[2,4,32,256]{3,2,1,0:T(8,128)S(1)}, u32[]{:S(2)}, u32[]{:S(2)}) collective-permute-start(f32[2,4,32,256]{3,2,1,0:T(8,128)S(1)} %dynamic-slice_bitcast_fusion.2), channel_id=1, source_target_pairs={{0,64},{64,0},{1,65},{65,1},{2,66},{66,2},{3,67},{67,3},{4,68},{68... | collective-permute-start | bytes 786440 | tf_op jit(solution)/shard_map/ppermute | solution.py:87
  116.3 23.9 %all-to-all-start.3 = ((f32[2,4,32,256]{3,2,0,1:T(8,128)}), f32[2,4,32,256]{3,2,0,1:T(8,128)S(1)}, u32[]{:S(2)}, u32[]{:S(2)}) async-start(f32[2,4,32,256]{3,2,0,1:T(8,128)} %copy.31), calls=%async_computation.3 | async-start | bytes 524288 | tf_op jit(solution)/shard_map/all_to_all | solution.py:88

commit v11 on v9

--- a/solution.py
+++ b/solution.py
@@ -114,7 +114,7 @@
     for h in range(halves):
         part = copies[..., h * span:(h + 1) * span]
         if previous is not None:
-            part, previous = lax.optimization_barrier((part, previous))
+            part, previous, stem_t = lax.optimization_barrier((part, previous, stem_t))
         gathered = lax.all_to_all(part, ("x", "y"), 2, 4, tiled=True)
         previous = gathered
         branch_t = gathered.reshape(slice_count, 2, -1, span)

time: 124 us -> 125 us (level)
  waiting for transfers between devices: 24.6 us -> 31.6 us
  starting transfers between devices: 70.9 us -> 65.1 us
    all_to_all x2, waiting for transfers between devices: 10.7 us -> 17.6 us  [body(): gathered = lax.all_to_all(part, ('x', 'y'), 2, 4, tiled=True)]
    ppermute x6, starting transfers between devices: 32 us -> 27.9 us  [halving_scatter(): shaped = keep + lax.ppermute(send, axis, pairs)]
    all_to_all x2, starting transfers between devices: 13.7 us -> 11.5 us  [body(): gathered = lax.all_to_all(part, ('x', 'y'), 2, 4, tiled=True)]
    ppermute x6, waiting for transfers between devices: 10.4 us -> 12.4 us  [halving_scatter(): shaped = keep + lax.ppermute(send, axis, pairs)]
    ppermute x1, waiting for transfers between devices: 1.84 us -> 0.01 us  [body(): other = lax.ppermute(permuted, 'zh', shift_pairs(2, 1))]
  transfers between devices with their start and end apart: 11 -> 11, of which waited for: 6 -> 7; matrix products, arithmetic and copies ran while one was open for 9% -> 8% of each run, Pallas kernels for 8% -> 8%
where the time goes in v11:
time: 125 us; the launch traced here: 123 us
  starting transfers between devices  65.1 us (52%)
  waiting for transfers between devices  31.6 us (25%)
  local copies, waits for them, and re-layouts  14 us (11%)
  Pallas kernels  9.38 us (8%)
  other arithmetic  1.81 us (1%)
    ppermute x6, starting transfers between devices, halving_scatter(): shaped = keep + lax.ppermute(send, axis, pairs)  27.9 us
    all_to_all x2, waiting for transfers between devices, body(): gathered = lax.all_to_all(part, ('x', 'y'), 2, 4, tiled=True)  17.6 us
    ppermute x1, starting transfers between devices, body(): other = lax.ppermute(permuted, 'zh', shift_pairs(2, 1))  16.3 us
    ppermute x6, waiting for transfers between devices, halving_scatter(): shaped = keep + lax.ppermute(send, axis, pairs)  12.4 us
    all_to_all x2, starting transfers between devices, body(): gathered = lax.all_to_all(part, ('x', 'y'), 2, 4, tiled=True)  11.5 us
    ppermute x2, starting transfers between devices, body(): mine = mine + lax.ppermute(theirs, 'core', shift_pairs(2, 1))  9.39 us
    pallas_call x2, Pallas kernels, contract(): pl.pallas_call(contract_kernel, out_shape=jax.ShapeDtypeStruct((2, rows,...  9.38 us
    squeeze x2, local copies, waits for them, and re-layouts, body(): theirs = lax.dynamic_index_in_dim(shaped, 1 - core, 2, keepdims=False)  3.9 us
  transfers between devices with their start and end apart: 11, of which 7 were waited for; matrix products, arithmetic and copies ran while one was open for 8% of the time, Pallas kernels for 8%

profile of v11, /device:TPU:1, one launch (start us, length us, event | category | flops | bytes accessed | tf_op | source)
XLA Modules:
  0.0 122.7 jit_solution(13595533713688148202)
XLA Ops:
  0.0 0.8 fusion.5
  0.8 0.8 fusion.6
  1.6 0.3 fusion
  2.0 0.3 fusion.1
  2.4 16.3 %collective-permute-start = (bf16[2,2,16,512]{3,1,2,0:T(2,128)(2,1)S(1)}, bf16[2,2,16,512]{3,1,2,0:T(2,128)(2,1)S(1)}, u32[]{:S(2)}, u32[]{:S(2)}) collective-permute-start(bf16[2,2,16,512]{3,1,2,0:T(2,128)(2,1)S(1)} %bitcast.79), channel_id=1, source_target_pairs={{0,16},{16,0},{1,17},{17,1},{2,18},{18,2},{3,19},{19,3},{4,20},{20... | collective-permute-start | bytes 196616 | tf_op jit(solution)/shard_map/ppermute | solution.py:100
  18.6 3.3 %copy.26 = bf16[2,512,2,512]{3,1,2,0:T(8,128)(2,1)} copy(bf16[2,512,2,512]{3,2,1,0:T(2,128)(2,1)} %param.4) | data formatting | bytes 4194304 | tf_op args[0]
  21.9 0.0 collective-permute-done
  21.9 0.2 broadcast_select_fusion
  22.1 0.1 fusion.4
  22.2 1.1 broadcast_in_dim.9
  23.3 6.8 %all-to-all-start.1 = ((bf16[2,2,16,2,16,256]{5,4,3,1,0,2:T(8,128)(2,1)}), bf16[2,2,16,2,16,256]{5,4,3,1,0,2:T(8,128)(2,1)S(1)}, u32[]{:S(2)}, u32[]{:S(2)}) async-start(bf16[2,2,16,2,16,256]{5,4,3,1,0,2:T(8,128)(2,1)} %broadcast_in_dim.9), calls=%async_computation.1 | async-start | bytes 2097152 | tf_op jit(solution)/shard_map/all_to_all | solution.py:118
  30.1 14.7 %all-to-all-done.1 = bf16[2,2,16,2,16,256]{5,4,3,1,0,2:T(8,128)(2,1)S(1)} async-done(((bf16[2,2,16,2,16,256]{5,4,3,1,0,2:T(8,128)(2,1)}), bf16[2,2,16,2,16,256]{5,4,3,1,0,2:T(8,128)(2,1)S(1)}, u32[]{:S(2)}, u32[]{:S(2)}) %all-to-all-start.1) | async-done | bytes 1048608 | tf_op jit(solution)/shard_map/all_to_all | solution.py:118
  44.8 1.1 broadcast_in_dim.8
  46.0 4.8 %all-to-all-start = ((bf16[2,2,16,2,16,256]{5,4,3,1,0,2:T(8,128)(2,1)}), bf16[2,2,16,2,16,256]{5,4,3,1,0,2:T(8,128)(2,1)S(1)}, u32[]{:S(2)}, u32[]{:S(2)}) async-start(bf16[2,2,16,2,16,256]{5,4,3,1,0,2:T(8,128)(2,1)} %broadcast_in_dim.8), calls=%async_computation | async-start | bytes 2097152 | tf_op jit(solution)/shard_map/all_to_all | solution.py:118
  50.7 1.1 copy.18
  51.8 4.6 %shard_map.47 = f32[2,512,256]{2,1,0:T(8,128)} custom-call(bf16[2,2,512,512]{3,2,1,0:T(8,128)(2,1)} %bitcast.65, bf16[2,2,512,256]{3,2,1,0:T(8,128)(2,1)} %bitcast.74, bf16[2,512,2,512]{3,2,1,0:T(2,128)(2,1)} %o_ref.3), custom_call_target="tpu_custom_call" | custom-call | flops 1073741824 | bytes 5242880 | tf_op jit(solution)/shard_map/pallas_call | solution.py:68
  56.5 1.9 %dynamic-slice_bitcast_fusion = f32[2,8,32,256]{3,2,1,0:T(8,128)} fusion(f32[2,8,2,32,256]{4,3,2,1,0:T(8,128)} %bitcast.69, s32[]{:T(128)S(6)} %select_n.51), kind=kLoop, calls=%fused_computation.9 | loop fusion | bytes 1048580 | tf_op jit(solution)/shard_map/jit(dynamic_index_in_dim)/squeeze | solution.py:124
  58.4 4.1 %collective-permute-start.5 = (f32[2,8,32,256]{3,2,1,0:T(8,128)}, f32[2,8,32,256]{3,2,1,0:T(8,128)S(1)}, u32[]{:S(2)}, u32[]{:S(2)}) collective-permute-start(f32[2,8,32,256]{3,2,1,0:T(8,128)} %dynamic-slice_bitcast_fusion), channel_id=1, source_target_pairs={{0,32},{32,0},{1,33},{33,1},{2,34},{34,2},{3,35},{35,3},{4,36},{36... | collective-permute-start | bytes 1572872 | tf_op jit(solution)/shard_map/ppermute | solution.py:125
  62.5 2.9 %all-to-all-done = bf16[2,2,16,2,16,256]{5,4,3,1,0,2:T(8,128)(2,1)S(1)} async-done(((bf16[2,2,16,2,16,256]{5,4,3,1,0,2:T(8,128)(2,1)}), bf16[2,2,16,2,16,256]{5,4,3,1,0,2:T(8,128)(2,1)S(1)}, u32[]{:S(2)}, u32[]{:S(2)}) %all-to-all-start) | async-done | bytes 1048608 | tf_op jit(solution)/shard_map/all_to_all | solution.py:118
  65.4 1.1 copy.14
  66.5 4.7 %shard_map.46 = f32[2,512,256]{2,1,0:T(8,128)} custom-call(bf16[2,2,512,512]{3,2,1,0:T(8,128)(2,1)} %bitcast.66, bf16[2,2,512,256]{3,2,1,0:T(8,128)(2,1)} %bitcast.73, bf16[2,512,2,512]{3,2,1,0:T(2,128)(2,1)} %o_ref.3), custom_call_target="tpu_custom_call" | custom-call | flops 1073741824 | bytes 5242880 | tf_op jit(solution)/shard_map/pallas_call | solution.py:68
  71.2 2.0 %dynamic-slice_bitcast_fusion.1 = f32[2,8,32,256]{3,2,1,0:T(8,128)} fusion(f32[2,8,2,32,256]{4,3,2,1,0:T(8,128)} %bitcast.71, s32[]{:T(128)S(6)} %select_n.51), kind=kLoop, calls=%fused_computation.10 | loop fusion | bytes 1048580 | tf_op jit(solution)/shard_map/jit(dynamic_index_in_dim)/squeeze | solution.py:124
  73.2 5.3 %collective-permute-start.1 = (f32[2,8,32,256]{3,2,1,0:T(8,128)}, f32[2,8,32,256]{3,2,1,0:T(8,128)S(1)}, u32[]{:S(2)}, u32[]{:S(2)}) collective-permute-start(f32[2,8,32,256]{3,2,1,0:T(8,128)} %dynamic-slice_bitcast_fusion.1), channel_id=1, source_target_pairs={{0,32},{32,0},{1,33},{33,1},{2,34},{34,2},{3,35},{35,3},{4,36},{36... | collective-permute-start | bytes 1572872 | tf_op jit(solution)/shard_map/ppermute | solution.py:125
  78.5 0.0 collective-permute-done.5
  78.5 0.0 copy-done
  78.5 0.1 bitcast_add_fusion
  78.6 1.6 %collective-permute-done.1 = f32[2,8,32,256]{3,2,1,0:T(8,128)S(1)} collective-permute-done((f32[2,8,32,256]{3,2,1,0:T(8,128)}, f32[2,8,32,256]{3,2,1,0:T(8,128)S(1)}, u32[]{:S(2)}, u32[]{:S(2)}) %collective-permute-start.1) | collective-permute-done | bytes 524320 | tf_op jit(solution)/shard_map/ppermute | solution.py:125
  80.2 0.1 bitcast_add_fusion.1
  80.3 0.1 constant_dynamic-slice_fusion.1
  80.4 0.2 copy.28
  80.6 2.3 %collective-permute-start.2 = (f32[2,2,2,32,256]{4,0,3,1,2:T(2,128)S(1)}, f32[2,2,2,32,256]{4,0,3,1,2:T(2,128)S(1)}, u32[]{:S(2)}, u32[]{:S(2)}) collective-permute-start(f32[2,2,2,32,256]{4,0,3,1,2:T(2,128)S(1)} %bitcast.77), channel_id=1, source_target_pairs={{0,64},{64,0},{128,192},{192,128},{256,320},{320,256},{384,448},{4... | collective-permute-start | bytes 786440 | tf_op jit(solution)/shard_map/ppermute | solution.py:92
  82.9 0.2 copy.27
  83.1 3.0 %collective-permute-start.6 = (f32[2,2,2,32,256]{4,0,3,1,2:T(2,128)S(1)}, f32[2,2,2,32,256]{4,0,3,1,2:T(2,128)S(1)}, u32[]{:S(2)}, u32[]{:S(2)}) collective-permute-start(f32[2,2,2,32,256]{4,0,3,1,2:T(2,128)S(1)} %bitcast.78), channel_id=1, source_target_pairs={{0,64},{64,0},{128,192},{192,128},{256,320},{320,256},{384,448},{4... | collective-permute-start | bytes 786440 | tf_op jit(solution)/shard_map/ppermute | solution.py:92
  86.1 3.9 %collective-permute-done.2 = f32[2,2,2,32,256]{4,0,3,1,2:T(2,128)S(1)} collective-permute-done((f32[2,2,2,32,256]{4,0,3,1,2:T(2,128)S(1)}, f32[2,2,2,32,256]{4,0,3,1,2:T(2,128)S(1)}, u32[]{:S(2)}, u32[]{:S(2)}) %collective-permute-start.2) | collective-permute-done | bytes 262176 | tf_op jit(solution)/shard_map/ppermute | solution.py:92
  90.0 0.3 bitcast_add_fusion.3
  90.3 2.7 %collective-permute-start.3 = (f32[2,2,32,256]{3,0,2,1:T(2,128)S(1)}, f32[2,2,32,256]{3,0,2,1:T(2,128)S(1)}, u32[]{:S(2)}, u32[]{:S(2)}) collective-permute-start(f32[2,2,32,256]{3,0,2,1:T(2,128)S(1)} %dynamic-slice_bitcast_fusion.3), channel_id=1, source_target_pairs={{0,128},{64,192},{128,0},{192,64},{256,384},{320,448},{384,256},{4... | collective-permute-start | bytes 393224 | tf_op jit(solution)/shard_map/ppermute | solution.py:92
  93.1 2.6 %collective-permute-done.6 = f32[2,2,2,32,256]{4,0,3,1,2:T(2,128)S(1)} collective-permute-done((f32[2,2,2,32,256]{4,0,3,1,2:T(2,128)S(1)}, f32[2,2,2,32,256]{4,0,3,1,2:T(2,128)S(1)}, u32[]{:S(2)}, u32[]{:S(2)}) %collective-permute-start.6) | collective-permute-done | bytes 262176 | tf_op jit(solution)/shard_map/ppermute | solution.py:92
  95.6 0.3 bitcast_add_fusion.2
  95.9 2.7 %collective-permute-start.7 = (f32[2,2,32,256]{3,0,2,1:T(2,128)S(1)}, f32[2,2,32,256]{3,0,2,1:T(2,128)S(1)}, u32[]{:S(2)}, u32[]{:S(2)}) collective-permute-start(f32[2,2,32,256]{3,0,2,1:T(2,128)S(1)} %dynamic-slice_bitcast_fusion.2), channel_id=1, source_target_pairs={{0,128},{64,192},{128,0},{192,64},{256,384},{320,448},{384,256},{4... | collective-permute-start | bytes 393224 | tf_op jit(solution)/shard_map/ppermute | solution.py:92
  98.7 1.4 %collective-permute-done.3 = f32[2,2,32,256]{3,0,2,1:T(2,128)S(1)} collective-permute-done((f32[2,2,32,256]{3,0,2,1:T(2,128)S(1)}, f32[2,2,32,256]{3,0,2,1:T(2,128)S(1)}, u32[]{:S(2)}, u32[]{:S(2)}) %collective-permute-start.3) | collective-permute-done | bytes 131104 | tf_op jit(solution)/shard_map/ppermute | solution.py:92
  100.1 0.1 bitcast_add_fusion.5
  100.2 8.9 %collective-permute-start.4 = (f32[2,32,256]{2,0,1:T(2,128)S(1)}, f32[2,32,256]{2,0,1:T(2,128)S(1)}, u32[]{:S(2)}, u32[]{:S(2)}) collective-permute-start(f32[2,32,256]{2,0,1:T(2,128)S(1)} %dynamic-slice_bitcast_fusion.5), channel_id=1, source_target_pairs={{0,256},{64,320},{128,384},{192,448},{256,0},{320,64},{384,128},{4... | collective-permute-start | bytes 196616 | tf_op jit(solution)/shard_map/ppermute | solution.py:92
  109.1 0.0 collective-permute-done.7
  109.1 0.1 bitcast_add_fusion.4
  109.2 8.2 %collective-permute-start.8 = (f32[2,32,256]{2,0,1:T(2,128)S(1)}, f32[2,32,256]{2,0,1:T(2,128)S(1)}, u32[]{:S(2)}, u32[]{:S(2)}) collective-permute-start(f32[2,32,256]{2,0,1:T(2,128)S(1)} %dynamic-slice_bitcast_fusion.4), channel_id=1, source_target_pairs={{0,256},{64,320},{128,384},{192,448},{256,0},{320,64},{384,128},{4... | collective-permute-start | bytes 196616 | tf_op jit(solution)/shard_map/ppermute | solution.py:92
  117.4 0.0 collective-permute-done.4
  117.5 4.5 %collective-permute-done.8 = f32[2,32,256]{2,0,1:T(2,128)S(1)} collective-permute-done((f32[2,32,256]{2,0,1:T(2,128)S(1)}, f32[2,32,256]{2,0,1:T(2,128)S(1)}, u32[]{:S(2)}, u32[]{:S(2)}) %collective-permute-start.8) | collective-permute-done | bytes 65568 | tf_op jit(solution)/shard_map/ppermute | solution.py:92
  122.0 0.7 maximum_bitcast_fusion
  (17 shorter events, 0.3 us)
Async XLA Ops:
  2.4 19.6 %collective-permute-start = (bf16[2,2,16,512]{3,1,2,0:T(2,128)(2,1)S(1)}, bf16[2,2,16,512]{3,1,2,0:T(2,128)(2,1)S(1)}, u32[]{:S(2)}, u32[]{:S(2)}) collective-permute-start(bf16[2,2,16,512]{3,1,2,0:T(2,128)(2,1)S(1)} %bitcast.79), channel_id=1, source_target_pairs={{0,16},{16,0},{1,17},{17,1},{2,18},{18,2},{3,19},{19,3},{4,20},{20... | collective-permute-start | bytes 196616 | tf_op jit(solution)/shard_map/ppermute | solution.py:100
  23.3 21.5 %all-to-all-start.1 = ((bf16[2,2,16,2,16,256]{5,4,3,1,0,2:T(8,128)(2,1)}), bf16[2,2,16,2,16,256]{5,4,3,1,0,2:T(8,128)(2,1)S(1)}, u32[]{:S(2)}, u32[]{:S(2)}) async-start(bf16[2,2,16,2,16,256]{5,4,3,1,0,2:T(8,128)(2,1)} %broadcast_in_dim.9), calls=%async_computation.1 | async-start | bytes 2097152 | tf_op jit(solution)/shard_map/all_to_all | solution.py:118
  46.0 19.4 %all-to-all-start = ((bf16[2,2,16,2,16,256]{5,4,3,1,0,2:T(8,128)(2,1)}), bf16[2,2,16,2,16,256]{5,4,3,1,0,2:T(8,128)(2,1)S(1)}, u32[]{:S(2)}, u32[]{:S(2)}) async-start(bf16[2,2,16,2,16,256]{5,4,3,1,0,2:T(8,128)(2,1)} %broadcast_in_dim.8), calls=%async_computation | async-start | bytes 2097152 | tf_op jit(solution)/shard_map/all_to_all | solution.py:118
  58.4 20.1 %collective-permute-start.5 = (f32[2,8,32,256]{3,2,1,0:T(8,128)}, f32[2,8,32,256]{3,2,1,0:T(8,128)S(1)}, u32[]{:S(2)}, u32[]{:S(2)}) collective-permute-start(f32[2,8,32,256]{3,2,1,0:T(8,128)} %dynamic-slice_bitcast_fusion), channel_id=1, source_target_pairs={{0,32},{32,0},{1,33},{33,1},{2,34},{34,2},{3,35},{35,3},{4,36},{36... | collective-permute-start | bytes 1572872 | tf_op jit(solution)/shard_map/ppermute | solution.py:125
  66.5 12.0 %copy-start = (f32[2,512,256]{2,1,0:T(8,128)S(1)}, f32[2,512,256]{2,1,0:T(8,128)}, u32[]{:S(2)}) copy-start(f32[2,512,256]{2,1,0:T(8,128)} %shard_map.47) | copy-start | bytes 3145732
  71.2 9.0 %copy-start.1 = (f32[2,512,256]{2,1,0:T(8,128)S(1)}, f32[2,512,256]{2,1,0:T(8,128)}, u32[]{:S(2)}) copy-start(f32[2,512,256]{2,1,0:T(8,128)} %shard_map.46) | copy-start | bytes 3145732
  73.2 7.0 %collective-permute-start.1 = (f32[2,8,32,256]{3,2,1,0:T(8,128)}, f32[2,8,32,256]{3,2,1,0:T(8,128)S(1)}, u32[]{:S(2)}, u32[]{:S(2)}) collective-permute-start(f32[2,8,32,256]{3,2,1,0:T(8,128)} %dynamic-slice_bitcast_fusion.1), channel_id=1, source_target_pairs={{0,32},{32,0},{1,33},{33,1},{2,34},{34,2},{3,35},{35,3},{4,36},{36... | collective-permute-start | bytes 1572872 | tf_op jit(solution)/shard_map/ppermute | solution.py:125
  80.6 9.4 %collective-permute-start.2 = (f32[2,2,2,32,256]{4,0,3,1,2:T(2,128)S(1)}, f32[2,2,2,32,256]{4,0,3,1,2:T(2,128)S(1)}, u32[]{:S(2)}, u32[]{:S(2)}) collective-permute-start(f32[2,2,2,32,256]{4,0,3,1,2:T(2,128)S(1)} %bitcast.77), channel_id=1, source_target_pairs={{0,64},{64,0},{128,192},{192,128},{256,320},{320,256},{384,448},{4... | collective-permute-start | bytes 786440 | tf_op jit(solution)/shard_map/ppermute | solution.py:92
  83.1 12.6 %collective-permute-start.6 = (f32[2,2,2,32,256]{4,0,3,1,2:T(2,128)S(1)}, f32[2,2,2,32,256]{4,0,3,1,2:T(2,128)S(1)}, u32[]{:S(2)}, u32[]{:S(2)}) collective-permute-start(f32[2,2,2,32,256]{4,0,3,1,2:T(2,128)S(1)} %bitcast.78), channel_id=1, source_target_pairs={{0,64},{64,0},{128,192},{192,128},{256,320},{320,256},{384,448},{4... | collective-permute-start | bytes 786440 | tf_op jit(solution)/shard_map/ppermute | solution.py:92
  90.3 9.8 %collective-permute-start.3 = (f32[2,2,32,256]{3,0,2,1:T(2,128)S(1)}, f32[2,2,32,256]{3,0,2,1:T(2,128)S(1)}, u32[]{:S(2)}, u32[]{:S(2)}) collective-permute-start(f32[2,2,32,256]{3,0,2,1:T(2,128)S(1)} %dynamic-slice_bitcast_fusion.3), channel_id=1, source_target_pairs={{0,128},{64,192},{128,0},{192,64},{256,384},{320,448},{384,256},{4... | collective-permute-start | bytes 393224 | tf_op jit(solution)/shard_map/ppermute | solution.py:92
  95.9 13.2 %collective-permute-start.7 = (f32[2,2,32,256]{3,0,2,1:T(2,128)S(1)}, f32[2,2,32,256]{3,0,2,1:T(2,128)S(1)}, u32[]{:S(2)}, u32[]{:S(2)}) collective-permute-start(f32[2,2,32,256]{3,0,2,1:T(2,128)S(1)} %dynamic-slice_bitcast_fusion.2), channel_id=1, source_target_pairs={{0,128},{64,192},{128,0},{192,64},{256,384},{320,448},{384,256},{4... | collective-permute-start | bytes 393224 | tf_op jit(solution)/shard_map/ppermute | solution.py:92
  100.2 17.3 %collective-permute-start.4 = (f32[2,32,256]{2,0,1:T(2,128)S(1)}, f32[2,32,256]{2,0,1:T(2,128)S(1)}, u32[]{:S(2)}, u32[]{:S(2)}) collective-permute-start(f32[2,32,256]{2,0,1:T(2,128)S(1)} %dynamic-slice_bitcast_fusion.5), channel_id=1, source_target_pairs={{0,256},{64,320},{128,384},{192,448},{256,0},{320,64},{384,128},{4... | collective-permute-start | bytes 196616 | tf_op jit(solution)/shard_map/ppermute | solution.py:92
  109.2 12.8 %collective-permute-start.8 = (f32[2,32,256]{2,0,1:T(2,128)S(1)}, f32[2,32,256]{2,0,1:T(2,128)S(1)}, u32[]{:S(2)}, u32[]{:S(2)}) collective-permute-start(f32[2,32,256]{2,0,1:T(2,128)S(1)} %dynamic-slice_bitcast_fusion.4), channel_id=1, source_target_pairs={{0,256},{64,320},{128,384},{192,448},{256,0},{320,64},{384,128},{4... | collective-permute-start | bytes 196616 | tf_op jit(solution)/shard_map/ppermute | solution.py:92

commit v12 on v11

--- a/solution.py
+++ b/solution.py
@@ -61,17 +61,17 @@
 
 def contract(stem_t, branch_t, open_t, column_block):
     slices, _, rows, depth = stem_t.shape
-    width = branch_t.shape[-1]
+    width = depth // 2
     tile = min(ROW_TILE, rows)
     flops = slices * 8 * rows * depth * width
-    moved = 2 * (stem_t.size + branch_t.size) + 2 * slices * 2 * rows * width + 4 * 2 * rows * width
+    moved = 2 * (stem_t.size + branch_t.size // 2) + 2 * slices * 2 * rows * width + 4 * 2 * rows * width
     return pl.pallas_call(
         contract_kernel,
         out_shape=jax.ShapeDtypeStruct((2, rows, width), jnp.float32),
         grid=(rows // tile,),
         in_specs=[
             pl.BlockSpec((slices, 2, tile, depth), lambda i: (0, 0, i, 0)),
-            pl.BlockSpec((slices, 2, depth, width), lambda i: (0, 0, 0, 0)),
+            pl.BlockSpec((slices, 2, depth, width), lambda i: (0, 0, 0, column_block)),
             pl.BlockSpec((slices, tile, 2, width), lambda i: (0, i, 0, column_block)),
         ],
         out_specs=pl.BlockSpec((2, tile, width), lambda i: (0, i, 0)),
@@ -102,6 +102,8 @@
     pair = jnp.where(low, jnp.stack([permuted, other], axis=2), jnp.stack([other, permuted], axis=2))
     plane = lax.axis_size("x") * lax.axis_size("y")
     copies = jnp.broadcast_to(pair[:, :, None], pair.shape[:2] + (plane,) + pair.shape[2:])
+    gathered = lax.all_to_all(copies, ("x", "y"), 2, 4, tiled=True)
+    branch_t = gathered.reshape(slice_count, 2, -1, width)
     halves = 2
     span = width // halves
     stem_t = jnp.transpose(stem_tensor, (0, 2, 1, 3))
@@ -110,14 +112,7 @@
     block_rows = row_count // (zl_count * 2)
     core = lax.axis_index("core")
     results = []
-    previous = None
     for h in range(halves):
-        part = copies[..., h * span:(h + 1) * span]
-        if previous is not None:
-            part, previous, stem_t = lax.optimization_barrier((part, previous, stem_t))
-        gathered = lax.all_to_all(part, ("x", "y"), 2, 4, tiled=True)
-        previous = gathered
-        branch_t = gathered.reshape(slice_count, 2, -1, span)
         local_sum = contract(stem_t, branch_t, open_t, h)
         shaped = local_sum.reshape(2, zl_count, 2, block_rows, span)
         mine = lax.dynamic_index_in_dim(shaped, core, 2, keepdims=False)

time: 125 us -> 125 us (level)
  the two profiles are of different devices: /device:TPU:1 before, /device:TPU:8 now
where the time goes in v12:
time: 125 us
  starting transfers between devices  57.9 us (46%)
  waiting for transfers between devices  42.1 us (34%)
  local copies, waits for them, and re-layouts  12.6 us (10%)
  Pallas kernels  9.37 us (7%)
  other arithmetic  1.81 us (1%)
    ppermute x6, starting transfers between devices, halving_scatter(): shaped = keep + lax.ppermute(send, axis, pairs)  30.4 us
    all_to_all x1, waiting for transfers between devices, body(): gathered = lax.all_to_all(copies, ('x', 'y'), 2, 4, tiled=True)  22.7 us
    ppermute x1, starting transfers between devices, body(): other = lax.ppermute(permuted, 'zh', shift_pairs(2, 1))  15.7 us
    ppermute x6, waiting for transfers between devices, halving_scatter(): shaped = keep + lax.ppermute(send, axis, pairs)  13.6 us
    pallas_call x2, Pallas kernels, contract(): pl.pallas_call(contract_kernel, out_shape=jax.ShapeDtypeStruct((2, rows,...  9.37 us
    all_to_all x1, starting transfers between devices, body(): gathered = lax.all_to_all(copies, ('x', 'y'), 2, 4, tiled=True)  7.39 us
    ppermute x2, starting transfers between devices, body(): mine = mine + lax.ppermute(theirs, 'core', shift_pairs(2, 1))  4.43 us
    ppermute x1, waiting for transfers between devices, body(): other = lax.ppermute(permuted, 'zh', shift_pairs(2, 1))  4.2 us
  transfers between devices with their start and end apart: 10, of which 8 were waited for; matrix products, arithmetic and copies ran while one was open for 5% of the time, Pallas kernels for 4%

profile of v12, /device:TPU:8, one launch (start us, length us, event | category | flops | bytes accessed | tf_op | source)
XLA Modules:
  0.0 124.6 jit_solution(6258458214099360456)
XLA Ops:
  0.0 0.8 fusion.5
  0.8 0.8 fusion.4
  1.6 0.3 fusion.1
  2.0 0.3 fusion
  2.3 15.7 %collective-permute-start = (bf16[2,2,16,512]{3,1,2,0:T(2,128)(2,1)S(1)}, bf16[2,2,16,512]{3,1,2,0:T(2,128)(2,1)S(1)}, u32[]{:S(2)}, u32[]{:S(2)}) collective-permute-start(bf16[2,2,16,512]{3,1,2,0:T(2,128)(2,1)S(1)} %bitcast.74), channel_id=1, source_target_pairs={{0,16},{16,0},{1,17},{17,1},{2,18},{18,2},{3,19},{19,3},{4,20},{20... | collective-permute-start | bytes 196616 | tf_op jit(solution)/shard_map/ppermute | solution.py:100
  18.1 4.2 %collective-permute-done = bf16[2,2,16,512]{3,1,2,0:T(2,128)(2,1)S(1)} collective-permute-done((bf16[2,2,16,512]{3,1,2,0:T(2,128)(2,1)S(1)}, bf16[2,2,16,512]{3,1,2,0:T(2,128)(2,1)S(1)}, u32[]{:S(2)}, u32[]{:S(2)}) %collective-permute-start) | collective-permute-done | bytes 65568 | tf_op jit(solution)/shard_map/ppermute | solution.py:100
  22.3 0.2 broadcast_select_fusion
  22.5 1.6 %broadcast_in_dim.2 = bf16[2,2,16,2,16,512]{5,4,3,1,0,2:T(8,128)(2,1)} broadcast(bf16[2,2,2,16,512]{4,3,2,1,0:T(8,128)(2,1)S(1)} %copy.12), dimensions={0,1,3,4,5} | broadcast | bytes 2228224 | tf_op jit(solution)/shard_map/broadcast_in_dim | solution.py:104
  24.1 7.4 %all-to-all-start = ((bf16[2,2,16,2,16,512]{5,4,3,1,0,2:T(8,128)(2,1)}), bf16[2,2,16,2,16,512]{5,4,3,1,0,2:T(8,128)(2,1)S(1)}, u32[]{:S(2)}, u32[]{:S(2)}) async-start(bf16[2,2,16,2,16,512]{5,4,3,1,0,2:T(8,128)(2,1)} %broadcast_in_dim.2), calls=%async_computation | async-start | bytes 4194304 | tf_op jit(solution)/shard_map/all_to_all | solution.py:105
  31.5 3.3 %copy.23 = bf16[2,512,2,512]{3,1,2,0:T(8,128)(2,1)} copy(bf16[2,512,2,512]{3,2,1,0:T(2,128)(2,1)} %param.4) | data formatting | bytes 4194304 | tf_op args[0]
  34.7 22.7 %all-to-all-done = bf16[2,2,16,2,16,512]{5,4,3,1,0,2:T(8,128)(2,1)S(1)} async-done(((bf16[2,2,16,2,16,512]{5,4,3,1,0,2:T(8,128)(2,1)}), bf16[2,2,16,2,16,512]{5,4,3,1,0,2:T(8,128)(2,1)S(1)}, u32[]{:S(2)}, u32[]{:S(2)}) %all-to-all-start) | async-done | bytes 2097184 | tf_op jit(solution)/shard_map/all_to_all | solution.py:105
  57.5 1.5 %copy.13 = bf16[2,2,1,2,16,16,512]{6,5,4,3,1,0,2:T(8,128)(2,1)} copy(bf16[2,2,1,2,16,16,512]{6,5,3,1,0,4,2:T(8,128)(2,1)S(1)} %bitcast.65) | data formatting | bytes 4194304 | tf_op jit(solution)/shard_map/all_to_all | solution.py:105
  59.0 4.7 %shard_map.46 = f32[2,512,256]{2,1,0:T(8,128)} custom-call(bf16[2,2,512,512]{3,2,1,0:T(8,128)(2,1)} %bitcast.61, bf16[2,2,512,512]{3,2,1,0:T(8,128)(2,1)} %bitcast.63, bf16[2,512,2,512]{3,2,1,0:T(2,128)(2,1)} %o_ref.3), custom_call_target="tpu_custom_call" | custom-call | flops 1073741824 | bytes 5242880 | tf_op jit(solution)/shard_map/pallas_call | solution.py:68
  63.7 1.9 %dynamic-slice_bitcast_fusion.1 = f32[2,8,32,256]{3,2,1,0:T(8,128)} fusion(f32[2,8,2,32,256]{4,3,2,1,0:T(8,128)} %bitcast.68, s32[]{:T(128)S(6)} %select_n.51), kind=kLoop, calls=%fused_computation.10 | loop fusion | bytes 1048580 | tf_op jit(solution)/shard_map/jit(dynamic_index_in_dim)/squeeze | solution.py:119
  65.6 0.0 copy-start.1
  65.6 2.0 %collective-permute-start.1 = (f32[2,8,32,256]{3,2,1,0:T(8,128)}, f32[2,8,32,256]{3,2,1,0:T(8,128)S(1)}, u32[]{:S(2)}, u32[]{:S(2)}) collective-permute-start(f32[2,8,32,256]{3,2,1,0:T(8,128)} %dynamic-slice_bitcast_fusion.1), channel_id=1, source_target_pairs={{0,32},{32,0},{1,33},{33,1},{2,34},{34,2},{3,35},{35,3},{4,36},{36... | collective-permute-start | bytes 1572872 | tf_op jit(solution)/shard_map/ppermute | solution.py:120
  67.6 4.7 %shard_map.47 = f32[2,512,256]{2,1,0:T(8,128)} custom-call(bf16[2,2,512,512]{3,2,1,0:T(8,128)(2,1)} %bitcast.62, bf16[2,2,512,512]{3,2,1,0:T(8,128)(2,1)} %bitcast.64, bf16[2,512,2,512]{3,2,1,0:T(2,128)(2,1)} %o_ref.3), custom_call_target="tpu_custom_call" | custom-call | flops 1073741824 | bytes 5242880 | tf_op jit(solution)/shard_map/pallas_call | solution.py:68
  72.3 0.0 copy-start
  72.3 2.0 %dynamic-slice_bitcast_fusion = f32[2,8,32,256]{3,2,1,0:T(8,128)} fusion(f32[2,8,2,32,256]{4,3,2,1,0:T(8,128)} %bitcast.66, s32[]{:T(128)S(6)} %select_n.51), kind=kLoop, calls=%fused_computation.9 | loop fusion | bytes 1048580 | tf_op jit(solution)/shard_map/jit(dynamic_index_in_dim)/squeeze | solution.py:119
  74.3 2.4 %collective-permute-start.5 = (f32[2,8,32,256]{3,2,1,0:T(8,128)}, f32[2,8,32,256]{3,2,1,0:T(8,128)S(1)}, u32[]{:S(2)}, u32[]{:S(2)}) collective-permute-start(f32[2,8,32,256]{3,2,1,0:T(8,128)} %dynamic-slice_bitcast_fusion), channel_id=1, source_target_pairs={{0,32},{32,0},{1,33},{33,1},{2,34},{34,2},{3,35},{35,3},{4,36},{36... | collective-permute-start | bytes 1572872 | tf_op jit(solution)/shard_map/ppermute | solution.py:120
  76.7 0.0 collective-permute-done.1
  76.7 0.0 copy-done.1
  76.7 0.1 bitcast_add_fusion.1
  76.8 1.6 %collective-permute-done.5 = f32[2,8,32,256]{3,2,1,0:T(8,128)S(1)} collective-permute-done((f32[2,8,32,256]{3,2,1,0:T(8,128)}, f32[2,8,32,256]{3,2,1,0:T(8,128)S(1)}, u32[]{:S(2)}, u32[]{:S(2)}) %collective-permute-start.5) | collective-permute-done | bytes 524320 | tf_op jit(solution)/shard_map/ppermute | solution.py:120
  78.4 0.0 copy-done
  78.4 0.1 bitcast_add_fusion
  78.5 0.1 constant_dynamic-slice_fusion.1
  78.6 0.2 copy.25
  78.8 2.8 %collective-permute-start.2 = (f32[2,2,2,32,256]{4,0,3,1,2:T(2,128)S(1)}, f32[2,2,2,32,256]{4,0,3,1,2:T(2,128)S(1)}, u32[]{:S(2)}, u32[]{:S(2)}) collective-permute-start(f32[2,2,2,32,256]{4,0,3,1,2:T(2,128)S(1)} %bitcast.72), channel_id=1, source_target_pairs={{0,64},{64,0},{128,192},{192,128},{256,320},{320,256},{384,448},{4... | collective-permute-start | bytes 786440 | tf_op jit(solution)/shard_map/ppermute | solution.py:92
  81.7 0.2 copy.24
  81.9 3.0 %collective-permute-start.6 = (f32[2,2,2,32,256]{4,0,3,1,2:T(2,128)S(1)}, f32[2,2,2,32,256]{4,0,3,1,2:T(2,128)S(1)}, u32[]{:S(2)}, u32[]{:S(2)}) collective-permute-start(f32[2,2,2,32,256]{4,0,3,1,2:T(2,128)S(1)} %bitcast.73), channel_id=1, source_target_pairs={{0,64},{64,0},{128,192},{192,128},{256,320},{320,256},{384,448},{4... | collective-permute-start | bytes 786440 | tf_op jit(solution)/shard_map/ppermute | solution.py:92
  84.9 4.9 %collective-permute-done.2 = f32[2,2,2,32,256]{4,0,3,1,2:T(2,128)S(1)} collective-permute-done((f32[2,2,2,32,256]{4,0,3,1,2:T(2,128)S(1)}, f32[2,2,2,32,256]{4,0,3,1,2:T(2,128)S(1)}, u32[]{:S(2)}, u32[]{:S(2)}) %collective-permute-start.2) | collective-permute-done | bytes 262176 | tf_op jit(solution)/shard_map/ppermute | solution.py:92
  89.9 0.3 bitcast_add_fusion.3
  90.2 3.4 %collective-permute-start.3 = (f32[2,2,32,256]{3,0,2,1:T(2,128)S(1)}, f32[2,2,32,256]{3,0,2,1:T(2,128)S(1)}, u32[]{:S(2)}, u32[]{:S(2)}) collective-permute-start(f32[2,2,32,256]{3,0,2,1:T(2,128)S(1)} %dynamic-slice_bitcast_fusion.3), channel_id=1, source_target_pairs={{0,128},{64,192},{128,0},{192,64},{256,384},{320,448},{384,256},{4... | collective-permute-start | bytes 393224 | tf_op jit(solution)/shard_map/ppermute | solution.py:92
  93.6 2.5 %collective-permute-done.6 = f32[2,2,2,32,256]{4,0,3,1,2:T(2,128)S(1)} collective-permute-done((f32[2,2,2,32,256]{4,0,3,1,2:T(2,128)S(1)}, f32[2,2,2,32,256]{4,0,3,1,2:T(2,128)S(1)}, u32[]{:S(2)}, u32[]{:S(2)}) %collective-permute-start.6) | collective-permute-done | bytes 262176 | tf_op jit(solution)/shard_map/ppermute | solution.py:92
  96.0 0.3 bitcast_add_fusion.2
  96.3 2.8 %collective-permute-start.7 = (f32[2,2,32,256]{3,0,2,1:T(2,128)S(1)}, f32[2,2,32,256]{3,0,2,1:T(2,128)S(1)}, u32[]{:S(2)}, u32[]{:S(2)}) collective-permute-start(f32[2,2,32,256]{3,0,2,1:T(2,128)S(1)} %dynamic-slice_bitcast_fusion.2), channel_id=1, source_target_pairs={{0,128},{64,192},{128,0},{192,64},{256,384},{320,448},{384,256},{4... | collective-permute-start | bytes 393224 | tf_op jit(solution)/shard_map/ppermute | solution.py:92
  99.2 1.0 collective-permute-done.3
  100.2 0.1 bitcast_add_fusion.5
  100.3 12.7 %collective-permute-start.4 = (f32[2,32,256]{2,0,1:T(2,128)S(1)}, f32[2,32,256]{2,0,1:T(2,128)S(1)}, u32[]{:S(2)}, u32[]{:S(2)}) collective-permute-start(f32[2,32,256]{2,0,1:T(2,128)S(1)} %dynamic-slice_bitcast_fusion.5), channel_id=1, source_target_pairs={{0,256},{64,320},{128,384},{192,448},{256,0},{320,64},{384,128},{4... | collective-permute-start | bytes 196616 | tf_op jit(solution)/shard_map/ppermute | solution.py:92
  113.0 0.0 collective-permute-done.7
  113.0 0.1 bitcast_add_fusion.4
  113.1 5.6 %collective-permute-start.8 = (f32[2,32,256]{2,0,1:T(2,128)S(1)}, f32[2,32,256]{2,0,1:T(2,128)S(1)}, u32[]{:S(2)}, u32[]{:S(2)}) collective-permute-start(f32[2,32,256]{2,0,1:T(2,128)S(1)} %dynamic-slice_bitcast_fusion.4), channel_id=1, source_target_pairs={{0,256},{64,320},{128,384},{192,448},{256,0},{320,64},{384,128},{4... | collective-permute-start | bytes 196616 | tf_op jit(solution)/shard_map/ppermute | solution.py:92
  118.7 0.6 collective-permute-done.4
  119.4 4.5 %collective-permute-done.8 = f32[2,32,256]{2,0,1:T(2,128)S(1)} collective-permute-done((f32[2,32,256]{2,0,1:T(2,128)S(1)}, f32[2,32,256]{2,0,1:T(2,128)S(1)}, u32[]{:S(2)}, u32[]{:S(2)}) %collective-permute-start.8) | collective-permute-done | bytes 65568 | tf_op jit(solution)/shard_map/ppermute | solution.py:92
  123.9 0.7 maximum_bitcast_fusion
  (13 shorter events, 0.3 us)
Async XLA Ops:
  2.3 19.9 %collective-permute-start = (bf16[2,2,16,512]{3,1,2,0:T(2,128)(2,1)S(1)}, bf16[2,2,16,512]{3,1,2,0:T(2,128)(2,1)S(1)}, u32[]{:S(2)}, u32[]{:S(2)}) collective-permute-start(bf16[2,2,16,512]{3,1,2,0:T(2,128)(2,1)S(1)} %bitcast.74), channel_id=1, source_target_pairs={{0,16},{16,0},{1,17},{17,1},{2,18},{18,2},{3,19},{19,3},{4,20},{20... | collective-permute-start | bytes 196616 | tf_op jit(solution)/shard_map/ppermute | solution.py:100
  24.1 33.4 %all-to-all-start = ((bf16[2,2,16,2,16,512]{5,4,3,1,0,2:T(8,128)(2,1)}), bf16[2,2,16,2,16,512]{5,4,3,1,0,2:T(8,128)(2,1)S(1)}, u32[]{:S(2)}, u32[]{:S(2)}) async-start(bf16[2,2,16,2,16,512]{5,4,3,1,0,2:T(8,128)(2,1)} %broadcast_in_dim.2), calls=%async_computation | async-start | bytes 4194304 | tf_op jit(solution)/shard_map/all_to_all | solution.py:105
  65.6 11.2 %copy-start.1 = (f32[2,512,256]{2,1,0:T(8,128)S(1)}, f32[2,512,256]{2,1,0:T(8,128)}, u32[]{:S(2)}) copy-start(f32[2,512,256]{2,1,0:T(8,128)} %shard_map.46) | copy-start | bytes 3145732
  65.6 11.1 %collective-permute-start.1 = (f32[2,8,32,256]{3,2,1,0:T(8,128)}, f32[2,8,32,256]{3,2,1,0:T(8,128)S(1)}, u32[]{:S(2)}, u32[]{:S(2)}) collective-permute-start(f32[2,8,32,256]{3,2,1,0:T(8,128)} %dynamic-slice_bitcast_fusion.1), channel_id=1, source_target_pairs={{0,32},{32,0},{1,33},{33,1},{2,34},{34,2},{3,35},{35,3},{4,36},{36... | collective-permute-start | bytes 1572872 | tf_op jit(solution)/shard_map/ppermute | solution.py:120
  72.3 6.1 %copy-start = (f32[2,512,256]{2,1,0:T(8,128)S(1)}, f32[2,512,256]{2,1,0:T(8,128)}, u32[]{:S(2)}) copy-start(f32[2,512,256]{2,1,0:T(8,128)} %shard_map.47) | copy-start | bytes 3145732
  74.3 4.1 %collective-permute-start.5 = (f32[2,8,32,256]{3,2,1,0:T(8,128)}, f32[2,8,32,256]{3,2,1,0:T(8,128)S(1)}, u32[]{:S(2)}, u32[]{:S(2)}) collective-permute-start(f32[2,8,32,256]{3,2,1,0:T(8,128)} %dynamic-slice_bitcast_fusion), channel_id=1, source_target_pairs={{0,32},{32,0},{1,33},{33,1},{2,34},{34,2},{3,35},{35,3},{4,36},{36... | collective-permute-start | bytes 1572872 | tf_op jit(solution)/shard_map/ppermute | solution.py:120
  78.8 11.0 %collective-permute-start.2 = (f32[2,2,2,32,256]{4,0,3,1,2:T(2,128)S(1)}, f32[2,2,2,32,256]{4,0,3,1,2:T(2,128)S(1)}, u32[]{:S(2)}, u32[]{:S(2)}) collective-permute-start(f32[2,2,2,32,256]{4,0,3,1,2:T(2,128)S(1)} %bitcast.72), channel_id=1, source_target_pairs={{0,64},{64,0},{128,192},{192,128},{256,320},{320,256},{384,448},{4... | collective-permute-start | bytes 786440 | tf_op jit(solution)/shard_map/ppermute | solution.py:92
  81.9 14.2 %collective-permute-start.6 = (f32[2,2,2,32,256]{4,0,3,1,2:T(2,128)S(1)}, f32[2,2,2,32,256]{4,0,3,1,2:T(2,128)S(1)}, u32[]{:S(2)}, u32[]{:S(2)}) collective-permute-start(f32[2,2,2,32,256]{4,0,3,1,2:T(2,128)S(1)} %bitcast.73), channel_id=1, source_target_pairs={{0,64},{64,0},{128,192},{192,128},{256,320},{320,256},{384,448},{4... | collective-permute-start | bytes 786440 | tf_op jit(solution)/shard_map/ppermute | solution.py:92
  90.2 10.0 %collective-permute-start.3 = (f32[2,2,32,256]{3,0,2,1:T(2,128)S(1)}, f32[2,2,32,256]{3,0,2,1:T(2,128)S(1)}, u32[]{:S(2)}, u32[]{:S(2)}) collective-permute-start(f32[2,2,32,256]{3,0,2,1:T(2,128)S(1)} %dynamic-slice_bitcast_fusion.3), channel_id=1, source_target_pairs={{0,128},{64,192},{128,0},{192,64},{256,384},{320,448},{384,256},{4... | collective-permute-start | bytes 393224 | tf_op jit(solution)/shard_map/ppermute | solution.py:92
  96.3 16.7 %collective-permute-start.7 = (f32[2,2,32,256]{3,0,2,1:T(2,128)S(1)}, f32[2,2,32,256]{3,0,2,1:T(2,128)S(1)}, u32[]{:S(2)}, u32[]{:S(2)}) collective-permute-start(f32[2,2,32,256]{3,0,2,1:T(2,128)S(1)} %dynamic-slice_bitcast_fusion.2), channel_id=1, source_target_pairs={{0,128},{64,192},{128,0},{192,64},{256,384},{320,448},{384,256},{4... | collective-permute-start | bytes 393224 | tf_op jit(solution)/shard_map/ppermute | solution.py:92
  100.3 19.1 %collective-permute-start.4 = (f32[2,32,256]{2,0,1:T(2,128)S(1)}, f32[2,32,256]{2,0,1:T(2,128)S(1)}, u32[]{:S(2)}, u32[]{:S(2)}) collective-permute-start(f32[2,32,256]{2,0,1:T(2,128)S(1)} %dynamic-slice_bitcast_fusion.5), channel_id=1, source_target_pairs={{0,256},{64,320},{128,384},{192,448},{256,0},{320,64},{384,128},{4... | collective-permute-start | bytes 196616 | tf_op jit(solution)/shard_map/ppermute | solution.py:92
  113.1 10.8 %collective-permute-start.8 = (f32[2,32,256]{2,0,1:T(2,128)S(1)}, f32[2,32,256]{2,0,1:T(2,128)S(1)}, u32[]{:S(2)}, u32[]{:S(2)}) collective-permute-start(f32[2,32,256]{2,0,1:T(2,128)S(1)} %dynamic-slice_bitcast_fusion.4), channel_id=1, source_target_pairs={{0,256},{64,320},{128,384},{192,448},{256,0},{320,64},{384,128},{4... | collective-permute-start | bytes 196616 | tf_op jit(solution)/shard_map/ppermute | solution.py:92

commit v13 on v12

--- a/solution.py
+++ b/solution.py
@@ -118,7 +118,11 @@
         mine = lax.dynamic_index_in_dim(shaped, core, 2, keepdims=False)
         theirs = lax.dynamic_index_in_dim(shaped, 1 - core, 2, keepdims=False)
         mine = mine + lax.ppermute(theirs, "core", shift_pairs(2, 1))
-        results.append(halving_scatter(mine, "zl"))
+        if h == 0:
+            results.append(halving_scatter(mine, "zl"))
+        else:
+            summed = lax.psum_scatter(mine, "zl", scatter_dimension=1, tiled=True)
+            results.append(summed.reshape(2, block_rows, span))
     result = jnp.concatenate(results, axis=-1)
     return jnp.transpose(result, (1, 0, 2)).reshape(1, block_rows, 2, width)
 

time: 125 us -> 161 us (1.29)
  the two profiles are of different devices: /device:TPU:8 before, /device:TPU:2 now
where the time goes in v13:
time: 161 us; the launch traced here: 160 us
  waiting for transfers between devices  79 us (49%)
  starting transfers between devices  43.3 us (27%)
  between operations  13.6 us (8%)
  local copies, waits for them, and re-layouts  12.3 us (8%)
  Pallas kernels  9.33 us (6%)
  other arithmetic  2.05 us (1%)
    reduce_scatter x1, waiting for transfers between devices, body(): summed = lax.psum_scatter(mine, 'zl', scatter_dimension=1, tiled=True)  31.8 us
    all_to_all x1, waiting for transfers between devices, body(): gathered = lax.all_to_all(copies, ('x', 'y'), 2, 4, tiled=True)  21.5 us
    ppermute x3, waiting for transfers between devices, halving_scatter(): shaped = keep + lax.ppermute(send, axis, pairs)  21.5 us
    ppermute x1, starting transfers between devices, body(): other = lax.ppermute(permuted, 'zh', shift_pairs(2, 1))  15.7 us
    ppermute x3, starting transfers between devices, halving_scatter(): shaped = keep + lax.ppermute(send, axis, pairs)  15.7 us
    pallas_call x2, Pallas kernels, contract(): pl.pallas_call(contract_kernel, out_shape=jax.ShapeDtypeStruct((2, rows,...  9.33 us
    all_to_all x1, starting transfers between devices, body(): gathered = lax.all_to_all(copies, ('x', 'y'), 2, 4, tiled=True)  7.48 us
    ppermute x2, starting transfers between devices, body(): mine = mine + lax.ppermute(theirs, 'core', shift_pairs(2, 1))  4.32 us
  transfers between devices with their start and end apart: 8, of which 6 were waited for; matrix products, arithmetic and copies ran while one was open for 4% of the time, Pallas kernels for 3%

profile of v13, /device:TPU:2, one launch (start us, length us, event | category | flops | bytes accessed | tf_op | source)
XLA Modules:
  0.0 160.2 jit_solution(4520227837350968952)
XLA Ops:
  6.5 0.8 fusion.5
  7.3 0.8 fusion.4
  8.2 0.3 fusion.1
  8.5 0.3 fusion
  8.9 15.7 %collective-permute-start = (bf16[2,2,16,512]{3,1,2,0:T(2,128)(2,1)S(1)}, bf16[2,2,16,512]{3,1,2,0:T(2,128)(2,1)S(1)}, u32[]{:S(2)}, u32[]{:S(2)}) collective-permute-start(bf16[2,2,16,512]{3,1,2,0:T(2,128)(2,1)S(1)} %bitcast.60), channel_id=1, source_target_pairs={{0,16},{16,0},{1,17},{17,1},{2,18},{18,2},{3,19},{19,3},{4,20},{20... | collective-permute-start | bytes 196616 | tf_op jit(solution)/shard_map/ppermute | solution.py:100
  24.6 4.2 %collective-permute-done = bf16[2,2,16,512]{3,1,2,0:T(2,128)(2,1)S(1)} collective-permute-done((bf16[2,2,16,512]{3,1,2,0:T(2,128)(2,1)S(1)}, bf16[2,2,16,512]{3,1,2,0:T(2,128)(2,1)S(1)}, u32[]{:S(2)}, u32[]{:S(2)}) %collective-permute-start) | collective-permute-done | bytes 65568 | tf_op jit(solution)/shard_map/ppermute | solution.py:100
  28.8 0.2 broadcast_select_fusion
  29.0 1.6 broadcast_in_dim.2
  30.6 7.5 %all-to-all-start = ((bf16[2,2,16,2,16,512]{5,4,3,1,0,2:T(8,128)(2,1)}), bf16[2,2,16,2,16,512]{5,4,3,1,0,2:T(8,128)(2,1)S(1)}, u32[]{:S(2)}, u32[]{:S(2)}) async-start(bf16[2,2,16,2,16,512]{5,4,3,1,0,2:T(8,128)(2,1)} %broadcast_in_dim.2), calls=%async_computation | async-start | bytes 4194304 | tf_op jit(solution)/shard_map/all_to_all | solution.py:105
  38.1 0.0 reduce-scatter.2.cloned.1.call-start
  38.1 3.3 %copy.24 = bf16[2,512,2,512]{3,1,2,0:T(8,128)(2,1)} copy(bf16[2,512,2,512]{3,2,1,0:T(2,128)(2,1)} %param.4) | data formatting | bytes 4194304 | tf_op args[0]
  41.4 21.5 %all-to-all-done = bf16[2,2,16,2,16,512]{5,4,3,1,0,2:T(8,128)(2,1)S(1)} async-done(((bf16[2,2,16,2,16,512]{5,4,3,1,0,2:T(8,128)(2,1)}), bf16[2,2,16,2,16,512]{5,4,3,1,0,2:T(8,128)(2,1)S(1)}, u32[]{:S(2)}, u32[]{:S(2)}) %all-to-all-start) | async-done | bytes 2097184 | tf_op jit(solution)/shard_map/all_to_all | solution.py:105
  62.9 1.5 copy.13
  64.4 4.7 %shard_map.46 = f32[2,512,256]{2,1,0:T(8,128)} custom-call(bf16[2,2,512,512]{3,2,1,0:T(8,128)(2,1)} %bitcast.49, bf16[2,2,512,512]{3,2,1,0:T(8,128)(2,1)} %bitcast.51, bf16[2,512,2,512]{3,2,1,0:T(2,128)(2,1)} %o_ref.3), custom_call_target="tpu_custom_call" | custom-call | flops 1073741824 | bytes 5242880 | tf_op jit(solution)/shard_map/pallas_call | solution.py:68
  69.1 1.9 %dynamic-slice_bitcast_fusion = f32[2,8,32,256]{3,2,1,0:T(8,128)} fusion(f32[2,8,2,32,256]{4,3,2,1,0:T(8,128)} %bitcast.54, s32[]{:T(128)S(6)} %select_n.45), kind=kLoop, calls=%fused_computation.10 | loop fusion | bytes 1048580 | tf_op jit(solution)/shard_map/jit(dynamic_index_in_dim)/squeeze | solution.py:119
  71.0 1.9 %collective-permute-start.1 = (f32[2,8,32,256]{3,2,1,0:T(8,128)}, f32[2,8,32,256]{3,2,1,0:T(8,128)S(1)}, u32[]{:S(2)}, u32[]{:S(2)}) collective-permute-start(f32[2,8,32,256]{3,2,1,0:T(8,128)} %dynamic-slice_bitcast_fusion), channel_id=1, source_target_pairs={{0,32},{32,0},{1,33},{33,1},{2,34},{34,2},{3,35},{35,3},{4,36},{36... | collective-permute-start | bytes 1572872 | tf_op jit(solution)/shard_map/ppermute | solution.py:120
  72.9 4.7 %shard_map.47 = f32[2,512,256]{2,1,0:T(8,128)} custom-call(bf16[2,2,512,512]{3,2,1,0:T(8,128)(2,1)} %bitcast.50, bf16[2,2,512,512]{3,2,1,0:T(8,128)(2,1)} %bitcast.52, bf16[2,512,2,512]{3,2,1,0:T(2,128)(2,1)} %o_ref.3), custom_call_target="tpu_custom_call" | custom-call | flops 1073741824 | bytes 5242880 | tf_op jit(solution)/shard_map/pallas_call | solution.py:68
  77.6 0.0 copy-start
  77.6 1.4 constant_dynamic-slice_fusion.1
  79.0 2.4 %collective-permute-start.5 = (f32[2,8,32,256]{3,2,0,1:T(8,128)S(1)}, f32[2,8,32,256]{3,2,0,1:T(8,128)S(1)}, u32[]{:S(2)}, u32[]{:S(2)}) collective-permute-start(f32[2,8,32,256]{3,2,0,1:T(8,128)S(1)} %bitcast.58), channel_id=1, source_target_pairs={{0,32},{32,0},{1,33},{33,1},{2,34},{34,2},{3,35},{35,3},{4,36},{36... | collective-permute-start | bytes 1572872 | tf_op jit(solution)/shard_map/ppermute | solution.py:120
  81.4 0.0 collective-permute-done.1
  81.4 0.0 copy-done
  81.5 0.1 bitcast_add_fusion.1
  81.6 2.5 %collective-permute-start.2 = (f32[2,2,2,32,256]{4,3,0,1,2:T(8,128)S(1)}, f32[2,2,2,32,256]{4,3,0,1,2:T(8,128)S(1)}, u32[]{:S(2)}, u32[]{:S(2)}) collective-permute-start(f32[2,2,2,32,256]{4,3,0,1,2:T(8,128)S(1)} %bitcast.59), channel_id=1, source_target_pairs={{0,64},{64,0},{128,192},{192,128},{256,320},{320,256},{384,448},{4... | collective-permute-start | bytes 786440 | tf_op jit(solution)/shard_map/ppermute | solution.py:92
  84.1 0.0 collective-permute-done.5
  84.1 0.9 bitcast_add_fusion
  85.0 0.0 reduce-scatter.2.cloned.1.call-update
  85.0 6.7 %collective-permute-done.2 = f32[2,2,2,32,256]{4,3,0,1,2:T(8,128)S(1)} collective-permute-done((f32[2,2,2,32,256]{4,3,0,1,2:T(8,128)S(1)}, f32[2,2,2,32,256]{4,3,0,1,2:T(8,128)S(1)}, u32[]{:S(2)}, u32[]{:S(2)}) %collective-permute-start.2) | collective-permute-done | bytes 262176 | tf_op jit(solution)/shard_map/ppermute | solution.py:92
  91.8 3.1 %collective-permute-start.3 = (f32[2,2,32,256]{3,2,0,1:T(8,128)S(1)}, f32[2,2,32,256]{3,2,0,1:T(8,128)S(1)}, u32[]{:S(2)}, u32[]{:S(2)}) collective-permute-start(f32[2,2,32,256]{3,2,0,1:T(8,128)S(1)} %dynamic-slice_bitcast_fusion.1), channel_id=1, source_target_pairs={{0,128},{64,192},{128,0},{192,64},{256,384},{320,448},{384,256},{4... | collective-permute-start | bytes 393224 | tf_op jit(solution)/shard_map/ppermute | solution.py:92
  94.9 7.1 %collective-permute-done.3 = f32[2,2,32,256]{3,2,0,1:T(8,128)S(1)} collective-permute-done((f32[2,2,32,256]{3,2,0,1:T(8,128)S(1)}, f32[2,2,32,256]{3,2,0,1:T(8,128)S(1)}, u32[]{:S(2)}, u32[]{:S(2)}) %collective-permute-start.3) | collective-permute-done | bytes 131104 | tf_op jit(solution)/shard_map/ppermute | solution.py:92
  102.0 10.1 %collective-permute-start.4 = (f32[2,32,256]{2,1,0:T(8,128)S(1)}, f32[2,32,256]{2,1,0:T(8,128)S(1)}, u32[]{:S(2)}, u32[]{:S(2)}) collective-permute-start(f32[2,32,256]{2,1,0:T(8,128)S(1)} %dynamic-slice_bitcast_fusion.2), channel_id=1, source_target_pairs={{0,256},{64,320},{128,384},{192,448},{256,0},{320,64},{384,128},{4... | collective-permute-start | bytes 196616 | tf_op jit(solution)/shard_map/ppermute | solution.py:92
  112.2 7.7 %collective-permute-done.4 = f32[2,32,256]{2,1,0:T(8,128)S(1)} collective-permute-done((f32[2,32,256]{2,1,0:T(8,128)S(1)}, f32[2,32,256]{2,1,0:T(8,128)S(1)}, u32[]{:S(2)}, u32[]{:S(2)}) %collective-permute-start.4) | collective-permute-done | bytes 65568 | tf_op jit(solution)/shard_map/ppermute | solution.py:92
  119.9 31.8 %reduce-scatter.2.cloned.1.call-done = f32[2,1,32,256]{3,2,0,1:T(8,128)} async-done(((f32[2,8,32,256]{3,2,0,1:T(8,128)}), f32[2,1,32,256]{3,2,0,1:T(8,128)}) %reduce-scatter.2.cloned.1.call-update) | async-done | bytes 65552 | tf_op jit(solution)/shard_map/reduce_scatter | solution.py:124
  151.7 0.8 maximum_bitcast_fusion
  152.5 0.8 copy.18
  (15 shorter events, 0.3 us)
Async XLA Ops:
  8.9 19.9 %collective-permute-start = (bf16[2,2,16,512]{3,1,2,0:T(2,128)(2,1)S(1)}, bf16[2,2,16,512]{3,1,2,0:T(2,128)(2,1)S(1)}, u32[]{:S(2)}, u32[]{:S(2)}) collective-permute-start(bf16[2,2,16,512]{3,1,2,0:T(2,128)(2,1)S(1)} %bitcast.60), channel_id=1, source_target_pairs={{0,16},{16,0},{1,17},{17,1},{2,18},{18,2},{3,19},{19,3},{4,20},{20... | collective-permute-start | bytes 196616 | tf_op jit(solution)/shard_map/ppermute | solution.py:100
  30.6 32.3 %all-to-all-start = ((bf16[2,2,16,2,16,512]{5,4,3,1,0,2:T(8,128)(2,1)}), bf16[2,2,16,2,16,512]{5,4,3,1,0,2:T(8,128)(2,1)S(1)}, u32[]{:S(2)}, u32[]{:S(2)}) async-start(bf16[2,2,16,2,16,512]{5,4,3,1,0,2:T(8,128)(2,1)} %broadcast_in_dim.2), calls=%async_computation | async-start | bytes 4194304 | tf_op jit(solution)/shard_map/all_to_all | solution.py:105
  38.1 113.6 %reduce-scatter.2.cloned.1.call-start = ((), (), s32[]{:S(2)}) async-start(), calls=%async_computation.2 | async-start | bytes 589824 | tf_op jit(solution)/shard_map/reduce_scatter | solution.py:124
  71.0 10.4 %collective-permute-start.1 = (f32[2,8,32,256]{3,2,1,0:T(8,128)}, f32[2,8,32,256]{3,2,1,0:T(8,128)S(1)}, u32[]{:S(2)}, u32[]{:S(2)}) collective-permute-start(f32[2,8,32,256]{3,2,1,0:T(8,128)} %dynamic-slice_bitcast_fusion), channel_id=1, source_target_pairs={{0,32},{32,0},{1,33},{33,1},{2,34},{34,2},{3,35},{35,3},{4,36},{36... | collective-permute-start | bytes 1572872 | tf_op jit(solution)/shard_map/ppermute | solution.py:120
  77.6 3.9 %copy-start = (f32[2,512,256]{2,1,0:T(8,128)S(1)}, f32[2,512,256]{2,1,0:T(8,128)}, u32[]{:S(2)}) copy-start(f32[2,512,256]{2,1,0:T(8,128)} %shard_map.46) | copy-start | bytes 3145732
  79.0 5.1 %collective-permute-start.5 = (f32[2,8,32,256]{3,2,0,1:T(8,128)S(1)}, f32[2,8,32,256]{3,2,0,1:T(8,128)S(1)}, u32[]{:S(2)}, u32[]{:S(2)}) collective-permute-start(f32[2,8,32,256]{3,2,0,1:T(8,128)S(1)} %bitcast.58), channel_id=1, source_target_pairs={{0,32},{32,0},{1,33},{33,1},{2,34},{34,2},{3,35},{35,3},{4,36},{36... | collective-permute-start | bytes 1572872 | tf_op jit(solution)/shard_map/ppermute | solution.py:120
  81.6 10.1 %collective-permute-start.2 = (f32[2,2,2,32,256]{4,3,0,1,2:T(8,128)S(1)}, f32[2,2,2,32,256]{4,3,0,1,2:T(8,128)S(1)}, u32[]{:S(2)}, u32[]{:S(2)}) collective-permute-start(f32[2,2,2,32,256]{4,3,0,1,2:T(8,128)S(1)} %bitcast.59), channel_id=1, source_target_pairs={{0,64},{64,0},{128,192},{192,128},{256,320},{320,256},{384,448},{4... | collective-permute-start | bytes 786440 | tf_op jit(solution)/shard_map/ppermute | solution.py:92
  91.8 10.2 %collective-permute-start.3 = (f32[2,2,32,256]{3,2,0,1:T(8,128)S(1)}, f32[2,2,32,256]{3,2,0,1:T(8,128)S(1)}, u32[]{:S(2)}, u32[]{:S(2)}) collective-permute-start(f32[2,2,32,256]{3,2,0,1:T(8,128)S(1)} %dynamic-slice_bitcast_fusion.1), channel_id=1, source_target_pairs={{0,128},{64,192},{128,0},{192,64},{256,384},{320,448},{384,256},{4... | collective-permute-start | bytes 393224 | tf_op jit(solution)/shard_map/ppermute | solution.py:92
  102.0 17.8 %collective-permute-start.4 = (f32[2,32,256]{2,1,0:T(8,128)S(1)}, f32[2,32,256]{2,1,0:T(8,128)S(1)}, u32[]{:S(2)}, u32[]{:S(2)}) collective-permute-start(f32[2,32,256]{2,1,0:T(8,128)S(1)} %dynamic-slice_bitcast_fusion.2), channel_id=1, source_target_pairs={{0,256},{64,320},{128,384},{192,448},{256,0},{320,64},{384,128},{4... | collective-permute-start | bytes 196616 | tf_op jit(solution)/shard_map/ppermute | solution.py:92
Sparse Core Ops, SparseCore 0:
  85.1 66.5 reduce-scatter.1

commit v14 on v9

--- a/solution.py
+++ b/solution.py
@@ -2,6 +2,7 @@
 import jax.numpy as jnp
 from jax import lax
 from jax.experimental import pallas as pl
+from jax.experimental.pallas import tpu as pltpu
 from jax.sharding import Mesh
 from jax.sharding import PartitionSpec as P
 
@@ -38,7 +39,7 @@
     return moved.astype(block.dtype).reshape(block.shape)
 
 
-def contract_kernel(s_ref, b_ref, o_ref, out_ref):
+def contract_kernel(core_ref, s_ref, b_ref, o_ref, out_ref, acc_ref):
     f32 = jnp.float32
     for t in range(s_ref.shape[0]):
         sr = s_ref[t, 0]
@@ -52,31 +53,44 @@
         re = pr * o_r - pi * o_i
         im = pr * o_i + pi * o_r
         if t == 0:
-            out_ref[0] = re
-            out_ref[1] = im
+            acc_ref[0] = re
+            acc_ref[1] = im
         else:
-            out_ref[0] += re
-            out_ref[1] += im
+            acc_ref[0] += re
+            acc_ref[1] += im
+    core = core_ref[0]
+    block = out_ref.shape[-2]
+    for chip in range(out_ref.shape[2]):
+        for slot in range(2):
+            owner = core if slot == 0 else 1 - core
+            start = pl.multiple_of((chip * 2 + owner) * block, block)
+            out_ref[:, slot, chip] = acc_ref[:, pl.ds(start, block), :]
 
 
-def contract(stem_t, branch_t, open_t, column_block):
+def contract(stem_t, branch_t, open_t, column_block, core, block_rows):
     slices, _, rows, depth = stem_t.shape
     width = branch_t.shape[-1]
     tile = min(ROW_TILE, rows)
+    chips = rows // (2 * block_rows)
+    per_tile = tile // (2 * block_rows)
     flops = slices * 8 * rows * depth * width
     moved = 2 * (stem_t.size + branch_t.size) + 2 * slices * 2 * rows * width + 4 * 2 * rows * width
     return pl.pallas_call(
         contract_kernel,
-        out_shape=jax.ShapeDtypeStruct((2, rows, width), jnp.float32),
-        grid=(rows // tile,),
-        in_specs=[
-            pl.BlockSpec((slices, 2, tile, depth), lambda i: (0, 0, i, 0)),
-            pl.BlockSpec((slices, 2, depth, width), lambda i: (0, 0, 0, 0)),
-            pl.BlockSpec((slices, tile, 2, width), lambda i: (0, i, 0, column_block)),
-        ],
-        out_specs=pl.BlockSpec((2, tile, width), lambda i: (0, i, 0)),
+        out_shape=jax.ShapeDtypeStruct((2, 2, chips, block_rows, width), jnp.float32),
+        grid_spec=pltpu.PrefetchScalarGridSpec(
+            num_scalar_prefetch=1,
+            grid=(rows // tile,),
+            in_specs=[
+                pl.BlockSpec((slices, 2, tile, depth), lambda i, c: (0, 0, i, 0)),
+                pl.BlockSpec((slices, 2, depth, width), lambda i, c: (0, 0, 0, 0)),
+                pl.BlockSpec((slices, tile, 2, width), lambda i, c: (0, i, 0, column_block)),
+            ],
+            out_specs=pl.BlockSpec((2, 2, per_tile, block_rows, width), lambda i, c: (0, 0, i, 0, 0)),
+            scratch_shapes=[pltpu.VMEM((2, tile, width), jnp.float32)],
+        ),
         cost_estimate=pl.CostEstimate(flops=flops, bytes_accessed=moved, transcendentals=0),
-    )(stem_t, branch_t, open_t)
+    )(core, stem_t, branch_t, open_t)
 
 
 def halving_scatter(blocks, axis):
@@ -108,7 +122,7 @@
     open_t = open_tensor
     zl_count = lax.axis_size("zl")
     block_rows = row_count // (zl_count * 2)
-    core = lax.axis_index("core")
+    core_index = jnp.reshape(lax.axis_index("core"), (1,)).astype(jnp.int32)
     results = []
     previous = None
     for h in range(halves):
@@ -118,11 +132,8 @@
         gathered = lax.all_to_all(part, ("x", "y"), 2, 4, tiled=True)
         previous = gathered
         branch_t = gathered.reshape(slice_count, 2, -1, span)
-        local_sum = contract(stem_t, branch_t, open_t, h)
-        shaped = local_sum.reshape(2, zl_count, 2, block_rows, span)
-        mine = lax.dynamic_index_in_dim(shaped, core, 2, keepdims=False)
-        theirs = lax.dynamic_index_in_dim(shaped, 1 - core, 2, keepdims=False)
-        mine = mine + lax.ppermute(theirs, "core", shift_pairs(2, 1))
+        local_sum = contract(stem_t, branch_t, open_t, h, core_index, block_rows)
+        mine = local_sum[:, 0] + lax.ppermute(local_sum[:, 1], "core", shift_pairs(2, 1))
         results.append(halving_scatter(mine, "zl"))
     result = jnp.concatenate(results, axis=-1)
     return jnp.transpose(result, (1, 0, 2)).reshape(1, block_rows, 2, width)

time: 124 us -> 129 us (1.040); the launches traced: 122 us -> 129 us
  waiting for transfers between devices: 24.6 us -> 37.4 us
  starting transfers between devices: 70.9 us -> 64.4 us
  other arithmetic: 1.82 us -> 3.54 us
    ppermute x6, waiting for transfers between devices: 10.4 us -> 24.8 us  [halving_scatter(): shaped = keep + lax.ppermute(send, axis, pairs)]
    ppermute x6, starting transfers between devices: 32 us -> 25.5 us  [halving_scatter(): shaped = keep + lax.ppermute(send, axis, pairs)]
    add x2, other arithmetic: 0.15 us -> 2.22 us  [body(): local_sum[:, 0] + lax.ppermute(local_sum[:, 1], 'core', shift_pairs(2, 1))]
    ppermute x2, waiting for transfers between devices: 1.62 us -> 0.01 us  [body(): lax.ppermute(local_sum[:, 1], 'core', shift_pairs(2, 1))]
  transfers between devices with their start and end apart: 11 -> 11, of which waited for: 6 -> 7; matrix products, arithmetic and copies ran while one was open for 9% -> 10% of each run, Pallas kernels for 8% -> 7%
where the time goes in v14:
time: 129 us
  starting transfers between devices  64.4 us (50%)
  waiting for transfers between devices  37.4 us (29%)
  local copies, waits for them, and re-layouts  12.9 us (10%)
  Pallas kernels  9.52 us (7%)
  other arithmetic  3.54 us (3%)
    ppermute x6, starting transfers between devices, halving_scatter(): shaped = keep + lax.ppermute(send, axis, pairs)  25.5 us
    ppermute x6, waiting for transfers between devices, halving_scatter(): shaped = keep + lax.ppermute(send, axis, pairs)  24.8 us
    ppermute x1, starting transfers between devices, body(): other = lax.ppermute(permuted, 'zh', shift_pairs(2, 1))  16.3 us
    all_to_all x2, starting transfers between devices, body(): gathered = lax.all_to_all(part, ('x', 'y'), 2, 4, tiled=True)  13.7 us
    all_to_all x2, waiting for transfers between devices, body(): gathered = lax.all_to_all(part, ('x', 'y'), 2, 4, tiled=True)  10.7 us
    pallas_call x2, Pallas kernels, contract(): pl.pallas_call(contract_kernel, out_shape=jax.ShapeDtypeStruct((2, 2, chi...  9.52 us
    ppermute x2, starting transfers between devices, body(): lax.ppermute(local_sum[:, 1], 'core', shift_pairs(2, 1))  9 us
    unnamed x6, local copies, waits for them, and re-layouts  3.31 us
  transfers between devices with their start and end apart: 11, of which 7 were waited for; matrix products, arithmetic and copies ran while one was open for 10% of the time, Pallas kernels for 7%

profile of v14, /device:TPU:1, one launch (start us, length us, event | category | flops | bytes accessed | tf_op | source)
XLA Modules:
  0.0 128.7 jit_solution(1823507535175957457)
XLA Ops:
  0.0 0.8 fusion.7
  0.8 0.8 fusion.8
  1.6 0.3 fusion
  2.0 0.3 fusion.1
  2.4 16.3 %collective-permute-start = (bf16[2,2,16,512]{3,1,2,0:T(2,128)(2,1)S(1)}, bf16[2,2,16,512]{3,1,2,0:T(2,128)(2,1)S(1)}, u32[]{:S(2)}, u32[]{:S(2)}) collective-permute-start(bf16[2,2,16,512]{3,1,2,0:T(2,128)(2,1)S(1)} %bitcast.82), channel_id=1, source_target_pairs={{0,16},{16,0},{1,17},{17,1},{2,18},{18,2},{3,19},{19,3},{4,20},{20... | collective-permute-start | bytes 196616 | tf_op jit(solution)/shard_map/ppermute | solution.py:114
  18.6 1.8 %collective-permute-done = bf16[2,2,16,512]{3,1,2,0:T(2,128)(2,1)S(1)} collective-permute-done((bf16[2,2,16,512]{3,1,2,0:T(2,128)(2,1)S(1)}, bf16[2,2,16,512]{3,1,2,0:T(2,128)(2,1)S(1)}, u32[]{:S(2)}, u32[]{:S(2)}) %collective-permute-start) | collective-permute-done | bytes 65568 | tf_op jit(solution)/shard_map/ppermute | solution.py:114
  20.5 0.2 broadcast_select_fusion
  20.7 0.1 fusion.6
  20.8 1.1 broadcast_in_dim.8
  21.9 6.8 %all-to-all-start = ((bf16[2,2,16,2,16,256]{5,4,3,1,0,2:T(8,128)(2,1)}), bf16[2,2,16,2,16,256]{5,4,3,1,0,2:T(8,128)(2,1)S(1)}, u32[]{:S(2)}, u32[]{:S(2)}) async-start(bf16[2,2,16,2,16,256]{5,4,3,1,0,2:T(8,128)(2,1)} %broadcast_in_dim.8), calls=%async_computation | async-start | bytes 2097152 | tf_op jit(solution)/shard_map/all_to_all | solution.py:132
  28.7 1.1 broadcast_in_dim.9
  29.8 10.7 %all-to-all-done = bf16[2,2,16,2,16,256]{5,4,3,1,0,2:T(8,128)(2,1)S(1)} async-done(((bf16[2,2,16,2,16,256]{5,4,3,1,0,2:T(8,128)(2,1)}), bf16[2,2,16,2,16,256]{5,4,3,1,0,2:T(8,128)(2,1)S(1)}, u32[]{:S(2)}, u32[]{:S(2)}) %all-to-all-start) | async-done | bytes 1048608 | tf_op jit(solution)/shard_map/all_to_all | solution.py:132
  40.5 6.9 %all-to-all-start.1 = ((bf16[2,2,16,2,16,256]{5,4,3,1,0,2:T(8,128)(2,1)}), bf16[2,2,16,2,16,256]{5,4,3,1,0,2:T(8,128)(2,1)S(1)}, u32[]{:S(2)}, u32[]{:S(2)}) async-start(bf16[2,2,16,2,16,256]{5,4,3,1,0,2:T(8,128)(2,1)} %broadcast_in_dim.9), calls=%async_computation.1 | async-start | bytes 2097152 | tf_op jit(solution)/shard_map/all_to_all | solution.py:132
  47.5 3.3 %copy.32 = bf16[2,512,2,512]{3,1,2,0:T(8,128)(2,1)} copy(bf16[2,512,2,512]{3,2,1,0:T(2,128)(2,1)} %param.4) | data formatting | bytes 4194304 | tf_op args[0]
  50.8 1.1 copy.16
  51.8 4.7 %shard_map.46 = f32[2,2,8,32,256]{4,3,2,1,0:T(8,128)} custom-call(s32[1]{0:T(128)} %bitcast.core_ref, bf16[2,2,512,512]{3,2,1,0:T(8,128)(2,1)} %bitcast.72, bf16[2,2,512,256]{3,2,1,0:T(8,128)(2,1)} %bitcast.75, bf16[2,512,2,512]{3,2,1,0:T(2,128)(2,1)} %o_ref.3), custom_call_target="tpu_custom_call" | custom-call | flops 1073741824 | bytes 5242880 | tf_op jit(solution)/shard_map/pallas_call | solution.py:78
  56.5 1.9 %slice_bitcast_fusion.2 = f32[2,8,32,256]{3,2,1,0:T(8,128)} fusion(f32[2,2,8,32,256]{4,3,2,1,0:T(8,128)} %shard_map.46), kind=kLoop, calls=%fused_computation.10 | loop fusion | bytes 1048576 | tf_op jit(solution)/shard_map/squeeze | solution.py:136
  58.4 4.8 %collective-permute-start.1 = (f32[2,8,32,256]{3,2,1,0:T(8,128)}, f32[2,8,32,256]{3,2,1,0:T(8,128)}, u32[]{:S(2)}, u32[]{:S(2)}) collective-permute-start(f32[2,8,32,256]{3,2,1,0:T(8,128)} %slice_bitcast_fusion.2), channel_id=1, source_target_pairs={{0,32},{32,0},{1,33},{33,1},{2,34},{34,2},{3,35},{35,3},{4,36},{36... | collective-permute-start | bytes 1572872 | tf_op jit(solution)/shard_map/ppermute | solution.py:136
  63.3 0.0 all-to-all-done.1
  63.3 1.1 copy.21
  64.3 0.0 copy-start
  64.4 4.8 %shard_map.47 = f32[2,2,8,32,256]{4,3,2,1,0:T(8,128)} custom-call(s32[1]{0:T(128)} %bitcast.core_ref, bf16[2,2,512,512]{3,2,1,0:T(8,128)(2,1)} %bitcast.73, bf16[2,2,512,256]{3,2,1,0:T(8,128)(2,1)} %bitcast.74, bf16[2,512,2,512]{3,2,1,0:T(2,128)(2,1)} %o_ref.3), custom_call_target="tpu_custom_call" | custom-call | flops 1073741824 | bytes 5242880 | tf_op jit(solution)/shard_map/pallas_call | solution.py:78
  69.2 0.0 copy-start.1
  69.2 1.2 slice_bitcast_fusion
  70.3 4.2 %collective-permute-start.5 = (f32[2,8,32,256]{3,2,1,0:T(8,128)S(1)}, f32[2,8,32,256]{3,2,1,0:T(8,128)}, u32[]{:S(2)}, u32[]{:S(2)}) collective-permute-start(f32[2,8,32,256]{3,2,1,0:T(8,128)S(1)} %slice_bitcast_fusion), channel_id=1, source_target_pairs={{0,32},{32,0},{1,33},{33,1},{2,34},{34,2},{3,35},{35,3},{4,36},{36... | collective-permute-start | bytes 1572872 | tf_op jit(solution)/shard_map/ppermute | solution.py:136
  74.5 0.0 collective-permute-done.1
  74.5 0.0 copy-done
  74.5 1.1 fusion.3
  75.7 2.7 %collective-permute-start.2 = (f32[2,2,2,32,256]{4,3,2,1,0:T(8,128)S(1)}, f32[2,2,2,32,256]{4,3,2,1,0:T(8,128)S(1)}, u32[]{:S(2)}, u32[]{:S(2)}) collective-permute-start(f32[2,2,2,32,256]{4,3,2,1,0:T(8,128)S(1)} %dynamic-slice_bitcast_fusion.1), channel_id=1, source_target_pairs={{0,64},{64,0},{128,192},{192,128},{256,320},{320,256},{384,448},{4... | collective-permute-start | bytes 786440 | tf_op jit(solution)/shard_map/ppermute | solution.py:106
  78.4 0.0 collective-permute-done.5
  78.4 0.0 copy-done.1
  78.4 1.1 fusion.2
  79.6 2.6 %collective-permute-start.6 = (f32[2,2,2,32,256]{4,3,2,1,0:T(8,128)S(1)}, f32[2,2,2,32,256]{4,3,2,1,0:T(8,128)S(1)}, u32[]{:S(2)}, u32[]{:S(2)}) collective-permute-start(f32[2,2,2,32,256]{4,3,2,1,0:T(8,128)S(1)} %dynamic-slice_bitcast_fusion), channel_id=1, source_target_pairs={{0,64},{64,0},{128,192},{192,128},{256,320},{320,256},{384,448},{4... | collective-permute-start | bytes 786440 | tf_op jit(solution)/shard_map/ppermute | solution.py:106
  82.2 3.3 %collective-permute-done.2 = f32[2,2,2,32,256]{4,3,2,1,0:T(8,128)S(1)} collective-permute-done((f32[2,2,2,32,256]{4,3,2,1,0:T(8,128)S(1)}, f32[2,2,2,32,256]{4,3,2,1,0:T(8,128)S(1)}, u32[]{:S(2)}, u32[]{:S(2)}) %collective-permute-start.2) | collective-permute-done | bytes 262176 | tf_op jit(solution)/shard_map/ppermute | solution.py:106
  85.6 5.6 %collective-permute-done.6 = f32[2,2,2,32,256]{4,3,2,1,0:T(8,128)S(1)} collective-permute-done((f32[2,2,2,32,256]{4,3,2,1,0:T(8,128)S(1)}, f32[2,2,2,32,256]{4,3,2,1,0:T(8,128)S(1)}, u32[]{:S(2)}, u32[]{:S(2)}) %collective-permute-start.6) | collective-permute-done | bytes 262176 | tf_op jit(solution)/shard_map/ppermute | solution.py:106
  91.2 0.1 copy.34
  91.3 3.3 %collective-permute-start.3 = (f32[2,2,32,256]{3,0,2,1:T(2,128)S(1)}, f32[2,2,32,256]{3,0,2,1:T(2,128)S(1)}, u32[]{:S(2)}, u32[]{:S(2)}) collective-permute-start(f32[2,2,32,256]{3,0,2,1:T(2,128)S(1)} %bitcast.84), channel_id=1, source_target_pairs={{0,128},{64,192},{128,0},{192,64},{256,384},{320,448},{384,256},{4... | collective-permute-start | bytes 393224 | tf_op jit(solution)/shard_map/ppermute | solution.py:106
  94.6 0.1 copy.33
  94.7 2.9 %collective-permute-start.7 = (f32[2,2,32,256]{3,0,2,1:T(2,128)S(1)}, f32[2,2,32,256]{3,0,2,1:T(2,128)S(1)}, u32[]{:S(2)}, u32[]{:S(2)}) collective-permute-start(f32[2,2,32,256]{3,0,2,1:T(2,128)S(1)} %bitcast.85), channel_id=1, source_target_pairs={{0,128},{64,192},{128,0},{192,64},{256,384},{320,448},{384,256},{4... | collective-permute-start | bytes 393224 | tf_op jit(solution)/shard_map/ppermute | solution.py:106
  97.6 7.0 %collective-permute-done.3 = f32[2,2,32,256]{3,0,2,1:T(2,128)S(1)} collective-permute-done((f32[2,2,32,256]{3,0,2,1:T(2,128)S(1)}, f32[2,2,32,256]{3,0,2,1:T(2,128)S(1)}, u32[]{:S(2)}, u32[]{:S(2)}) %collective-permute-start.3) | collective-permute-done | bytes 131104 | tf_op jit(solution)/shard_map/ppermute | solution.py:106
  104.6 0.1 bitcast_add_fusion.3
  104.8 11.4 %collective-permute-start.4 = (f32[2,32,256]{2,0,1:T(2,128)S(1)}, f32[2,32,256]{2,0,1:T(2,128)S(1)}, u32[]{:S(2)}, u32[]{:S(2)}) collective-permute-start(f32[2,32,256]{2,0,1:T(2,128)S(1)} %dynamic-slice_bitcast_fusion.3), channel_id=1, source_target_pairs={{0,256},{64,320},{128,384},{192,448},{256,0},{320,64},{384,128},{4... | collective-permute-start | bytes 196616 | tf_op jit(solution)/shard_map/ppermute | solution.py:106
  116.2 0.0 collective-permute-done.7
  116.2 0.1 bitcast_add_fusion.2
  116.4 2.6 %collective-permute-start.8 = (f32[2,32,256]{2,0,1:T(2,128)S(1)}, f32[2,32,256]{2,0,1:T(2,128)S(1)}, u32[]{:S(2)}, u32[]{:S(2)}) collective-permute-start(f32[2,32,256]{2,0,1:T(2,128)S(1)} %dynamic-slice_bitcast_fusion.2), channel_id=1, source_target_pairs={{0,256},{64,320},{128,384},{192,448},{256,0},{320,64},{384,128},{4... | collective-permute-start | bytes 196616 | tf_op jit(solution)/shard_map/ppermute | solution.py:106
  119.0 3.3 %collective-permute-done.4 = f32[2,32,256]{2,0,1:T(2,128)S(1)} collective-permute-done((f32[2,32,256]{2,0,1:T(2,128)S(1)}, f32[2,32,256]{2,0,1:T(2,128)S(1)}, u32[]{:S(2)}, u32[]{:S(2)}) %collective-permute-start.4) | collective-permute-done | bytes 65568 | tf_op jit(solution)/shard_map/ppermute | solution.py:106
  122.3 5.6 %collective-permute-done.8 = f32[2,32,256]{2,0,1:T(2,128)S(1)} collective-permute-done((f32[2,32,256]{2,0,1:T(2,128)S(1)}, f32[2,32,256]{2,0,1:T(2,128)S(1)}, u32[]{:S(2)}, u32[]{:S(2)}) %collective-permute-start.8) | collective-permute-done | bytes 65568 | tf_op jit(solution)/shard_map/ppermute | solution.py:106
  128.0 0.7 maximum_bitcast_fusion
  (17 shorter events, 0.4 us)
Async XLA Ops:
  2.4 18.1 %collective-permute-start = (bf16[2,2,16,512]{3,1,2,0:T(2,128)(2,1)S(1)}, bf16[2,2,16,512]{3,1,2,0:T(2,128)(2,1)S(1)}, u32[]{:S(2)}, u32[]{:S(2)}) collective-permute-start(bf16[2,2,16,512]{3,1,2,0:T(2,128)(2,1)S(1)} %bitcast.82), channel_id=1, source_target_pairs={{0,16},{16,0},{1,17},{17,1},{2,18},{18,2},{3,19},{19,3},{4,20},{20... | collective-permute-start | bytes 196616 | tf_op jit(solution)/shard_map/ppermute | solution.py:114
  21.9 18.6 %all-to-all-start = ((bf16[2,2,16,2,16,256]{5,4,3,1,0,2:T(8,128)(2,1)}), bf16[2,2,16,2,16,256]{5,4,3,1,0,2:T(8,128)(2,1)S(1)}, u32[]{:S(2)}, u32[]{:S(2)}) async-start(bf16[2,2,16,2,16,256]{5,4,3,1,0,2:T(8,128)(2,1)} %broadcast_in_dim.8), calls=%async_computation | async-start | bytes 2097152 | tf_op jit(solution)/shard_map/all_to_all | solution.py:132
  40.5 22.7 %all-to-all-start.1 = ((bf16[2,2,16,2,16,256]{5,4,3,1,0,2:T(8,128)(2,1)}), bf16[2,2,16,2,16,256]{5,4,3,1,0,2:T(8,128)(2,1)S(1)}, u32[]{:S(2)}, u32[]{:S(2)}) async-start(bf16[2,2,16,2,16,256]{5,4,3,1,0,2:T(8,128)(2,1)} %broadcast_in_dim.9), calls=%async_computation.1 | async-start | bytes 2097152 | tf_op jit(solution)/shard_map/all_to_all | solution.py:132
  58.4 16.1 %collective-permute-start.1 = (f32[2,8,32,256]{3,2,1,0:T(8,128)}, f32[2,8,32,256]{3,2,1,0:T(8,128)}, u32[]{:S(2)}, u32[]{:S(2)}) collective-permute-start(f32[2,8,32,256]{3,2,1,0:T(8,128)} %slice_bitcast_fusion.2), channel_id=1, source_target_pairs={{0,32},{32,0},{1,33},{33,1},{2,34},{34,2},{3,35},{35,3},{4,36},{36... | collective-permute-start | bytes 1572872 | tf_op jit(solution)/shard_map/ppermute | solution.py:136
  64.3 10.2 %copy-start = (f32[2,2,8,32,256]{4,3,2,1,0:T(8,128)S(1)}, f32[2,2,8,32,256]{4,3,2,1,0:T(8,128)}, u32[]{:S(2)}) copy-start(f32[2,2,8,32,256]{4,3,2,1,0:T(8,128)} %shard_map.46) | copy-start | bytes 3145732
  69.2 9.2 %copy-start.1 = (f32[2,2,8,32,256]{4,3,2,1,0:T(8,128)S(1)}, f32[2,2,8,32,256]{4,3,2,1,0:T(8,128)}, u32[]{:S(2)}) copy-start(f32[2,2,8,32,256]{4,3,2,1,0:T(8,128)} %shard_map.47) | copy-start | bytes 3145732
  70.3 8.0 %collective-permute-start.5 = (f32[2,8,32,256]{3,2,1,0:T(8,128)S(1)}, f32[2,8,32,256]{3,2,1,0:T(8,128)}, u32[]{:S(2)}, u32[]{:S(2)}) collective-permute-start(f32[2,8,32,256]{3,2,1,0:T(8,128)S(1)} %slice_bitcast_fusion), channel_id=1, source_target_pairs={{0,32},{32,0},{1,33},{33,1},{2,34},{34,2},{3,35},{35,3},{4,36},{36... | collective-permute-start | bytes 1572872 | tf_op jit(solution)/shard_map/ppermute | solution.py:136
  75.7 9.8 %collective-permute-start.2 = (f32[2,2,2,32,256]{4,3,2,1,0:T(8,128)S(1)}, f32[2,2,2,32,256]{4,3,2,1,0:T(8,128)S(1)}, u32[]{:S(2)}, u32[]{:S(2)}) collective-permute-start(f32[2,2,2,32,256]{4,3,2,1,0:T(8,128)S(1)} %dynamic-slice_bitcast_fusion.1), channel_id=1, source_target_pairs={{0,64},{64,0},{128,192},{192,128},{256,320},{320,256},{384,448},{4... | collective-permute-start | bytes 786440 | tf_op jit(solution)/shard_map/ppermute | solution.py:106
  79.6 11.6 %collective-permute-start.6 = (f32[2,2,2,32,256]{4,3,2,1,0:T(8,128)S(1)}, f32[2,2,2,32,256]{4,3,2,1,0:T(8,128)S(1)}, u32[]{:S(2)}, u32[]{:S(2)}) collective-permute-start(f32[2,2,2,32,256]{4,3,2,1,0:T(8,128)S(1)} %dynamic-slice_bitcast_fusion), channel_id=1, source_target_pairs={{0,64},{64,0},{128,192},{192,128},{256,320},{320,256},{384,448},{4... | collective-permute-start | bytes 786440 | tf_op jit(solution)/shard_map/ppermute | solution.py:106
  91.3 13.3 %collective-permute-start.3 = (f32[2,2,32,256]{3,0,2,1:T(2,128)S(1)}, f32[2,2,32,256]{3,0,2,1:T(2,128)S(1)}, u32[]{:S(2)}, u32[]{:S(2)}) collective-permute-start(f32[2,2,32,256]{3,0,2,1:T(2,128)S(1)} %bitcast.84), channel_id=1, source_target_pairs={{0,128},{64,192},{128,0},{192,64},{256,384},{320,448},{384,256},{4... | collective-permute-start | bytes 393224 | tf_op jit(solution)/shard_map/ppermute | solution.py:106
  94.7 21.4 %collective-permute-start.7 = (f32[2,2,32,256]{3,0,2,1:T(2,128)S(1)}, f32[2,2,32,256]{3,0,2,1:T(2,128)S(1)}, u32[]{:S(2)}, u32[]{:S(2)}) collective-permute-start(f32[2,2,32,256]{3,0,2,1:T(2,128)S(1)} %bitcast.85), channel_id=1, source_target_pairs={{0,128},{64,192},{128,0},{192,64},{256,384},{320,448},{384,256},{4... | collective-permute-start | bytes 393224 | tf_op jit(solution)/shard_map/ppermute | solution.py:106
  104.8 17.5 %collective-permute-start.4 = (f32[2,32,256]{2,0,1:T(2,128)S(1)}, f32[2,32,256]{2,0,1:T(2,128)S(1)}, u32[]{:S(2)}, u32[]{:S(2)}) collective-permute-start(f32[2,32,256]{2,0,1:T(2,128)S(1)} %dynamic-slice_bitcast_fusion.3), channel_id=1, source_target_pairs={{0,256},{64,320},{128,384},{192,448},{256,0},{320,64},{384,128},{4... | collective-permute-start | bytes 196616 | tf_op jit(solution)/shard_map/ppermute | solution.py:106
  116.4 11.6 %collective-permute-start.8 = (f32[2,32,256]{2,0,1:T(2,128)S(1)}, f32[2,32,256]{2,0,1:T(2,128)S(1)}, u32[]{:S(2)}, u32[]{:S(2)}) collective-permute-start(f32[2,32,256]{2,0,1:T(2,128)S(1)} %dynamic-slice_bitcast_fusion.2), channel_id=1, source_target_pairs={{0,256},{64,320},{128,384},{192,448},{256,0},{320,64},{384,128},{4... | collective-permute-start | bytes 196616 | tf_op jit(solution)/shard_map/ppermute | solution.py:106

commit v15 on v9

--- a/solution.py
+++ b/solution.py
@@ -102,7 +102,7 @@
     pair = jnp.where(low, jnp.stack([permuted, other], axis=2), jnp.stack([other, permuted], axis=2))
     plane = lax.axis_size("x") * lax.axis_size("y")
     copies = jnp.broadcast_to(pair[:, :, None], pair.shape[:2] + (plane,) + pair.shape[2:])
-    halves = 2
+    halves = 4
     span = width // halves
     stem_t = jnp.transpose(stem_tensor, (0, 2, 1, 3))
     open_t = open_tensor

time: 124 us -> 163 us (1.31)
  the two profiles are of different devices: /device:TPU:1 before, /device:TPU:2 now
where the time goes in v15:
time: 163 us; the launch traced here: 162 us
  starting transfers between devices  95.9 us (59%)
  waiting for transfers between devices  30.4 us (19%)
  local copies, waits for them, and re-layouts  16.2 us (10%)
  Pallas kernels  16.2 us (10%)
  other arithmetic  1.87 us (1%)
    ppermute x12, starting transfers between devices, halving_scatter(): shaped = keep + lax.ppermute(send, axis, pairs)  45.9 us
    all_to_all x4, starting transfers between devices, body(): gathered = lax.all_to_all(part, ('x', 'y'), 2, 4, tiled=True)  25.4 us
    all_to_all x4, waiting for transfers between devices, body(): gathered = lax.all_to_all(part, ('x', 'y'), 2, 4, tiled=True)  18.4 us
    pallas_call x4, Pallas kernels, contract(): pl.pallas_call(contract_kernel, out_shape=jax.ShapeDtypeStruct((2, rows,...  16.2 us
    ppermute x1, starting transfers between devices, body(): other = lax.ppermute(permuted, 'zh', shift_pairs(2, 1))  15.7 us
    ppermute x4, starting transfers between devices, body(): mine = mine + lax.ppermute(theirs, 'core', shift_pairs(2, 1))  8.78 us
    ppermute x12, waiting for transfers between devices, halving_scatter(): shaped = keep + lax.ppermute(send, axis, pairs)  7.71 us
    all_to_all x4, local copies, waits for them, and re-layouts, body(): gathered = lax.all_to_all(part, ('x', 'y'), 2, 4, tiled=True)  4.45 us
  transfers between devices with their start and end apart: 21, of which 6 were waited for; matrix products, arithmetic and copies ran while one was open for 9% of the time, Pallas kernels for 10%

profile of v15, /device:TPU:2, one launch (start us, length us, event | category | flops | bytes accessed | tf_op | source)
XLA Modules:
  0.0 161.7 jit_solution(5734896598540922347)
XLA Ops:
  0.0 0.8 fusion.5
  0.8 0.8 fusion.6
  1.6 0.3 fusion
  2.4 15.7 %collective-permute-start = (bf16[2,2,16,512]{3,1,2,0:T(2,128)(2,1)S(1)}, bf16[2,2,16,512]{3,1,2,0:T(2,128)(2,1)S(1)}, u32[]{:S(2)}, u32[]{:S(2)}) collective-permute-start(bf16[2,2,16,512]{3,1,2,0:T(2,128)(2,1)S(1)} %bitcast.134), channel_id=1, source_target_pairs={{0,16},{16,0},{1,17},{17,1},{2,18},{18,2},{3,19},{19,3},{4,20},{20... | collective-permute-start | bytes 196616 | tf_op jit(solution)/shard_map/ppermute | solution.py:100
  18.1 4.2 %collective-permute-done = bf16[2,2,16,512]{3,1,2,0:T(2,128)(2,1)S(1)} collective-permute-done((bf16[2,2,16,512]{3,1,2,0:T(2,128)(2,1)S(1)}, bf16[2,2,16,512]{3,1,2,0:T(2,128)(2,1)S(1)}, u32[]{:S(2)}, u32[]{:S(2)}) %collective-permute-start) | collective-permute-done | bytes 65568 | tf_op jit(solution)/shard_map/ppermute | solution.py:100
  22.6 0.9 broadcast_in_dim.12
  23.5 7.6 %all-to-all-start = ((bf16[2,2,16,2,16,128]{5,4,3,1,0,2:T(8,128)(2,1)}), bf16[2,2,16,2,16,128]{5,4,3,1,0,2:T(8,128)(2,1)S(1)}, u32[]{:S(2)}, u32[]{:S(2)}) async-start(bf16[2,2,16,2,16,128]{5,4,3,1,0,2:T(8,128)(2,1)} %broadcast_in_dim.12), calls=%async_computation | async-start | bytes 1048576 | tf_op jit(solution)/shard_map/all_to_all | solution.py:118
  31.1 0.9 broadcast_in_dim.13
  32.0 7.0 %all-to-all-done = bf16[2,2,16,2,16,128]{5,4,3,1,0,2:T(8,128)(2,1)S(1)} async-done(((bf16[2,2,16,2,16,128]{5,4,3,1,0,2:T(8,128)(2,1)}), bf16[2,2,16,2,16,128]{5,4,3,1,0,2:T(8,128)(2,1)S(1)}, u32[]{:S(2)}, u32[]{:S(2)}) %all-to-all-start) | async-done | bytes 524320 | tf_op jit(solution)/shard_map/all_to_all | solution.py:118
  39.0 5.7 %all-to-all-start.1 = ((bf16[2,2,16,2,16,128]{5,4,3,1,0,2:T(8,128)(2,1)}), bf16[2,2,16,2,16,128]{5,4,3,1,0,2:T(8,128)(2,1)S(1)}, u32[]{:S(2)}, u32[]{:S(2)}) async-start(bf16[2,2,16,2,16,128]{5,4,3,1,0,2:T(8,128)(2,1)} %broadcast_in_dim.13), calls=%async_computation.1 | async-start | bytes 1048576 | tf_op jit(solution)/shard_map/all_to_all | solution.py:118
  44.7 0.9 broadcast_in_dim.14
  45.6 7.0 %all-to-all-done.1 = bf16[2,2,16,2,16,128]{5,4,3,1,0,2:T(8,128)(2,1)S(1)} async-done(((bf16[2,2,16,2,16,128]{5,4,3,1,0,2:T(8,128)(2,1)}), bf16[2,2,16,2,16,128]{5,4,3,1,0,2:T(8,128)(2,1)S(1)}, u32[]{:S(2)}, u32[]{:S(2)}) %all-to-all-start.1) | async-done | bytes 524320 | tf_op jit(solution)/shard_map/all_to_all | solution.py:118
  52.6 6.4 %all-to-all-start.2 = ((bf16[2,2,16,2,16,128]{5,4,3,1,0,2:T(8,128)(2,1)}), bf16[2,2,16,2,16,128]{5,4,3,1,0,2:T(8,128)(2,1)}, u32[]{:S(2)}, u32[]{:S(2)}) async-start(bf16[2,2,16,2,16,128]{5,4,3,1,0,2:T(8,128)(2,1)} %broadcast_in_dim.14), calls=%async_computation.2 | async-start | bytes 1048576 | tf_op jit(solution)/shard_map/all_to_all | solution.py:118
  59.0 1.7 %copy.44 = bf16[2,512,2,512]{3,1,2,0:T(8,128)(2,1)} copy(bf16[2,512,2,512]{3,2,1,0:T(2,128)(2,1)S(1)} %copy-done.4) | data formatting | bytes 4194304 | tf_op args[0]
  60.7 0.9 broadcast_in_dim.15
  61.6 0.8 copy.20
  62.4 4.5 %all-to-all-done.2 = bf16[2,2,16,2,16,128]{5,4,3,1,0,2:T(8,128)(2,1)} async-done(((bf16[2,2,16,2,16,128]{5,4,3,1,0,2:T(8,128)(2,1)}), bf16[2,2,16,2,16,128]{5,4,3,1,0,2:T(8,128)(2,1)}, u32[]{:S(2)}, u32[]{:S(2)}) %all-to-all-start.2) | async-done | bytes 524320 | tf_op jit(solution)/shard_map/all_to_all | solution.py:118
  66.9 5.8 %all-to-all-start.3 = ((bf16[2,2,16,2,16,128]{5,4,3,1,0,2:T(8,128)(2,1)}), bf16[2,2,16,2,16,128]{5,4,3,1,0,2:T(8,128)(2,1)S(1)}, u32[]{:S(2)}, u32[]{:S(2)}) async-start(bf16[2,2,16,2,16,128]{5,4,3,1,0,2:T(8,128)(2,1)} %broadcast_in_dim.15), calls=%async_computation.3 | async-start | bytes 1048576 | tf_op jit(solution)/shard_map/all_to_all | solution.py:118
  72.7 4.0 %shard_map.46 = f32[2,512,128]{2,1,0:T(8,128)} custom-call(bf16[2,2,512,512]{3,2,1,0:T(8,128)(2,1)} %bitcast.111, bf16[2,2,512,128]{3,2,1,0:T(8,128)(2,1)} %bitcast.123, bf16[2,512,2,512]{3,2,1,0:T(2,128)(2,1)} %o_ref.7), custom_call_target="tpu_custom_call" | custom-call | flops 536870912 | bytes 3670016 | tf_op jit(solution)/shard_map/pallas_call | solution.py:68
  76.7 1.0 dynamic-slice_bitcast_fusion.3
  77.7 1.9 %collective-permute-start.1 = (f32[2,8,32,128]{3,2,1,0:T(8,128)S(1)}, f32[2,8,32,128]{3,2,1,0:T(8,128)S(1)}, u32[]{:S(2)}, u32[]{:S(2)}) collective-permute-start(f32[2,8,32,128]{3,2,1,0:T(8,128)S(1)} %dynamic-slice_bitcast_fusion.3), channel_id=1, source_target_pairs={{0,32},{32,0},{1,33},{33,1},{2,34},{34,2},{3,35},{35,3},{4,36},{36... | collective-permute-start | bytes 786440 | tf_op jit(solution)/shard_map/ppermute | solution.py:125
  79.6 0.9 copy.24
  80.5 4.0 %shard_map.47 = f32[2,512,128]{2,1,0:T(8,128)} custom-call(bf16[2,2,512,512]{3,2,1,0:T(8,128)(2,1)} %bitcast.112, bf16[2,2,512,128]{3,2,1,0:T(8,128)(2,1)} %bitcast.125, bf16[2,512,2,512]{3,2,1,0:T(2,128)(2,1)} %o_ref.7), custom_call_target="tpu_custom_call" | custom-call | flops 536870912 | bytes 3670016 | tf_op jit(solution)/shard_map/pallas_call | solution.py:68
  84.5 1.0 dynamic-slice_bitcast_fusion.2
  85.5 2.4 %collective-permute-start.5 = (f32[2,8,32,128]{3,2,1,0:T(8,128)S(1)}, f32[2,8,32,128]{3,2,1,0:T(8,128)S(1)}, u32[]{:S(2)}, u32[]{:S(2)}) collective-permute-start(f32[2,8,32,128]{3,2,1,0:T(8,128)S(1)} %dynamic-slice_bitcast_fusion.2), channel_id=1, source_target_pairs={{0,32},{32,0},{1,33},{33,1},{2,34},{34,2},{3,35},{35,3},{4,36},{36... | collective-permute-start | bytes 786440 | tf_op jit(solution)/shard_map/ppermute | solution.py:125
  87.9 1.9 %copy.28 = bf16[2,2,1,2,16,16,128]{6,5,4,3,1,0,2:T(8,128)(2,1)} copy(bf16[2,2,1,2,16,16,128]{6,5,3,1,0,4,2:T(8,128)(2,1)} %bitcast.36) | data formatting | bytes 1048576 | tf_op jit(solution)/shard_map/all_to_all | solution.py:118
  89.8 4.0 %shard_map.48 = f32[2,512,128]{2,1,0:T(8,128)} custom-call(bf16[2,2,512,512]{3,2,1,0:T(8,128)(2,1)} %bitcast.113, bf16[2,2,512,128]{3,2,1,0:T(8,128)(2,1)} %bitcast.126, bf16[2,512,2,512]{3,2,1,0:T(2,128)(2,1)} %o_ref.7), custom_call_target="tpu_custom_call" | custom-call | flops 536870912 | bytes 3670016 | tf_op jit(solution)/shard_map/pallas_call | solution.py:68
  93.8 1.0 dynamic-slice_bitcast_fusion.1
  94.8 1.9 %collective-permute-start.9 = (f32[2,8,32,128]{3,2,1,0:T(8,128)S(1)}, f32[2,8,32,128]{3,2,1,0:T(8,128)S(1)}, u32[]{:S(2)}, u32[]{:S(2)}) collective-permute-start(f32[2,8,32,128]{3,2,1,0:T(8,128)S(1)} %dynamic-slice_bitcast_fusion.1), channel_id=1, source_target_pairs={{0,32},{32,0},{1,33},{33,1},{2,34},{34,2},{3,35},{35,3},{4,36},{36... | collective-permute-start | bytes 786440 | tf_op jit(solution)/shard_map/ppermute | solution.py:125
  96.7 0.9 copy.32
  97.6 4.1 %shard_map.49 = f32[2,512,128]{2,1,0:T(8,128)} custom-call(bf16[2,2,512,512]{3,2,1,0:T(8,128)(2,1)} %bitcast.114, bf16[2,2,512,128]{3,2,1,0:T(8,128)(2,1)} %bitcast.124, bf16[2,512,2,512]{3,2,1,0:T(2,128)(2,1)} %o_ref.7), custom_call_target="tpu_custom_call" | custom-call | flops 536870912 | bytes 3670016 | tf_op jit(solution)/shard_map/pallas_call | solution.py:68
  101.7 1.0 dynamic-slice_bitcast_fusion
  102.7 2.5 %collective-permute-start.13 = (f32[2,8,32,128]{3,2,1,0:T(8,128)S(1)}, f32[2,8,32,128]{3,2,1,0:T(8,128)S(1)}, u32[]{:S(2)}, u32[]{:S(2)}) collective-permute-start(f32[2,8,32,128]{3,2,1,0:T(8,128)S(1)} %dynamic-slice_bitcast_fusion), channel_id=1, source_target_pairs={{0,32},{32,0},{1,33},{33,1},{2,34},{34,2},{3,35},{35,3},{4,36},{36... | collective-permute-start | bytes 786440 | tf_op jit(solution)/shard_map/ppermute | solution.py:125
  105.6 2.4 %collective-permute-start.2 = (f32[2,2,2,32,128]{4,0,3,1,2:T(2,128)S(1)}, f32[2,2,2,32,128]{4,0,3,1,2:T(2,128)S(1)}, u32[]{:S(2)}, u32[]{:S(2)}) collective-permute-start(f32[2,2,2,32,128]{4,0,3,1,2:T(2,128)S(1)} %bitcast.137), channel_id=1, source_target_pairs={{0,64},{64,0},{128,192},{192,128},{256,320},{320,256},{384,448},{4... | collective-permute-start | bytes 393224 | tf_op jit(solution)/shard_map/ppermute | solution.py:92
  108.1 3.4 %collective-permute-start.6 = (f32[2,2,2,32,128]{4,0,3,1,2:T(2,128)S(1)}, f32[2,2,2,32,128]{4,0,3,1,2:T(2,128)S(1)}, u32[]{:S(2)}, u32[]{:S(2)}) collective-permute-start(f32[2,2,2,32,128]{4,0,3,1,2:T(2,128)S(1)} %bitcast.136), channel_id=1, source_target_pairs={{0,64},{64,0},{128,192},{192,128},{256,320},{320,256},{384,448},{4... | collective-permute-start | bytes 393224 | tf_op jit(solution)/shard_map/ppermute | solution.py:92
  111.8 2.4 %collective-permute-start.10 = (f32[2,2,2,32,128]{4,0,3,1,2:T(2,128)S(1)}, f32[2,2,2,32,128]{4,0,3,1,2:T(2,128)S(1)}, u32[]{:S(2)}, u32[]{:S(2)}) collective-permute-start(f32[2,2,2,32,128]{4,0,3,1,2:T(2,128)S(1)} %bitcast.139), channel_id=1, source_target_pairs={{0,64},{64,0},{128,192},{192,128},{256,320},{320,256},{384,448},{4... | collective-permute-start | bytes 393224 | tf_op jit(solution)/shard_map/ppermute | solution.py:92
  114.4 3.4 %collective-permute-start.14 = (f32[2,2,2,32,128]{4,0,3,1,2:T(2,128)S(1)}, f32[2,2,2,32,128]{4,0,3,1,2:T(2,128)S(1)}, u32[]{:S(2)}, u32[]{:S(2)}) collective-permute-start(f32[2,2,2,32,128]{4,0,3,1,2:T(2,128)S(1)} %bitcast.138), channel_id=1, source_target_pairs={{0,64},{64,0},{128,192},{192,128},{256,320},{320,256},{384,448},{4... | collective-permute-start | bytes 393224 | tf_op jit(solution)/shard_map/ppermute | solution.py:92
  118.0 3.0 %collective-permute-start.3 = (f32[2,2,32,128]{3,0,2,1:T(2,128)S(1)}, f32[2,2,32,128]{3,0,2,1:T(2,128)S(1)}, u32[]{:S(2)}, u32[]{:S(2)}) collective-permute-start(f32[2,2,32,128]{3,0,2,1:T(2,128)S(1)} %dynamic-slice_bitcast_fusion.7), channel_id=1, source_target_pairs={{0,128},{64,192},{128,0},{192,64},{256,384},{320,448},{384,256},{4... | collective-permute-start | bytes 196616 | tf_op jit(solution)/shard_map/ppermute | solution.py:92
  121.2 3.7 %collective-permute-start.7 = (f32[2,2,32,128]{3,0,2,1:T(2,128)S(1)}, f32[2,2,32,128]{3,0,2,1:T(2,128)S(1)}, u32[]{:S(2)}, u32[]{:S(2)}) collective-permute-start(f32[2,2,32,128]{3,0,2,1:T(2,128)S(1)} %dynamic-slice_bitcast_fusion.6), channel_id=1, source_target_pairs={{0,128},{64,192},{128,0},{192,64},{256,384},{320,448},{384,256},{4... | collective-permute-start | bytes 196616 | tf_op jit(solution)/shard_map/ppermute | solution.py:92
  125.1 3.0 %collective-permute-start.11 = (f32[2,2,32,128]{3,0,2,1:T(2,128)S(1)}, f32[2,2,32,128]{3,0,2,1:T(2,128)S(1)}, u32[]{:S(2)}, u32[]{:S(2)}) collective-permute-start(f32[2,2,32,128]{3,0,2,1:T(2,128)S(1)} %dynamic-slice_bitcast_fusion.5), channel_id=1, source_target_pairs={{0,128},{64,192},{128,0},{192,64},{256,384},{320,448},{384,256},{4... | collective-permute-start | bytes 196616 | tf_op jit(solution)/shard_map/ppermute | solution.py:92
  128.3 3.7 %collective-permute-start.15 = (f32[2,2,32,128]{3,0,2,1:T(2,128)S(1)}, f32[2,2,32,128]{3,0,2,1:T(2,128)S(1)}, u32[]{:S(2)}, u32[]{:S(2)}) collective-permute-start(f32[2,2,32,128]{3,0,2,1:T(2,128)S(1)} %dynamic-slice_bitcast_fusion.4), channel_id=1, source_target_pairs={{0,128},{64,192},{128,0},{192,64},{256,384},{320,448},{384,256},{4... | collective-permute-start | bytes 196616 | tf_op jit(solution)/shard_map/ppermute | solution.py:92
  132.1 9.1 %collective-permute-start.4 = (f32[2,32,128]{2,0,1:T(2,128)S(1)}, f32[2,32,128]{2,0,1:T(2,128)S(1)}, u32[]{:S(2)}, u32[]{:S(2)}) collective-permute-start(f32[2,32,128]{2,0,1:T(2,128)S(1)} %dynamic-slice_bitcast_fusion.11), channel_id=1, source_target_pairs={{0,256},{64,320},{128,384},{192,448},{256,0},{320,64},{384,128},{4... | collective-permute-start | bytes 98312 | tf_op jit(solution)/shard_map/ppermute | solution.py:92
  141.3 1.9 %collective-permute-start.8 = (f32[2,32,128]{2,0,1:T(2,128)S(1)}, f32[2,32,128]{2,0,1:T(2,128)S(1)}, u32[]{:S(2)}, u32[]{:S(2)}) collective-permute-start(f32[2,32,128]{2,0,1:T(2,128)S(1)} %dynamic-slice_bitcast_fusion.10), channel_id=1, source_target_pairs={{0,256},{64,320},{128,384},{192,448},{256,0},{320,64},{384,128},{4... | collective-permute-start | bytes 98312 | tf_op jit(solution)/shard_map/ppermute | solution.py:92
  143.3 7.8 %collective-permute-start.12 = (f32[2,32,128]{2,0,1:T(2,128)S(1)}, f32[2,32,128]{2,0,1:T(2,128)S(1)}, u32[]{:S(2)}, u32[]{:S(2)}) collective-permute-start(f32[2,32,128]{2,0,1:T(2,128)S(1)} %dynamic-slice_bitcast_fusion.9), channel_id=1, source_target_pairs={{0,256},{64,320},{128,384},{192,448},{256,0},{320,64},{384,128},{4... | collective-permute-start | bytes 98312 | tf_op jit(solution)/shard_map/ppermute | solution.py:92
  151.2 1.9 %collective-permute-start.16 = (f32[2,32,128]{2,0,1:T(2,128)S(1)}, f32[2,32,128]{2,0,1:T(2,128)S(1)}, u32[]{:S(2)}, u32[]{:S(2)}) collective-permute-start(f32[2,32,128]{2,0,1:T(2,128)S(1)} %dynamic-slice_bitcast_fusion.8), channel_id=1, source_target_pairs={{0,256},{64,320},{128,384},{192,448},{256,0},{320,64},{384,128},{4... | collective-permute-start | bytes 98312 | tf_op jit(solution)/shard_map/ppermute | solution.py:92
  153.2 0.3 collective-permute-done.12
  153.5 7.4 %collective-permute-done.16 = f32[2,32,128]{2,0,1:T(2,128)S(1)} collective-permute-done((f32[2,32,128]{2,0,1:T(2,128)S(1)}, f32[2,32,128]{2,0,1:T(2,128)S(1)}, u32[]{:S(2)}, u32[]{:S(2)}) %collective-permute-start.16) | collective-permute-done | bytes 32800 | tf_op jit(solution)/shard_map/ppermute | solution.py:92
  161.0 0.7 maximum_bitcast_fusion
  (68 shorter events, 2.4 us)
Async XLA Ops:
  2.4 19.9 %collective-permute-start = (bf16[2,2,16,512]{3,1,2,0:T(2,128)(2,1)S(1)}, bf16[2,2,16,512]{3,1,2,0:T(2,128)(2,1)S(1)}, u32[]{:S(2)}, u32[]{:S(2)}) collective-permute-start(bf16[2,2,16,512]{3,1,2,0:T(2,128)(2,1)S(1)} %bitcast.134), channel_id=1, source_target_pairs={{0,16},{16,0},{1,17},{17,1},{2,18},{18,2},{3,19},{19,3},{4,20},{20... | collective-permute-start | bytes 196616 | tf_op jit(solution)/shard_map/ppermute | solution.py:100
  23.5 35.4 %copy-start.4 = (bf16[2,512,2,512]{3,2,1,0:T(2,128)(2,1)S(1)}, bf16[2,512,2,512]{3,2,1,0:T(2,128)(2,1)}, u32[]{:S(2)}) copy-start(bf16[2,512,2,512]{3,2,1,0:T(2,128)(2,1)} %param.4) | copy-start | bytes 6291460
  23.5 15.5 %all-to-all-start = ((bf16[2,2,16,2,16,128]{5,4,3,1,0,2:T(8,128)(2,1)}), bf16[2,2,16,2,16,128]{5,4,3,1,0,2:T(8,128)(2,1)S(1)}, u32[]{:S(2)}, u32[]{:S(2)}) async-start(bf16[2,2,16,2,16,128]{5,4,3,1,0,2:T(8,128)(2,1)} %broadcast_in_dim.12), calls=%async_computation | async-start | bytes 1048576 | tf_op jit(solution)/shard_map/all_to_all | solution.py:118
  39.0 13.6 %all-to-all-start.1 = ((bf16[2,2,16,2,16,128]{5,4,3,1,0,2:T(8,128)(2,1)}), bf16[2,2,16,2,16,128]{5,4,3,1,0,2:T(8,128)(2,1)S(1)}, u32[]{:S(2)}, u32[]{:S(2)}) async-start(bf16[2,2,16,2,16,128]{5,4,3,1,0,2:T(8,128)(2,1)} %broadcast_in_dim.13), calls=%async_computation.1 | async-start | bytes 1048576 | tf_op jit(solution)/shard_map/all_to_all | solution.py:118
  52.6 14.4 %all-to-all-start.2 = ((bf16[2,2,16,2,16,128]{5,4,3,1,0,2:T(8,128)(2,1)}), bf16[2,2,16,2,16,128]{5,4,3,1,0,2:T(8,128)(2,1)}, u32[]{:S(2)}, u32[]{:S(2)}) async-start(bf16[2,2,16,2,16,128]{5,4,3,1,0,2:T(8,128)(2,1)} %broadcast_in_dim.14), calls=%async_computation.2 | async-start | bytes 1048576 | tf_op jit(solution)/shard_map/all_to_all | solution.py:118
  66.9 29.8 %all-to-all-start.3 = ((bf16[2,2,16,2,16,128]{5,4,3,1,0,2:T(8,128)(2,1)}), bf16[2,2,16,2,16,128]{5,4,3,1,0,2:T(8,128)(2,1)S(1)}, u32[]{:S(2)}, u32[]{:S(2)}) async-start(bf16[2,2,16,2,16,128]{5,4,3,1,0,2:T(8,128)(2,1)} %broadcast_in_dim.15), calls=%async_computation.3 | async-start | bytes 1048576 | tf_op jit(solution)/shard_map/all_to_all | solution.py:118
  77.7 27.6 %collective-permute-start.1 = (f32[2,8,32,128]{3,2,1,0:T(8,128)S(1)}, f32[2,8,32,128]{3,2,1,0:T(8,128)S(1)}, u32[]{:S(2)}, u32[]{:S(2)}) collective-permute-start(f32[2,8,32,128]{3,2,1,0:T(8,128)S(1)} %dynamic-slice_bitcast_fusion.3), channel_id=1, source_target_pairs={{0,32},{32,0},{1,33},{33,1},{2,34},{34,2},{3,35},{35,3},{4,36},{36... | collective-permute-start | bytes 786440 | tf_op jit(solution)/shard_map/ppermute | solution.py:125
  85.5 19.9 %collective-permute-start.5 = (f32[2,8,32,128]{3,2,1,0:T(8,128)S(1)}, f32[2,8,32,128]{3,2,1,0:T(8,128)S(1)}, u32[]{:S(2)}, u32[]{:S(2)}) collective-permute-start(f32[2,8,32,128]{3,2,1,0:T(8,128)S(1)} %dynamic-slice_bitcast_fusion.2), channel_id=1, source_target_pairs={{0,32},{32,0},{1,33},{33,1},{2,34},{34,2},{3,35},{35,3},{4,36},{36... | collective-permute-start | bytes 786440 | tf_op jit(solution)/shard_map/ppermute | solution.py:125
  94.8 16.8 %collective-permute-start.9 = (f32[2,8,32,128]{3,2,1,0:T(8,128)S(1)}, f32[2,8,32,128]{3,2,1,0:T(8,128)S(1)}, u32[]{:S(2)}, u32[]{:S(2)}) collective-permute-start(f32[2,8,32,128]{3,2,1,0:T(8,128)S(1)} %dynamic-slice_bitcast_fusion.1), channel_id=1, source_target_pairs={{0,32},{32,0},{1,33},{33,1},{2,34},{34,2},{3,35},{35,3},{4,36},{36... | collective-permute-start | bytes 786440 | tf_op jit(solution)/shard_map/ppermute | solution.py:125
  97.6 7.7 %copy-start.2 = (f32[2,512,128]{2,1,0:T(8,128)S(1)}, f32[2,512,128]{2,1,0:T(8,128)}, u32[]{:S(2)}) copy-start(f32[2,512,128]{2,1,0:T(8,128)} %shard_map.46) | copy-start | bytes 1572868
  97.6 7.8 %copy-start.3 = (f32[2,512,128]{2,1,0:T(8,128)S(1)}, f32[2,512,128]{2,1,0:T(8,128)}, u32[]{:S(2)}) copy-start(f32[2,512,128]{2,1,0:T(8,128)} %shard_map.47) | copy-start | bytes 1572868
  101.7 9.9 %copy-start = (f32[2,512,128]{2,1,0:T(8,128)S(1)}, f32[2,512,128]{2,1,0:T(8,128)}, u32[]{:S(2)}) copy-start(f32[2,512,128]{2,1,0:T(8,128)} %shard_map.48) | copy-start | bytes 1572868
  102.7 8.9 %copy-start.1 = (f32[2,512,128]{2,1,0:T(8,128)S(1)}, f32[2,512,128]{2,1,0:T(8,128)}, u32[]{:S(2)}) copy-start(f32[2,512,128]{2,1,0:T(8,128)} %shard_map.49) | copy-start | bytes 1572868
  102.7 8.9 %collective-permute-start.13 = (f32[2,8,32,128]{3,2,1,0:T(8,128)S(1)}, f32[2,8,32,128]{3,2,1,0:T(8,128)S(1)}, u32[]{:S(2)}, u32[]{:S(2)}) collective-permute-start(f32[2,8,32,128]{3,2,1,0:T(8,128)S(1)} %dynamic-slice_bitcast_fusion), channel_id=1, source_target_pairs={{0,32},{32,0},{1,33},{33,1},{2,34},{34,2},{3,35},{35,3},{4,36},{36... | collective-permute-start | bytes 786440 | tf_op jit(solution)/shard_map/ppermute | solution.py:125
  105.6 12.2 %collective-permute-start.2 = (f32[2,2,2,32,128]{4,0,3,1,2:T(2,128)S(1)}, f32[2,2,2,32,128]{4,0,3,1,2:T(2,128)S(1)}, u32[]{:S(2)}, u32[]{:S(2)}) collective-permute-start(f32[2,2,2,32,128]{4,0,3,1,2:T(2,128)S(1)} %bitcast.137), channel_id=1, source_target_pairs={{0,64},{64,0},{128,192},{192,128},{256,320},{320,256},{384,448},{4... | collective-permute-start | bytes 393224 | tf_op jit(solution)/shard_map/ppermute | solution.py:92
  108.1 12.9 %collective-permute-start.6 = (f32[2,2,2,32,128]{4,0,3,1,2:T(2,128)S(1)}, f32[2,2,2,32,128]{4,0,3,1,2:T(2,128)S(1)}, u32[]{:S(2)}, u32[]{:S(2)}) collective-permute-start(f32[2,2,2,32,128]{4,0,3,1,2:T(2,128)S(1)} %bitcast.136), channel_id=1, source_target_pairs={{0,64},{64,0},{128,192},{192,128},{256,320},{320,256},{384,448},{4... | collective-permute-start | bytes 393224 | tf_op jit(solution)/shard_map/ppermute | solution.py:92
  111.8 13.1 %collective-permute-start.10 = (f32[2,2,2,32,128]{4,0,3,1,2:T(2,128)S(1)}, f32[2,2,2,32,128]{4,0,3,1,2:T(2,128)S(1)}, u32[]{:S(2)}, u32[]{:S(2)}) collective-permute-start(f32[2,2,2,32,128]{4,0,3,1,2:T(2,128)S(1)} %bitcast.139), channel_id=1, source_target_pairs={{0,64},{64,0},{128,192},{192,128},{256,320},{320,256},{384,448},{4... | collective-permute-start | bytes 393224 | tf_op jit(solution)/shard_map/ppermute | solution.py:92
  114.4 13.7 %collective-permute-start.14 = (f32[2,2,2,32,128]{4,0,3,1,2:T(2,128)S(1)}, f32[2,2,2,32,128]{4,0,3,1,2:T(2,128)S(1)}, u32[]{:S(2)}, u32[]{:S(2)}) collective-permute-start(f32[2,2,2,32,128]{4,0,3,1,2:T(2,128)S(1)} %bitcast.138), channel_id=1, source_target_pairs={{0,64},{64,0},{128,192},{192,128},{256,320},{320,256},{384,448},{4... | collective-permute-start | bytes 393224 | tf_op jit(solution)/shard_map/ppermute | solution.py:92
  118.0 14.1 %collective-permute-start.3 = (f32[2,2,32,128]{3,0,2,1:T(2,128)S(1)}, f32[2,2,32,128]{3,0,2,1:T(2,128)S(1)}, u32[]{:S(2)}, u32[]{:S(2)}) collective-permute-start(f32[2,2,32,128]{3,0,2,1:T(2,128)S(1)} %dynamic-slice_bitcast_fusion.7), channel_id=1, source_target_pairs={{0,128},{64,192},{128,0},{192,64},{256,384},{320,448},{384,256},{4... | collective-permute-start | bytes 196616 | tf_op jit(solution)/shard_map/ppermute | solution.py:92
  121.2 20.0 %collective-permute-start.7 = (f32[2,2,32,128]{3,0,2,1:T(2,128)S(1)}, f32[2,2,32,128]{3,0,2,1:T(2,128)S(1)}, u32[]{:S(2)}, u32[]{:S(2)}) collective-permute-start(f32[2,2,32,128]{3,0,2,1:T(2,128)S(1)} %dynamic-slice_bitcast_fusion.6), channel_id=1, source_target_pairs={{0,128},{64,192},{128,0},{192,64},{256,384},{320,448},{384,256},{4... | collective-permute-start | bytes 196616 | tf_op jit(solution)/shard_map/ppermute | solution.py:92
  125.1 18.1 %collective-permute-start.11 = (f32[2,2,32,128]{3,0,2,1:T(2,128)S(1)}, f32[2,2,32,128]{3,0,2,1:T(2,128)S(1)}, u32[]{:S(2)}, u32[]{:S(2)}) collective-permute-start(f32[2,2,32,128]{3,0,2,1:T(2,128)S(1)} %dynamic-slice_bitcast_fusion.5), channel_id=1, source_target_pairs={{0,128},{64,192},{128,0},{192,64},{256,384},{320,448},{384,256},{4... | collective-permute-start | bytes 196616 | tf_op jit(solution)/shard_map/ppermute | solution.py:92
  128.3 22.8 %collective-permute-start.15 = (f32[2,2,32,128]{3,0,2,1:T(2,128)S(1)}, f32[2,2,32,128]{3,0,2,1:T(2,128)S(1)}, u32[]{:S(2)}, u32[]{:S(2)}) collective-permute-start(f32[2,2,32,128]{3,0,2,1:T(2,128)S(1)} %dynamic-slice_bitcast_fusion.4), channel_id=1, source_target_pairs={{0,128},{64,192},{128,0},{192,64},{256,384},{320,448},{384,256},{4... | collective-permute-start | bytes 196616 | tf_op jit(solution)/shard_map/ppermute | solution.py:92
  132.1 21.0 %collective-permute-start.4 = (f32[2,32,128]{2,0,1:T(2,128)S(1)}, f32[2,32,128]{2,0,1:T(2,128)S(1)}, u32[]{:S(2)}, u32[]{:S(2)}) collective-permute-start(f32[2,32,128]{2,0,1:T(2,128)S(1)} %dynamic-slice_bitcast_fusion.11), channel_id=1, source_target_pairs={{0,256},{64,320},{128,384},{192,448},{256,0},{320,64},{384,128},{4... | collective-permute-start | bytes 98312 | tf_op jit(solution)/shard_map/ppermute | solution.py:92
  141.3 11.9 %collective-permute-start.8 = (f32[2,32,128]{2,0,1:T(2,128)S(1)}, f32[2,32,128]{2,0,1:T(2,128)S(1)}, u32[]{:S(2)}, u32[]{:S(2)}) collective-permute-start(f32[2,32,128]{2,0,1:T(2,128)S(1)} %dynamic-slice_bitcast_fusion.10), channel_id=1, source_target_pairs={{0,256},{64,320},{128,384},{192,448},{256,0},{320,64},{384,128},{4... | collective-permute-start | bytes 98312 | tf_op jit(solution)/shard_map/ppermute | solution.py:92
  143.3 10.2 %collective-permute-start.12 = (f32[2,32,128]{2,0,1:T(2,128)S(1)}, f32[2,32,128]{2,0,1:T(2,128)S(1)}, u32[]{:S(2)}, u32[]{:S(2)}) collective-permute-start(f32[2,32,128]{2,0,1:T(2,128)S(1)} %dynamic-slice_bitcast_fusion.9), channel_id=1, source_target_pairs={{0,256},{64,320},{128,384},{192,448},{256,0},{320,64},{384,128},{4... | collective-permute-start | bytes 98312 | tf_op jit(solution)/shard_map/ppermute | solution.py:92
  151.2 9.7 %collective-permute-start.16 = (f32[2,32,128]{2,0,1:T(2,128)S(1)}, f32[2,32,128]{2,0,1:T(2,128)S(1)}, u32[]{:S(2)}, u32[]{:S(2)}) collective-permute-start(f32[2,32,128]{2,0,1:T(2,128)S(1)} %dynamic-slice_bitcast_fusion.8), channel_id=1, source_target_pairs={{0,256},{64,320},{128,384},{192,448},{256,0},{320,64},{384,128},{4... | collective-permute-start | bytes 98312 | tf_op jit(solution)/shard_map/ppermute | solution.py:92

commit v16 on v15

--- a/solution.py
+++ b/solution.py
@@ -102,8 +102,7 @@
     pair = jnp.where(low, jnp.stack([permuted, other], axis=2), jnp.stack([other, permuted], axis=2))
     plane = lax.axis_size("x") * lax.axis_size("y")
     copies = jnp.broadcast_to(pair[:, :, None], pair.shape[:2] + (plane,) + pair.shape[2:])
-    halves = 4
-    span = width // halves
+    spans = [3 * width // 4, width // 4]
     stem_t = jnp.transpose(stem_tensor, (0, 2, 1, 3))
     open_t = open_tensor
     zl_count = lax.axis_size("zl")
@@ -111,14 +110,17 @@
     core = lax.axis_index("core")
     results = []
     previous = None
-    for h in range(halves):
-        part = copies[..., h * span:(h + 1) * span]
+    offset = 0
+    for span in spans:
+        part = copies[..., offset:offset + span]
         if previous is not None:
             part, previous = lax.optimization_barrier((part, previous))
         gathered = lax.all_to_all(part, ("x", "y"), 2, 4, tiled=True)
         previous = gathered
         branch_t = gathered.reshape(slice_count, 2, -1, span)
-        local_sum = contract(stem_t, branch_t, open_t, h)
+        column_block = offset // span
+        offset += span
+        local_sum = contract(stem_t, branch_t, open_t, column_block)
         shaped = local_sum.reshape(2, zl_count, 2, block_rows, span)
         mine = lax.dynamic_index_in_dim(shaped, core, 2, keepdims=False)
         theirs = lax.dynamic_index_in_dim(shaped, 1 - core, 2, keepdims=False)

time: 163 us -> 136 us (0.83)
  the two profiles are of different devices: /device:TPU:2 before, /device:TPU:8 now
where the time goes in v16:
time: 136 us; the launch traced here: 135 us
  starting transfers between devices  66.5 us (49%)
  waiting for transfers between devices  42.8 us (31%)
  local copies, waits for them, and re-layouts  12.5 us (9%)
  Pallas kernels  9.7 us (7%)
  other arithmetic  2.84 us (2%)
    ppermute x6, starting transfers between devices, halving_scatter(): shaped = keep + lax.ppermute(send, axis, pairs)  34.1 us
    all_to_all x2, waiting for transfers between devices, body(): gathered = lax.all_to_all(part, ('x', 'y'), 2, 4, tiled=True)  22.8 us
    ppermute x1, starting transfers between devices, body(): other = lax.ppermute(permuted, 'zh', shift_pairs(2, 1))  15.7 us
    ppermute x6, waiting for transfers between devices, halving_scatter(): shaped = keep + lax.ppermute(send, axis, pairs)  14.6 us
    all_to_all x2, starting transfers between devices, body(): gathered = lax.all_to_all(part, ('x', 'y'), 2, 4, tiled=True)  12.3 us
    pallas_call x2, Pallas kernels, contract(): pl.pallas_call(contract_kernel, out_shape=jax.ShapeDtypeStruct((2, rows,...  9.7 us
    ppermute x2, starting transfers between devices, body(): mine = mine + lax.ppermute(theirs, 'core', shift_pairs(2, 1))  4.33 us
    ppermute x1, waiting for transfers between devices, body(): other = lax.ppermute(permuted, 'zh', shift_pairs(2, 1))  4.2 us
  transfers between devices with their start and end apart: 11, of which 7 were waited for; matrix products, arithmetic and copies ran while one was open for 6% of the time, Pallas kernels for 3%

profile of v16, /device:TPU:8, one launch (start us, length us, event | category | flops | bytes accessed | tf_op | source)
XLA Modules:
  0.0 135.3 jit_solution(1491496039520953435)
XLA Ops:
  0.0 0.8 fusion.4
  0.8 0.8 fusion.5
  1.6 0.3 fusion
  2.0 0.3 fusion.1
  2.4 15.7 %collective-permute-start = (bf16[2,2,16,512]{3,1,2,0:T(2,128)(2,1)S(1)}, bf16[2,2,16,512]{3,1,2,0:T(2,128)(2,1)S(1)}, u32[]{:S(2)}, u32[]{:S(2)}) collective-permute-start(bf16[2,2,16,512]{3,1,2,0:T(2,128)(2,1)S(1)} %bitcast.78), channel_id=1, source_target_pairs={{0,16},{16,0},{1,17},{17,1},{2,18},{18,2},{3,19},{19,3},{4,20},{20... | collective-permute-start | bytes 196616 | tf_op jit(solution)/shard_map/ppermute | solution.py:100
  18.1 4.2 %collective-permute-done = bf16[2,2,16,512]{3,1,2,0:T(2,128)(2,1)S(1)} collective-permute-done((bf16[2,2,16,512]{3,1,2,0:T(2,128)(2,1)S(1)}, bf16[2,2,16,512]{3,1,2,0:T(2,128)(2,1)S(1)}, u32[]{:S(2)}, u32[]{:S(2)}) %collective-permute-start) | collective-permute-done | bytes 65568 | tf_op jit(solution)/shard_map/ppermute | solution.py:100
  22.3 0.2 broadcast_select_fusion
  22.5 0.9 broadcast_in_dim.9
  23.4 7.4 %all-to-all-start.1 = ((bf16[2,2,16,2,16,128]{5,4,3,1,0,2:T(8,128)(2,1)}), bf16[2,2,16,2,16,128]{5,4,3,1,0,2:T(8,128)(2,1)S(1)}, u32[]{:S(2)}, u32[]{:S(2)}) async-start(bf16[2,2,16,2,16,128]{5,4,3,1,0,2:T(8,128)(2,1)} %broadcast_in_dim.9), calls=%async_computation.1 | async-start | bytes 1048576 | tf_op jit(solution)/shard_map/all_to_all | solution.py:118
  30.8 0.1 slice.26
  30.9 8.6 %all-to-all-done.1 = bf16[2,2,16,2,16,128]{5,4,3,1,0,2:T(8,128)(2,1)S(1)} async-done(((bf16[2,2,16,2,16,128]{5,4,3,1,0,2:T(8,128)(2,1)}), bf16[2,2,16,2,16,128]{5,4,3,1,0,2:T(8,128)(2,1)S(1)}, u32[]{:S(2)}, u32[]{:S(2)}) %all-to-all-start.1) | async-done | bytes 524320 | tf_op jit(solution)/shard_map/all_to_all | solution.py:118
  39.6 1.4 %broadcast_in_dim.8 = bf16[2,2,16,2,16,384]{5,4,3,1,0,2:T(8,128)(2,1)} broadcast(bf16[2,2,2,16,384]{4,3,2,1,0:T(8,128)(2,1)S(1)} %copy.13), dimensions={0,1,3,4,5} | broadcast | bytes 1671168 | tf_op jit(solution)/shard_map/broadcast_in_dim | solution.py:104
  41.0 5.0 %all-to-all-start = ((bf16[2,2,16,2,16,384]{5,4,3,1,0,2:T(8,128)(2,1)}), bf16[2,2,16,2,16,384]{5,4,3,1,0,2:T(8,128)(2,1)S(1)}, u32[]{:S(2)}, u32[]{:S(2)}) async-start(bf16[2,2,16,2,16,384]{5,4,3,1,0,2:T(8,128)(2,1)} %broadcast_in_dim.8), calls=%async_computation | async-start | bytes 3145728 | tf_op jit(solution)/shard_map/all_to_all | solution.py:118
  45.9 3.3 %copy.26 = bf16[2,512,2,512]{3,1,2,0:T(8,128)(2,1)} copy(bf16[2,512,2,512]{3,2,1,0:T(2,128)(2,1)} %param.4) | data formatting | bytes 4194304 | tf_op args[0]
  49.2 0.9 copy.18
  50.1 14.2 %all-to-all-done = bf16[2,2,16,2,16,384]{5,4,3,1,0,2:T(8,128)(2,1)S(1)} async-done(((bf16[2,2,16,2,16,384]{5,4,3,1,0,2:T(8,128)(2,1)}), bf16[2,2,16,2,16,384]{5,4,3,1,0,2:T(8,128)(2,1)S(1)}, u32[]{:S(2)}, u32[]{:S(2)}) %all-to-all-start) | async-done | bytes 1572896 | tf_op jit(solution)/shard_map/all_to_all | solution.py:118
  64.2 1.3 copy.14
  65.6 5.7 %shard_map.46 = f32[2,512,384]{2,1,0:T(8,128)} custom-call(bf16[2,2,512,512]{3,2,1,0:T(8,128)(2,1)} %bitcast.65, bf16[2,2,512,384]{3,2,1,0:T(8,128)(2,1)} %bitcast.70, bf16[2,512,2,512]{3,2,1,0:T(2,128)(2,1)} %o_ref.3), custom_call_target="tpu_custom_call" | custom-call | flops 1610612736 | bytes 6815744 | tf_op jit(solution)/shard_map/pallas_call | solution.py:68
  71.2 1.2 dynamic-slice_bitcast_fusion
  72.4 1.9 %collective-permute-start.1 = (f32[2,8,32,384]{3,2,1,0:T(8,128)S(1)}, f32[2,8,32,384]{3,2,1,0:T(8,128)S(1)}, u32[]{:S(2)}, u32[]{:S(2)}) collective-permute-start(f32[2,8,32,384]{3,2,1,0:T(8,128)S(1)} %dynamic-slice_bitcast_fusion), channel_id=1, source_target_pairs={{0,32},{32,0},{1,33},{33,1},{2,34},{34,2},{3,35},{35,3},{4,36},{36... | collective-permute-start | bytes 2359304 | tf_op jit(solution)/shard_map/ppermute | solution.py:127
  74.4 4.0 %shard_map.47 = f32[2,512,128]{2,1,0:T(8,128)} custom-call(bf16[2,2,512,512]{3,2,1,0:T(8,128)(2,1)} %bitcast.66, bf16[2,2,512,128]{3,2,1,0:T(8,128)(2,1)} %bitcast.74, bf16[2,512,2,512]{3,2,1,0:T(2,128)(2,1)} %o_ref.3), custom_call_target="tpu_custom_call" | custom-call | flops 536870912 | bytes 3670016 | tf_op jit(solution)/shard_map/pallas_call | solution.py:68
  78.4 1.1 dynamic-slice_bitcast_fusion.1
  79.5 2.4 %collective-permute-start.5 = (f32[2,8,32,128]{3,2,1,0:T(8,128)S(1)}, f32[2,8,32,128]{3,2,1,0:T(8,128)}, u32[]{:S(2)}, u32[]{:S(2)}) collective-permute-start(f32[2,8,32,128]{3,2,1,0:T(8,128)S(1)} %dynamic-slice_bitcast_fusion.1), channel_id=1, source_target_pairs={{0,32},{32,0},{1,33},{33,1},{2,34},{34,2},{3,35},{35,3},{4,36},{36... | collective-permute-start | bytes 786440 | tf_op jit(solution)/shard_map/ppermute | solution.py:127
  81.9 1.3 collective-permute-done.5
  83.2 1.1 bitcast_add_fusion.2
  84.3 0.1 copy.28
  84.4 3.1 %collective-permute-start.6 = (f32[2,2,2,32,128]{4,0,3,1,2:T(2,128)S(1)}, f32[2,2,2,32,128]{4,0,3,1,2:T(2,128)S(1)}, u32[]{:S(2)}, u32[]{:S(2)}) collective-permute-start(f32[2,2,2,32,128]{4,0,3,1,2:T(2,128)S(1)} %bitcast.80), channel_id=1, source_target_pairs={{0,64},{64,0},{128,192},{192,128},{256,320},{320,256},{384,448},{4... | collective-permute-start | bytes 393224 | tf_op jit(solution)/shard_map/ppermute | solution.py:92
  87.5 0.0 collective-permute-done.1
  87.5 0.1 bitcast_add_fusion
  87.6 0.1 constant_dynamic-slice_fusion.3
  87.7 0.3 copy.27
  88.0 2.8 %collective-permute-start.2 = (f32[2,2,2,32,384]{4,0,3,1,2:T(2,128)S(1)}, f32[2,2,2,32,384]{4,0,3,1,2:T(2,128)S(1)}, u32[]{:S(2)}, u32[]{:S(2)}) collective-permute-start(f32[2,2,2,32,384]{4,0,3,1,2:T(2,128)S(1)} %bitcast.77), channel_id=1, source_target_pairs={{0,64},{64,0},{128,192},{192,128},{256,320},{320,256},{384,448},{4... | collective-permute-start | bytes 1179656 | tf_op jit(solution)/shard_map/ppermute | solution.py:92
  90.8 1.3 collective-permute-done.6
  92.0 0.1 bitcast_add_fusion.4
  92.2 3.7 %collective-permute-start.7 = (f32[2,2,32,128]{3,0,2,1:T(2,128)S(1)}, f32[2,2,32,128]{3,0,2,1:T(2,128)S(1)}, u32[]{:S(2)}, u32[]{:S(2)}) collective-permute-start(f32[2,2,32,128]{3,0,2,1:T(2,128)S(1)} %dynamic-slice_bitcast_fusion.4), channel_id=1, source_target_pairs={{0,128},{64,192},{128,0},{192,64},{256,384},{320,448},{384,256},{4... | collective-permute-start | bytes 196616 | tf_op jit(solution)/shard_map/ppermute | solution.py:92
  95.9 6.5 %collective-permute-done.2 = f32[2,2,2,32,384]{4,0,3,1,2:T(2,128)S(1)} collective-permute-done((f32[2,2,2,32,384]{4,0,3,1,2:T(2,128)S(1)}, f32[2,2,2,32,384]{4,0,3,1,2:T(2,128)S(1)}, u32[]{:S(2)}, u32[]{:S(2)}) %collective-permute-start.2) | collective-permute-done | bytes 393248 | tf_op jit(solution)/shard_map/ppermute | solution.py:92
  102.4 0.4 bitcast_add_fusion.1
  102.8 0.1 dynamic-slice_bitcast_fusion.2
  102.8 2.7 %collective-permute-start.3 = (f32[2,2,32,384]{3,0,2,1:T(2,128)S(1)}, f32[2,2,32,384]{3,0,2,1:T(2,128)S(1)}, u32[]{:S(2)}, u32[]{:S(2)}) collective-permute-start(f32[2,2,32,384]{3,0,2,1:T(2,128)S(1)} %dynamic-slice_bitcast_fusion.2), channel_id=1, source_target_pairs={{0,128},{64,192},{128,0},{192,64},{256,384},{320,448},{384,256},{4... | collective-permute-start | bytes 589832 | tf_op jit(solution)/shard_map/ppermute | solution.py:92
  105.5 0.0 collective-permute-done.7
  105.6 12.2 %collective-permute-start.8 = (f32[2,32,128]{2,0,1:T(2,128)S(1)}, f32[2,32,128]{2,0,1:T(2,128)S(1)}, u32[]{:S(2)}, u32[]{:S(2)}) collective-permute-start(f32[2,32,128]{2,0,1:T(2,128)S(1)} %dynamic-slice_bitcast_fusion.5), channel_id=1, source_target_pairs={{0,256},{64,320},{128,384},{192,448},{256,0},{320,64},{384,128},{4... | collective-permute-start | bytes 98312 | tf_op jit(solution)/shard_map/ppermute | solution.py:92
  117.8 0.0 collective-permute-done.3
  117.8 0.1 bitcast_add_fusion.3
  118.0 9.7 %collective-permute-start.4 = (f32[2,32,384]{2,0,1:T(2,128)S(1)}, f32[2,32,384]{2,0,1:T(2,128)S(1)}, u32[]{:S(2)}, u32[]{:S(2)}) collective-permute-start(f32[2,32,384]{2,0,1:T(2,128)S(1)} %dynamic-slice_bitcast_fusion.3), channel_id=1, source_target_pairs={{0,256},{64,320},{128,384},{192,448},{256,0},{320,64},{384,128},{4... | collective-permute-start | bytes 294920 | tf_op jit(solution)/shard_map/ppermute | solution.py:92
  127.7 0.0 collective-permute-done.8
  127.8 6.8 %collective-permute-done.4 = f32[2,32,384]{2,0,1:T(2,128)S(1)} collective-permute-done((f32[2,32,384]{2,0,1:T(2,128)S(1)}, f32[2,32,384]{2,0,1:T(2,128)S(1)}, u32[]{:S(2)}, u32[]{:S(2)}) %collective-permute-start.4) | collective-permute-done | bytes 98336 | tf_op jit(solution)/shard_map/ppermute | solution.py:92
  134.6 0.1 bitcast_add_fusion.5
  134.6 0.7 maximum_bitcast_fusion
  (17 shorter events, 0.3 us)
Async XLA Ops:
  2.4 19.9 %collective-permute-start = (bf16[2,2,16,512]{3,1,2,0:T(2,128)(2,1)S(1)}, bf16[2,2,16,512]{3,1,2,0:T(2,128)(2,1)S(1)}, u32[]{:S(2)}, u32[]{:S(2)}) collective-permute-start(bf16[2,2,16,512]{3,1,2,0:T(2,128)(2,1)S(1)} %bitcast.78), channel_id=1, source_target_pairs={{0,16},{16,0},{1,17},{17,1},{2,18},{18,2},{3,19},{19,3},{4,20},{20... | collective-permute-start | bytes 196616 | tf_op jit(solution)/shard_map/ppermute | solution.py:100
  23.4 16.1 %all-to-all-start.1 = ((bf16[2,2,16,2,16,128]{5,4,3,1,0,2:T(8,128)(2,1)}), bf16[2,2,16,2,16,128]{5,4,3,1,0,2:T(8,128)(2,1)S(1)}, u32[]{:S(2)}, u32[]{:S(2)}) async-start(bf16[2,2,16,2,16,128]{5,4,3,1,0,2:T(8,128)(2,1)} %broadcast_in_dim.9), calls=%async_computation.1 | async-start | bytes 1048576 | tf_op jit(solution)/shard_map/all_to_all | solution.py:118
  41.0 23.3 %all-to-all-start = ((bf16[2,2,16,2,16,384]{5,4,3,1,0,2:T(8,128)(2,1)}), bf16[2,2,16,2,16,384]{5,4,3,1,0,2:T(8,128)(2,1)S(1)}, u32[]{:S(2)}, u32[]{:S(2)}) async-start(bf16[2,2,16,2,16,384]{5,4,3,1,0,2:T(8,128)(2,1)} %broadcast_in_dim.8), calls=%async_computation | async-start | bytes 3145728 | tf_op jit(solution)/shard_map/all_to_all | solution.py:118
  72.4 15.0 %collective-permute-start.1 = (f32[2,8,32,384]{3,2,1,0:T(8,128)S(1)}, f32[2,8,32,384]{3,2,1,0:T(8,128)S(1)}, u32[]{:S(2)}, u32[]{:S(2)}) collective-permute-start(f32[2,8,32,384]{3,2,1,0:T(8,128)S(1)} %dynamic-slice_bitcast_fusion), channel_id=1, source_target_pairs={{0,32},{32,0},{1,33},{33,1},{2,34},{34,2},{3,35},{35,3},{4,36},{36... | collective-permute-start | bytes 2359304 | tf_op jit(solution)/shard_map/ppermute | solution.py:127
  78.4 9.1 %copy-start = (f32[2,512,384]{2,1,0:T(8,128)S(1)}, f32[2,512,384]{2,1,0:T(8,128)}, u32[]{:S(2)}) copy-start(f32[2,512,384]{2,1,0:T(8,128)} %shard_map.46) | copy-start | bytes 4718596
  79.5 3.7 %collective-permute-start.5 = (f32[2,8,32,128]{3,2,1,0:T(8,128)S(1)}, f32[2,8,32,128]{3,2,1,0:T(8,128)}, u32[]{:S(2)}, u32[]{:S(2)}) collective-permute-start(f32[2,8,32,128]{3,2,1,0:T(8,128)S(1)} %dynamic-slice_bitcast_fusion.1), channel_id=1, source_target_pairs={{0,32},{32,0},{1,33},{33,1},{2,34},{34,2},{3,35},{35,3},{4,36},{36... | collective-permute-start | bytes 786440 | tf_op jit(solution)/shard_map/ppermute | solution.py:127
  84.4 7.7 %collective-permute-start.6 = (f32[2,2,2,32,128]{4,0,3,1,2:T(2,128)S(1)}, f32[2,2,2,32,128]{4,0,3,1,2:T(2,128)S(1)}, u32[]{:S(2)}, u32[]{:S(2)}) collective-permute-start(f32[2,2,2,32,128]{4,0,3,1,2:T(2,128)S(1)} %bitcast.80), channel_id=1, source_target_pairs={{0,64},{64,0},{128,192},{192,128},{256,320},{320,256},{384,448},{4... | collective-permute-start | bytes 393224 | tf_op jit(solution)/shard_map/ppermute | solution.py:92
  88.0 14.4 %collective-permute-start.2 = (f32[2,2,2,32,384]{4,0,3,1,2:T(2,128)S(1)}, f32[2,2,2,32,384]{4,0,3,1,2:T(2,128)S(1)}, u32[]{:S(2)}, u32[]{:S(2)}) collective-permute-start(f32[2,2,2,32,384]{4,0,3,1,2:T(2,128)S(1)} %bitcast.77), channel_id=1, source_target_pairs={{0,64},{64,0},{128,192},{192,128},{256,320},{320,256},{384,448},{4... | collective-permute-start | bytes 1179656 | tf_op jit(solution)/shard_map/ppermute | solution.py:92
  92.2 13.3 %collective-permute-start.7 = (f32[2,2,32,128]{3,0,2,1:T(2,128)S(1)}, f32[2,2,32,128]{3,0,2,1:T(2,128)S(1)}, u32[]{:S(2)}, u32[]{:S(2)}) collective-permute-start(f32[2,2,32,128]{3,0,2,1:T(2,128)S(1)} %dynamic-slice_bitcast_fusion.4), channel_id=1, source_target_pairs={{0,128},{64,192},{128,0},{192,64},{256,384},{320,448},{384,256},{4... | collective-permute-start | bytes 196616 | tf_op jit(solution)/shard_map/ppermute | solution.py:92
  102.8 15.0 %collective-permute-start.3 = (f32[2,2,32,384]{3,0,2,1:T(2,128)S(1)}, f32[2,2,32,384]{3,0,2,1:T(2,128)S(1)}, u32[]{:S(2)}, u32[]{:S(2)}) collective-permute-start(f32[2,2,32,384]{3,0,2,1:T(2,128)S(1)} %dynamic-slice_bitcast_fusion.2), channel_id=1, source_target_pairs={{0,128},{64,192},{128,0},{192,64},{256,384},{320,448},{384,256},{4... | collective-permute-start | bytes 589832 | tf_op jit(solution)/shard_map/ppermute | solution.py:92
  105.6 22.1 %collective-permute-start.8 = (f32[2,32,128]{2,0,1:T(2,128)S(1)}, f32[2,32,128]{2,0,1:T(2,128)S(1)}, u32[]{:S(2)}, u32[]{:S(2)}) collective-permute-start(f32[2,32,128]{2,0,1:T(2,128)S(1)} %dynamic-slice_bitcast_fusion.5), channel_id=1, source_target_pairs={{0,256},{64,320},{128,384},{192,448},{256,0},{320,64},{384,128},{4... | collective-permute-start | bytes 98312 | tf_op jit(solution)/shard_map/ppermute | solution.py:92
  118.0 16.6 %collective-permute-start.4 = (f32[2,32,384]{2,0,1:T(2,128)S(1)}, f32[2,32,384]{2,0,1:T(2,128)S(1)}, u32[]{:S(2)}, u32[]{:S(2)}) collective-permute-start(f32[2,32,384]{2,0,1:T(2,128)S(1)} %dynamic-slice_bitcast_fusion.3), channel_id=1, source_target_pairs={{0,256},{64,320},{128,384},{192,448},{256,0},{320,64},{384,128},{4... | collective-permute-start | bytes 294920 | tf_op jit(solution)/shard_map/ppermute | solution.py:92

commit v17 on v9

--- a/solution.py
+++ b/solution.py
@@ -95,9 +95,14 @@
 
 def body(stem_tensor, branch_tensor, open_tensor, open_order):
     slice_count, row_count, _, width = stem_tensor.shape
-    permuted = jnp.stack([permute_columns(branch_tensor[t], open_order[t]) for t in range(slice_count)])
-    permuted = jnp.transpose(permuted, (0, 2, 1, 3))
-    other = lax.ppermute(permuted, "zh", shift_pairs(2, 1))
+    other_raw = lax.ppermute(branch_tensor, "zh", shift_pairs(2, 1))
+
+    def permuted_of(shard):
+        moved = jnp.stack([permute_columns(shard[t], open_order[t]) for t in range(slice_count)])
+        return jnp.transpose(moved, (0, 2, 1, 3))
+
+    permuted = permuted_of(branch_tensor)
+    other = permuted_of(other_raw)
     low = lax.axis_index("zh") == 0
     pair = jnp.where(low, jnp.stack([permuted, other], axis=2), jnp.stack([other, permuted], axis=2))
     plane = lax.axis_size("x") * lax.axis_size("y")

time: 124 us -> 121 us (0.976); the launches traced: 122 us -> 121 us
  waiting for transfers between devices: 24.6 us -> 22.7 us
    ppermute x1, waiting for transfers between devices: 1.84 us -> 0.01 us  [body(): other_raw = lax.ppermute(branch_tensor, 'zh', shift_pairs(2, 1))]
    ppermute x2, waiting for transfers between devices: 1.62 us -> 0.01 us  [body(): mine = mine + lax.ppermute(theirs, 'core', shift_pairs(2, 1))]
    ppermute x6, waiting for transfers between devices: 10.4 us -> 12 us  [halving_scatter(): shaped = keep + lax.ppermute(send, axis, pairs)]
    unnamed x6 -> x5, local copies, waits for them, and re-layouts: 3.31 us -> 3.28 us
  transfers between devices with their start and end apart: 11 -> 11, of which waited for: 6 -> 4; matrix products, arithmetic and copies ran while one was open for 9% -> 12% of each run, Pallas kernels for 8% -> 8%
where the time goes in v17:
time: 121 us
  starting transfers between devices  70.9 us (59%)
  waiting for transfers between devices  22.7 us (19%)
  local copies, waits for them, and re-layouts  14 us (12%)
  Pallas kernels  9.36 us (8%)
  other arithmetic  2 us (2%)
    ppermute x6, starting transfers between devices, halving_scatter(): shaped = keep + lax.ppermute(send, axis, pairs)  31.7 us
    ppermute x1, starting transfers between devices, body(): other_raw = lax.ppermute(branch_tensor, 'zh', shift_pairs(2, 1))  16.3 us
    all_to_all x2, starting transfers between devices, body(): gathered = lax.all_to_all(part, ('x', 'y'), 2, 4, tiled=True)  13.9 us
    ppermute x6, waiting for transfers between devices, halving_scatter(): shaped = keep + lax.ppermute(send, axis, pairs)  12 us
    all_to_all x2, waiting for transfers between devices, body(): gathered = lax.all_to_all(part, ('x', 'y'), 2, 4, tiled=True)  10.7 us
    pallas_call x2, Pallas kernels, contract(): pl.pallas_call(contract_kernel, out_shape=jax.ShapeDtypeStruct((2, rows,...  9.36 us
    ppermute x2, starting transfers between devices, body(): mine = mine + lax.ppermute(theirs, 'core', shift_pairs(2, 1))  9.05 us
    squeeze x2, local copies, waits for them, and re-layouts, body(): theirs = lax.dynamic_index_in_dim(shaped, 1 - core, 2, keepdims=False)  3.88 us
  transfers between devices with their start and end apart: 11, of which 4 were waited for; matrix products, arithmetic and copies ran while one was open for 12% of the time, Pallas kernels for 8%

profile of v17, /device:TPU:1, one launch (start us, length us, event | category | flops | bytes accessed | tf_op | source)
XLA Modules:
  0.0 120.5 jit_solution(4418400671714283530)
XLA Ops:
  0.0 16.3 %collective-permute-start = (bf16[2,16,2,512]{3,2,1,0:T(2,128)(2,1)}, bf16[2,16,2,512]{3,2,1,0:T(2,128)(2,1)S(1)}, u32[]{:S(2)}, u32[]{:S(2)}) collective-permute-start(bf16[2,16,2,512]{3,2,1,0:T(2,128)(2,1)} %param.5), channel_id=1, source_target_pairs={{0,16},{16,0},{1,17},{17,1},{2,18},{18,2},{3,19},{19,3},{4,20},{20... | collective-permute-start | bytes 196616 | tf_op jit(solution)/shard_map/ppermute | solution.py:98
  16.3 0.9 fusion.9
  17.1 0.8 fusion.11
  17.9 0.3 fusion
  18.2 0.3 fusion.1
  18.6 0.0 collective-permute-done
  18.7 0.3 fusion.2
  19.0 0.3 fusion.3
  19.3 0.2 maximum_bitcast_fusion.1
  19.5 0.2 broadcast_select_fusion
  19.7 0.1 fusion.8
  19.9 1.1 broadcast_in_dim.8
  21.0 6.8 %all-to-all-start = ((bf16[2,2,16,2,16,256]{5,4,3,1,0,2:T(8,128)(2,1)}), bf16[2,2,16,2,16,256]{5,4,3,1,0,2:T(8,128)(2,1)S(1)}, u32[]{:S(2)}, u32[]{:S(2)}) async-start(bf16[2,2,16,2,16,256]{5,4,3,1,0,2:T(8,128)(2,1)} %broadcast_in_dim.8), calls=%async_computation | async-start | bytes 2097152 | tf_op jit(solution)/shard_map/all_to_all | solution.py:123
  27.7 1.1 broadcast_in_dim.9
  28.9 10.7 %all-to-all-done = bf16[2,2,16,2,16,256]{5,4,3,1,0,2:T(8,128)(2,1)S(1)} async-done(((bf16[2,2,16,2,16,256]{5,4,3,1,0,2:T(8,128)(2,1)}), bf16[2,2,16,2,16,256]{5,4,3,1,0,2:T(8,128)(2,1)S(1)}, u32[]{:S(2)}, u32[]{:S(2)}) %all-to-all-start) | async-done | bytes 1048608 | tf_op jit(solution)/shard_map/all_to_all | solution.py:123
  39.5 7.1 %all-to-all-start.1 = ((bf16[2,2,16,2,16,256]{5,4,3,1,0,2:T(8,128)(2,1)}), bf16[2,2,16,2,16,256]{5,4,3,1,0,2:T(8,128)(2,1)S(1)}, u32[]{:S(2)}, u32[]{:S(2)}) async-start(bf16[2,2,16,2,16,256]{5,4,3,1,0,2:T(8,128)(2,1)} %broadcast_in_dim.9), calls=%async_computation.1 | async-start | bytes 2097152 | tf_op jit(solution)/shard_map/all_to_all | solution.py:123
  46.7 3.3 %copy.26 = bf16[2,512,2,512]{3,1,2,0:T(8,128)(2,1)} copy(bf16[2,512,2,512]{3,2,1,0:T(2,128)(2,1)} %param.4) | data formatting | bytes 4194304 | tf_op args[0]
  50.0 1.1 copy.14
  51.0 4.6 %shard_map.46 = f32[2,512,256]{2,1,0:T(8,128)} custom-call(bf16[2,2,512,512]{3,2,1,0:T(8,128)(2,1)} %bitcast.75, bf16[2,2,512,256]{3,2,1,0:T(8,128)(2,1)} %bitcast.84, bf16[2,512,2,512]{3,2,1,0:T(2,128)(2,1)} %o_ref.3), custom_call_target="tpu_custom_call" | custom-call | flops 1073741824 | bytes 5242880 | tf_op jit(solution)/shard_map/pallas_call | solution.py:68
  55.7 1.9 %dynamic-slice_bitcast_fusion.1 = f32[2,8,32,256]{3,2,1,0:T(8,128)} fusion(f32[2,8,2,32,256]{4,3,2,1,0:T(8,128)} %bitcast.81, s32[]{:T(128)S(6)} %select_n.51), kind=kLoop, calls=%fused_computation.14 | loop fusion | bytes 1048580 | tf_op jit(solution)/shard_map/jit(dynamic_index_in_dim)/squeeze | solution.py:129
  57.6 4.7 %collective-permute-start.1 = (f32[2,8,32,256]{3,2,1,0:T(8,128)}, f32[2,8,32,256]{3,2,1,0:T(8,128)S(1)}, u32[]{:S(2)}, u32[]{:S(2)}) collective-permute-start(f32[2,8,32,256]{3,2,1,0:T(8,128)} %dynamic-slice_bitcast_fusion.1), channel_id=1, source_target_pairs={{0,32},{32,0},{1,33},{33,1},{2,34},{34,2},{3,35},{35,3},{4,36},{36... | collective-permute-start | bytes 1572872 | tf_op jit(solution)/shard_map/ppermute | solution.py:130
  62.3 0.0 all-to-all-done.1
  62.3 1.1 copy.18
  63.4 4.7 %shard_map.47 = f32[2,512,256]{2,1,0:T(8,128)} custom-call(bf16[2,2,512,512]{3,2,1,0:T(8,128)(2,1)} %bitcast.76, bf16[2,2,512,256]{3,2,1,0:T(8,128)(2,1)} %bitcast.83, bf16[2,512,2,512]{3,2,1,0:T(2,128)(2,1)} %o_ref.3), custom_call_target="tpu_custom_call" | custom-call | flops 1073741824 | bytes 5242880 | tf_op jit(solution)/shard_map/pallas_call | solution.py:68
  68.1 2.0 %dynamic-slice_bitcast_fusion = f32[2,8,32,256]{3,2,1,0:T(8,128)} fusion(f32[2,8,2,32,256]{4,3,2,1,0:T(8,128)} %bitcast.79, s32[]{:T(128)S(6)} %select_n.51), kind=kLoop, calls=%fused_computation.13 | loop fusion | bytes 1048580 | tf_op jit(solution)/shard_map/jit(dynamic_index_in_dim)/squeeze | solution.py:129
  70.1 4.3 %collective-permute-start.5 = (f32[2,8,32,256]{3,2,1,0:T(8,128)}, f32[2,8,32,256]{3,2,1,0:T(8,128)S(1)}, u32[]{:S(2)}, u32[]{:S(2)}) collective-permute-start(f32[2,8,32,256]{3,2,1,0:T(8,128)} %dynamic-slice_bitcast_fusion), channel_id=1, source_target_pairs={{0,32},{32,0},{1,33},{33,1},{2,34},{34,2},{3,35},{35,3},{4,36},{36... | collective-permute-start | bytes 1572872 | tf_op jit(solution)/shard_map/ppermute | solution.py:130
  74.4 0.0 collective-permute-done.1
  74.5 0.1 bitcast_add_fusion.1
  74.5 0.1 constant_dynamic-slice_fusion.3
  74.6 0.2 copy.28
  74.8 3.2 %collective-permute-start.2 = (f32[2,2,2,32,256]{4,0,3,1,2:T(2,128)S(1)}, f32[2,2,2,32,256]{4,0,3,1,2:T(2,128)S(1)}, u32[]{:S(2)}, u32[]{:S(2)}) collective-permute-start(f32[2,2,2,32,256]{4,0,3,1,2:T(2,128)S(1)} %bitcast.87), channel_id=1, source_target_pairs={{0,64},{64,0},{128,192},{192,128},{256,320},{320,256},{384,448},{4... | collective-permute-start | bytes 786440 | tf_op jit(solution)/shard_map/ppermute | solution.py:92
  78.0 0.0 collective-permute-done.5
  78.0 0.1 bitcast_add_fusion
  78.2 0.2 copy.27
  78.4 2.1 %collective-permute-start.6 = (f32[2,2,2,32,256]{4,0,3,1,2:T(2,128)S(1)}, f32[2,2,2,32,256]{4,0,3,1,2:T(2,128)S(1)}, u32[]{:S(2)}, u32[]{:S(2)}) collective-permute-start(f32[2,2,2,32,256]{4,0,3,1,2:T(2,128)S(1)} %bitcast.88), channel_id=1, source_target_pairs={{0,64},{64,0},{128,192},{192,128},{256,320},{320,256},{384,448},{4... | collective-permute-start | bytes 786440 | tf_op jit(solution)/shard_map/ppermute | solution.py:92
  80.5 4.2 %collective-permute-done.2 = f32[2,2,2,32,256]{4,0,3,1,2:T(2,128)S(1)} collective-permute-done((f32[2,2,2,32,256]{4,0,3,1,2:T(2,128)S(1)}, f32[2,2,2,32,256]{4,0,3,1,2:T(2,128)S(1)}, u32[]{:S(2)}, u32[]{:S(2)}) %collective-permute-start.2) | collective-permute-done | bytes 262176 | tf_op jit(solution)/shard_map/ppermute | solution.py:92
  84.6 0.3 bitcast_add_fusion.3
  84.9 3.5 %collective-permute-start.3 = (f32[2,2,32,256]{3,0,2,1:T(2,128)S(1)}, f32[2,2,32,256]{3,0,2,1:T(2,128)S(1)}, u32[]{:S(2)}, u32[]{:S(2)}) collective-permute-start(f32[2,2,32,256]{3,0,2,1:T(2,128)S(1)} %dynamic-slice_bitcast_fusion.3), channel_id=1, source_target_pairs={{0,128},{64,192},{128,0},{192,64},{256,384},{320,448},{384,256},{4... | collective-permute-start | bytes 393224 | tf_op jit(solution)/shard_map/ppermute | solution.py:92
  88.5 1.8 %collective-permute-done.6 = f32[2,2,2,32,256]{4,0,3,1,2:T(2,128)S(1)} collective-permute-done((f32[2,2,2,32,256]{4,0,3,1,2:T(2,128)S(1)}, f32[2,2,2,32,256]{4,0,3,1,2:T(2,128)S(1)}, u32[]{:S(2)}, u32[]{:S(2)}) %collective-permute-start.6) | collective-permute-done | bytes 262176 | tf_op jit(solution)/shard_map/ppermute | solution.py:92
  90.3 0.3 bitcast_add_fusion.2
  90.6 3.5 %collective-permute-start.7 = (f32[2,2,32,256]{3,0,2,1:T(2,128)S(1)}, f32[2,2,32,256]{3,0,2,1:T(2,128)S(1)}, u32[]{:S(2)}, u32[]{:S(2)}) collective-permute-start(f32[2,2,32,256]{3,0,2,1:T(2,128)S(1)} %dynamic-slice_bitcast_fusion.2), channel_id=1, source_target_pairs={{0,128},{64,192},{128,0},{192,64},{256,384},{320,448},{384,256},{4... | collective-permute-start | bytes 393224 | tf_op jit(solution)/shard_map/ppermute | solution.py:92
  94.1 0.0 collective-permute-done.3
  94.1 0.1 bitcast_add_fusion.5
  94.2 11.2 %collective-permute-start.4 = (f32[2,32,256]{2,0,1:T(2,128)S(1)}, f32[2,32,256]{2,0,1:T(2,128)S(1)}, u32[]{:S(2)}, u32[]{:S(2)}) collective-permute-start(f32[2,32,256]{2,0,1:T(2,128)S(1)} %dynamic-slice_bitcast_fusion.5), channel_id=1, source_target_pairs={{0,256},{64,320},{128,384},{192,448},{256,0},{320,64},{384,128},{4... | collective-permute-start | bytes 196616 | tf_op jit(solution)/shard_map/ppermute | solution.py:92
  105.4 0.1 bitcast_add_fusion.4
  105.5 8.2 %collective-permute-start.8 = (f32[2,32,256]{2,0,1:T(2,128)S(1)}, f32[2,32,256]{2,0,1:T(2,128)S(1)}, u32[]{:S(2)}, u32[]{:S(2)}) collective-permute-start(f32[2,32,256]{2,0,1:T(2,128)S(1)} %dynamic-slice_bitcast_fusion.4), channel_id=1, source_target_pairs={{0,256},{64,320},{128,384},{192,448},{256,0},{320,64},{384,128},{4... | collective-permute-start | bytes 196616 | tf_op jit(solution)/shard_map/ppermute | solution.py:92
  113.8 6.0 %collective-permute-done.8 = f32[2,32,256]{2,0,1:T(2,128)S(1)} collective-permute-done((f32[2,32,256]{2,0,1:T(2,128)S(1)}, f32[2,32,256]{2,0,1:T(2,128)S(1)}, u32[]{:S(2)}, u32[]{:S(2)}) %collective-permute-start.8) | collective-permute-done | bytes 65568 | tf_op jit(solution)/shard_map/ppermute | solution.py:92
  119.8 0.7 maximum_bitcast_fusion
  (24 shorter events, 0.4 us)
Async XLA Ops:
  0.0 18.6 %collective-permute-start = (bf16[2,16,2,512]{3,2,1,0:T(2,128)(2,1)}, bf16[2,16,2,512]{3,2,1,0:T(2,128)(2,1)S(1)}, u32[]{:S(2)}, u32[]{:S(2)}) collective-permute-start(bf16[2,16,2,512]{3,2,1,0:T(2,128)(2,1)} %param.5), channel_id=1, source_target_pairs={{0,16},{16,0},{1,17},{17,1},{2,18},{18,2},{3,19},{19,3},{4,20},{20... | collective-permute-start | bytes 196616 | tf_op jit(solution)/shard_map/ppermute | solution.py:98
  21.0 18.6 %all-to-all-start = ((bf16[2,2,16,2,16,256]{5,4,3,1,0,2:T(8,128)(2,1)}), bf16[2,2,16,2,16,256]{5,4,3,1,0,2:T(8,128)(2,1)S(1)}, u32[]{:S(2)}, u32[]{:S(2)}) async-start(bf16[2,2,16,2,16,256]{5,4,3,1,0,2:T(8,128)(2,1)} %broadcast_in_dim.8), calls=%async_computation | async-start | bytes 2097152 | tf_op jit(solution)/shard_map/all_to_all | solution.py:123
  39.5 22.8 %all-to-all-start.1 = ((bf16[2,2,16,2,16,256]{5,4,3,1,0,2:T(8,128)(2,1)}), bf16[2,2,16,2,16,256]{5,4,3,1,0,2:T(8,128)(2,1)S(1)}, u32[]{:S(2)}, u32[]{:S(2)}) async-start(bf16[2,2,16,2,16,256]{5,4,3,1,0,2:T(8,128)(2,1)} %broadcast_in_dim.9), calls=%async_computation.1 | async-start | bytes 2097152 | tf_op jit(solution)/shard_map/all_to_all | solution.py:123
  57.6 16.9 %collective-permute-start.1 = (f32[2,8,32,256]{3,2,1,0:T(8,128)}, f32[2,8,32,256]{3,2,1,0:T(8,128)S(1)}, u32[]{:S(2)}, u32[]{:S(2)}) collective-permute-start(f32[2,8,32,256]{3,2,1,0:T(8,128)} %dynamic-slice_bitcast_fusion.1), channel_id=1, source_target_pairs={{0,32},{32,0},{1,33},{33,1},{2,34},{34,2},{3,35},{35,3},{4,36},{36... | collective-permute-start | bytes 1572872 | tf_op jit(solution)/shard_map/ppermute | solution.py:130
  63.4 11.1 %copy-start.1 = (f32[2,512,256]{2,1,0:T(8,128)S(1)}, f32[2,512,256]{2,1,0:T(8,128)}, u32[]{:S(2)}) copy-start(f32[2,512,256]{2,1,0:T(8,128)} %shard_map.46) | copy-start | bytes 3145732
  68.1 9.9 %copy-start = (f32[2,512,256]{2,1,0:T(8,128)S(1)}, f32[2,512,256]{2,1,0:T(8,128)}, u32[]{:S(2)}) copy-start(f32[2,512,256]{2,1,0:T(8,128)} %shard_map.47) | copy-start | bytes 3145732
  70.1 7.9 %collective-permute-start.5 = (f32[2,8,32,256]{3,2,1,0:T(8,128)}, f32[2,8,32,256]{3,2,1,0:T(8,128)S(1)}, u32[]{:S(2)}, u32[]{:S(2)}) collective-permute-start(f32[2,8,32,256]{3,2,1,0:T(8,128)} %dynamic-slice_bitcast_fusion), channel_id=1, source_target_pairs={{0,32},{32,0},{1,33},{33,1},{2,34},{34,2},{3,35},{35,3},{4,36},{36... | collective-permute-start | bytes 1572872 | tf_op jit(solution)/shard_map/ppermute | solution.py:130
  74.8 9.8 %collective-permute-start.2 = (f32[2,2,2,32,256]{4,0,3,1,2:T(2,128)S(1)}, f32[2,2,2,32,256]{4,0,3,1,2:T(2,128)S(1)}, u32[]{:S(2)}, u32[]{:S(2)}) collective-permute-start(f32[2,2,2,32,256]{4,0,3,1,2:T(2,128)S(1)} %bitcast.87), channel_id=1, source_target_pairs={{0,64},{64,0},{128,192},{192,128},{256,320},{320,256},{384,448},{4... | collective-permute-start | bytes 786440 | tf_op jit(solution)/shard_map/ppermute | solution.py:92
  78.4 11.9 %collective-permute-start.6 = (f32[2,2,2,32,256]{4,0,3,1,2:T(2,128)S(1)}, f32[2,2,2,32,256]{4,0,3,1,2:T(2,128)S(1)}, u32[]{:S(2)}, u32[]{:S(2)}) collective-permute-start(f32[2,2,2,32,256]{4,0,3,1,2:T(2,128)S(1)} %bitcast.88), channel_id=1, source_target_pairs={{0,64},{64,0},{128,192},{192,128},{256,320},{320,256},{384,448},{4... | collective-permute-start | bytes 786440 | tf_op jit(solution)/shard_map/ppermute | solution.py:92
  84.9 9.1 %collective-permute-start.3 = (f32[2,2,32,256]{3,0,2,1:T(2,128)S(1)}, f32[2,2,32,256]{3,0,2,1:T(2,128)S(1)}, u32[]{:S(2)}, u32[]{:S(2)}) collective-permute-start(f32[2,2,32,256]{3,0,2,1:T(2,128)S(1)} %dynamic-slice_bitcast_fusion.3), channel_id=1, source_target_pairs={{0,128},{64,192},{128,0},{192,64},{256,384},{320,448},{384,256},{4... | collective-permute-start | bytes 393224 | tf_op jit(solution)/shard_map/ppermute | solution.py:92
  90.6 14.9 %collective-permute-start.7 = (f32[2,2,32,256]{3,0,2,1:T(2,128)S(1)}, f32[2,2,32,256]{3,0,2,1:T(2,128)S(1)}, u32[]{:S(2)}, u32[]{:S(2)}) collective-permute-start(f32[2,2,32,256]{3,0,2,1:T(2,128)S(1)} %dynamic-slice_bitcast_fusion.2), channel_id=1, source_target_pairs={{0,128},{64,192},{128,0},{192,64},{256,384},{320,448},{384,256},{4... | collective-permute-start | bytes 393224 | tf_op jit(solution)/shard_map/ppermute | solution.py:92
  94.2 19.5 %collective-permute-start.4 = (f32[2,32,256]{2,0,1:T(2,128)S(1)}, f32[2,32,256]{2,0,1:T(2,128)S(1)}, u32[]{:S(2)}, u32[]{:S(2)}) collective-permute-start(f32[2,32,256]{2,0,1:T(2,128)S(1)} %dynamic-slice_bitcast_fusion.5), channel_id=1, source_target_pairs={{0,256},{64,320},{128,384},{192,448},{256,0},{320,64},{384,128},{4... | collective-permute-start | bytes 196616 | tf_op jit(solution)/shard_map/ppermute | solution.py:92
  105.5 14.3 %collective-permute-start.8 = (f32[2,32,256]{2,0,1:T(2,128)S(1)}, f32[2,32,256]{2,0,1:T(2,128)S(1)}, u32[]{:S(2)}, u32[]{:S(2)}) collective-permute-start(f32[2,32,256]{2,0,1:T(2,128)S(1)} %dynamic-slice_bitcast_fusion.4), channel_id=1, source_target_pairs={{0,256},{64,320},{128,384},{192,448},{256,0},{320,64},{384,128},{4... | collective-permute-start | bytes 196616 | tf_op jit(solution)/shard_map/ppermute | solution.py:92

commit v18 on v17

--- a/solution.py
+++ b/solution.py
@@ -7,7 +7,7 @@
 
 CUTS = ("zl", "core")
 STEM = ("zh", "x", "y")
-ROW_TILE = 256
+ROW_TILE = 128
 
 
 def split_mesh(mesh):

time: 121 us -> 122 us (level)
  no operation moved by 1% of the time
where the time goes in v18:
time: 122 us; the launch traced here: 121 us
  starting transfers between devices  70.4 us (58%)
  waiting for transfers between devices  22.7 us (19%)
  local copies, waits for them, and re-layouts  14 us (11%)
  Pallas kernels  10.3 us (8%)
  other arithmetic  2 us (2%)
    ppermute x6, starting transfers between devices, halving_scatter(): shaped = keep + lax.ppermute(send, axis, pairs)  31.7 us
    ppermute x1, starting transfers between devices, body(): other_raw = lax.ppermute(branch_tensor, 'zh', shift_pairs(2, 1))  16.3 us
    all_to_all x2, starting transfers between devices, body(): gathered = lax.all_to_all(part, ('x', 'y'), 2, 4, tiled=True)  13.9 us
    ppermute x6, waiting for transfers between devices, halving_scatter(): shaped = keep + lax.ppermute(send, axis, pairs)  12 us
    all_to_all x2, waiting for transfers between devices, body(): gathered = lax.all_to_all(part, ('x', 'y'), 2, 4, tiled=True)  10.7 us
    pallas_call x2, Pallas kernels, contract(): pl.pallas_call(contract_kernel, out_shape=jax.ShapeDtypeStruct((2, rows,...  10.3 us
    ppermute x2, starting transfers between devices, body(): mine = mine + lax.ppermute(theirs, 'core', shift_pairs(2, 1))  8.6 us
    squeeze x2, local copies, waits for them, and re-layouts, body(): theirs = lax.dynamic_index_in_dim(shaped, 1 - core, 2, keepdims=False)  3.88 us
  transfers between devices with their start and end apart: 11, of which 4 were waited for; matrix products, arithmetic and copies ran while one was open for 12% of the time, Pallas kernels for 8%

profile of v18, /device:TPU:1, one launch (start us, length us, event | category | flops | bytes accessed | tf_op | source)
XLA Modules:
  0.0 121.0 jit_solution(2832336227919980169)
XLA Ops:
  0.0 16.3 %collective-permute-start = (bf16[2,16,2,512]{3,2,1,0:T(2,128)(2,1)}, bf16[2,16,2,512]{3,2,1,0:T(2,128)(2,1)S(1)}, u32[]{:S(2)}, u32[]{:S(2)}) collective-permute-start(bf16[2,16,2,512]{3,2,1,0:T(2,128)(2,1)} %param.5), channel_id=1, source_target_pairs={{0,16},{16,0},{1,17},{17,1},{2,18},{18,2},{3,19},{19,3},{4,20},{20... | collective-permute-start | bytes 196616 | tf_op jit(solution)/shard_map/ppermute | solution.py:98
  16.3 0.9 fusion.9
  17.1 0.8 fusion.11
  17.9 0.3 fusion
  18.2 0.3 fusion.1
  18.6 0.0 collective-permute-done
  18.7 0.3 fusion.2
  19.0 0.3 fusion.3
  19.3 0.2 maximum_bitcast_fusion.1
  19.5 0.2 broadcast_select_fusion
  19.7 0.1 fusion.8
  19.9 1.1 broadcast_in_dim.8
  21.0 6.8 %all-to-all-start = ((bf16[2,2,16,2,16,256]{5,4,3,1,0,2:T(8,128)(2,1)}), bf16[2,2,16,2,16,256]{5,4,3,1,0,2:T(8,128)(2,1)S(1)}, u32[]{:S(2)}, u32[]{:S(2)}) async-start(bf16[2,2,16,2,16,256]{5,4,3,1,0,2:T(8,128)(2,1)} %broadcast_in_dim.8), calls=%async_computation | async-start | bytes 2097152 | tf_op jit(solution)/shard_map/all_to_all | solution.py:123
  27.7 1.1 broadcast_in_dim.9
  28.9 10.7 %all-to-all-done = bf16[2,2,16,2,16,256]{5,4,3,1,0,2:T(8,128)(2,1)S(1)} async-done(((bf16[2,2,16,2,16,256]{5,4,3,1,0,2:T(8,128)(2,1)}), bf16[2,2,16,2,16,256]{5,4,3,1,0,2:T(8,128)(2,1)S(1)}, u32[]{:S(2)}, u32[]{:S(2)}) %all-to-all-start) | async-done | bytes 1048608 | tf_op jit(solution)/shard_map/all_to_all | solution.py:123
  39.5 7.1 %all-to-all-start.1 = ((bf16[2,2,16,2,16,256]{5,4,3,1,0,2:T(8,128)(2,1)}), bf16[2,2,16,2,16,256]{5,4,3,1,0,2:T(8,128)(2,1)S(1)}, u32[]{:S(2)}, u32[]{:S(2)}) async-start(bf16[2,2,16,2,16,256]{5,4,3,1,0,2:T(8,128)(2,1)} %broadcast_in_dim.9), calls=%async_computation.1 | async-start | bytes 2097152 | tf_op jit(solution)/shard_map/all_to_all | solution.py:123
  46.7 3.3 %copy.26 = bf16[2,512,2,512]{3,1,2,0:T(8,128)(2,1)} copy(bf16[2,512,2,512]{3,2,1,0:T(2,128)(2,1)} %param.4) | data formatting | bytes 4194304 | tf_op args[0]
  50.0 1.1 copy.14
  51.0 5.1 %shard_map.46 = f32[2,512,256]{2,1,0:T(8,128)} custom-call(bf16[2,2,512,512]{3,2,1,0:T(8,128)(2,1)} %bitcast.75, bf16[2,2,512,256]{3,2,1,0:T(8,128)(2,1)} %bitcast.84, bf16[2,512,2,512]{3,2,1,0:T(2,128)(2,1)} %o_ref.3), custom_call_target="tpu_custom_call" | custom-call | flops 1073741824 | bytes 5242880 | tf_op jit(solution)/shard_map/pallas_call | solution.py:68
  56.1 1.9 %dynamic-slice_bitcast_fusion.1 = f32[2,8,32,256]{3,2,1,0:T(8,128)} fusion(f32[2,8,2,32,256]{4,3,2,1,0:T(8,128)} %bitcast.81, s32[]{:T(128)S(6)} %select_n.51), kind=kLoop, calls=%fused_computation.14 | loop fusion | bytes 1048580 | tf_op jit(solution)/shard_map/jit(dynamic_index_in_dim)/squeeze | solution.py:129
  58.0 4.7 %collective-permute-start.1 = (f32[2,8,32,256]{3,2,1,0:T(8,128)}, f32[2,8,32,256]{3,2,1,0:T(8,128)S(1)}, u32[]{:S(2)}, u32[]{:S(2)}) collective-permute-start(f32[2,8,32,256]{3,2,1,0:T(8,128)} %dynamic-slice_bitcast_fusion.1), channel_id=1, source_target_pairs={{0,32},{32,0},{1,33},{33,1},{2,34},{34,2},{3,35},{35,3},{4,36},{36... | collective-permute-start | bytes 1572872 | tf_op jit(solution)/shard_map/ppermute | solution.py:130
  62.8 0.0 all-to-all-done.1
  62.8 1.1 copy.18
  63.8 5.2 %shard_map.47 = f32[2,512,256]{2,1,0:T(8,128)} custom-call(bf16[2,2,512,512]{3,2,1,0:T(8,128)(2,1)} %bitcast.76, bf16[2,2,512,256]{3,2,1,0:T(8,128)(2,1)} %bitcast.83, bf16[2,512,2,512]{3,2,1,0:T(2,128)(2,1)} %o_ref.3), custom_call_target="tpu_custom_call" | custom-call | flops 1073741824 | bytes 5242880 | tf_op jit(solution)/shard_map/pallas_call | solution.py:68
  69.0 2.0 %dynamic-slice_bitcast_fusion = f32[2,8,32,256]{3,2,1,0:T(8,128)} fusion(f32[2,8,2,32,256]{4,3,2,1,0:T(8,128)} %bitcast.79, s32[]{:T(128)S(6)} %select_n.51), kind=kLoop, calls=%fused_computation.13 | loop fusion | bytes 1048580 | tf_op jit(solution)/shard_map/jit(dynamic_index_in_dim)/squeeze | solution.py:129
  71.0 3.9 %collective-permute-start.5 = (f32[2,8,32,256]{3,2,1,0:T(8,128)}, f32[2,8,32,256]{3,2,1,0:T(8,128)S(1)}, u32[]{:S(2)}, u32[]{:S(2)}) collective-permute-start(f32[2,8,32,256]{3,2,1,0:T(8,128)} %dynamic-slice_bitcast_fusion), channel_id=1, source_target_pairs={{0,32},{32,0},{1,33},{33,1},{2,34},{34,2},{3,35},{35,3},{4,36},{36... | collective-permute-start | bytes 1572872 | tf_op jit(solution)/shard_map/ppermute | solution.py:130
  74.9 0.0 collective-permute-done.1
  74.9 0.1 bitcast_add_fusion.1
  75.0 0.1 constant_dynamic-slice_fusion.3
  75.1 0.2 copy.28
  75.3 3.2 %collective-permute-start.2 = (f32[2,2,2,32,256]{4,0,3,1,2:T(2,128)S(1)}, f32[2,2,2,32,256]{4,0,3,1,2:T(2,128)S(1)}, u32[]{:S(2)}, u32[]{:S(2)}) collective-permute-start(f32[2,2,2,32,256]{4,0,3,1,2:T(2,128)S(1)} %bitcast.87), channel_id=1, source_target_pairs={{0,64},{64,0},{128,192},{192,128},{256,320},{320,256},{384,448},{4... | collective-permute-start | bytes 786440 | tf_op jit(solution)/shard_map/ppermute | solution.py:92
  78.5 0.0 collective-permute-done.5
  78.5 0.1 bitcast_add_fusion
  78.6 0.2 copy.27
  78.8 2.1 %collective-permute-start.6 = (f32[2,2,2,32,256]{4,0,3,1,2:T(2,128)S(1)}, f32[2,2,2,32,256]{4,0,3,1,2:T(2,128)S(1)}, u32[]{:S(2)}, u32[]{:S(2)}) collective-permute-start(f32[2,2,2,32,256]{4,0,3,1,2:T(2,128)S(1)} %bitcast.88), channel_id=1, source_target_pairs={{0,64},{64,0},{128,192},{192,128},{256,320},{320,256},{384,448},{4... | collective-permute-start | bytes 786440 | tf_op jit(solution)/shard_map/ppermute | solution.py:92
  80.9 4.2 %collective-permute-done.2 = f32[2,2,2,32,256]{4,0,3,1,2:T(2,128)S(1)} collective-permute-done((f32[2,2,2,32,256]{4,0,3,1,2:T(2,128)S(1)}, f32[2,2,2,32,256]{4,0,3,1,2:T(2,128)S(1)}, u32[]{:S(2)}, u32[]{:S(2)}) %collective-permute-start.2) | collective-permute-done | bytes 262176 | tf_op jit(solution)/shard_map/ppermute | solution.py:92
  85.1 0.3 bitcast_add_fusion.3
  85.4 3.5 %collective-permute-start.3 = (f32[2,2,32,256]{3,0,2,1:T(2,128)S(1)}, f32[2,2,32,256]{3,0,2,1:T(2,128)S(1)}, u32[]{:S(2)}, u32[]{:S(2)}) collective-permute-start(f32[2,2,32,256]{3,0,2,1:T(2,128)S(1)} %dynamic-slice_bitcast_fusion.3), channel_id=1, source_target_pairs={{0,128},{64,192},{128,0},{192,64},{256,384},{320,448},{384,256},{4... | collective-permute-start | bytes 393224 | tf_op jit(solution)/shard_map/ppermute | solution.py:92
  88.9 1.8 %collective-permute-done.6 = f32[2,2,2,32,256]{4,0,3,1,2:T(2,128)S(1)} collective-permute-done((f32[2,2,2,32,256]{4,0,3,1,2:T(2,128)S(1)}, f32[2,2,2,32,256]{4,0,3,1,2:T(2,128)S(1)}, u32[]{:S(2)}, u32[]{:S(2)}) %collective-permute-start.6) | collective-permute-done | bytes 262176 | tf_op jit(solution)/shard_map/ppermute | solution.py:92
  90.7 0.3 bitcast_add_fusion.2
  91.0 3.5 %collective-permute-start.7 = (f32[2,2,32,256]{3,0,2,1:T(2,128)S(1)}, f32[2,2,32,256]{3,0,2,1:T(2,128)S(1)}, u32[]{:S(2)}, u32[]{:S(2)}) collective-permute-start(f32[2,2,32,256]{3,0,2,1:T(2,128)S(1)} %dynamic-slice_bitcast_fusion.2), channel_id=1, source_target_pairs={{0,128},{64,192},{128,0},{192,64},{256,384},{320,448},{384,256},{4... | collective-permute-start | bytes 393224 | tf_op jit(solution)/shard_map/ppermute | solution.py:92
  94.5 0.1 bitcast_add_fusion.5
  94.6 11.2 %collective-permute-start.4 = (f32[2,32,256]{2,0,1:T(2,128)S(1)}, f32[2,32,256]{2,0,1:T(2,128)S(1)}, u32[]{:S(2)}, u32[]{:S(2)}) collective-permute-start(f32[2,32,256]{2,0,1:T(2,128)S(1)} %dynamic-slice_bitcast_fusion.5), channel_id=1, source_target_pairs={{0,256},{64,320},{128,384},{192,448},{256,0},{320,64},{384,128},{4... | collective-permute-start | bytes 196616 | tf_op jit(solution)/shard_map/ppermute | solution.py:92
  105.9 0.0 collective-permute-done.7
  105.9 0.1 bitcast_add_fusion.4
  106.0 8.2 %collective-permute-start.8 = (f32[2,32,256]{2,0,1:T(2,128)S(1)}, f32[2,32,256]{2,0,1:T(2,128)S(1)}, u32[]{:S(2)}, u32[]{:S(2)}) collective-permute-start(f32[2,32,256]{2,0,1:T(2,128)S(1)} %dynamic-slice_bitcast_fusion.4), channel_id=1, source_target_pairs={{0,256},{64,320},{128,384},{192,448},{256,0},{320,64},{384,128},{4... | collective-permute-start | bytes 196616 | tf_op jit(solution)/shard_map/ppermute | solution.py:92
  114.2 6.0 %collective-permute-done.8 = f32[2,32,256]{2,0,1:T(2,128)S(1)} collective-permute-done((f32[2,32,256]{2,0,1:T(2,128)S(1)}, f32[2,32,256]{2,0,1:T(2,128)S(1)}, u32[]{:S(2)}, u32[]{:S(2)}) %collective-permute-start.8) | collective-permute-done | bytes 65568 | tf_op jit(solution)/shard_map/ppermute | solution.py:92
  120.3 0.7 maximum_bitcast_fusion
  (24 shorter events, 0.4 us)
Async XLA Ops:
  0.0 18.6 %collective-permute-start = (bf16[2,16,2,512]{3,2,1,0:T(2,128)(2,1)}, bf16[2,16,2,512]{3,2,1,0:T(2,128)(2,1)S(1)}, u32[]{:S(2)}, u32[]{:S(2)}) collective-permute-start(bf16[2,16,2,512]{3,2,1,0:T(2,128)(2,1)} %param.5), channel_id=1, source_target_pairs={{0,16},{16,0},{1,17},{17,1},{2,18},{18,2},{3,19},{19,3},{4,20},{20... | collective-permute-start | bytes 196616 | tf_op jit(solution)/shard_map/ppermute | solution.py:98
  21.0 18.6 %all-to-all-start = ((bf16[2,2,16,2,16,256]{5,4,3,1,0,2:T(8,128)(2,1)}), bf16[2,2,16,2,16,256]{5,4,3,1,0,2:T(8,128)(2,1)S(1)}, u32[]{:S(2)}, u32[]{:S(2)}) async-start(bf16[2,2,16,2,16,256]{5,4,3,1,0,2:T(8,128)(2,1)} %broadcast_in_dim.8), calls=%async_computation | async-start | bytes 2097152 | tf_op jit(solution)/shard_map/all_to_all | solution.py:123
  39.5 23.2 %all-to-all-start.1 = ((bf16[2,2,16,2,16,256]{5,4,3,1,0,2:T(8,128)(2,1)}), bf16[2,2,16,2,16,256]{5,4,3,1,0,2:T(8,128)(2,1)S(1)}, u32[]{:S(2)}, u32[]{:S(2)}) async-start(bf16[2,2,16,2,16,256]{5,4,3,1,0,2:T(8,128)(2,1)} %broadcast_in_dim.9), calls=%async_computation.1 | async-start | bytes 2097152 | tf_op jit(solution)/shard_map/all_to_all | solution.py:123
  58.0 16.9 %collective-permute-start.1 = (f32[2,8,32,256]{3,2,1,0:T(8,128)}, f32[2,8,32,256]{3,2,1,0:T(8,128)S(1)}, u32[]{:S(2)}, u32[]{:S(2)}) collective-permute-start(f32[2,8,32,256]{3,2,1,0:T(8,128)} %dynamic-slice_bitcast_fusion.1), channel_id=1, source_target_pairs={{0,32},{32,0},{1,33},{33,1},{2,34},{34,2},{3,35},{35,3},{4,36},{36... | collective-permute-start | bytes 1572872 | tf_op jit(solution)/shard_map/ppermute | solution.py:130
  63.8 11.1 %copy-start.1 = (f32[2,512,256]{2,1,0:T(8,128)S(1)}, f32[2,512,256]{2,1,0:T(8,128)}, u32[]{:S(2)}) copy-start(f32[2,512,256]{2,1,0:T(8,128)} %shard_map.46) | copy-start | bytes 3145732
  69.0 9.5 %copy-start = (f32[2,512,256]{2,1,0:T(8,128)S(1)}, f32[2,512,256]{2,1,0:T(8,128)}, u32[]{:S(2)}) copy-start(f32[2,512,256]{2,1,0:T(8,128)} %shard_map.47) | copy-start | bytes 3145732
  71.0 7.5 %collective-permute-start.5 = (f32[2,8,32,256]{3,2,1,0:T(8,128)}, f32[2,8,32,256]{3,2,1,0:T(8,128)S(1)}, u32[]{:S(2)}, u32[]{:S(2)}) collective-permute-start(f32[2,8,32,256]{3,2,1,0:T(8,128)} %dynamic-slice_bitcast_fusion), channel_id=1, source_target_pairs={{0,32},{32,0},{1,33},{33,1},{2,34},{34,2},{3,35},{35,3},{4,36},{36... | collective-permute-start | bytes 1572872 | tf_op jit(solution)/shard_map/ppermute | solution.py:130
  75.3 9.8 %collective-permute-start.2 = (f32[2,2,2,32,256]{4,0,3,1,2:T(2,128)S(1)}, f32[2,2,2,32,256]{4,0,3,1,2:T(2,128)S(1)}, u32[]{:S(2)}, u32[]{:S(2)}) collective-permute-start(f32[2,2,2,32,256]{4,0,3,1,2:T(2,128)S(1)} %bitcast.87), channel_id=1, source_target_pairs={{0,64},{64,0},{128,192},{192,128},{256,320},{320,256},{384,448},{4... | collective-permute-start | bytes 786440 | tf_op jit(solution)/shard_map/ppermute | solution.py:92
  78.8 11.9 %collective-permute-start.6 = (f32[2,2,2,32,256]{4,0,3,1,2:T(2,128)S(1)}, f32[2,2,2,32,256]{4,0,3,1,2:T(2,128)S(1)}, u32[]{:S(2)}, u32[]{:S(2)}) collective-permute-start(f32[2,2,2,32,256]{4,0,3,1,2:T(2,128)S(1)} %bitcast.88), channel_id=1, source_target_pairs={{0,64},{64,0},{128,192},{192,128},{256,320},{320,256},{384,448},{4... | collective-permute-start | bytes 786440 | tf_op jit(solution)/shard_map/ppermute | solution.py:92
  85.4 9.1 %collective-permute-start.3 = (f32[2,2,32,256]{3,0,2,1:T(2,128)S(1)}, f32[2,2,32,256]{3,0,2,1:T(2,128)S(1)}, u32[]{:S(2)}, u32[]{:S(2)}) collective-permute-start(f32[2,2,32,256]{3,0,2,1:T(2,128)S(1)} %dynamic-slice_bitcast_fusion.3), channel_id=1, source_target_pairs={{0,128},{64,192},{128,0},{192,64},{256,384},{320,448},{384,256},{4... | collective-permute-start | bytes 393224 | tf_op jit(solution)/shard_map/ppermute | solution.py:92
  91.0 14.9 %collective-permute-start.7 = (f32[2,2,32,256]{3,0,2,1:T(2,128)S(1)}, f32[2,2,32,256]{3,0,2,1:T(2,128)S(1)}, u32[]{:S(2)}, u32[]{:S(2)}) collective-permute-start(f32[2,2,32,256]{3,0,2,1:T(2,128)S(1)} %dynamic-slice_bitcast_fusion.2), channel_id=1, source_target_pairs={{0,128},{64,192},{128,0},{192,64},{256,384},{320,448},{384,256},{4... | collective-permute-start | bytes 393224 | tf_op jit(solution)/shard_map/ppermute | solution.py:92
  94.6 19.5 %collective-permute-start.4 = (f32[2,32,256]{2,0,1:T(2,128)S(1)}, f32[2,32,256]{2,0,1:T(2,128)S(1)}, u32[]{:S(2)}, u32[]{:S(2)}) collective-permute-start(f32[2,32,256]{2,0,1:T(2,128)S(1)} %dynamic-slice_bitcast_fusion.5), channel_id=1, source_target_pairs={{0,256},{64,320},{128,384},{192,448},{256,0},{320,64},{384,128},{4... | collective-permute-start | bytes 196616 | tf_op jit(solution)/shard_map/ppermute | solution.py:92
  106.0 14.3 %collective-permute-start.8 = (f32[2,32,256]{2,0,1:T(2,128)S(1)}, f32[2,32,256]{2,0,1:T(2,128)S(1)}, u32[]{:S(2)}, u32[]{:S(2)}) collective-permute-start(f32[2,32,256]{2,0,1:T(2,128)S(1)} %dynamic-slice_bitcast_fusion.4), channel_id=1, source_target_pairs={{0,256},{64,320},{128,384},{192,448},{256,0},{320,64},{384,128},{4... | collective-permute-start | bytes 196616 | tf_op jit(solution)/shard_map/ppermute | solution.py:92

commit v19 on v18

--- a/solution.py
+++ b/solution.py
@@ -7,7 +7,7 @@
 
 CUTS = ("zl", "core")
 STEM = ("zh", "x", "y")
-ROW_TILE = 128
+ROW_TILE = 512
 
 
 def split_mesh(mesh):

time: 122 us -> 122 us (level)
  transfers between devices with their start and end apart: 11 -> 11, of which waited for: 4 -> 4; matrix products, arithmetic and copies ran while one was open for 12% -> 12% of each run, Pallas kernels for 8% -> 9%
where the time goes in v19:
time: 122 us; the launch traced here: 121 us
  starting transfers between devices  70.3 us (58%)
  waiting for transfers between devices  22.7 us (19%)
  local copies, waits for them, and re-layouts  14 us (11%)
  Pallas kernels  10.6 us (9%)
  other arithmetic  2 us (2%)
    ppermute x6, starting transfers between devices, halving_scatter(): shaped = keep + lax.ppermute(send, axis, pairs)  31.7 us
    ppermute x1, starting transfers between devices, body(): other_raw = lax.ppermute(branch_tensor, 'zh', shift_pairs(2, 1))  16.3 us
    all_to_all x2, starting transfers between devices, body(): gathered = lax.all_to_all(part, ('x', 'y'), 2, 4, tiled=True)  13.9 us
    ppermute x6, waiting for transfers between devices, halving_scatter(): shaped = keep + lax.ppermute(send, axis, pairs)  12 us
    all_to_all x2, waiting for transfers between devices, body(): gathered = lax.all_to_all(part, ('x', 'y'), 2, 4, tiled=True)  10.7 us
    pallas_call x2, Pallas kernels, contract(): pl.pallas_call(contract_kernel, out_shape=jax.ShapeDtypeStruct((2, rows,...  10.6 us
    ppermute x2, starting transfers between devices, body(): mine = mine + lax.ppermute(theirs, 'core', shift_pairs(2, 1))  8.43 us
    squeeze x2, local copies, waits for them, and re-layouts, body(): theirs = lax.dynamic_index_in_dim(shaped, 1 - core, 2, keepdims=False)  3.88 us
  transfers between devices with their start and end apart: 11, of which 4 were waited for; matrix products, arithmetic and copies ran while one was open for 12% of the time, Pallas kernels for 9%

profile of v19, /device:TPU:1, one launch (start us, length us, event | category | flops | bytes accessed | tf_op | source)
XLA Modules:
  0.0 121.2 jit_solution(4812111650680707920)
XLA Ops:
  0.0 16.3 %collective-permute-start = (bf16[2,16,2,512]{3,2,1,0:T(2,128)(2,1)}, bf16[2,16,2,512]{3,2,1,0:T(2,128)(2,1)S(1)}, u32[]{:S(2)}, u32[]{:S(2)}) collective-permute-start(bf16[2,16,2,512]{3,2,1,0:T(2,128)(2,1)} %param.5), channel_id=1, source_target_pairs={{0,16},{16,0},{1,17},{17,1},{2,18},{18,2},{3,19},{19,3},{4,20},{20... | collective-permute-start | bytes 196616 | tf_op jit(solution)/shard_map/ppermute | solution.py:98
  16.3 0.9 fusion.9
  17.1 0.8 fusion.11
  17.9 0.3 fusion
  18.2 0.3 fusion.1
  18.7 0.3 fusion.2
  19.0 0.3 fusion.3
  19.3 0.2 maximum_bitcast_fusion.1
  19.5 0.2 broadcast_select_fusion
  19.7 0.1 fusion.8
  19.9 1.1 broadcast_in_dim.8
  21.0 6.8 %all-to-all-start = ((bf16[2,2,16,2,16,256]{5,4,3,1,0,2:T(8,128)(2,1)}), bf16[2,2,16,2,16,256]{5,4,3,1,0,2:T(8,128)(2,1)S(1)}, u32[]{:S(2)}, u32[]{:S(2)}) async-start(bf16[2,2,16,2,16,256]{5,4,3,1,0,2:T(8,128)(2,1)} %broadcast_in_dim.8), calls=%async_computation | async-start | bytes 2097152 | tf_op jit(solution)/shard_map/all_to_all | solution.py:123
  27.7 1.1 broadcast_in_dim.9
  28.9 10.7 %all-to-all-done = bf16[2,2,16,2,16,256]{5,4,3,1,0,2:T(8,128)(2,1)S(1)} async-done(((bf16[2,2,16,2,16,256]{5,4,3,1,0,2:T(8,128)(2,1)}), bf16[2,2,16,2,16,256]{5,4,3,1,0,2:T(8,128)(2,1)S(1)}, u32[]{:S(2)}, u32[]{:S(2)}) %all-to-all-start) | async-done | bytes 1048608 | tf_op jit(solution)/shard_map/all_to_all | solution.py:123
  39.5 7.1 %all-to-all-start.1 = ((bf16[2,2,16,2,16,256]{5,4,3,1,0,2:T(8,128)(2,1)}), bf16[2,2,16,2,16,256]{5,4,3,1,0,2:T(8,128)(2,1)S(1)}, u32[]{:S(2)}, u32[]{:S(2)}) async-start(bf16[2,2,16,2,16,256]{5,4,3,1,0,2:T(8,128)(2,1)} %broadcast_in_dim.9), calls=%async_computation.1 | async-start | bytes 2097152 | tf_op jit(solution)/shard_map/all_to_all | solution.py:123
  46.7 3.3 %copy.26 = bf16[2,512,2,512]{3,1,2,0:T(8,128)(2,1)} copy(bf16[2,512,2,512]{3,2,1,0:T(2,128)(2,1)} %param.4) | data formatting | bytes 4194304 | tf_op args[0]
  50.0 1.1 copy.14
  51.0 5.3 %shard_map.46 = f32[2,512,256]{2,1,0:T(8,128)} custom-call(bf16[2,2,512,512]{3,2,1,0:T(8,128)(2,1)} %bitcast.75, bf16[2,2,512,256]{3,2,1,0:T(8,128)(2,1)} %bitcast.84, bf16[2,512,2,512]{3,2,1,0:T(2,128)(2,1)} %o_ref.3), custom_call_target="tpu_custom_call" | custom-call | flops 1073741824 | bytes 5242880 | tf_op jit(solution)/shard_map/pallas_call | solution.py:68
  56.3 1.9 %dynamic-slice_bitcast_fusion.1 = f32[2,8,32,256]{3,2,1,0:T(8,128)} fusion(f32[2,8,2,32,256]{4,3,2,1,0:T(8,128)} %bitcast.81, s32[]{:T(128)S(6)} %select_n.51), kind=kLoop, calls=%fused_computation.14 | loop fusion | bytes 1048580 | tf_op jit(solution)/shard_map/jit(dynamic_index_in_dim)/squeeze | solution.py:129
  58.2 4.7 %collective-permute-start.1 = (f32[2,8,32,256]{3,2,1,0:T(8,128)}, f32[2,8,32,256]{3,2,1,0:T(8,128)S(1)}, u32[]{:S(2)}, u32[]{:S(2)}) collective-permute-start(f32[2,8,32,256]{3,2,1,0:T(8,128)} %dynamic-slice_bitcast_fusion.1), channel_id=1, source_target_pairs={{0,32},{32,0},{1,33},{33,1},{2,34},{34,2},{3,35},{35,3},{4,36},{36... | collective-permute-start | bytes 1572872 | tf_op jit(solution)/shard_map/ppermute | solution.py:130
  62.9 0.0 all-to-all-done.1
  62.9 1.1 copy.18
  64.0 5.3 %shard_map.47 = f32[2,512,256]{2,1,0:T(8,128)} custom-call(bf16[2,2,512,512]{3,2,1,0:T(8,128)(2,1)} %bitcast.76, bf16[2,2,512,256]{3,2,1,0:T(8,128)(2,1)} %bitcast.83, bf16[2,512,2,512]{3,2,1,0:T(2,128)(2,1)} %o_ref.3), custom_call_target="tpu_custom_call" | custom-call | flops 1073741824 | bytes 5242880 | tf_op jit(solution)/shard_map/pallas_call | solution.py:68
  69.4 2.0 %dynamic-slice_bitcast_fusion = f32[2,8,32,256]{3,2,1,0:T(8,128)} fusion(f32[2,8,2,32,256]{4,3,2,1,0:T(8,128)} %bitcast.79, s32[]{:T(128)S(6)} %select_n.51), kind=kLoop, calls=%fused_computation.13 | loop fusion | bytes 1048580 | tf_op jit(solution)/shard_map/jit(dynamic_index_in_dim)/squeeze | solution.py:129
  71.3 3.7 %collective-permute-start.5 = (f32[2,8,32,256]{3,2,1,0:T(8,128)}, f32[2,8,32,256]{3,2,1,0:T(8,128)S(1)}, u32[]{:S(2)}, u32[]{:S(2)}) collective-permute-start(f32[2,8,32,256]{3,2,1,0:T(8,128)} %dynamic-slice_bitcast_fusion), channel_id=1, source_target_pairs={{0,32},{32,0},{1,33},{33,1},{2,34},{34,2},{3,35},{35,3},{4,36},{36... | collective-permute-start | bytes 1572872 | tf_op jit(solution)/shard_map/ppermute | solution.py:130
  75.1 0.1 bitcast_add_fusion.1
  75.2 0.1 constant_dynamic-slice_fusion.3
  75.2 0.2 copy.28
  75.4 3.2 %collective-permute-start.2 = (f32[2,2,2,32,256]{4,0,3,1,2:T(2,128)S(1)}, f32[2,2,2,32,256]{4,0,3,1,2:T(2,128)S(1)}, u32[]{:S(2)}, u32[]{:S(2)}) collective-permute-start(f32[2,2,2,32,256]{4,0,3,1,2:T(2,128)S(1)} %bitcast.87), channel_id=1, source_target_pairs={{0,64},{64,0},{128,192},{192,128},{256,320},{320,256},{384,448},{4... | collective-permute-start | bytes 786440 | tf_op jit(solution)/shard_map/ppermute | solution.py:92
  78.7 0.0 collective-permute-done.5
  78.7 0.1 bitcast_add_fusion
  78.8 0.2 copy.27
  79.0 2.1 %collective-permute-start.6 = (f32[2,2,2,32,256]{4,0,3,1,2:T(2,128)S(1)}, f32[2,2,2,32,256]{4,0,3,1,2:T(2,128)S(1)}, u32[]{:S(2)}, u32[]{:S(2)}) collective-permute-start(f32[2,2,2,32,256]{4,0,3,1,2:T(2,128)S(1)} %bitcast.88), channel_id=1, source_target_pairs={{0,64},{64,0},{128,192},{192,128},{256,320},{320,256},{384,448},{4... | collective-permute-start | bytes 786440 | tf_op jit(solution)/shard_map/ppermute | solution.py:92
  81.1 4.2 %collective-permute-done.2 = f32[2,2,2,32,256]{4,0,3,1,2:T(2,128)S(1)} collective-permute-done((f32[2,2,2,32,256]{4,0,3,1,2:T(2,128)S(1)}, f32[2,2,2,32,256]{4,0,3,1,2:T(2,128)S(1)}, u32[]{:S(2)}, u32[]{:S(2)}) %collective-permute-start.2) | collective-permute-done | bytes 262176 | tf_op jit(solution)/shard_map/ppermute | solution.py:92
  85.3 0.3 bitcast_add_fusion.3
  85.6 3.5 %collective-permute-start.3 = (f32[2,2,32,256]{3,0,2,1:T(2,128)S(1)}, f32[2,2,32,256]{3,0,2,1:T(2,128)S(1)}, u32[]{:S(2)}, u32[]{:S(2)}) collective-permute-start(f32[2,2,32,256]{3,0,2,1:T(2,128)S(1)} %dynamic-slice_bitcast_fusion.3), channel_id=1, source_target_pairs={{0,128},{64,192},{128,0},{192,64},{256,384},{320,448},{384,256},{4... | collective-permute-start | bytes 393224 | tf_op jit(solution)/shard_map/ppermute | solution.py:92
  89.1 1.8 %collective-permute-done.6 = f32[2,2,2,32,256]{4,0,3,1,2:T(2,128)S(1)} collective-permute-done((f32[2,2,2,32,256]{4,0,3,1,2:T(2,128)S(1)}, f32[2,2,2,32,256]{4,0,3,1,2:T(2,128)S(1)}, u32[]{:S(2)}, u32[]{:S(2)}) %collective-permute-start.6) | collective-permute-done | bytes 262176 | tf_op jit(solution)/shard_map/ppermute | solution.py:92
  90.9 0.3 bitcast_add_fusion.2
  91.2 3.5 %collective-permute-start.7 = (f32[2,2,32,256]{3,0,2,1:T(2,128)S(1)}, f32[2,2,32,256]{3,0,2,1:T(2,128)S(1)}, u32[]{:S(2)}, u32[]{:S(2)}) collective-permute-start(f32[2,2,32,256]{3,0,2,1:T(2,128)S(1)} %dynamic-slice_bitcast_fusion.2), channel_id=1, source_target_pairs={{0,128},{64,192},{128,0},{192,64},{256,384},{320,448},{384,256},{4... | collective-permute-start | bytes 393224 | tf_op jit(solution)/shard_map/ppermute | solution.py:92
  94.7 0.0 collective-permute-done.3
  94.7 0.1 bitcast_add_fusion.5
  94.8 11.2 %collective-permute-start.4 = (f32[2,32,256]{2,0,1:T(2,128)S(1)}, f32[2,32,256]{2,0,1:T(2,128)S(1)}, u32[]{:S(2)}, u32[]{:S(2)}) collective-permute-start(f32[2,32,256]{2,0,1:T(2,128)S(1)} %dynamic-slice_bitcast_fusion.5), channel_id=1, source_target_pairs={{0,256},{64,320},{128,384},{192,448},{256,0},{320,64},{384,128},{4... | collective-permute-start | bytes 196616 | tf_op jit(solution)/shard_map/ppermute | solution.py:92
  106.0 0.0 collective-permute-done.7
  106.1 0.1 bitcast_add_fusion.4
  106.2 8.2 %collective-permute-start.8 = (f32[2,32,256]{2,0,1:T(2,128)S(1)}, f32[2,32,256]{2,0,1:T(2,128)S(1)}, u32[]{:S(2)}, u32[]{:S(2)}) collective-permute-start(f32[2,32,256]{2,0,1:T(2,128)S(1)} %dynamic-slice_bitcast_fusion.4), channel_id=1, source_target_pairs={{0,256},{64,320},{128,384},{192,448},{256,0},{320,64},{384,128},{4... | collective-permute-start | bytes 196616 | tf_op jit(solution)/shard_map/ppermute | solution.py:92
  114.3 0.0 collective-permute-done.4
  114.4 6.0 %collective-permute-done.8 = f32[2,32,256]{2,0,1:T(2,128)S(1)} collective-permute-done((f32[2,32,256]{2,0,1:T(2,128)S(1)}, f32[2,32,256]{2,0,1:T(2,128)S(1)}, u32[]{:S(2)}, u32[]{:S(2)}) %collective-permute-start.8) | collective-permute-done | bytes 65568 | tf_op jit(solution)/shard_map/ppermute | solution.py:92
  120.5 0.7 maximum_bitcast_fusion
  (24 shorter events, 0.4 us)
Async XLA Ops:
  0.0 18.6 %collective-permute-start = (bf16[2,16,2,512]{3,2,1,0:T(2,128)(2,1)}, bf16[2,16,2,512]{3,2,1,0:T(2,128)(2,1)S(1)}, u32[]{:S(2)}, u32[]{:S(2)}) collective-permute-start(bf16[2,16,2,512]{3,2,1,0:T(2,128)(2,1)} %param.5), channel_id=1, source_target_pairs={{0,16},{16,0},{1,17},{17,1},{2,18},{18,2},{3,19},{19,3},{4,20},{20... | collective-permute-start | bytes 196616 | tf_op jit(solution)/shard_map/ppermute | solution.py:98
  21.0 18.6 %all-to-all-start = ((bf16[2,2,16,2,16,256]{5,4,3,1,0,2:T(8,128)(2,1)}), bf16[2,2,16,2,16,256]{5,4,3,1,0,2:T(8,128)(2,1)S(1)}, u32[]{:S(2)}, u32[]{:S(2)}) async-start(bf16[2,2,16,2,16,256]{5,4,3,1,0,2:T(8,128)(2,1)} %broadcast_in_dim.8), calls=%async_computation | async-start | bytes 2097152 | tf_op jit(solution)/shard_map/all_to_all | solution.py:123
  39.5 23.4 %all-to-all-start.1 = ((bf16[2,2,16,2,16,256]{5,4,3,1,0,2:T(8,128)(2,1)}), bf16[2,2,16,2,16,256]{5,4,3,1,0,2:T(8,128)(2,1)S(1)}, u32[]{:S(2)}, u32[]{:S(2)}) async-start(bf16[2,2,16,2,16,256]{5,4,3,1,0,2:T(8,128)(2,1)} %broadcast_in_dim.9), calls=%async_computation.1 | async-start | bytes 2097152 | tf_op jit(solution)/shard_map/all_to_all | solution.py:123
  58.2 16.9 %collective-permute-start.1 = (f32[2,8,32,256]{3,2,1,0:T(8,128)}, f32[2,8,32,256]{3,2,1,0:T(8,128)S(1)}, u32[]{:S(2)}, u32[]{:S(2)}) collective-permute-start(f32[2,8,32,256]{3,2,1,0:T(8,128)} %dynamic-slice_bitcast_fusion.1), channel_id=1, source_target_pairs={{0,32},{32,0},{1,33},{33,1},{2,34},{34,2},{3,35},{35,3},{4,36},{36... | collective-permute-start | bytes 1572872 | tf_op jit(solution)/shard_map/ppermute | solution.py:130
  64.0 11.1 %copy-start.1 = (f32[2,512,256]{2,1,0:T(8,128)S(1)}, f32[2,512,256]{2,1,0:T(8,128)}, u32[]{:S(2)}) copy-start(f32[2,512,256]{2,1,0:T(8,128)} %shard_map.46) | copy-start | bytes 3145732
  69.4 9.3 %copy-start = (f32[2,512,256]{2,1,0:T(8,128)S(1)}, f32[2,512,256]{2,1,0:T(8,128)}, u32[]{:S(2)}) copy-start(f32[2,512,256]{2,1,0:T(8,128)} %shard_map.47) | copy-start | bytes 3145732
  71.3 7.3 %collective-permute-start.5 = (f32[2,8,32,256]{3,2,1,0:T(8,128)}, f32[2,8,32,256]{3,2,1,0:T(8,128)S(1)}, u32[]{:S(2)}, u32[]{:S(2)}) collective-permute-start(f32[2,8,32,256]{3,2,1,0:T(8,128)} %dynamic-slice_bitcast_fusion), channel_id=1, source_target_pairs={{0,32},{32,0},{1,33},{33,1},{2,34},{34,2},{3,35},{35,3},{4,36},{36... | collective-permute-start | bytes 1572872 | tf_op jit(solution)/shard_map/ppermute | solution.py:130
  75.4 9.8 %collective-permute-start.2 = (f32[2,2,2,32,256]{4,0,3,1,2:T(2,128)S(1)}, f32[2,2,2,32,256]{4,0,3,1,2:T(2,128)S(1)}, u32[]{:S(2)}, u32[]{:S(2)}) collective-permute-start(f32[2,2,2,32,256]{4,0,3,1,2:T(2,128)S(1)} %bitcast.87), channel_id=1, source_target_pairs={{0,64},{64,0},{128,192},{192,128},{256,320},{320,256},{384,448},{4... | collective-permute-start | bytes 786440 | tf_op jit(solution)/shard_map/ppermute | solution.py:92
  79.0 11.9 %collective-permute-start.6 = (f32[2,2,2,32,256]{4,0,3,1,2:T(2,128)S(1)}, f32[2,2,2,32,256]{4,0,3,1,2:T(2,128)S(1)}, u32[]{:S(2)}, u32[]{:S(2)}) collective-permute-start(f32[2,2,2,32,256]{4,0,3,1,2:T(2,128)S(1)} %bitcast.88), channel_id=1, source_target_pairs={{0,64},{64,0},{128,192},{192,128},{256,320},{320,256},{384,448},{4... | collective-permute-start | bytes 786440 | tf_op jit(solution)/shard_map/ppermute | solution.py:92
  85.6 9.2 %collective-permute-start.3 = (f32[2,2,32,256]{3,0,2,1:T(2,128)S(1)}, f32[2,2,32,256]{3,0,2,1:T(2,128)S(1)}, u32[]{:S(2)}, u32[]{:S(2)}) collective-permute-start(f32[2,2,32,256]{3,0,2,1:T(2,128)S(1)} %dynamic-slice_bitcast_fusion.3), channel_id=1, source_target_pairs={{0,128},{64,192},{128,0},{192,64},{256,384},{320,448},{384,256},{4... | collective-permute-start | bytes 393224 | tf_op jit(solution)/shard_map/ppermute | solution.py:92
  91.2 14.9 %collective-permute-start.7 = (f32[2,2,32,256]{3,0,2,1:T(2,128)S(1)}, f32[2,2,32,256]{3,0,2,1:T(2,128)S(1)}, u32[]{:S(2)}, u32[]{:S(2)}) collective-permute-start(f32[2,2,32,256]{3,0,2,1:T(2,128)S(1)} %dynamic-slice_bitcast_fusion.2), channel_id=1, source_target_pairs={{0,128},{64,192},{128,0},{192,64},{256,384},{320,448},{384,256},{4... | collective-permute-start | bytes 393224 | tf_op jit(solution)/shard_map/ppermute | solution.py:92
  94.8 19.5 %collective-permute-start.4 = (f32[2,32,256]{2,0,1:T(2,128)S(1)}, f32[2,32,256]{2,0,1:T(2,128)S(1)}, u32[]{:S(2)}, u32[]{:S(2)}) collective-permute-start(f32[2,32,256]{2,0,1:T(2,128)S(1)} %dynamic-slice_bitcast_fusion.5), channel_id=1, source_target_pairs={{0,256},{64,320},{128,384},{192,448},{256,0},{320,64},{384,128},{4... | collective-permute-start | bytes 196616 | tf_op jit(solution)/shard_map/ppermute | solution.py:92
  106.2 14.3 %collective-permute-start.8 = (f32[2,32,256]{2,0,1:T(2,128)S(1)}, f32[2,32,256]{2,0,1:T(2,128)S(1)}, u32[]{:S(2)}, u32[]{:S(2)}) collective-permute-start(f32[2,32,256]{2,0,1:T(2,128)S(1)} %dynamic-slice_bitcast_fusion.4), channel_id=1, source_target_pairs={{0,256},{64,320},{128,384},{192,448},{256,0},{320,64},{384,128},{4... | collective-permute-start | bytes 196616 | tf_op jit(solution)/shard_map/ppermute | solution.py:92

commit v20 on v17

--- a/solution.py
+++ b/solution.py
@@ -102,6 +102,8 @@
         return jnp.transpose(moved, (0, 2, 1, 3))
 
     permuted = permuted_of(branch_tensor)
+    stem_t = jnp.transpose(stem_tensor, (0, 2, 1, 3))
+    other_raw, stem_t = lax.optimization_barrier((other_raw, stem_t))
     other = permuted_of(other_raw)
     low = lax.axis_index("zh") == 0
     pair = jnp.where(low, jnp.stack([permuted, other], axis=2), jnp.stack([other, permuted], axis=2))
@@ -109,7 +111,6 @@
     copies = jnp.broadcast_to(pair[:, :, None], pair.shape[:2] + (plane,) + pair.shape[2:])
     halves = 2
     span = width // halves
-    stem_t = jnp.transpose(stem_tensor, (0, 2, 1, 3))
     open_t = open_tensor
     zl_count = lax.axis_size("zl")
     block_rows = row_count // (zl_count * 2)

time: 121 us -> 122 us (level)
  waiting for transfers between devices: 22.7 us -> 30.5 us
  starting transfers between devices: 70.9 us -> 64.2 us
    all_to_all x2, waiting for transfers between devices: 10.7 us -> 17 us  [body(): gathered = lax.all_to_all(part, ('x', 'y'), 2, 4, tiled=True)]
    ppermute x6, starting transfers between devices: 31.7 us -> 26.7 us  [halving_scatter(): shaped = keep + lax.ppermute(send, axis, pairs)]
    all_to_all x2, starting transfers between devices: 13.9 us -> 10.6 us  [body(): gathered = lax.all_to_all(part, ('x', 'y'), 2, 4, tiled=True)]
    ppermute x2, starting transfers between devices: 9.05 us -> 10.6 us  [body(): mine = mine + lax.ppermute(theirs, 'core', shift_pairs(2, 1))]
    ppermute x6, waiting for transfers between devices: 12 us -> 13.5 us  [halving_scatter(): shaped = keep + lax.ppermute(send, axis, pairs)]
  transfers between devices with their start and end apart: 11 -> 11, of which waited for: 4 -> 6; matrix products, arithmetic and copies ran while one was open for 12% -> 11% of each run, Pallas kernels for 8% -> 8%
where the time goes in v20:
time: 122 us
  starting transfers between devices  64.2 us (53%)
  waiting for transfers between devices  30.5 us (25%)
  local copies, waits for them, and re-layouts  14 us (11%)
  Pallas kernels  9.37 us (8%)
  other arithmetic  1.99 us (2%)
    ppermute x6, starting transfers between devices, halving_scatter(): shaped = keep + lax.ppermute(send, axis, pairs)  26.7 us
    all_to_all x2, waiting for transfers between devices, body(): gathered = lax.all_to_all(part, ('x', 'y'), 2, 4, tiled=True)  17 us
    ppermute x1, starting transfers between devices, body(): other_raw = lax.ppermute(branch_tensor, 'zh', shift_pairs(2, 1))  16.3 us
    ppermute x6, waiting for transfers between devices, halving_scatter(): shaped = keep + lax.ppermute(send, axis, pairs)  13.5 us
    all_to_all x2, starting transfers between devices, body(): gathered = lax.all_to_all(part, ('x', 'y'), 2, 4, tiled=True)  10.6 us
    ppermute x2, starting transfers between devices, body(): mine = mine + lax.ppermute(theirs, 'core', shift_pairs(2, 1))  10.6 us
    pallas_call x2, Pallas kernels, contract(): pl.pallas_call(contract_kernel, out_shape=jax.ShapeDtypeStruct((2, rows,...  9.37 us
    squeeze x2, local copies, waits for them, and re-layouts, body(): theirs = lax.dynamic_index_in_dim(shaped, 1 - core, 2, keepdims=False)  3.88 us
  transfers between devices with their start and end apart: 11, of which 6 were waited for; matrix products, arithmetic and copies ran while one was open for 11% of the time, Pallas kernels for 8%

profile of v20, /device:TPU:1, one launch (start us, length us, event | category | flops | bytes accessed | tf_op | source)
XLA Modules:
  0.0 121.6 jit_solution(13049481606606267822)
XLA Ops:
  0.0 16.3 %collective-permute-start = (bf16[2,16,2,512]{3,2,1,0:T(2,128)(2,1)}, bf16[2,16,2,512]{3,2,1,0:T(2,128)(2,1)S(1)}, u32[]{:S(2)}, u32[]{:S(2)}) collective-permute-start(bf16[2,16,2,512]{3,2,1,0:T(2,128)(2,1)} %param.5), channel_id=1, source_target_pairs={{0,16},{16,0},{1,17},{17,1},{2,18},{18,2},{3,19},{19,3},{4,20},{20... | collective-permute-start | bytes 196616 | tf_op jit(solution)/shard_map/ppermute | solution.py:98
  16.3 0.9 fusion.7
  17.1 0.8 fusion.9
  17.9 0.3 fusion
  18.2 0.3 fusion.1
  18.6 3.3 %copy.26 = bf16[2,512,2,512]{3,1,2,0:T(8,128)(2,1)} copy(bf16[2,512,2,512]{3,2,1,0:T(2,128)(2,1)} %param.4) | data formatting | bytes 4194304 | tf_op args[0]
  21.9 0.3 convolution_convert_fusion.1
  22.3 0.3 convolution_convert_fusion
  22.6 0.2 maximum_bitcast_fusion.1
  22.8 0.2 broadcast_select_fusion
  23.0 0.1 fusion.6
  23.1 1.1 broadcast_in_dim.9
  24.2 6.8 %all-to-all-start.1 = ((bf16[2,2,16,2,16,256]{5,4,3,1,0,2:T(8,128)(2,1)}), bf16[2,2,16,2,16,256]{5,4,3,1,0,2:T(8,128)(2,1)S(1)}, u32[]{:S(2)}, u32[]{:S(2)}) async-start(bf16[2,2,16,2,16,256]{5,4,3,1,0,2:T(8,128)(2,1)} %broadcast_in_dim.9), calls=%async_computation.1 | async-start | bytes 2097152 | tf_op jit(solution)/shard_map/all_to_all | solution.py:124
  31.0 15.3 %all-to-all-done.1 = bf16[2,2,16,2,16,256]{5,4,3,1,0,2:T(8,128)(2,1)S(1)} async-done(((bf16[2,2,16,2,16,256]{5,4,3,1,0,2:T(8,128)(2,1)}), bf16[2,2,16,2,16,256]{5,4,3,1,0,2:T(8,128)(2,1)S(1)}, u32[]{:S(2)}, u32[]{:S(2)}) %all-to-all-start.1) | async-done | bytes 1048608 | tf_op jit(solution)/shard_map/all_to_all | solution.py:124
  46.3 1.1 broadcast_in_dim.8
  47.4 3.9 %all-to-all-start = ((bf16[2,2,16,2,16,256]{5,4,3,1,0,2:T(8,128)(2,1)}), bf16[2,2,16,2,16,256]{5,4,3,1,0,2:T(8,128)(2,1)S(1)}, u32[]{:S(2)}, u32[]{:S(2)}) async-start(bf16[2,2,16,2,16,256]{5,4,3,1,0,2:T(8,128)(2,1)} %broadcast_in_dim.8), calls=%async_computation | async-start | bytes 2097152 | tf_op jit(solution)/shard_map/all_to_all | solution.py:124
  51.3 1.1 copy.18
  52.3 4.6 %shard_map.47 = f32[2,512,256]{2,1,0:T(8,128)} custom-call(bf16[2,2,512,512]{3,2,1,0:T(8,128)(2,1)} %bitcast.71, bf16[2,2,512,256]{3,2,1,0:T(8,128)(2,1)} %bitcast.80, bf16[2,512,2,512]{3,2,1,0:T(2,128)(2,1)} %o_ref.3), custom_call_target="tpu_custom_call" | custom-call | flops 1073741824 | bytes 5242880 | tf_op jit(solution)/shard_map/pallas_call | solution.py:68
  57.0 1.9 %dynamic-slice_bitcast_fusion = f32[2,8,32,256]{3,2,1,0:T(8,128)} fusion(f32[2,8,2,32,256]{4,3,2,1,0:T(8,128)} %bitcast.77, s32[]{:T(128)S(6)} %select_n.51), kind=kLoop, calls=%fused_computation.11 | loop fusion | bytes 1048580 | tf_op jit(solution)/shard_map/jit(dynamic_index_in_dim)/squeeze | solution.py:130
  58.9 4.9 %collective-permute-start.5 = (f32[2,8,32,256]{3,2,1,0:T(8,128)}, f32[2,8,32,256]{3,2,1,0:T(8,128)S(1)}, u32[]{:S(2)}, u32[]{:S(2)}) collective-permute-start(f32[2,8,32,256]{3,2,1,0:T(8,128)} %dynamic-slice_bitcast_fusion), channel_id=1, source_target_pairs={{0,32},{32,0},{1,33},{33,1},{2,34},{34,2},{3,35},{35,3},{4,36},{36... | collective-permute-start | bytes 1572872 | tf_op jit(solution)/shard_map/ppermute | solution.py:131
  63.8 1.7 %all-to-all-done = bf16[2,2,16,2,16,256]{5,4,3,1,0,2:T(8,128)(2,1)S(1)} async-done(((bf16[2,2,16,2,16,256]{5,4,3,1,0,2:T(8,128)(2,1)}), bf16[2,2,16,2,16,256]{5,4,3,1,0,2:T(8,128)(2,1)S(1)}, u32[]{:S(2)}, u32[]{:S(2)}) %all-to-all-start) | async-done | bytes 1048608 | tf_op jit(solution)/shard_map/all_to_all | solution.py:124
  65.5 1.1 copy.14
  66.6 4.7 %shard_map.46 = f32[2,512,256]{2,1,0:T(8,128)} custom-call(bf16[2,2,512,512]{3,2,1,0:T(8,128)(2,1)} %bitcast.72, bf16[2,2,512,256]{3,2,1,0:T(8,128)(2,1)} %bitcast.79, bf16[2,512,2,512]{3,2,1,0:T(2,128)(2,1)} %o_ref.3), custom_call_target="tpu_custom_call" | custom-call | flops 1073741824 | bytes 5242880 | tf_op jit(solution)/shard_map/pallas_call | solution.py:68
  71.3 2.0 %dynamic-slice_bitcast_fusion.1 = f32[2,8,32,256]{3,2,1,0:T(8,128)} fusion(f32[2,8,2,32,256]{4,3,2,1,0:T(8,128)} %bitcast.75, s32[]{:T(128)S(6)} %select_n.51), kind=kLoop, calls=%fused_computation.12 | loop fusion | bytes 1048580 | tf_op jit(solution)/shard_map/jit(dynamic_index_in_dim)/squeeze | solution.py:130
  73.3 5.7 %collective-permute-start.1 = (f32[2,8,32,256]{3,2,1,0:T(8,128)}, f32[2,8,32,256]{3,2,1,0:T(8,128)S(1)}, u32[]{:S(2)}, u32[]{:S(2)}) collective-permute-start(f32[2,8,32,256]{3,2,1,0:T(8,128)} %dynamic-slice_bitcast_fusion.1), channel_id=1, source_target_pairs={{0,32},{32,0},{1,33},{33,1},{2,34},{34,2},{3,35},{35,3},{4,36},{36... | collective-permute-start | bytes 1572872 | tf_op jit(solution)/shard_map/ppermute | solution.py:131
  79.0 0.1 bitcast_add_fusion
  79.1 0.1 constant_dynamic-slice_fusion.1
  79.2 0.2 copy.27
  79.4 2.7 %collective-permute-start.6 = (f32[2,2,2,32,256]{4,0,3,1,2:T(2,128)S(1)}, f32[2,2,2,32,256]{4,0,3,1,2:T(2,128)S(1)}, u32[]{:S(2)}, u32[]{:S(2)}) collective-permute-start(f32[2,2,2,32,256]{4,0,3,1,2:T(2,128)S(1)} %bitcast.83), channel_id=1, source_target_pairs={{0,64},{64,0},{128,192},{192,128},{256,320},{320,256},{384,448},{4... | collective-permute-start | bytes 786440 | tf_op jit(solution)/shard_map/ppermute | solution.py:92
  82.0 0.0 collective-permute-done.1
  82.1 0.1 bitcast_add_fusion.1
  82.2 0.1 constant_dynamic-slice_fusion.3
  82.2 0.2 copy.28
  82.4 2.6 %collective-permute-start.2 = (f32[2,2,2,32,256]{4,0,3,1,2:T(2,128)S(1)}, f32[2,2,2,32,256]{4,0,3,1,2:T(2,128)S(1)}, u32[]{:S(2)}, u32[]{:S(2)}) collective-permute-start(f32[2,2,2,32,256]{4,0,3,1,2:T(2,128)S(1)} %bitcast.84), channel_id=1, source_target_pairs={{0,64},{64,0},{128,192},{192,128},{256,320},{320,256},{384,448},{4... | collective-permute-start | bytes 786440 | tf_op jit(solution)/shard_map/ppermute | solution.py:92
  85.1 4.2 %collective-permute-done.6 = f32[2,2,2,32,256]{4,0,3,1,2:T(2,128)S(1)} collective-permute-done((f32[2,2,2,32,256]{4,0,3,1,2:T(2,128)S(1)}, f32[2,2,2,32,256]{4,0,3,1,2:T(2,128)S(1)}, u32[]{:S(2)}, u32[]{:S(2)}) %collective-permute-start.6) | collective-permute-done | bytes 262176 | tf_op jit(solution)/shard_map/ppermute | solution.py:92
  89.2 0.3 bitcast_add_fusion.2
  89.5 3.1 %collective-permute-start.7 = (f32[2,2,32,256]{3,0,2,1:T(2,128)S(1)}, f32[2,2,32,256]{3,0,2,1:T(2,128)S(1)}, u32[]{:S(2)}, u32[]{:S(2)}) collective-permute-start(f32[2,2,32,256]{3,0,2,1:T(2,128)S(1)} %dynamic-slice_bitcast_fusion.2), channel_id=1, source_target_pairs={{0,128},{64,192},{128,0},{192,64},{256,384},{320,448},{384,256},{4... | collective-permute-start | bytes 393224 | tf_op jit(solution)/shard_map/ppermute | solution.py:92
  92.6 2.2 %collective-permute-done.2 = f32[2,2,2,32,256]{4,0,3,1,2:T(2,128)S(1)} collective-permute-done((f32[2,2,2,32,256]{4,0,3,1,2:T(2,128)S(1)}, f32[2,2,2,32,256]{4,0,3,1,2:T(2,128)S(1)}, u32[]{:S(2)}, u32[]{:S(2)}) %collective-permute-start.2) | collective-permute-done | bytes 262176 | tf_op jit(solution)/shard_map/ppermute | solution.py:92
  94.8 0.3 bitcast_add_fusion.3
  95.1 3.1 %collective-permute-start.3 = (f32[2,2,32,256]{3,0,2,1:T(2,128)S(1)}, f32[2,2,32,256]{3,0,2,1:T(2,128)S(1)}, u32[]{:S(2)}, u32[]{:S(2)}) collective-permute-start(f32[2,2,32,256]{3,0,2,1:T(2,128)S(1)} %dynamic-slice_bitcast_fusion.3), channel_id=1, source_target_pairs={{0,128},{64,192},{128,0},{192,64},{256,384},{320,448},{384,256},{4... | collective-permute-start | bytes 393224 | tf_op jit(solution)/shard_map/ppermute | solution.py:92
  98.2 1.1 collective-permute-done.7
  99.3 0.1 bitcast_add_fusion.4
  99.4 7.1 %collective-permute-start.8 = (f32[2,32,256]{2,0,1:T(2,128)S(1)}, f32[2,32,256]{2,0,1:T(2,128)S(1)}, u32[]{:S(2)}, u32[]{:S(2)}) collective-permute-start(f32[2,32,256]{2,0,1:T(2,128)S(1)} %dynamic-slice_bitcast_fusion.4), channel_id=1, source_target_pairs={{0,256},{64,320},{128,384},{192,448},{256,0},{320,64},{384,128},{4... | collective-permute-start | bytes 196616 | tf_op jit(solution)/shard_map/ppermute | solution.py:92
  106.5 0.1 bitcast_add_fusion.5
  106.6 8.2 %collective-permute-start.4 = (f32[2,32,256]{2,0,1:T(2,128)S(1)}, f32[2,32,256]{2,0,1:T(2,128)S(1)}, u32[]{:S(2)}, u32[]{:S(2)}) collective-permute-start(f32[2,32,256]{2,0,1:T(2,128)S(1)} %dynamic-slice_bitcast_fusion.5), channel_id=1, source_target_pairs={{0,256},{64,320},{128,384},{192,448},{256,0},{320,64},{384,128},{4... | collective-permute-start | bytes 196616 | tf_op jit(solution)/shard_map/ppermute | solution.py:92
  114.8 0.0 collective-permute-done.8
  114.9 6.0 %collective-permute-done.4 = f32[2,32,256]{2,0,1:T(2,128)S(1)} collective-permute-done((f32[2,32,256]{2,0,1:T(2,128)S(1)}, f32[2,32,256]{2,0,1:T(2,128)S(1)}, u32[]{:S(2)}, u32[]{:S(2)}) %collective-permute-start.4) | collective-permute-done | bytes 65568 | tf_op jit(solution)/shard_map/ppermute | solution.py:92
  120.9 0.7 maximum_bitcast_fusion
  (24 shorter events, 0.4 us)
Async XLA Ops:
  0.0 21.9 %collective-permute-start = (bf16[2,16,2,512]{3,2,1,0:T(2,128)(2,1)}, bf16[2,16,2,512]{3,2,1,0:T(2,128)(2,1)S(1)}, u32[]{:S(2)}, u32[]{:S(2)}) collective-permute-start(bf16[2,16,2,512]{3,2,1,0:T(2,128)(2,1)} %param.5), channel_id=1, source_target_pairs={{0,16},{16,0},{1,17},{17,1},{2,18},{18,2},{3,19},{19,3},{4,20},{20... | collective-permute-start | bytes 196616 | tf_op jit(solution)/shard_map/ppermute | solution.py:98
  24.2 22.0 %all-to-all-start.1 = ((bf16[2,2,16,2,16,256]{5,4,3,1,0,2:T(8,128)(2,1)}), bf16[2,2,16,2,16,256]{5,4,3,1,0,2:T(8,128)(2,1)S(1)}, u32[]{:S(2)}, u32[]{:S(2)}) async-start(bf16[2,2,16,2,16,256]{5,4,3,1,0,2:T(8,128)(2,1)} %broadcast_in_dim.9), calls=%async_computation.1 | async-start | bytes 2097152 | tf_op jit(solution)/shard_map/all_to_all | solution.py:124
  47.4 18.2 %all-to-all-start = ((bf16[2,2,16,2,16,256]{5,4,3,1,0,2:T(8,128)(2,1)}), bf16[2,2,16,2,16,256]{5,4,3,1,0,2:T(8,128)(2,1)S(1)}, u32[]{:S(2)}, u32[]{:S(2)}) async-start(bf16[2,2,16,2,16,256]{5,4,3,1,0,2:T(8,128)(2,1)} %broadcast_in_dim.8), calls=%async_computation | async-start | bytes 2097152 | tf_op jit(solution)/shard_map/all_to_all | solution.py:124
  58.9 20.1 %collective-permute-start.5 = (f32[2,8,32,256]{3,2,1,0:T(8,128)}, f32[2,8,32,256]{3,2,1,0:T(8,128)S(1)}, u32[]{:S(2)}, u32[]{:S(2)}) collective-permute-start(f32[2,8,32,256]{3,2,1,0:T(8,128)} %dynamic-slice_bitcast_fusion), channel_id=1, source_target_pairs={{0,32},{32,0},{1,33},{33,1},{2,34},{34,2},{3,35},{35,3},{4,36},{36... | collective-permute-start | bytes 1572872 | tf_op jit(solution)/shard_map/ppermute | solution.py:131
  66.6 12.4 %copy-start.1 = (f32[2,512,256]{2,1,0:T(8,128)S(1)}, f32[2,512,256]{2,1,0:T(8,128)}, u32[]{:S(2)}) copy-start(f32[2,512,256]{2,1,0:T(8,128)} %shard_map.47) | copy-start | bytes 3145732
  71.3 10.7 %copy-start = (f32[2,512,256]{2,1,0:T(8,128)S(1)}, f32[2,512,256]{2,1,0:T(8,128)}, u32[]{:S(2)}) copy-start(f32[2,512,256]{2,1,0:T(8,128)} %shard_map.46) | copy-start | bytes 3145732
  73.3 8.8 %collective-permute-start.1 = (f32[2,8,32,256]{3,2,1,0:T(8,128)}, f32[2,8,32,256]{3,2,1,0:T(8,128)S(1)}, u32[]{:S(2)}, u32[]{:S(2)}) collective-permute-start(f32[2,8,32,256]{3,2,1,0:T(8,128)} %dynamic-slice_bitcast_fusion.1), channel_id=1, source_target_pairs={{0,32},{32,0},{1,33},{33,1},{2,34},{34,2},{3,35},{35,3},{4,36},{36... | collective-permute-start | bytes 1572872 | tf_op jit(solution)/shard_map/ppermute | solution.py:131
  79.4 9.8 %collective-permute-start.6 = (f32[2,2,2,32,256]{4,0,3,1,2:T(2,128)S(1)}, f32[2,2,2,32,256]{4,0,3,1,2:T(2,128)S(1)}, u32[]{:S(2)}, u32[]{:S(2)}) collective-permute-start(f32[2,2,2,32,256]{4,0,3,1,2:T(2,128)S(1)} %bitcast.83), channel_id=1, source_target_pairs={{0,64},{64,0},{128,192},{192,128},{256,320},{320,256},{384,448},{4... | collective-permute-start | bytes 786440 | tf_op jit(solution)/shard_map/ppermute | solution.py:92
  82.4 12.4 %collective-permute-start.2 = (f32[2,2,2,32,256]{4,0,3,1,2:T(2,128)S(1)}, f32[2,2,2,32,256]{4,0,3,1,2:T(2,128)S(1)}, u32[]{:S(2)}, u32[]{:S(2)}) collective-permute-start(f32[2,2,2,32,256]{4,0,3,1,2:T(2,128)S(1)} %bitcast.84), channel_id=1, source_target_pairs={{0,64},{64,0},{128,192},{192,128},{256,320},{320,256},{384,448},{4... | collective-permute-start | bytes 786440 | tf_op jit(solution)/shard_map/ppermute | solution.py:92
  89.5 9.8 %collective-permute-start.7 = (f32[2,2,32,256]{3,0,2,1:T(2,128)S(1)}, f32[2,2,32,256]{3,0,2,1:T(2,128)S(1)}, u32[]{:S(2)}, u32[]{:S(2)}) collective-permute-start(f32[2,2,32,256]{3,0,2,1:T(2,128)S(1)} %dynamic-slice_bitcast_fusion.2), channel_id=1, source_target_pairs={{0,128},{64,192},{128,0},{192,64},{256,384},{320,448},{384,256},{4... | collective-permute-start | bytes 393224 | tf_op jit(solution)/shard_map/ppermute | solution.py:92
  95.1 11.4 %collective-permute-start.3 = (f32[2,2,32,256]{3,0,2,1:T(2,128)S(1)}, f32[2,2,32,256]{3,0,2,1:T(2,128)S(1)}, u32[]{:S(2)}, u32[]{:S(2)}) collective-permute-start(f32[2,2,32,256]{3,0,2,1:T(2,128)S(1)} %dynamic-slice_bitcast_fusion.3), channel_id=1, source_target_pairs={{0,128},{64,192},{128,0},{192,64},{256,384},{320,448},{384,256},{4... | collective-permute-start | bytes 393224 | tf_op jit(solution)/shard_map/ppermute | solution.py:92
  99.4 15.4 %collective-permute-start.8 = (f32[2,32,256]{2,0,1:T(2,128)S(1)}, f32[2,32,256]{2,0,1:T(2,128)S(1)}, u32[]{:S(2)}, u32[]{:S(2)}) collective-permute-start(f32[2,32,256]{2,0,1:T(2,128)S(1)} %dynamic-slice_bitcast_fusion.4), channel_id=1, source_target_pairs={{0,256},{64,320},{128,384},{192,448},{256,0},{320,64},{384,128},{4... | collective-permute-start | bytes 196616 | tf_op jit(solution)/shard_map/ppermute | solution.py:92
  106.6 14.3 %collective-permute-start.4 = (f32[2,32,256]{2,0,1:T(2,128)S(1)}, f32[2,32,256]{2,0,1:T(2,128)S(1)}, u32[]{:S(2)}, u32[]{:S(2)}) collective-permute-start(f32[2,32,256]{2,0,1:T(2,128)S(1)} %dynamic-slice_bitcast_fusion.5), channel_id=1, source_target_pairs={{0,256},{64,320},{128,384},{192,448},{256,0},{320,64},{384,128},{4... | collective-permute-start | bytes 196616 | tf_op jit(solution)/shard_map/ppermute | solution.py:92
